TPU v7x, 32 devices: a whole 2x2x4 slice. The times are simulated.
32 devices in a mesh: seg: 4 (over y, x), fibre: 8 (over z, core).
Axes of the slice: x: 2, y: 2, z: 4, core: 2. Of those that a mesh axis runs over, the one named last changes fastest.
Arguments:
- record: bfloat16 [4, 128, 27648], P('seg', 'fibre'), may hold values from -6 to 6
- offsets: int32 [4, 16], P('seg'), may hold values from 0 to 24576
- live_mask: int32 [128], P('fibre'), may hold values 0 or 1
Outputs:
- stacked: float32 [256, 128, 128], P('seg', 'fibre')
All inputs are finite; a program needn't handle non-finite values. No bound on the sum of `live_mask` on one device may be relied on, other than what follows from the above.
Results may differ from a plain program's by a relative error of at most 0.0036.
Values may be sent and summed in bfloat16 or wider, within the bound.
No kernel may reach another device: no remote copies, remote signals or barrier semaphores. Data moves between devices by JAX's collectives and lax.ppermute only.
A program may use at most 64 MiB of HBM per device.

v0:
```python
import math

import jax
import jax.numpy as jnp
from jax import lax
from jax.sharding import PartitionSpec as P

NF = 64
NT = 3072
BIN0 = 32
BAND = 256


def passed_along(value, axis, steps):
    count = lax.axis_size(axis)
    first, last = (max(0, -steps), min(count, count - steps))
    return lax.ppermute(value, axis, [(source, source + steps) for source in range(first, last)])


def spectral_table():
    sample_idx = jnp.arange(NT, dtype=jnp.int32)
    bin_idx = BIN0 + jnp.arange(NF, dtype=jnp.int32)
    phase_int = sample_idx[:, None] * bin_idx[None, :] % NT
    angle_rad = 2.0 * math.pi / NT * phase_int.astype(jnp.float32)
    return jnp.concatenate([jnp.cos(angle_rad), -jnp.sin(angle_rad)], axis=1).astype(jnp.bfloat16)


def whiten(record_rows, starts, live_mask):
    windows = jax.vmap(
        lambda first_sample: lax.dynamic_slice_in_dim(record_rows, first_sample, NT, axis=1)
    )(starts)
    spectra = jnp.dot(windows, spectral_table(), preferred_element_type=jnp.float32)
    real_part = spectra[..., :NF]
    imag_part = spectra[..., NF:]
    power_bins = real_part * real_part + imag_part * imag_part
    bin_index = jnp.arange(NF, dtype=jnp.int32)
    nearby = (jnp.abs(bin_index[:, None] - bin_index[None, :]) <= 4).astype(jnp.float32)
    smooth = jnp.dot(power_bins, nearby, precision=lax.Precision.HIGHEST) / jnp.sum(nearby, axis=0)
    water_level = jnp.mean(power_bins, axis=-1, keepdims=True)
    gain_of = live_mask.astype(jnp.float32)[None, :, None] / jnp.sqrt(
        smooth + 0.1 * water_level + 1e-06
    )
    return jnp.concatenate([real_part * gain_of, imag_part * gain_of], axis=-1).astype(jnp.bfloat16)


def band_terms(own_part, slab, count):
    channels = own_part.shape[1]
    own_float = own_part.astype(jnp.float32)
    own_re = own_float[..., :NF]
    own_im = own_float[..., NF:]
    swapped = jnp.concatenate([own_im, -own_re], axis=-1)

    def shifted_at(offset_idx):
        return lax.dynamic_slice_in_dim(slab, offset_idx + 1, channels, 1)

    partners = jax.vmap(shifted_at)(jnp.arange(count, dtype=jnp.int32)).astype(jnp.float32)
    direct = jnp.sum(own_float[None] * partners, axis=1)
    crossed = jnp.sum(swapped[None] * partners, axis=1)
    real_sum = direct[..., :NF] + direct[..., NF:]
    imag_sum = crossed[..., :NF] + crossed[..., NF:]
    return jnp.concatenate([real_sum, imag_sum], axis=-1)


def shards(record, offsets, live_mask):
    own_block = whiten(record[0], offsets[0], live_mask)
    windows_count = own_block.shape[0]
    channels = own_block.shape[1]
    width = own_block.shape[2]
    hops = BAND // channels

    def one_hop(step_idx, state_pair):
        block, buffer = state_pair
        block = passed_along(block, "fibre", -1)
        buffer = lax.dynamic_update_slice_in_dim(buffer, block, step_idx * channels, 1)
        return (block, buffer)

    empty_buffer = jnp.zeros((windows_count, hops * channels, width), jnp.bfloat16)
    halo_part = lax.fori_loop(0, hops, one_hop, (own_block, empty_buffer))[1]
    extended = jnp.concatenate([own_block, halo_part], axis=1)
    seg_count = lax.axis_size("seg")
    per_owner = BAND // seg_count
    norm_factor = 1.0 / math.sqrt(seg_count * windows_count)
    summed = lax.psum_scatter(
        band_terms(own_block, extended, per_owner * lax.axis_size("seg")),
        "seg",
        scatter_dimension=0,
        tiled=True,
    )
    return summed * norm_factor


def solution(mesh):
    placed = (P("seg", "fibre", None), P("seg", None), P("fibre"))
    return jax.shard_map(
        shards, mesh=mesh, in_specs=placed, out_specs=P("seg", "fibre", None), check_vma=False
    )
```

profile of v0, /device:TPU:0, one launch (start us, length us, event | category | flops | bytes accessed | tf_op | source)
XLA Modules:
  0.0 224.7 jit_solution(14129159320196185386)
XLA Ops:
  7.9 3.6 %cosine_convert_fusion = (bf16[3072,64]{0,1:T(8,128)(2,1)S(1)}, bf16[3072,64]{0,1:T(8,128)(2,1)S(1)}) fusion(s32[64]{0:T(128)S(1)} %iota_add_fusion.2), kind=kLoop, calls=%fused_computation.25 | loop fusion | flops 2359296 | bytes 786688 | tf_op jit(solution)/shard_map/convert.2
  11.5 38.0 %while.17 = (s32[]{:T(128)}, bf16[16,27648]{1,0:T(8,128)(2,1)}, s32[16,2]{0,1:T(2,128)S(1)}, bf16[16,16,3072]{2,1,0:T(8,128)(2,1)S(1)}, s32[]{:T(128)}) while((s32[]{:T(128)}, bf16[16,27648]{1,0:T(8,128)(2,1)}, s32[16,2]{0,1:T(2,128)S(1)}, bf16[16,16,3072]{2,1,0:T(8,128)(2,1)S(1)}, s32[]{:T(128)}) %tuple.52), condition=%wide.while_cond, body=%wide.while_body.sunk | while | flops 2 | bytes 196713 | solution.py:30
  12.2 1.7 bitcast_dynamic-update-slice_fusion.2
  14.6 1.7 bitcast_dynamic-update-slice_fusion.2
  16.9 1.7 bitcast_dynamic-update-slice_fusion.2
  19.3 1.7 bitcast_dynamic-update-slice_fusion.2
  21.7 1.7 bitcast_dynamic-update-slice_fusion.2
  24.0 1.7 bitcast_dynamic-update-slice_fusion.2
  26.4 1.7 bitcast_dynamic-update-slice_fusion.2
  28.8 1.7 bitcast_dynamic-update-slice_fusion.2
  51.1 88.6 %while.16 = (s32[]{:T(128)}, bf16[16,16,128]{2,1,0:T(8,128)(2,1)S(1)}, bf16[16,256,128]{2,0,1:T(8,128)(2,1)S(1)}, s32[]{:T(128)}, s32[]{:T(128)}, /*index=5*/s32[]{:T(128)}, s32[]{:T(128)}) while((s32[]{:T(128)}, bf16[16,16,128]{2,1,0:T(8,128)(2,1)S(1)}, bf16[16,256,128]{2,0,1:T(8,128)(2,1)S(1)}, s32[]{:T(128)}, s32[]{:T(128)}, ...), condition=%wide.region_3.4_spmd, body=%wide.region_2.3_spmd.sunk | while | flops 6 | bytes 524455 | solution.py:78
  52.4 1.8 collective-permute-done
  55.6 5.2 %collective-permute-done = bf16[16,16,128]{2,1,0:T(8,128)(2,1)S(1)} collective-permute-done((bf16[16,16,128]{2,1,0:T(8,128)(2,1)S(1)}, bf16[16,16,128]{2,1,0:T(8,128)(2,1)S(1)}, u32[]{:S(2)}, u32[]{:S(2)}) %collective-permute-start) | collective-permute-done | bytes 65568 | tf_op jit(solution)/shard_map/while/body/eval_jaxpr/ppermute | solution.py:17
  62.2 4.3 %collective-permute-done = bf16[16,16,128]{2,1,0:T(8,128)(2,1)S(1)} collective-permute-done((bf16[16,16,128]{2,1,0:T(8,128)(2,1)S(1)}, bf16[16,16,128]{2,1,0:T(8,128)(2,1)S(1)}, u32[]{:S(2)}, u32[]{:S(2)}) %collective-permute-start) | collective-permute-done | bytes 65568 | tf_op jit(solution)/shard_map/while/body/eval_jaxpr/ppermute | solution.py:17
  67.8 4.3 %collective-permute-done = bf16[16,16,128]{2,1,0:T(8,128)(2,1)S(1)} collective-permute-done((bf16[16,16,128]{2,1,0:T(8,128)(2,1)S(1)}, bf16[16,16,128]{2,1,0:T(8,128)(2,1)S(1)}, u32[]{:S(2)}, u32[]{:S(2)}) %collective-permute-start) | collective-permute-done | bytes 65568 | tf_op jit(solution)/shard_map/while/body/eval_jaxpr/ppermute | solution.py:17
  73.4 4.3 %collective-permute-done = bf16[16,16,128]{2,1,0:T(8,128)(2,1)S(1)} collective-permute-done((bf16[16,16,128]{2,1,0:T(8,128)(2,1)S(1)}, bf16[16,16,128]{2,1,0:T(8,128)(2,1)S(1)}, u32[]{:S(2)}, u32[]{:S(2)}) %collective-permute-start) | collective-permute-done | bytes 65568 | tf_op jit(solution)/shard_map/while/body/eval_jaxpr/ppermute | solution.py:17
  79.1 4.3 %collective-permute-done = bf16[16,16,128]{2,1,0:T(8,128)(2,1)S(1)} collective-permute-done((bf16[16,16,128]{2,1,0:T(8,128)(2,1)S(1)}, bf16[16,16,128]{2,1,0:T(8,128)(2,1)S(1)}, u32[]{:S(2)}, u32[]{:S(2)}) %collective-permute-start) | collective-permute-done | bytes 65568 | tf_op jit(solution)/shard_map/while/body/eval_jaxpr/ppermute | solution.py:17
  84.7 4.3 %collective-permute-done = bf16[16,16,128]{2,1,0:T(8,128)(2,1)S(1)} collective-permute-done((bf16[16,16,128]{2,1,0:T(8,128)(2,1)S(1)}, bf16[16,16,128]{2,1,0:T(8,128)(2,1)S(1)}, u32[]{:S(2)}, u32[]{:S(2)}) %collective-permute-start) | collective-permute-done | bytes 65568 | tf_op jit(solution)/shard_map/while/body/eval_jaxpr/ppermute | solution.py:17
  90.3 4.3 %collective-permute-done = bf16[16,16,128]{2,1,0:T(8,128)(2,1)S(1)} collective-permute-done((bf16[16,16,128]{2,1,0:T(8,128)(2,1)S(1)}, bf16[16,16,128]{2,1,0:T(8,128)(2,1)S(1)}, u32[]{:S(2)}, u32[]{:S(2)}) %collective-permute-start) | collective-permute-done | bytes 65568 | tf_op jit(solution)/shard_map/while/body/eval_jaxpr/ppermute | solution.py:17
  96.0 4.3 %collective-permute-done = bf16[16,16,128]{2,1,0:T(8,128)(2,1)S(1)} collective-permute-done((bf16[16,16,128]{2,1,0:T(8,128)(2,1)S(1)}, bf16[16,16,128]{2,1,0:T(8,128)(2,1)S(1)}, u32[]{:S(2)}, u32[]{:S(2)}) %collective-permute-start) | collective-permute-done | bytes 65568 | tf_op jit(solution)/shard_map/while/body/eval_jaxpr/ppermute | solution.py:17
  101.6 4.3 %collective-permute-done = bf16[16,16,128]{2,1,0:T(8,128)(2,1)S(1)} collective-permute-done((bf16[16,16,128]{2,1,0:T(8,128)(2,1)S(1)}, bf16[16,16,128]{2,1,0:T(8,128)(2,1)S(1)}, u32[]{:S(2)}, u32[]{:S(2)}) %collective-permute-start) | collective-permute-done | bytes 65568 | tf_op jit(solution)/shard_map/while/body/eval_jaxpr/ppermute | solution.py:17
  107.2 4.3 %collective-permute-done = bf16[16,16,128]{2,1,0:T(8,128)(2,1)S(1)} collective-permute-done((bf16[16,16,128]{2,1,0:T(8,128)(2,1)S(1)}, bf16[16,16,128]{2,1,0:T(8,128)(2,1)S(1)}, u32[]{:S(2)}, u32[]{:S(2)}) %collective-permute-start) | collective-permute-done | bytes 65568 | tf_op jit(solution)/shard_map/while/body/eval_jaxpr/ppermute | solution.py:17
  112.9 4.3 %collective-permute-done = bf16[16,16,128]{2,1,0:T(8,128)(2,1)S(1)} collective-permute-done((bf16[16,16,128]{2,1,0:T(8,128)(2,1)S(1)}, bf16[16,16,128]{2,1,0:T(8,128)(2,1)S(1)}, u32[]{:S(2)}, u32[]{:S(2)}) %collective-permute-start) | collective-permute-done | bytes 65568 | tf_op jit(solution)/shard_map/while/body/eval_jaxpr/ppermute | solution.py:17
  118.5 4.3 %collective-permute-done = bf16[16,16,128]{2,1,0:T(8,128)(2,1)S(1)} collective-permute-done((bf16[16,16,128]{2,1,0:T(8,128)(2,1)S(1)}, bf16[16,16,128]{2,1,0:T(8,128)(2,1)S(1)}, u32[]{:S(2)}, u32[]{:S(2)}) %collective-permute-start) | collective-permute-done | bytes 65568 | tf_op jit(solution)/shard_map/while/body/eval_jaxpr/ppermute | solution.py:17
  124.1 4.3 %collective-permute-done = bf16[16,16,128]{2,1,0:T(8,128)(2,1)S(1)} collective-permute-done((bf16[16,16,128]{2,1,0:T(8,128)(2,1)S(1)}, bf16[16,16,128]{2,1,0:T(8,128)(2,1)S(1)}, u32[]{:S(2)}, u32[]{:S(2)}) %collective-permute-start) | collective-permute-done | bytes 65568 | tf_op jit(solution)/shard_map/while/body/eval_jaxpr/ppermute | solution.py:17
  129.8 4.3 %collective-permute-done = bf16[16,16,128]{2,1,0:T(8,128)(2,1)S(1)} collective-permute-done((bf16[16,16,128]{2,1,0:T(8,128)(2,1)S(1)}, bf16[16,16,128]{2,1,0:T(8,128)(2,1)S(1)}, u32[]{:S(2)}, u32[]{:S(2)}) %collective-permute-start) | collective-permute-done | bytes 65568 | tf_op jit(solution)/shard_map/while/body/eval_jaxpr/ppermute | solution.py:17
  135.4 4.3 %collective-permute-done = bf16[16,16,128]{2,1,0:T(8,128)(2,1)S(1)} collective-permute-done((bf16[16,16,128]{2,1,0:T(8,128)(2,1)S(1)}, bf16[16,16,128]{2,1,0:T(8,128)(2,1)S(1)}, u32[]{:S(2)}, u32[]{:S(2)}) %collective-permute-start) | collective-permute-done | bytes 65568 | tf_op jit(solution)/shard_map/while/body/eval_jaxpr/ppermute | solution.py:17
  139.8 11.4 %gather_fusion = bf16[256,16,16,128]{3,1,2,0:T(8,128)(2,1)} fusion(bf16[16,272,128]{2,0,1:T(8,128)(2,1)S(1)} %pad_maximum_fusion.1, s32[256]{0:T(256)S(1)} %bitcast.20), kind=kCustom, calls=%fused_computation | custom fusion | bytes 33557504 | tf_op jit(solution)/shard_map/vmap()/gather | solution.py:54
  151.2 23.5 %fusion = (f32[256,16,128]{2,1,0:T(8,128)S(1)}, f32[256,16,128]{2,1,0:T(8,128)S(1)}) fusion(bf16[256,16,16,128]{3,1,2,0:T(8,128)(2,1)} %gather_fusion, f32[16,16,128]{2,0,1:T(8,128)S(1)} %copy.13, f32[16,16,128]{2,0,1:T(8,128)S(1)} %copy.16), kind=kLoop, calls=%fused_computation.6 | loop fusion | flops 40894464 | bytes 21233664 | tf_op jit(solution)/shard_map/reduce_sum | solution.py:57
  175.9 2.0 pad_maximum_fusion
  177.8 38.2 %reduce-scatter.2.cloned.1.call-done = f32[64,16,128]{2,1,0:T(8,128)} async-done(((f32[256,16,128]{2,1,0:T(8,128)}), f32[64,16,128]{2,1,0:T(8,128)}) %reduce-scatter.2.cloned.1.call-update) | async-done | bytes 524304 | tf_op jit(solution)/shard_map/reduce_scatter | solution.py:83
  216.0 1.9 broadcast_multiply_fusion
  (111 shorter events, 49.5 us)
Async XLA Ops:
  6.5 209.5 %reduce-scatter.2.cloned.1.call-start = ((), (), s32[]{:S(2)}) async-start(), calls=%async_computation.1 | async-start | bytes 2621440 | tf_op jit(solution)/shard_map/reduce_scatter | solution.py:83
  51.1 3.1 %collective-permute-start = (bf16[16,16,128]{2,1,0:T(8,128)(2,1)S(1)}, bf16[16,16,128]{2,1,0:T(8,128)(2,1)S(1)}, u32[]{:S(2)}, u32[]{:S(2)}) collective-permute-start(bf16[16,16,128]{2,1,0:T(8,128)(2,1)S(1)} %get-tuple-element.169), channel_id=1, source_target_pairs={{1,0},{2,1},{3,2},{4,3},{5,4},{6,5},{7,6},{9,8},{10,9},{11,10},{12... | collective-permute-start | bytes 196616 | tf_op jit(solution)/shard_map/while/body/eval_jaxpr/ppermute | solution.py:17
  54.3 6.5 %collective-permute-start = (bf16[16,16,128]{2,1,0:T(8,128)(2,1)S(1)}, bf16[16,16,128]{2,1,0:T(8,128)(2,1)S(1)}, u32[]{:S(2)}, u32[]{:S(2)}) collective-permute-start(bf16[16,16,128]{2,1,0:T(8,128)(2,1)S(1)} %get-tuple-element.169), channel_id=1, source_target_pairs={{1,0},{2,1},{3,2},{4,3},{5,4},{6,5},{7,6},{9,8},{10,9},{11,10},{12... | collective-permute-start | bytes 196616 | tf_op jit(solution)/shard_map/while/body/eval_jaxpr/ppermute | solution.py:17
  60.9 5.6 %collective-permute-start = (bf16[16,16,128]{2,1,0:T(8,128)(2,1)S(1)}, bf16[16,16,128]{2,1,0:T(8,128)(2,1)S(1)}, u32[]{:S(2)}, u32[]{:S(2)}) collective-permute-start(bf16[16,16,128]{2,1,0:T(8,128)(2,1)S(1)} %get-tuple-element.169), channel_id=1, source_target_pairs={{1,0},{2,1},{3,2},{4,3},{5,4},{6,5},{7,6},{9,8},{10,9},{11,10},{12... | collective-permute-start | bytes 196616 | tf_op jit(solution)/shard_map/while/body/eval_jaxpr/ppermute | solution.py:17
  66.5 5.6 %collective-permute-start = (bf16[16,16,128]{2,1,0:T(8,128)(2,1)S(1)}, bf16[16,16,128]{2,1,0:T(8,128)(2,1)S(1)}, u32[]{:S(2)}, u32[]{:S(2)}) collective-permute-start(bf16[16,16,128]{2,1,0:T(8,128)(2,1)S(1)} %get-tuple-element.169), channel_id=1, source_target_pairs={{1,0},{2,1},{3,2},{4,3},{5,4},{6,5},{7,6},{9,8},{10,9},{11,10},{12... | collective-permute-start | bytes 196616 | tf_op jit(solution)/shard_map/while/body/eval_jaxpr/ppermute | solution.py:17
  72.1 5.6 %collective-permute-start = (bf16[16,16,128]{2,1,0:T(8,128)(2,1)S(1)}, bf16[16,16,128]{2,1,0:T(8,128)(2,1)S(1)}, u32[]{:S(2)}, u32[]{:S(2)}) collective-permute-start(bf16[16,16,128]{2,1,0:T(8,128)(2,1)S(1)} %get-tuple-element.169), channel_id=1, source_target_pairs={{1,0},{2,1},{3,2},{4,3},{5,4},{6,5},{7,6},{9,8},{10,9},{11,10},{12... | collective-permute-start | bytes 196616 | tf_op jit(solution)/shard_map/while/body/eval_jaxpr/ppermute | solution.py:17
  77.8 5.6 %collective-permute-start = (bf16[16,16,128]{2,1,0:T(8,128)(2,1)S(1)}, bf16[16,16,128]{2,1,0:T(8,128)(2,1)S(1)}, u32[]{:S(2)}, u32[]{:S(2)}) collective-permute-start(bf16[16,16,128]{2,1,0:T(8,128)(2,1)S(1)} %get-tuple-element.169), channel_id=1, source_target_pairs={{1,0},{2,1},{3,2},{4,3},{5,4},{6,5},{7,6},{9,8},{10,9},{11,10},{12... | collective-permute-start | bytes 196616 | tf_op jit(solution)/shard_map/while/body/eval_jaxpr/ppermute | solution.py:17
  83.4 5.6 %collective-permute-start = (bf16[16,16,128]{2,1,0:T(8,128)(2,1)S(1)}, bf16[16,16,128]{2,1,0:T(8,128)(2,1)S(1)}, u32[]{:S(2)}, u32[]{:S(2)}) collective-permute-start(bf16[16,16,128]{2,1,0:T(8,128)(2,1)S(1)} %get-tuple-element.169), channel_id=1, source_target_pairs={{1,0},{2,1},{3,2},{4,3},{5,4},{6,5},{7,6},{9,8},{10,9},{11,10},{12... | collective-permute-start | bytes 196616 | tf_op jit(solution)/shard_map/while/body/eval_jaxpr/ppermute | solution.py:17
  89.0 5.6 %collective-permute-start = (bf16[16,16,128]{2,1,0:T(8,128)(2,1)S(1)}, bf16[16,16,128]{2,1,0:T(8,128)(2,1)S(1)}, u32[]{:S(2)}, u32[]{:S(2)}) collective-permute-start(bf16[16,16,128]{2,1,0:T(8,128)(2,1)S(1)} %get-tuple-element.169), channel_id=1, source_target_pairs={{1,0},{2,1},{3,2},{4,3},{5,4},{6,5},{7,6},{9,8},{10,9},{11,10},{12... | collective-permute-start | bytes 196616 | tf_op jit(solution)/shard_map/while/body/eval_jaxpr/ppermute | solution.py:17
  94.7 5.6 %collective-permute-start = (bf16[16,16,128]{2,1,0:T(8,128)(2,1)S(1)}, bf16[16,16,128]{2,1,0:T(8,128)(2,1)S(1)}, u32[]{:S(2)}, u32[]{:S(2)}) collective-permute-start(bf16[16,16,128]{2,1,0:T(8,128)(2,1)S(1)} %get-tuple-element.169), channel_id=1, source_target_pairs={{1,0},{2,1},{3,2},{4,3},{5,4},{6,5},{7,6},{9,8},{10,9},{11,10},{12... | collective-permute-start | bytes 196616 | tf_op jit(solution)/shard_map/while/body/eval_jaxpr/ppermute | solution.py:17
  100.3 5.6 %collective-permute-start = (bf16[16,16,128]{2,1,0:T(8,128)(2,1)S(1)}, bf16[16,16,128]{2,1,0:T(8,128)(2,1)S(1)}, u32[]{:S(2)}, u32[]{:S(2)}) collective-permute-start(bf16[16,16,128]{2,1,0:T(8,128)(2,1)S(1)} %get-tuple-element.169), channel_id=1, source_target_pairs={{1,0},{2,1},{3,2},{4,3},{5,4},{6,5},{7,6},{9,8},{10,9},{11,10},{12... | collective-permute-start | bytes 196616 | tf_op jit(solution)/shard_map/while/body/eval_jaxpr/ppermute | solution.py:17
  105.9 5.6 %collective-permute-start = (bf16[16,16,128]{2,1,0:T(8,128)(2,1)S(1)}, bf16[16,16,128]{2,1,0:T(8,128)(2,1)S(1)}, u32[]{:S(2)}, u32[]{:S(2)}) collective-permute-start(bf16[16,16,128]{2,1,0:T(8,128)(2,1)S(1)} %get-tuple-element.169), channel_id=1, source_target_pairs={{1,0},{2,1},{3,2},{4,3},{5,4},{6,5},{7,6},{9,8},{10,9},{11,10},{12... | collective-permute-start | bytes 196616 | tf_op jit(solution)/shard_map/while/body/eval_jaxpr/ppermute | solution.py:17
  111.6 5.6 %collective-permute-start = (bf16[16,16,128]{2,1,0:T(8,128)(2,1)S(1)}, bf16[16,16,128]{2,1,0:T(8,128)(2,1)S(1)}, u32[]{:S(2)}, u32[]{:S(2)}) collective-permute-start(bf16[16,16,128]{2,1,0:T(8,128)(2,1)S(1)} %get-tuple-element.169), channel_id=1, source_target_pairs={{1,0},{2,1},{3,2},{4,3},{5,4},{6,5},{7,6},{9,8},{10,9},{11,10},{12... | collective-permute-start | bytes 196616 | tf_op jit(solution)/shard_map/while/body/eval_jaxpr/ppermute | solution.py:17
  117.2 5.6 %collective-permute-start = (bf16[16,16,128]{2,1,0:T(8,128)(2,1)S(1)}, bf16[16,16,128]{2,1,0:T(8,128)(2,1)S(1)}, u32[]{:S(2)}, u32[]{:S(2)}) collective-permute-start(bf16[16,16,128]{2,1,0:T(8,128)(2,1)S(1)} %get-tuple-element.169), channel_id=1, source_target_pairs={{1,0},{2,1},{3,2},{4,3},{5,4},{6,5},{7,6},{9,8},{10,9},{11,10},{12... | collective-permute-start | bytes 196616 | tf_op jit(solution)/shard_map/while/body/eval_jaxpr/ppermute | solution.py:17
  122.8 5.6 %collective-permute-start = (bf16[16,16,128]{2,1,0:T(8,128)(2,1)S(1)}, bf16[16,16,128]{2,1,0:T(8,128)(2,1)S(1)}, u32[]{:S(2)}, u32[]{:S(2)}) collective-permute-start(bf16[16,16,128]{2,1,0:T(8,128)(2,1)S(1)} %get-tuple-element.169), channel_id=1, source_target_pairs={{1,0},{2,1},{3,2},{4,3},{5,4},{6,5},{7,6},{9,8},{10,9},{11,10},{12... | collective-permute-start | bytes 196616 | tf_op jit(solution)/shard_map/while/body/eval_jaxpr/ppermute | solution.py:17
  128.5 5.6 %collective-permute-start = (bf16[16,16,128]{2,1,0:T(8,128)(2,1)S(1)}, bf16[16,16,128]{2,1,0:T(8,128)(2,1)S(1)}, u32[]{:S(2)}, u32[]{:S(2)}) collective-permute-start(bf16[16,16,128]{2,1,0:T(8,128)(2,1)S(1)} %get-tuple-element.169), channel_id=1, source_target_pairs={{1,0},{2,1},{3,2},{4,3},{5,4},{6,5},{7,6},{9,8},{10,9},{11,10},{12... | collective-permute-start | bytes 196616 | tf_op jit(solution)/shard_map/while/body/eval_jaxpr/ppermute | solution.py:17
  134.1 5.6 %collective-permute-start = (bf16[16,16,128]{2,1,0:T(8,128)(2,1)S(1)}, bf16[16,16,128]{2,1,0:T(8,128)(2,1)S(1)}, u32[]{:S(2)}, u32[]{:S(2)}) collective-permute-start(bf16[16,16,128]{2,1,0:T(8,128)(2,1)S(1)} %get-tuple-element.169), channel_id=1, source_target_pairs={{1,0},{2,1},{3,2},{4,3},{5,4},{6,5},{7,6},{9,8},{10,9},{11,10},{12... | collective-permute-start | bytes 196616 | tf_op jit(solution)/shard_map/while/body/eval_jaxpr/ppermute | solution.py:17
Sparse Core Ops, SparseCore 0:
  178.0 38.0 reduce-scatter.1
where the time goes:
time: 226 us; the launch traced here: 225 us
  waiting for transfers between devices  105 us (46%)
  local copies, waits for them, and re-layouts  49.8 us (22%)
  other arithmetic  33.9 us (15%)
  starting transfers between devices  20.7 us (9%)
  between operations  13.5 us (6%)
    ppermute x16, waiting for transfers between devices, passed_along(): lax.ppermute(value, axis, [(source, source + steps) for source in range(f...  66.9 us
    reduce_scatter x1, waiting for transfers between devices, shards(): lax.psum_scatter(band_terms(own_block, extended, per_owner * lax.axis_siz...  38.2 us
    gather x48, local copies, waits for them, and re-layouts  37.6 us
    reduce_sum x1, other arithmetic, band_terms(): direct = jnp.sum(own_float[None] * partners, axis=1)  23.5 us
    ppermute x16, starting transfers between devices, passed_along(): lax.ppermute(value, axis, [(source, source + steps) for source in range(f...  20.7 us
    gather x1, local copies, waits for them, and re-layouts, shifted_at(): return lax.dynamic_slice_in_dim(slab, offset_idx + 1, channels, 1)  11.4 us
  transfers between devices with their start and end apart: 17, of which 17 were waited for; matrix products, arithmetic and copies ran while one was open for 0% of the time, Pallas kernels for 0%

commit v1 on v0

v1 whole, which is shorter than its diff:
```python
import math

import jax
import jax.numpy as jnp
import ml_dtypes
import numpy as np
from jax import lax
from jax.sharding import PartitionSpec as P

NF = 64
NT = 3072
BIN0 = 32
BAND = 256
LANES = 128


def spectral_table():
    sample_idx = np.arange(NT, dtype=np.int64)
    bin_idx = BIN0 + np.arange(NF, dtype=np.int64)
    phase_int = sample_idx[:, None] * bin_idx[None, :] % NT
    angle_rad = np.float32(2.0 * math.pi / NT) * phase_int.astype(np.float32)
    angle = angle_rad.astype(np.float64)
    table = np.concatenate([np.cos(angle), -np.sin(angle)], axis=1)
    return table.astype(ml_dtypes.bfloat16)


def window_spectra(record_rows, starts):
    channels, length = record_rows.shape
    blocks = length // LANES
    per_window = NT // LANES
    by_block = record_rows.reshape(channels, blocks, LANES).transpose(1, 0, 2)
    by_block = jnp.concatenate([by_block, jnp.zeros((1, channels, LANES), by_block.dtype)], axis=0)
    first_block = starts // LANES
    shift = starts % LANES
    chunks = jax.vmap(lambda q: lax.dynamic_slice_in_dim(by_block, q, per_window + 1, axis=0))(first_block)
    pairs = jnp.concatenate([chunks[:, :per_window], chunks[:, 1:]], axis=-1)
    src = lax.broadcasted_iota(jnp.int32, (2 * LANES, LANES), 0)
    dst = lax.broadcasted_iota(jnp.int32, (2 * LANES, LANES), 1)
    pick = (src[None] == dst[None] + shift[:, None, None]).astype(jnp.bfloat16)
    windows = jnp.einsum(
        "wbcm,wmi->wcbi", pairs, pick, preferred_element_type=jnp.float32
    ).astype(jnp.bfloat16)
    table = jnp.asarray(spectral_table()).reshape(per_window, LANES, 2 * NF)
    return jnp.einsum("wcbi,bif->wcf", windows, table, preferred_element_type=jnp.float32)


def whiten(record_rows, starts, live_mask):
    spectra = window_spectra(record_rows, starts)
    real_part = spectra[..., :NF]
    imag_part = spectra[..., NF:]
    power_bins = real_part * real_part + imag_part * imag_part
    bin_index = jnp.arange(NF, dtype=jnp.int32)
    nearby = (jnp.abs(bin_index[:, None] - bin_index[None, :]) <= 4).astype(jnp.float32)
    smooth = jnp.dot(power_bins, nearby, precision=lax.Precision.HIGHEST) / jnp.sum(nearby, axis=0)
    water_level = jnp.mean(power_bins, axis=-1, keepdims=True)
    gain_of = live_mask.astype(jnp.float32)[None, :, None] / jnp.sqrt(
        smooth + 0.1 * water_level + 1e-06
    )
    return jnp.concatenate([real_part * gain_of, imag_part * gain_of], axis=-1).astype(jnp.bfloat16)


def shards(record, offsets, live_mask):
    seg_count = lax.axis_size("seg")
    fibre_count = lax.axis_size("fibre")
    own_block = whiten(record[0], offsets[0], live_mask)
    windows_count, block, _ = own_block.shape
    channels = block * fibre_count
    per_owner = BAND // seg_count
    bins_each = NF // seg_count
    live_offsets = min(BAND, channels - 1)
    live_owners = -(-live_offsets // per_owner)
    kept = live_owners * per_owner
    span = block + kept
    hops = min(-(-span // block) - 1, fibre_count - 1)
    me = lax.axis_index("seg")

    split = own_block.reshape(windows_count, block, 2, seg_count, bins_each).transpose(3, 0, 1, 2, 4)
    gathered = [lax.dynamic_index_in_dim(split, me, 0, keepdims=False)]
    for step in range(1, seg_count):
        sent = lax.dynamic_index_in_dim(split, (me + step) % seg_count, 0, keepdims=False)
        pairs = [(i, (i + step) % seg_count) for i in range(seg_count)]
        gathered.append(lax.ppermute(sent, "seg", pairs))
    mine = jnp.stack(gathered)

    columns = [mine]
    for step in range(1, hops + 1):
        pairs = [(i, i - step) for i in range(step, fibre_count)]
        columns.append(lax.ppermute(mine, "fibre", pairs))
    columns = jnp.concatenate(columns, axis=2)
    if columns.shape[2] < span:
        pad = jnp.zeros(columns.shape[:2] + (span - columns.shape[2],) + columns.shape[3:], columns.dtype)
        columns = jnp.concatenate([columns, pad], axis=2)
    columns = columns.reshape((seg_count * windows_count,) + columns.shape[2:])
    re_all = columns[:, :, 0]
    im_all = columns[:, :, 1]
    re_own = re_all[:, :block]
    im_own = im_all[:, :block]
    right = jnp.stack([re_all, im_all])
    left = jnp.stack([jnp.stack([re_own, im_own]), jnp.stack([im_own, -re_own])])
    cross = jnp.einsum("opscn,psjn->nocj", left, right, preferred_element_type=jnp.float32)
    band = jnp.stack([cross[:, :, c, c + 1 : c + 1 + kept] for c in range(block)])
    band = band.transpose(3, 0, 2, 1) * (1.0 / math.sqrt(seg_count * windows_count))
    if kept < BAND:
        band = jnp.concatenate([band, jnp.zeros((BAND - kept,) + band.shape[1:], band.dtype)], axis=0)
    band = band.reshape((seg_count, per_owner) + band.shape[1:])

    collected = [lax.dynamic_index_in_dim(band, me, 0, keepdims=False)]
    for step in range(1, seg_count):
        sent = lax.dynamic_index_in_dim(band, (me + step) % seg_count, 0, keepdims=False)
        pairs = [(i, (i + step) % seg_count) for i in range(seg_count) if (i + step) % seg_count < live_owners]
        if pairs:
            collected.append(lax.ppermute(sent, "seg", pairs))
        else:
            collected.append(jnp.zeros_like(sent))
    collected = jnp.stack(collected)
    holder = (me - jnp.arange(seg_count, dtype=jnp.int32)) % seg_count
    by_bins = jnp.take(collected, holder, axis=0)
    return by_bins.transpose(1, 2, 3, 0, 4).reshape(per_owner, block, 2 * NF)


def solution(mesh):
    placed = (P("seg", "fibre", None), P("seg", None), P("fibre"))
    return jax.shard_map(
        shards, mesh=mesh, in_specs=placed, out_specs=P("seg", "fibre", None), check_vma=False
    )
```

time: 226 us -> 146 us (0.65)
  other arithmetic: 33.9 us -> 3.23 us
  local copies, waits for them, and re-layouts: 49.8 us -> 22.6 us
  between operations: 13.5 us -> 0.46 us
  waiting for transfers between devices: 105 us -> 94.6 us
  matrix products: 0.86 us -> 3.83 us
    gather x49 -> x2, local copies, waits for them, and re-layouts: 49 us -> 1.48 us  [the longest x1 0.87 us: window_spectra(): lax.dynamic_slice_in_dim(by_block, q, per_window + 1, axis=0)]
    reduce_scatter x1 -> x0, waiting for transfers between devices: 38.2 us -> none  [shards(): lax.psum_scatter(band_terms(own_block, extended, per_owner * lax.axis_siz...]
    ppermute x16 -> x13, waiting for transfers between devices: 66.9 us -> 94.6 us  [the longest x7 83.1 us: shards(): columns.append(lax.ppermute(mine, 'fibre', pairs))]
    reduce_sum x1 -> x0, other arithmetic: 23.5 us -> none  [band_terms(): direct = jnp.sum(own_float[None] * partners, axis=1)]
    unnamed x0 -> x27, local copies, waits for them, and re-layouts: none -> 7.95 us
    concatenate x2 -> x4, local copies, waits for them, and re-layouts: 0.06 us -> 6.33 us  [the longest x2 5.97 us: shards(): columns = jnp.concatenate([columns, pad], axis=2)]
    dot_general x1 -> x2, matrix products: 0.57 us -> 3.54 us  [the longest x1 3.13 us: window_spectra(): jnp.einsum('wcbi,bif->wcf', windows, table, preferred_element_type=jnp.fl...]
    another operation x1 -> x5, other arithmetic: 3.57 us -> 1.3 us  [the longest x1 1.04 us: shards(): mine = jnp.stack(gathered)]
  transfers between devices with their start and end apart: 17 -> 13, of which waited for: 17 -> 10; matrix products, arithmetic and copies ran while one was open for 0% -> 4% of each run, Pallas kernels for 0% -> 0%
where the time goes in v1:
time: 146 us
  waiting for transfers between devices  94.6 us (65%)
  local copies, waits for them, and re-layouts  22.6 us (15%)
  starting transfers between devices  21.2 us (15%)
  matrix products  3.83 us (3%)
  other arithmetic  3.23 us (2%)
    ppermute x7, waiting for transfers between devices, shards(): columns.append(lax.ppermute(mine, 'fibre', pairs))  83.1 us
    ppermute x7, starting transfers between devices, shards(): columns.append(lax.ppermute(mine, 'fibre', pairs))  9.02 us
    unnamed x27, local copies, waits for them, and re-layouts  7.95 us
    ppermute x3, waiting for transfers between devices, shards(): collected.append(lax.ppermute(sent, 'seg', pairs))  6.91 us
    ppermute x3, starting transfers between devices, shards(): collected.append(lax.ppermute(sent, 'seg', pairs))  6.24 us
    concatenate x2, local copies, waits for them, and re-layouts, shards(): columns = jnp.concatenate([columns, pad], axis=2)  5.97 us
    ppermute x3, starting transfers between devices, shards(): gathered.append(lax.ppermute(sent, 'seg', pairs))  5.94 us
    ppermute x3, waiting for transfers between devices, shards(): gathered.append(lax.ppermute(sent, 'seg', pairs))  4.56 us
  transfers between devices with their start and end apart: 13, of which 10 were waited for; matrix products, arithmetic and copies ran while one was open for 4% of the time, Pallas kernels for 0%

profile of v1, /device:TPU:0, one launch (start us, length us, event | category | flops | bytes accessed | tf_op | source)
XLA Modules:
  0.0 145.9 jit_solution(18371625276664661040)
XLA Ops:
  1.4 1.3 copy.140
  3.8 1.7 %fusion.51 = (bf16[16,24,16,128]{3,2,1,0:T(8,128)(2,1)S(1)}, bf16[16,24,16,128]{3,2,1,0:T(8,128)(2,1)}) fusion(bf16[16,25,16,128]{3,2,1,0:T(8,128)(2,1)S(1)} %gather_fusion), kind=kLoop, calls=%fused_computation.114 | loop fusion | bytes 6291456 | tf_op jit(solution)/shard_map/slice | solution.py:36
  5.5 3.1 %fusion.21 = f32[16,16,128]{2,1,0:T(8,128)S(1)} fusion(bf16[24,128,128,1]{2,1,0,3:T(8,128)(2,1)} %constant.161, bf16[16,24,16,128]{3,2,1,0:T(8,128)(2,1)} %get-tuple-element.6, bf16[16,24,16,128]{3,2,1,0:T(8,128)(2,1)S(1)} %get-tuple-element.5, s32[16]{0:T(128)S(1)} %and_select_fusion.2), kind=kOutput, calls=%fused_computation.12 | convolution fusion | flops 612106240 | bytes 4063296 | tf_op jit(solution)/shard_map/wcbi,bif->wcf/dot_general | solution.py:44
  9.7 3.0 %collective-permute-start = (bf16[16,16,2,16]{3,1,2,0:T(8,128)(2,1)S(1)}, bf16[16,16,2,16]{3,1,2,0:T(8,128)(2,1)S(1)}, u32[]{:S(2)}, u32[]{:S(2)}) collective-permute-start(bf16[16,16,2,16]{3,1,2,0:T(8,128)(2,1)S(1)} %get-tuple-element.38), channel_id=1, source_target_pairs={{0,8},{8,16},{16,24},{24,0},{1,9},{9,17},{17,25},{25,1},{2,10},{10... | collective-permute-start | bytes 49160 | tf_op jit(solution)/shard_map/ppermute | solution.py:82
  12.7 1.5 %collective-permute-start.1 = (bf16[16,16,2,16]{3,1,2,0:T(8,128)(2,1)S(1)}, bf16[16,16,2,16]{3,1,2,0:T(8,128)(2,1)S(1)}, u32[]{:S(2)}, u32[]{:S(2)}) collective-permute-start(bf16[16,16,2,16]{3,1,2,0:T(8,128)(2,1)S(1)} %get-tuple-element.37), channel_id=1, source_target_pairs={{0,16},{8,24},{16,0},{24,8},{1,17},{9,25},{17,1},{25,9},{2,18},{10... | collective-permute-start | bytes 49160 | tf_op jit(solution)/shard_map/ppermute | solution.py:82
  14.3 1.4 collective-permute-start.2
  15.7 2.3 %collective-permute-done = bf16[16,16,2,16]{3,1,2,0:T(8,128)(2,1)S(1)} collective-permute-done((bf16[16,16,2,16]{3,1,2,0:T(8,128)(2,1)S(1)}, bf16[16,16,2,16]{3,1,2,0:T(8,128)(2,1)S(1)}, u32[]{:S(2)}, u32[]{:S(2)}) %collective-permute-start) | collective-permute-done | bytes 16416 | tf_op jit(solution)/shard_map/ppermute | solution.py:82
  18.0 2.0 %collective-permute-done.1 = bf16[16,16,2,16]{3,1,2,0:T(8,128)(2,1)S(1)} collective-permute-done((bf16[16,16,2,16]{3,1,2,0:T(8,128)(2,1)S(1)}, bf16[16,16,2,16]{3,1,2,0:T(8,128)(2,1)S(1)}, u32[]{:S(2)}, u32[]{:S(2)}) %collective-permute-start.1) | collective-permute-done | bytes 16416 | tf_op jit(solution)/shard_map/ppermute | solution.py:82
  20.3 1.0 pad_maximum_fusion.1
  21.3 1.3 collective-permute-start.3
  22.6 1.3 collective-permute-start.4
  23.9 1.3 collective-permute-start.5
  25.2 1.3 collective-permute-start.6
  26.5 1.3 collective-permute-start.7
  27.8 1.3 collective-permute-start.8
  29.1 0.9 constant_dynamic-update-slice_fusion.6
  30.0 16.7 %collective-permute-done.4 = bf16[4,16,16,2,16]{4,2,3,1,0:T(8,128)(2,1)S(1)} collective-permute-done((bf16[4,16,16,2,16]{4,2,3,1,0:T(8,128)(2,1)S(1)}, bf16[4,16,16,2,16]{4,2,3,1,0:T(8,128)(2,1)S(1)}, u32[]{:S(2)}, u32[]{:S(2)}) %collective-permute-start.4) | collective-permute-done | bytes 65568 | tf_op jit(solution)/shard_map/ppermute | solution.py:88
  46.8 1.3 collective-permute-start.9
  48.1 0.9 constant_dynamic-update-slice_fusion.5
  50.3 64.9 %collective-permute-done.6 = bf16[4,16,16,2,16]{4,2,3,1,0:T(8,128)(2,1)S(1)} collective-permute-done((bf16[4,16,16,2,16]{4,2,3,1,0:T(8,128)(2,1)S(1)}, bf16[4,16,16,2,16]{4,2,3,1,0:T(8,128)(2,1)S(1)}, u32[]{:S(2)}, u32[]{:S(2)}) %collective-permute-start.6) | collective-permute-done | bytes 65568 | tf_op jit(solution)/shard_map/ppermute | solution.py:88
  116.1 1.1 collective-permute-done.7
  119.0 0.9 constant_dynamic-update-slice_fusion
  120.0 1.0 broadcast_dynamic-update-slice_fusion
  120.9 5.0 %copy.92 = bf16[4,16,144,2,16]{2,1,0,4,3:T(8,128)(2,1)S(1)} copy(bf16[4,16,144,2,16]{4,2,3,1,0:T(8,128)(2,1)} %broadcast_dynamic-update-slice_fusion) | data formatting | bytes 1179648 | tf_op jit(solution)/shard_map/concatenate | solution.py:92
  129.3 1.2 constant_dynamic-slice_fusion.3
  130.4 3.7 %collective-permute-start.10 = (f32[64,16,2,16]{0,3,2,1:T(8,128)S(1)}, f32[64,16,2,16]{0,3,2,1:T(8,128)S(1)}, u32[]{:S(2)}, u32[]{:S(2)}) collective-permute-start(f32[64,16,2,16]{0,3,2,1:T(8,128)S(1)} %bitcast.160), channel_id=1, source_target_pairs={{0,8},{24,0},{1,9},{25,1},{2,10},{26,2},{3,11},{27,3},{4,12},{28,4... | collective-permute-start | bytes 393224 | tf_op jit(solution)/shard_map/ppermute | solution.py:112
  134.1 1.3 collective-permute-start.11
  135.5 1.3 collective-permute-start.12
  136.8 2.8 %collective-permute-done.10 = f32[64,16,2,16]{0,3,2,1:T(8,128)S(1)} collective-permute-done((f32[64,16,2,16]{0,3,2,1:T(8,128)S(1)}, f32[64,16,2,16]{0,3,2,1:T(8,128)S(1)}, u32[]{:S(2)}, u32[]{:S(2)}) %collective-permute-start.10) | collective-permute-done | bytes 131104 | tf_op jit(solution)/shard_map/ppermute | solution.py:112
  139.6 2.8 %collective-permute-done.11 = f32[64,16,2,16]{0,3,2,1:T(8,128)S(1)} collective-permute-done((f32[64,16,2,16]{0,3,2,1:T(8,128)S(1)}, f32[64,16,2,16]{0,3,2,1:T(8,128)S(1)}, u32[]{:S(2)}, u32[]{:S(2)}) %collective-permute-start.11) | collective-permute-done | bytes 131104 | tf_op jit(solution)/shard_map/ppermute | solution.py:112
  142.4 1.3 collective-permute-done.12
  144.8 1.1 copy.119
  (65 shorter events, 12.1 us)
Async XLA Ops:
  5.5 3.3 %copy-start = (s32[16]{0:T(128)S(1)}, s32[16]{0:T(128)}, u32[]{:S(2)}) copy-start(s32[16]{0:T(128)} %param.6) | copy-start | bytes 196
  9.7 8.3 %collective-permute-start = (bf16[16,16,2,16]{3,1,2,0:T(8,128)(2,1)S(1)}, bf16[16,16,2,16]{3,1,2,0:T(8,128)(2,1)S(1)}, u32[]{:S(2)}, u32[]{:S(2)}) collective-permute-start(bf16[16,16,2,16]{3,1,2,0:T(8,128)(2,1)S(1)} %get-tuple-element.38), channel_id=1, source_target_pairs={{0,8},{8,16},{16,24},{24,0},{1,9},{9,17},{17,25},{25,1},{2,10},{10... | collective-permute-start | bytes 49160 | tf_op jit(solution)/shard_map/ppermute | solution.py:82
  12.7 7.3 %collective-permute-start.1 = (bf16[16,16,2,16]{3,1,2,0:T(8,128)(2,1)S(1)}, bf16[16,16,2,16]{3,1,2,0:T(8,128)(2,1)S(1)}, u32[]{:S(2)}, u32[]{:S(2)}) collective-permute-start(bf16[16,16,2,16]{3,1,2,0:T(8,128)(2,1)S(1)} %get-tuple-element.37), channel_id=1, source_target_pairs={{0,16},{8,24},{16,0},{24,8},{1,17},{9,25},{17,1},{25,9},{2,18},{10... | collective-permute-start | bytes 49160 | tf_op jit(solution)/shard_map/ppermute | solution.py:82
  14.3 6.0 %collective-permute-start.2 = (bf16[16,16,2,16]{3,1,2,0:T(8,128)(2,1)S(1)}, bf16[16,16,2,16]{3,1,2,0:T(8,128)(2,1)S(1)}, u32[]{:S(2)}, u32[]{:S(2)}) collective-permute-start(bf16[16,16,2,16]{3,1,2,0:T(8,128)(2,1)S(1)} %get-tuple-element.36), channel_id=1, source_target_pairs={{0,24},{8,0},{16,8},{24,16},{1,25},{9,1},{17,9},{25,17},{2,26},{10... | collective-permute-start | bytes 49160 | tf_op jit(solution)/shard_map/ppermute | solution.py:82
  21.3 6.5 %collective-permute-start.3 = (bf16[4,16,16,2,16]{4,2,3,1,0:T(8,128)(2,1)S(1)}, bf16[4,16,16,2,16]{4,2,3,1,0:T(8,128)(2,1)S(1)}, u32[]{:S(2)}, u32[]{:S(2)}) collective-permute-start(bf16[4,16,16,2,16]{4,2,3,1,0:T(8,128)(2,1)S(1)} %get-tuple-element.33), channel_id=1, source_target_pairs={{1,0},{2,1},{3,2},{4,3},{5,4},{6,5},{7,6},{9,8},{10,9},{11,10},{12... | collective-permute-start | bytes 196616 | tf_op jit(solution)/shard_map/ppermute | solution.py:88
  22.6 24.2 %collective-permute-start.4 = (bf16[4,16,16,2,16]{4,2,3,1,0:T(8,128)(2,1)S(1)}, bf16[4,16,16,2,16]{4,2,3,1,0:T(8,128)(2,1)S(1)}, u32[]{:S(2)}, u32[]{:S(2)}) collective-permute-start(bf16[4,16,16,2,16]{4,2,3,1,0:T(8,128)(2,1)S(1)} %get-tuple-element.33), channel_id=1, source_target_pairs={{2,0},{3,1},{4,2},{5,3},{6,4},{7,5},{10,8},{11,9},{12,10},{13,11},... | collective-permute-start | bytes 196616 | tf_op jit(solution)/shard_map/ppermute | solution.py:88
  23.9 25.5 %collective-permute-start.5 = (bf16[4,16,16,2,16]{4,2,3,1,0:T(8,128)(2,1)S(1)}, bf16[4,16,16,2,16]{4,2,3,1,0:T(8,128)(2,1)S(1)}, u32[]{:S(2)}, u32[]{:S(2)}) collective-permute-start(bf16[4,16,16,2,16]{4,2,3,1,0:T(8,128)(2,1)S(1)} %get-tuple-element.33), channel_id=1, source_target_pairs={{3,0},{4,1},{5,2},{6,3},{7,4},{11,8},{12,9},{13,10},{14,11},{15,12... | collective-permute-start | bytes 196616 | tf_op jit(solution)/shard_map/ppermute | solution.py:88
  25.2 90.0 %collective-permute-start.6 = (bf16[4,16,16,2,16]{4,2,3,1,0:T(8,128)(2,1)S(1)}, bf16[4,16,16,2,16]{4,2,3,1,0:T(8,128)(2,1)S(1)}, u32[]{:S(2)}, u32[]{:S(2)}) collective-permute-start(bf16[4,16,16,2,16]{4,2,3,1,0:T(8,128)(2,1)S(1)} %get-tuple-element.33), channel_id=1, source_target_pairs={{4,0},{5,1},{6,2},{7,3},{12,8},{13,9},{14,10},{15,11},{20,16},{21,... | collective-permute-start | bytes 196616 | tf_op jit(solution)/shard_map/ppermute | solution.py:88
  26.5 90.7 %collective-permute-start.7 = (bf16[4,16,16,2,16]{4,2,3,1,0:T(8,128)(2,1)S(1)}, bf16[4,16,16,2,16]{4,2,3,1,0:T(8,128)(2,1)S(1)}, u32[]{:S(2)}, u32[]{:S(2)}) collective-permute-start(bf16[4,16,16,2,16]{4,2,3,1,0:T(8,128)(2,1)S(1)} %get-tuple-element.33), channel_id=1, source_target_pairs={{5,0},{6,1},{7,2},{13,8},{14,9},{15,10},{21,16},{22,17},{23,18},{2... | collective-permute-start | bytes 196616 | tf_op jit(solution)/shard_map/ppermute | solution.py:88
  27.8 90.3 %collective-permute-start.8 = (bf16[4,16,16,2,16]{4,2,3,1,0:T(8,128)(2,1)S(1)}, bf16[4,16,16,2,16]{4,2,3,1,0:T(8,128)(2,1)S(1)}, u32[]{:S(2)}, u32[]{:S(2)}) collective-permute-start(bf16[4,16,16,2,16]{4,2,3,1,0:T(8,128)(2,1)S(1)} %get-tuple-element.33), channel_id=1, source_target_pairs={{6,0},{7,1},{14,8},{15,9},{22,16},{23,17},{30,24},{31,25}} | collective-permute-start | bytes 196616 | tf_op jit(solution)/shard_map/ppermute | solution.py:88
  46.8 72.3 %collective-permute-start.9 = (bf16[4,16,16,2,16]{4,2,3,1,0:T(8,128)(2,1)S(1)}, bf16[4,16,16,2,16]{4,2,3,1,0:T(8,128)(2,1)S(1)}, u32[]{:S(2)}, u32[]{:S(2)}) collective-permute-start(bf16[4,16,16,2,16]{4,2,3,1,0:T(8,128)(2,1)S(1)} %get-tuple-element.33), channel_id=1, source_target_pairs={{7,0},{15,8},{23,16},{31,24}} | collective-permute-start | bytes 196616 | tf_op jit(solution)/shard_map/ppermute | solution.py:88
  130.4 9.2 %collective-permute-start.10 = (f32[64,16,2,16]{0,3,2,1:T(8,128)S(1)}, f32[64,16,2,16]{0,3,2,1:T(8,128)S(1)}, u32[]{:S(2)}, u32[]{:S(2)}) collective-permute-start(f32[64,16,2,16]{0,3,2,1:T(8,128)S(1)} %bitcast.160), channel_id=1, source_target_pairs={{0,8},{24,0},{1,9},{25,1},{2,10},{26,2},{3,11},{27,3},{4,12},{28,4... | collective-permute-start | bytes 393224 | tf_op jit(solution)/shard_map/ppermute | solution.py:112
  134.1 8.3 %collective-permute-start.11 = (f32[64,16,2,16]{0,3,2,1:T(8,128)S(1)}, f32[64,16,2,16]{0,3,2,1:T(8,128)S(1)}, u32[]{:S(2)}, u32[]{:S(2)}) collective-permute-start(f32[64,16,2,16]{0,3,2,1:T(8,128)S(1)} %bitcast.161), channel_id=1, source_target_pairs={{16,0},{24,8},{17,1},{25,9},{18,2},{26,10},{19,3},{27,11},{20,4},{... | collective-permute-start | bytes 393224 | tf_op jit(solution)/shard_map/ppermute | solution.py:112
  135.5 8.3 %collective-permute-start.12 = (f32[64,16,2,16]{0,3,2,1:T(8,128)S(1)}, f32[64,16,2,16]{0,3,2,1:T(8,128)S(1)}, u32[]{:S(2)}, u32[]{:S(2)}) collective-permute-start(f32[64,16,2,16]{0,3,2,1:T(8,128)S(1)} %bitcast.162), channel_id=1, source_target_pairs={{8,0},{16,8},{9,1},{17,9},{10,2},{18,10},{11,3},{19,11},{12,4},{20... | collective-permute-start | bytes 393224 | tf_op jit(solution)/shard_map/ppermute | solution.py:112

commit v2 on v1

--- a/solution.py
+++ b/solution.py
@@ -73,36 +73,37 @@
     span = block + kept
     hops = min(-(-span // block) - 1, fibre_count - 1)
     me = lax.axis_index("seg")
+    rows = seg_count * windows_count
 
-    split = own_block.reshape(windows_count, block, 2, seg_count, bins_each).transpose(3, 0, 1, 2, 4)
+    split = own_block.reshape(windows_count, block, 2, seg_count, bins_each).transpose(3, 1, 0, 2, 4)
+    split = split.reshape(seg_count, block, windows_count * 2 * bins_each)
     gathered = [lax.dynamic_index_in_dim(split, me, 0, keepdims=False)]
     for step in range(1, seg_count):
         sent = lax.dynamic_index_in_dim(split, (me + step) % seg_count, 0, keepdims=False)
         pairs = [(i, (i + step) % seg_count) for i in range(seg_count)]
         gathered.append(lax.ppermute(sent, "seg", pairs))
-    mine = jnp.stack(gathered)
+    mine = jnp.concatenate(gathered, axis=1)
 
     columns = [mine]
     for step in range(1, hops + 1):
         pairs = [(i, i - step) for i in range(step, fibre_count)]
         columns.append(lax.ppermute(mine, "fibre", pairs))
-    columns = jnp.concatenate(columns, axis=2)
-    if columns.shape[2] < span:
-        pad = jnp.zeros(columns.shape[:2] + (span - columns.shape[2],) + columns.shape[3:], columns.dtype)
-        columns = jnp.concatenate([columns, pad], axis=2)
-    columns = columns.reshape((seg_count * windows_count,) + columns.shape[2:])
-    re_all = columns[:, :, 0]
-    im_all = columns[:, :, 1]
-    re_own = re_all[:, :block]
-    im_own = im_all[:, :block]
-    right = jnp.stack([re_all, im_all])
-    left = jnp.stack([jnp.stack([re_own, im_own]), jnp.stack([im_own, -re_own])])
-    cross = jnp.einsum("opscn,psjn->nocj", left, right, preferred_element_type=jnp.float32)
+    columns = jnp.concatenate(columns, axis=0)
+    if columns.shape[0] < span:
+        columns = jnp.concatenate(
+            [columns, jnp.zeros((span - columns.shape[0], columns.shape[1]), columns.dtype)], axis=0
+        )
+    right = columns.reshape(span, rows, 2, bins_each)
+    re_own = right[:block, :, 0]
+    im_own = right[:block, :, 1]
+    left = jnp.stack([jnp.stack([re_own, im_own], axis=2), jnp.stack([im_own, -re_own], axis=2)])
+    cross = jnp.einsum("ocspn,jspn->nocj", left, right, preferred_element_type=jnp.float32)
     band = jnp.stack([cross[:, :, c, c + 1 : c + 1 + kept] for c in range(block)])
     band = band.transpose(3, 0, 2, 1) * (1.0 / math.sqrt(seg_count * windows_count))
+    band = band.reshape(kept, block * 2 * bins_each)
     if kept < BAND:
-        band = jnp.concatenate([band, jnp.zeros((BAND - kept,) + band.shape[1:], band.dtype)], axis=0)
-    band = band.reshape((seg_count, per_owner) + band.shape[1:])
+        band = jnp.concatenate([band, jnp.zeros((BAND - kept, band.shape[1]), band.dtype)], axis=0)
+    band = band.reshape(seg_count, per_owner, band.shape[1])
 
     collected = [lax.dynamic_index_in_dim(band, me, 0, keepdims=False)]
     for step in range(1, seg_count):
@@ -114,7 +115,7 @@
             collected.append(jnp.zeros_like(sent))
     collected = jnp.stack(collected)
     holder = (me - jnp.arange(seg_count, dtype=jnp.int32)) % seg_count
-    by_bins = jnp.take(collected, holder, axis=0)
+    by_bins = jnp.take(collected, holder, axis=0).reshape(seg_count, per_owner, block, 2, bins_each)
     return by_bins.transpose(1, 2, 3, 0, 4).reshape(per_owner, block, 2 * NF)
 
 

time: 146 us -> 58.2 us (0.40)
  waiting for transfers between devices: 94.6 us -> 17.3 us
  local copies, waits for them, and re-layouts: 22.6 us -> 11.2 us
    ppermute x7, waiting for transfers between devices: 83.1 us -> 8.86 us  [shards(): columns.append(lax.ppermute(mine, 'fibre', pairs))]
    unnamed x27 -> x28, local copies, waits for them, and re-layouts: 7.95 us -> 2.13 us
    concatenate x3, local copies, waits for them, and re-layouts: 6.18 us -> 0.55 us  [the longest x2 0.5 us: shards(): jnp.concatenate([columns, jnp.zeros((span - columns.shape[0], columns.sha...]
    ppermute x3, waiting for transfers between devices: 6.91 us -> 4.35 us  [shards(): collected.append(lax.ppermute(sent, 'seg', pairs))]
    transpose x0 -> x2, other arithmetic: none -> 1.58 us  [the longest x1 1.38 us: shards(): own_block.reshape(windows_count, block, 2, seg_count, bins_each)]
  transfers between devices with their start and end apart: 13 -> 13, of which waited for: 10 -> 7; matrix products, arithmetic and copies ran while one was open for 4% -> 2% of each run, Pallas kernels for 0% -> 0%
where the time goes in v2:
time: 58.2 us; the launch traced here: 57.8 us
  starting transfers between devices  21.2 us (36%)
  waiting for transfers between devices  17.3 us (30%)
  local copies, waits for them, and re-layouts  11.2 us (19%)
  matrix products  4.14 us (7%)
  other arithmetic  3.41 us (6%)
    ppermute x7, starting transfers between devices, shards(): columns.append(lax.ppermute(mine, 'fibre', pairs))  9.04 us
    ppermute x7, waiting for transfers between devices, shards(): columns.append(lax.ppermute(mine, 'fibre', pairs))  8.86 us
    ppermute x3, starting transfers between devices, shards(): collected.append(lax.ppermute(sent, 'seg', pairs))  7.13 us
    ppermute x3, starting transfers between devices, shards(): gathered.append(lax.ppermute(sent, 'seg', pairs))  5.04 us
    ppermute x3, waiting for transfers between devices, shards(): collected.append(lax.ppermute(sent, 'seg', pairs))  4.35 us
    ppermute x3, waiting for transfers between devices, shards(): gathered.append(lax.ppermute(sent, 'seg', pairs))  4.04 us
    dot_general x1, matrix products, window_spectra(): jnp.einsum('wcbi,bif->wcf', windows, table, preferred_element_type=jnp.fl...  3.13 us
    unnamed x28, local copies, waits for them, and re-layouts  2.13 us
  transfers between devices with their start and end apart: 13, of which 7 were waited for; matrix products, arithmetic and copies ran while one was open for 2% of the time, Pallas kernels for 0%

profile of v2, /device:TPU:0, one launch (start us, length us, event | category | flops | bytes accessed | tf_op | source)
XLA Modules:
  0.0 57.8 jit_solution(11770031650157485888)
XLA Ops:
  0.0 0.7 %fusion.46 = s32[16]{0:T(128)S(1)} fusion(s32[1,16]{1,0:T(1,128)} %param.5), kind=kLoop, calls=%fused_computation.95 | loop fusion | flops 320 | bytes 128 | tf_op jit(solution)/shard_map/vmap()/concatenate | solution.py:35
  0.7 0.7 %and_select_fusion.2 = s32[16]{0:T(128)S(1)} fusion(s32[1,16]{1,0:T(1,128)} %param.5), kind=kLoop, calls=%fused_computation.84 | loop fusion | flops 176 | bytes 128 | tf_op jit(solution)/shard_map/jit(remainder)/select_n | solution.py:34
  1.4 1.3 %copy.99 = bf16[2,8,216,128]{3,2,1,0:T(8,128)(2,1)S(1)} copy(bf16[2,8,216,128]{3,1,2,0:T(8,128)(2,1)} %bitcast.139) | data formatting | bytes 1769472
  3.0 0.9 %gather_fusion = bf16[16,25,16,128]{3,2,1,0:T(8,128)(2,1)S(1)} fusion(bf16[217,16,128]{2,1,0:T(8,128)(2,1)S(1)} %concatenate.28, s32[16]{0:T(128)S(1)} %fusion.46), kind=kCustom, calls=%fused_computation | custom fusion | bytes 3276992 | tf_op jit(solution)/shard_map/vmap()/gather | solution.py:35
  3.8 1.7 %fusion.52 = (bf16[16,24,16,128]{3,2,1,0:T(8,128)(2,1)S(1)}, bf16[16,24,16,128]{3,2,1,0:T(8,128)(2,1)}) fusion(bf16[16,25,16,128]{3,2,1,0:T(8,128)(2,1)S(1)} %gather_fusion), kind=kLoop, calls=%fused_computation.101 | loop fusion | bytes 6291456 | tf_op jit(solution)/shard_map/slice | solution.py:36
  5.6 3.1 %fusion.21 = f32[16,16,128]{2,1,0:T(8,128)S(1)} fusion(bf16[24,128,128,1]{2,1,0,3:T(8,128)(2,1)} %constant.161, bf16[16,24,16,128]{3,2,1,0:T(8,128)(2,1)} %get-tuple-element.6, bf16[16,24,16,128]{3,2,1,0:T(8,128)(2,1)S(1)} %get-tuple-element.5, s32[16]{0:T(128)S(1)} %and_select_fusion.2), kind=kOutput, calls=%fused_computation.12 | convolution fusion | flops 612106240 | bytes 4063296 | tf_op jit(solution)/shard_map/wcbi,bif->wcf/dot_general | solution.py:44
  10.4 1.4 %maximum_bitcast_fusion = bf16[4,16,16,2,16]{4,3,2,1,0:T(2,128)(2,1)S(1)} fusion(bf16[16,16,1,4,16]{4,2,0,1,3:T(2,128)(2,1)S(1)} %copy.49, bf16[16,16,1,4,16]{4,2,0,1,3:T(2,128)(2,1)S(1)} %copy.48), kind=kLoop, calls=%fused_computation.22 | loop fusion | flops 131072 | bytes 131072 | tf_op jit(solution)/shard_map/transpose | solution.py:78
  11.8 0.8 %reshape.188 = bf16[4,16,512]{2,1,0:T(8,128)(2,1)S(1)} reshape(bf16[4,16,16,2,16]{4,3,2,1,0:T(2,128)(2,1)S(1)} %maximum_bitcast_fusion) | data formatting | bytes 131072 | tf_op jit(solution)/shard_map/reshape | solution.py:79
  12.6 3.9 %collective-permute-start.2 = (bf16[16,512]{1,0:T(8,128)(2,1)S(1)}, bf16[16,512]{1,0:T(8,128)(2,1)S(1)}, u32[]{:S(2)}, u32[]{:S(2)}) collective-permute-start(bf16[16,512]{1,0:T(8,128)(2,1)S(1)} %get-tuple-element.34), channel_id=1, source_target_pairs={{0,24},{8,0},{16,8},{24,16},{1,25},{9,1},{17,9},{25,17},{2,26},{10... | collective-permute-start | bytes 49160 | tf_op jit(solution)/shard_map/ppermute | solution.py:84
  16.5 0.5 collective-permute-start.1
  17.0 0.6 %collective-permute-start = (bf16[16,512]{1,0:T(8,128)(2,1)S(1)}, bf16[16,512]{1,0:T(8,128)(2,1)S(1)}, u32[]{:S(2)}, u32[]{:S(2)}) collective-permute-start(bf16[16,512]{1,0:T(8,128)(2,1)S(1)} %get-tuple-element.36), channel_id=1, source_target_pairs={{0,8},{8,16},{16,24},{24,0},{1,9},{9,17},{17,25},{25,1},{2,10},{10... | collective-permute-start | bytes 49160 | tf_op jit(solution)/shard_map/ppermute | solution.py:84
  17.9 2.3 %collective-permute-done.1 = bf16[16,512]{1,0:T(8,128)(2,1)S(1)} collective-permute-done((bf16[16,512]{1,0:T(8,128)(2,1)S(1)}, bf16[16,512]{1,0:T(8,128)(2,1)S(1)}, u32[]{:S(2)}, u32[]{:S(2)}) %collective-permute-start.1) | collective-permute-done | bytes 16416 | tf_op jit(solution)/shard_map/ppermute | solution.py:84
  20.2 1.4 %collective-permute-done = bf16[16,512]{1,0:T(8,128)(2,1)S(1)} collective-permute-done((bf16[16,512]{1,0:T(8,128)(2,1)S(1)}, bf16[16,512]{1,0:T(8,128)(2,1)S(1)}, u32[]{:S(2)}, u32[]{:S(2)}) %collective-permute-start) | collective-permute-done | bytes 16416 | tf_op jit(solution)/shard_map/ppermute | solution.py:84
  21.7 1.3 %collective-permute-start.3 = (bf16[16,2048]{1,0:T(8,128)(2,1)S(1)}, bf16[16,2048]{1,0:T(8,128)(2,1)S(1)}, u32[]{:S(2)}, u32[]{:S(2)}) collective-permute-start(bf16[16,2048]{1,0:T(8,128)(2,1)S(1)} %get-tuple-element.31), channel_id=1, source_target_pairs={{1,0},{2,1},{3,2},{4,3},{5,4},{6,5},{7,6},{9,8},{10,9},{11,10},{12... | collective-permute-start | bytes 196616 | tf_op jit(solution)/shard_map/ppermute | solution.py:90
  23.0 1.3 %collective-permute-start.4 = (bf16[16,2048]{1,0:T(8,128)(2,1)S(1)}, bf16[16,2048]{1,0:T(8,128)(2,1)S(1)}, u32[]{:S(2)}, u32[]{:S(2)}) collective-permute-start(bf16[16,2048]{1,0:T(8,128)(2,1)S(1)} %get-tuple-element.31), channel_id=1, source_target_pairs={{2,0},{3,1},{4,2},{5,3},{6,4},{7,5},{10,8},{11,9},{12,10},{13,11},... | collective-permute-start | bytes 196616 | tf_op jit(solution)/shard_map/ppermute | solution.py:90
  24.3 1.3 %collective-permute-start.5 = (bf16[16,2048]{1,0:T(8,128)(2,1)S(1)}, bf16[16,2048]{1,0:T(8,128)(2,1)S(1)}, u32[]{:S(2)}, u32[]{:S(2)}) collective-permute-start(bf16[16,2048]{1,0:T(8,128)(2,1)S(1)} %get-tuple-element.31), channel_id=1, source_target_pairs={{3,0},{4,1},{5,2},{6,3},{7,4},{11,8},{12,9},{13,10},{14,11},{15,12... | collective-permute-start | bytes 196616 | tf_op jit(solution)/shard_map/ppermute | solution.py:90
  25.6 1.3 %collective-permute-start.6 = (bf16[16,2048]{1,0:T(8,128)(2,1)S(1)}, bf16[16,2048]{1,0:T(8,128)(2,1)S(1)}, u32[]{:S(2)}, u32[]{:S(2)}) collective-permute-start(bf16[16,2048]{1,0:T(8,128)(2,1)S(1)} %get-tuple-element.31), channel_id=1, source_target_pairs={{4,0},{5,1},{6,2},{7,3},{12,8},{13,9},{14,10},{15,11},{20,16},{21,... | collective-permute-start | bytes 196616 | tf_op jit(solution)/shard_map/ppermute | solution.py:90
  26.9 1.3 %collective-permute-start.7 = (bf16[16,2048]{1,0:T(8,128)(2,1)S(1)}, bf16[16,2048]{1,0:T(8,128)(2,1)S(1)}, u32[]{:S(2)}, u32[]{:S(2)}) collective-permute-start(bf16[16,2048]{1,0:T(8,128)(2,1)S(1)} %get-tuple-element.31), channel_id=1, source_target_pairs={{5,0},{6,1},{7,2},{13,8},{14,9},{15,10},{21,16},{22,17},{23,18},{2... | collective-permute-start | bytes 196616 | tf_op jit(solution)/shard_map/ppermute | solution.py:90
  28.6 0.4 copy.53
  29.0 1.3 %collective-permute-start.8 = (bf16[16,2048]{1,0:T(8,128)(2,1)S(1)}, bf16[16,2048]{1,0:T(8,128)(2,1)S(1)}, u32[]{:S(2)}, u32[]{:S(2)}) collective-permute-start(bf16[16,2048]{1,0:T(8,128)(2,1)S(1)} %get-tuple-element.31), channel_id=1, source_target_pairs={{6,0},{7,1},{14,8},{15,9},{22,16},{23,17},{30,24},{31,25}} | collective-permute-start | bytes 196616 | tf_op jit(solution)/shard_map/ppermute | solution.py:90
  30.4 1.3 %collective-permute-start.9 = (bf16[16,2048]{1,0:T(8,128)(2,1)S(1)}, bf16[16,2048]{1,0:T(8,128)(2,1)S(1)}, u32[]{:S(2)}, u32[]{:S(2)}) collective-permute-start(bf16[16,2048]{1,0:T(8,128)(2,1)S(1)} %get-tuple-element.31), channel_id=1, source_target_pairs={{7,0},{15,8},{23,16},{31,24}} | collective-permute-start | bytes 196616 | tf_op jit(solution)/shard_map/ppermute | solution.py:90
  31.7 8.5 %collective-permute-done.6 = bf16[16,2048]{1,0:T(8,128)(2,1)S(1)} collective-permute-done((bf16[16,2048]{1,0:T(8,128)(2,1)S(1)}, bf16[16,2048]{1,0:T(8,128)(2,1)S(1)}, u32[]{:S(2)}, u32[]{:S(2)}) %collective-permute-start.6) | collective-permute-done | bytes 65568 | tf_op jit(solution)/shard_map/ppermute | solution.py:90
  40.6 0.5 copy.50
  41.8 0.7 %convolution_bitcast_fusion = f32[16,2,16,144]{3,2,1,0:T(8,128)S(1)} fusion(bf16[144,64,2,16,1]{0,3,2,1,4:T(8,128)(2,1)S(1)} %bitcast.132, bf16[1,16,64,2,16]{2,1,3,0,4:T(8,128)(2,1)S(1)} %maximum_bitcast_fusion.1, bf16[1,16,64,2,16]{2,1,3,0,4:T(8,128)(2,1)S(1)} %copy.53), kind=kOutput, calls=%fused_computation.11 | convolution fusion | flops 18939904 | bytes 1015808 | tf_op jit(solution)/shard_map/ocspn,jspn->nocj/dot_general | solution.py:100
  42.5 0.6 %fusion.54 = (f32[16,2,1,128]{3,2,1,0:T(1,128)S(1)}, f32[16,2,1,128]{3,2,1,0:T(1,128)S(1)}, f32[16,2,1,128]{3,2,1,0:T(1,128)S(1)}, f32[16,2,1,128]{3,2,1,0:T(1,1...) fusion(f32[16,2,16,144]{3,2,1,0:T(8,128)S(1)} %convolution_bitc, ...), kind=kLoop, calls=%fused_computation.103 | loop fusion | bytes 524288 | tf_op jit(solution)/shard_map/slice | solution.py:101
  43.8 1.3 %collective-permute-start.12 = (f32[64,512]{1,0:T(8,128)S(1)}, f32[64,512]{1,0:T(8,128)S(1)}, u32[]{:S(2)}, u32[]{:S(2)}) collective-permute-start(f32[64,512]{1,0:T(8,128)S(1)} %get-tuple-element.10), channel_id=1, source_target_pairs={{8,0},{16,8},{9,1},{17,9},{10,2},{18,10},{11,3},{19,11},{12,4},{20... | collective-permute-start | bytes 393224 | tf_op jit(solution)/shard_map/ppermute | solution.py:113
  45.1 1.3 %collective-permute-start.11 = (f32[64,512]{1,0:T(8,128)S(1)}, f32[64,512]{1,0:T(8,128)S(1)}, u32[]{:S(2)}, u32[]{:S(2)}) collective-permute-start(f32[64,512]{1,0:T(8,128)S(1)} %get-tuple-element.11), channel_id=1, source_target_pairs={{16,0},{24,8},{17,1},{25,9},{18,2},{26,10},{19,3},{27,11},{20,4},{... | collective-permute-start | bytes 393224 | tf_op jit(solution)/shard_map/ppermute | solution.py:113
  46.4 4.6 %collective-permute-start.10 = (f32[64,512]{1,0:T(8,128)S(1)}, f32[64,512]{1,0:T(8,128)S(1)}, u32[]{:S(2)}, u32[]{:S(2)}) collective-permute-start(f32[64,512]{1,0:T(8,128)S(1)} %get-tuple-element.12), channel_id=1, source_target_pairs={{0,8},{24,0},{1,9},{25,1},{2,10},{26,2},{3,11},{27,3},{4,12},{28,4... | collective-permute-start | bytes 393224 | tf_op jit(solution)/shard_map/ppermute | solution.py:113
  51.0 2.4 %collective-permute-done.11 = f32[64,512]{1,0:T(8,128)S(1)} collective-permute-done((f32[64,512]{1,0:T(8,128)S(1)}, f32[64,512]{1,0:T(8,128)S(1)}, u32[]{:S(2)}, u32[]{:S(2)}) %collective-permute-start.11) | collective-permute-done | bytes 131104 | tf_op jit(solution)/shard_map/ppermute | solution.py:113
  53.3 2.0 %collective-permute-done.10 = f32[64,512]{1,0:T(8,128)S(1)} collective-permute-done((f32[64,512]{1,0:T(8,128)S(1)}, f32[64,512]{1,0:T(8,128)S(1)}, u32[]{:S(2)}, u32[]{:S(2)}) %collective-permute-start.10) | collective-permute-done | bytes 131104 | tf_op jit(solution)/shard_map/ppermute | solution.py:113
  55.4 0.6 %gather_fusion.1 = f32[4,64,512]{2,1,0:T(8,128)S(1)} fusion(f32[4,64,512]{2,1,0:T(8,128)S(1)} %pad_maximum_fusion, s32[1024]{0:T(1024)S(1)} %pad_clamp_fusion), kind=kCustom, calls=%fused_computation.1 | custom fusion | bytes 1048592 | tf_op jit(solution)/shard_map/jit(_take)/gather | solution.py:118
  56.6 1.1 %copy.74 = f32[64,16,128]{2,1,0:T(8,128)} copy(f32[64,16,128]{0,2,1:T(8,128)S(1)} %bitcast.134) | data formatting | bytes 1048576 | tf_op jit(solution)/shard_map/reshape | solution.py:119
  (65 shorter events, 5.0 us)
Async XLA Ops:
  5.6 3.3 %copy-start = (s32[16]{0:T(128)S(1)}, s32[16]{0:T(128)}, u32[]{:S(2)}) copy-start(s32[16]{0:T(128)} %param.6) | copy-start | bytes 196
  12.6 5.4 %collective-permute-start.2 = (bf16[16,512]{1,0:T(8,128)(2,1)S(1)}, bf16[16,512]{1,0:T(8,128)(2,1)S(1)}, u32[]{:S(2)}, u32[]{:S(2)}) collective-permute-start(bf16[16,512]{1,0:T(8,128)(2,1)S(1)} %get-tuple-element.34), channel_id=1, source_target_pairs={{0,24},{8,0},{16,8},{24,16},{1,25},{9,1},{17,9},{25,17},{2,26},{10... | collective-permute-start | bytes 49160 | tf_op jit(solution)/shard_map/ppermute | solution.py:84
  16.5 3.7 %collective-permute-start.1 = (bf16[16,512]{1,0:T(8,128)(2,1)S(1)}, bf16[16,512]{1,0:T(8,128)(2,1)S(1)}, u32[]{:S(2)}, u32[]{:S(2)}) collective-permute-start(bf16[16,512]{1,0:T(8,128)(2,1)S(1)} %get-tuple-element.35), channel_id=1, source_target_pairs={{0,16},{8,24},{16,0},{24,8},{1,17},{9,25},{17,1},{25,9},{2,18},{10... | collective-permute-start | bytes 49160 | tf_op jit(solution)/shard_map/ppermute | solution.py:84
  17.0 4.6 %collective-permute-start = (bf16[16,512]{1,0:T(8,128)(2,1)S(1)}, bf16[16,512]{1,0:T(8,128)(2,1)S(1)}, u32[]{:S(2)}, u32[]{:S(2)}) collective-permute-start(bf16[16,512]{1,0:T(8,128)(2,1)S(1)} %get-tuple-element.36), channel_id=1, source_target_pairs={{0,8},{8,16},{16,24},{24,0},{1,9},{9,17},{17,25},{25,1},{2,10},{10... | collective-permute-start | bytes 49160 | tf_op jit(solution)/shard_map/ppermute | solution.py:84
  21.7 7.4 %collective-permute-start.3 = (bf16[16,2048]{1,0:T(8,128)(2,1)S(1)}, bf16[16,2048]{1,0:T(8,128)(2,1)S(1)}, u32[]{:S(2)}, u32[]{:S(2)}) collective-permute-start(bf16[16,2048]{1,0:T(8,128)(2,1)S(1)} %get-tuple-element.31), channel_id=1, source_target_pairs={{1,0},{2,1},{3,2},{4,3},{5,4},{6,5},{7,6},{9,8},{10,9},{11,10},{12... | collective-permute-start | bytes 196616 | tf_op jit(solution)/shard_map/ppermute | solution.py:90
  23.0 7.4 %collective-permute-start.4 = (bf16[16,2048]{1,0:T(8,128)(2,1)S(1)}, bf16[16,2048]{1,0:T(8,128)(2,1)S(1)}, u32[]{:S(2)}, u32[]{:S(2)}) collective-permute-start(bf16[16,2048]{1,0:T(8,128)(2,1)S(1)} %get-tuple-element.31), channel_id=1, source_target_pairs={{2,0},{3,1},{4,2},{5,3},{6,4},{7,5},{10,8},{11,9},{12,10},{13,11},... | collective-permute-start | bytes 196616 | tf_op jit(solution)/shard_map/ppermute | solution.py:90
  24.3 7.4 %collective-permute-start.5 = (bf16[16,2048]{1,0:T(8,128)(2,1)S(1)}, bf16[16,2048]{1,0:T(8,128)(2,1)S(1)}, u32[]{:S(2)}, u32[]{:S(2)}) collective-permute-start(bf16[16,2048]{1,0:T(8,128)(2,1)S(1)} %get-tuple-element.31), channel_id=1, source_target_pairs={{3,0},{4,1},{5,2},{6,3},{7,4},{11,8},{12,9},{13,10},{14,11},{15,12... | collective-permute-start | bytes 196616 | tf_op jit(solution)/shard_map/ppermute | solution.py:90
  25.6 14.6 %collective-permute-start.6 = (bf16[16,2048]{1,0:T(8,128)(2,1)S(1)}, bf16[16,2048]{1,0:T(8,128)(2,1)S(1)}, u32[]{:S(2)}, u32[]{:S(2)}) collective-permute-start(bf16[16,2048]{1,0:T(8,128)(2,1)S(1)} %get-tuple-element.31), channel_id=1, source_target_pairs={{4,0},{5,1},{6,2},{7,3},{12,8},{13,9},{14,10},{15,11},{20,16},{21,... | collective-permute-start | bytes 196616 | tf_op jit(solution)/shard_map/ppermute | solution.py:90
  26.9 13.7 %collective-permute-start.7 = (bf16[16,2048]{1,0:T(8,128)(2,1)S(1)}, bf16[16,2048]{1,0:T(8,128)(2,1)S(1)}, u32[]{:S(2)}, u32[]{:S(2)}) collective-permute-start(bf16[16,2048]{1,0:T(8,128)(2,1)S(1)} %get-tuple-element.31), channel_id=1, source_target_pairs={{5,0},{6,1},{7,2},{13,8},{14,9},{15,10},{21,16},{22,17},{23,18},{2... | collective-permute-start | bytes 196616 | tf_op jit(solution)/shard_map/ppermute | solution.py:90
  29.0 11.5 %collective-permute-start.8 = (bf16[16,2048]{1,0:T(8,128)(2,1)S(1)}, bf16[16,2048]{1,0:T(8,128)(2,1)S(1)}, u32[]{:S(2)}, u32[]{:S(2)}) collective-permute-start(bf16[16,2048]{1,0:T(8,128)(2,1)S(1)} %get-tuple-element.31), channel_id=1, source_target_pairs={{6,0},{7,1},{14,8},{15,9},{22,16},{23,17},{30,24},{31,25}} | collective-permute-start | bytes 196616 | tf_op jit(solution)/shard_map/ppermute | solution.py:90
  30.4 10.2 %collective-permute-start.9 = (bf16[16,2048]{1,0:T(8,128)(2,1)S(1)}, bf16[16,2048]{1,0:T(8,128)(2,1)S(1)}, u32[]{:S(2)}, u32[]{:S(2)}) collective-permute-start(bf16[16,2048]{1,0:T(8,128)(2,1)S(1)} %get-tuple-element.31), channel_id=1, source_target_pairs={{7,0},{15,8},{23,16},{31,24}} | collective-permute-start | bytes 196616 | tf_op jit(solution)/shard_map/ppermute | solution.py:90
  43.8 7.2 %collective-permute-start.12 = (f32[64,512]{1,0:T(8,128)S(1)}, f32[64,512]{1,0:T(8,128)S(1)}, u32[]{:S(2)}, u32[]{:S(2)}) collective-permute-start(f32[64,512]{1,0:T(8,128)S(1)} %get-tuple-element.10), channel_id=1, source_target_pairs={{8,0},{16,8},{9,1},{17,9},{10,2},{18,10},{11,3},{19,11},{12,4},{20... | collective-permute-start | bytes 393224 | tf_op jit(solution)/shard_map/ppermute | solution.py:113
  45.1 8.3 %collective-permute-start.11 = (f32[64,512]{1,0:T(8,128)S(1)}, f32[64,512]{1,0:T(8,128)S(1)}, u32[]{:S(2)}, u32[]{:S(2)}) collective-permute-start(f32[64,512]{1,0:T(8,128)S(1)} %get-tuple-element.11), channel_id=1, source_target_pairs={{16,0},{24,8},{17,1},{25,9},{18,2},{26,10},{19,3},{27,11},{20,4},{... | collective-permute-start | bytes 393224 | tf_op jit(solution)/shard_map/ppermute | solution.py:113
  46.4 8.9 %collective-permute-start.10 = (f32[64,512]{1,0:T(8,128)S(1)}, f32[64,512]{1,0:T(8,128)S(1)}, u32[]{:S(2)}, u32[]{:S(2)}) collective-permute-start(f32[64,512]{1,0:T(8,128)S(1)} %get-tuple-element.12), channel_id=1, source_target_pairs={{0,8},{24,0},{1,9},{25,1},{2,10},{26,2},{3,11},{27,3},{4,12},{28,4... | collective-permute-start | bytes 393224 | tf_op jit(solution)/shard_map/ppermute | solution.py:113

commit v3 on v2

--- a/solution.py
+++ b/solution.py
@@ -59,6 +59,26 @@
     return jnp.concatenate([real_part * gain_of, imag_part * gain_of], axis=-1).astype(jnp.bfloat16)
 
 
+def halo(mine, hops, fibre_count):
+    if fibre_count % 2:
+        columns = [mine]
+        for step in range(1, hops + 1):
+            pairs = [(i, i - step) for i in range(step, fibre_count)]
+            columns.append(lax.ppermute(mine, "fibre", pairs))
+        return jnp.concatenate(columns, axis=0)
+    strides = min(-(-hops // 2), (fibre_count - 1) // 2)
+    own = [mine]
+    for step in range(1, strides + 1):
+        pairs = [(i, i - 2 * step) for i in range(2 * step, fibre_count)]
+        own.append(lax.ppermute(mine, "fibre", pairs))
+    swapped = lax.ppermute(jnp.concatenate(own, axis=0), "fibre", [(i, i ^ 1) for i in range(fibre_count)])
+    swapped = jnp.split(swapped, strides + 1, axis=0)
+    even = [part for pair in zip(own, swapped) for part in pair]
+    odd = [part for pair in zip(own, swapped[1:] + [jnp.zeros_like(mine)]) for part in pair]
+    odd_side = lax.axis_index("fibre") % 2 == 1
+    return jnp.where(odd_side, jnp.concatenate(odd, axis=0), jnp.concatenate(even, axis=0))
+
+
 def shards(record, offsets, live_mask):
     seg_count = lax.axis_size("seg")
     fibre_count = lax.axis_size("fibre")
@@ -84,11 +104,7 @@
         gathered.append(lax.ppermute(sent, "seg", pairs))
     mine = jnp.concatenate(gathered, axis=1)
 
-    columns = [mine]
-    for step in range(1, hops + 1):
-        pairs = [(i, i - step) for i in range(step, fibre_count)]
-        columns.append(lax.ppermute(mine, "fibre", pairs))
-    columns = jnp.concatenate(columns, axis=0)
+    columns = halo(mine, hops, fibre_count)[:span]
     if columns.shape[0] < span:
         columns = jnp.concatenate(
             [columns, jnp.zeros((span - columns.shape[0], columns.shape[1]), columns.dtype)], axis=0

time: 58.2 us -> 51.6 us (0.89)
  starting transfers between devices: 21.2 us -> 16.1 us
  waiting for transfers between devices: 17.3 us -> 15.8 us
    ppermute x7 -> x4, starting transfers between devices: 9.04 us -> 3.95 us  [the longest x3 3.88 us: halo(): own.append(lax.ppermute(mine, 'fibre', pairs))]
    ppermute x7 -> x4, waiting for transfers between devices: 8.86 us -> 7.1 us  [the longest x3 5.65 us: halo(): own.append(lax.ppermute(mine, 'fibre', pairs))]
    unnamed x28 -> x31, local copies, waits for them, and re-layouts: 2.13 us -> 2.48 us
  transfers between devices with their start and end apart: 13 -> 10, of which waited for: 7 -> 9; matrix products, arithmetic and copies ran while one was open for 2% -> 0% of each run, Pallas kernels for 0% -> 0%
where the time goes in v3:
time: 51.6 us; the launch traced here: 51.3 us
  starting transfers between devices  16.1 us (31%)
  waiting for transfers between devices  15.8 us (31%)
  local copies, waits for them, and re-layouts  11.2 us (22%)
  matrix products  4.14 us (8%)
  other arithmetic  3.51 us (7%)
  between operations  0.54 us (1%)
    ppermute x3, starting transfers between devices, shards(): collected.append(lax.ppermute(sent, 'seg', pairs))  7.13 us
    ppermute x3, waiting for transfers between devices, halo(): own.append(lax.ppermute(mine, 'fibre', pairs))  5.65 us
    ppermute x3, starting transfers between devices, shards(): gathered.append(lax.ppermute(sent, 'seg', pairs))  5.04 us
    ppermute x3, waiting for transfers between devices, shards(): collected.append(lax.ppermute(sent, 'seg', pairs))  4.64 us
    ppermute x3, waiting for transfers between devices, shards(): gathered.append(lax.ppermute(sent, 'seg', pairs))  4.04 us
    ppermute x3, starting transfers between devices, halo(): own.append(lax.ppermute(mine, 'fibre', pairs))  3.88 us
    dot_general x1, matrix products, window_spectra(): jnp.einsum('wcbi,bif->wcf', windows, table, preferred_element_type=jnp.fl...  3.13 us
    unnamed x31, local copies, waits for them, and re-layouts  2.48 us
  transfers between devices with their start and end apart: 10, of which 9 were waited for; matrix products, arithmetic and copies ran while one was open for 0% of the time, Pallas kernels for 0%

profile of v3, /device:TPU:0, one launch (start us, length us, event | category | flops | bytes accessed | tf_op | source)
XLA Modules:
  0.0 51.3 jit_solution(234289283784448275)
XLA Ops:
  0.0 0.7 %fusion.46 = s32[16]{0:T(128)S(1)} fusion(s32[1,16]{1,0:T(1,128)} %param.5), kind=kLoop, calls=%fused_computation.104 | loop fusion | flops 320 | bytes 128 | tf_op jit(solution)/shard_map/vmap()/concatenate | solution.py:35
  0.7 0.7 %and_select_fusion.2 = s32[16]{0:T(128)S(1)} fusion(s32[1,16]{1,0:T(1,128)} %param.5), kind=kLoop, calls=%fused_computation.93 | loop fusion | flops 176 | bytes 128 | tf_op jit(solution)/shard_map/jit(remainder)/select_n | solution.py:34
  1.4 1.3 %copy.100 = bf16[2,8,216,128]{3,2,1,0:T(8,128)(2,1)S(1)} copy(bf16[2,8,216,128]{3,1,2,0:T(8,128)(2,1)} %bitcast.139) | data formatting | bytes 1769472
  3.0 0.9 %gather_fusion = bf16[16,25,16,128]{3,2,1,0:T(8,128)(2,1)S(1)} fusion(bf16[217,16,128]{2,1,0:T(8,128)(2,1)S(1)} %concatenate.37, s32[16]{0:T(128)S(1)} %fusion.46), kind=kCustom, calls=%fused_computation | custom fusion | bytes 3276992 | tf_op jit(solution)/shard_map/vmap()/gather | solution.py:35
  3.9 1.7 %fusion.52 = (bf16[16,24,16,128]{3,2,1,0:T(8,128)(2,1)S(1)}, bf16[16,24,16,128]{3,2,1,0:T(8,128)(2,1)}) fusion(bf16[16,25,16,128]{3,2,1,0:T(8,128)(2,1)S(1)} %gather_fusion), kind=kLoop, calls=%fused_computation.110 | loop fusion | bytes 6291456 | tf_op jit(solution)/shard_map/slice | solution.py:36
  5.6 3.1 %fusion.21 = f32[16,16,128]{2,1,0:T(8,128)S(1)} fusion(bf16[24,128,128,1]{2,1,0,3:T(8,128)(2,1)} %constant.173, bf16[16,24,16,128]{3,2,1,0:T(8,128)(2,1)} %get-tuple-element.6, bf16[16,24,16,128]{3,2,1,0:T(8,128)(2,1)S(1)} %get-tuple-element.5, s32[16]{0:T(128)S(1)} %and_select_fusion.2), kind=kOutput, calls=%fused_computation.12 | convolution fusion | flops 612106240 | bytes 4063296 | tf_op jit(solution)/shard_map/wcbi,bif->wcf/dot_general | solution.py:44
  9.4 0.4 copy.49
  10.0 0.4 copy.48
  10.4 1.4 %maximum_bitcast_fusion = bf16[4,16,16,2,16]{4,3,2,1,0:T(2,128)(2,1)S(1)} fusion(bf16[16,16,1,4,16]{4,2,0,1,3:T(2,128)(2,1)S(1)} %copy.49, bf16[16,16,1,4,16]{4,2,0,1,3:T(2,128)(2,1)S(1)} %copy.48), kind=kLoop, calls=%fused_computation.22 | loop fusion | flops 131072 | bytes 131072 | tf_op jit(solution)/shard_map/transpose | solution.py:98
  11.8 0.8 %reshape.188 = bf16[4,16,512]{2,1,0:T(8,128)(2,1)S(1)} reshape(bf16[4,16,16,2,16]{4,3,2,1,0:T(2,128)(2,1)S(1)} %maximum_bitcast_fusion) | data formatting | bytes 131072 | tf_op jit(solution)/shard_map/reshape | solution.py:99
  12.6 3.9 %collective-permute-start.2 = (bf16[16,512]{1,0:T(8,128)(2,1)S(1)}, bf16[16,512]{1,0:T(8,128)(2,1)S(1)}, u32[]{:S(2)}, u32[]{:S(2)}) collective-permute-start(bf16[16,512]{1,0:T(8,128)(2,1)S(1)} %get-tuple-element.40), channel_id=1, source_target_pairs={{0,24},{8,0},{16,8},{24,16},{1,25},{9,1},{17,9},{25,17},{2,26},{10... | collective-permute-start | bytes 49160 | tf_op jit(solution)/shard_map/ppermute | solution.py:104
  16.5 0.5 collective-permute-start.1
  17.0 0.6 %collective-permute-start = (bf16[16,512]{1,0:T(8,128)(2,1)S(1)}, bf16[16,512]{1,0:T(8,128)(2,1)S(1)}, u32[]{:S(2)}, u32[]{:S(2)}) collective-permute-start(bf16[16,512]{1,0:T(8,128)(2,1)S(1)} %get-tuple-element.42), channel_id=1, source_target_pairs={{0,8},{8,16},{16,24},{24,0},{1,9},{9,17},{17,25},{25,1},{2,10},{10... | collective-permute-start | bytes 49160 | tf_op jit(solution)/shard_map/ppermute | solution.py:104
  18.0 2.3 %collective-permute-done.1 = bf16[16,512]{1,0:T(8,128)(2,1)S(1)} collective-permute-done((bf16[16,512]{1,0:T(8,128)(2,1)S(1)}, bf16[16,512]{1,0:T(8,128)(2,1)S(1)}, u32[]{:S(2)}, u32[]{:S(2)}) %collective-permute-start.1) | collective-permute-done | bytes 16416 | tf_op jit(solution)/shard_map/ppermute | solution.py:104
  20.3 1.4 %collective-permute-done = bf16[16,512]{1,0:T(8,128)(2,1)S(1)} collective-permute-done((bf16[16,512]{1,0:T(8,128)(2,1)S(1)}, bf16[16,512]{1,0:T(8,128)(2,1)S(1)}, u32[]{:S(2)}, u32[]{:S(2)}) %collective-permute-start) | collective-permute-done | bytes 16416 | tf_op jit(solution)/shard_map/ppermute | solution.py:104
  21.7 1.3 %collective-permute-start.5 = (bf16[16,2048]{1,0:T(8,128)(2,1)S(1)}, bf16[16,2048]{1,0:T(8,128)(2,1)S(1)}, u32[]{:S(2)}, u32[]{:S(2)}) collective-permute-start(bf16[16,2048]{1,0:T(8,128)(2,1)S(1)} %get-tuple-element.37), channel_id=1, source_target_pairs={{6,0},{7,1},{14,8},{15,9},{22,16},{23,17},{30,24},{31,25}} | collective-permute-start | bytes 196616 | tf_op jit(solution)/shard_map/ppermute | solution.py:73
  23.0 1.3 %collective-permute-start.4 = (bf16[16,2048]{1,0:T(8,128)(2,1)S(1)}, bf16[16,2048]{1,0:T(8,128)(2,1)S(1)}, u32[]{:S(2)}, u32[]{:S(2)}) collective-permute-start(bf16[16,2048]{1,0:T(8,128)(2,1)S(1)} %get-tuple-element.37), channel_id=1, source_target_pairs={{4,0},{5,1},{6,2},{7,3},{12,8},{13,9},{14,10},{15,11},{20,16},{21,... | collective-permute-start | bytes 196616 | tf_op jit(solution)/shard_map/ppermute | solution.py:73
  24.3 1.3 %collective-permute-start.3 = (bf16[16,2048]{1,0:T(8,128)(2,1)S(1)}, bf16[16,2048]{1,0:T(8,128)(2,1)S(1)}, u32[]{:S(2)}, u32[]{:S(2)}) collective-permute-start(bf16[16,2048]{1,0:T(8,128)(2,1)S(1)} %get-tuple-element.37), channel_id=1, source_target_pairs={{2,0},{3,1},{4,2},{5,3},{6,4},{7,5},{10,8},{11,9},{12,10},{13,11},... | collective-permute-start | bytes 196616 | tf_op jit(solution)/shard_map/ppermute | solution.py:73
  25.6 4.2 %collective-permute-done.5 = bf16[16,2048]{1,0:T(8,128)(2,1)S(1)} collective-permute-done((bf16[16,2048]{1,0:T(8,128)(2,1)S(1)}, bf16[16,2048]{1,0:T(8,128)(2,1)S(1)}, u32[]{:S(2)}, u32[]{:S(2)}) %collective-permute-start.5) | collective-permute-done | bytes 65568 | tf_op jit(solution)/shard_map/ppermute | solution.py:73
  29.7 1.5 %collective-permute-done.4 = bf16[16,2048]{1,0:T(8,128)(2,1)S(1)} collective-permute-done((bf16[16,2048]{1,0:T(8,128)(2,1)S(1)}, bf16[16,2048]{1,0:T(8,128)(2,1)S(1)}, u32[]{:S(2)}, u32[]{:S(2)}) %collective-permute-start.4) | collective-permute-done | bytes 65568 | tf_op jit(solution)/shard_map/ppermute | solution.py:73
  31.4 1.4 %collective-permute-done.6 = bf16[64,2048]{1,0:T(8,128)(2,1)S(1)} collective-permute-done((bf16[64,2048]{1,0:T(8,128)(2,1)S(1)}, bf16[64,2048]{1,0:T(8,128)(2,1)S(1)}, u32[]{:S(2)}, u32[]{:S(2)}) %collective-permute-start.6) | collective-permute-done | bytes 262176 | tf_op jit(solution)/shard_map/ppermute | solution.py:74
  34.1 0.4 stack.33
  34.6 0.4 copy.53
  35.0 0.7 %convolution_bitcast_fusion = f32[16,2,16,144]{3,2,1,0:T(8,128)S(1)} fusion(bf16[144,64,2,16,1]{0,3,2,1,4:T(8,128)(2,1)S(1)} %bitcast.132, bf16[1,16,64,2,16]{2,1,3,0,4:T(8,128)(2,1)S(1)} %maximum_bitcast_fusion.1, bf16[1,16,64,2,16]{2,1,3,0,4:T(8,128)(2,1)S(1)} %copy.53), kind=kOutput, calls=%fused_computation.11 | convolution fusion | flops 18939904 | bytes 1015808 | tf_op jit(solution)/shard_map/ocspn,jspn->nocj/dot_general | solution.py:116
  35.8 0.6 %fusion.54 = (f32[16,2,1,128]{3,2,1,0:T(1,128)S(1)}, f32[16,2,1,128]{3,2,1,0:T(1,128)S(1)}, f32[16,2,1,128]{3,2,1,0:T(1,128)S(1)}, f32[16,2,1,128]{3,2,1,0:T(1,1...) fusion(f32[16,2,16,144]{3,2,1,0:T(8,128)S(1)} %convolution_bitc, ...), kind=kLoop, calls=%fused_computation.112 | loop fusion | bytes 524288 | tf_op jit(solution)/shard_map/slice | solution.py:117
  37.0 1.3 %collective-permute-start.9 = (f32[64,512]{1,0:T(8,128)S(1)}, f32[64,512]{1,0:T(8,128)S(1)}, u32[]{:S(2)}, u32[]{:S(2)}) collective-permute-start(f32[64,512]{1,0:T(8,128)S(1)} %get-tuple-element.10), channel_id=1, source_target_pairs={{8,0},{16,8},{9,1},{17,9},{10,2},{18,10},{11,3},{19,11},{12,4},{20... | collective-permute-start | bytes 393224 | tf_op jit(solution)/shard_map/ppermute | solution.py:129
  38.3 1.3 %collective-permute-start.8 = (f32[64,512]{1,0:T(8,128)S(1)}, f32[64,512]{1,0:T(8,128)S(1)}, u32[]{:S(2)}, u32[]{:S(2)}) collective-permute-start(f32[64,512]{1,0:T(8,128)S(1)} %get-tuple-element.11), channel_id=1, source_target_pairs={{16,0},{24,8},{17,1},{25,9},{18,2},{26,10},{19,3},{27,11},{20,4},{... | collective-permute-start | bytes 393224 | tf_op jit(solution)/shard_map/ppermute | solution.py:129
  39.6 4.6 %collective-permute-start.7 = (f32[64,512]{1,0:T(8,128)S(1)}, f32[64,512]{1,0:T(8,128)S(1)}, u32[]{:S(2)}, u32[]{:S(2)}) collective-permute-start(f32[64,512]{1,0:T(8,128)S(1)} %get-tuple-element.12), channel_id=1, source_target_pairs={{0,8},{24,0},{1,9},{25,1},{2,10},{26,2},{3,11},{27,3},{4,12},{28,4... | collective-permute-start | bytes 393224 | tf_op jit(solution)/shard_map/ppermute | solution.py:129
  44.4 1.3 %collective-permute-done.8 = f32[64,512]{1,0:T(8,128)S(1)} collective-permute-done((f32[64,512]{1,0:T(8,128)S(1)}, f32[64,512]{1,0:T(8,128)S(1)}, u32[]{:S(2)}, u32[]{:S(2)}) %collective-permute-start.8) | collective-permute-done | bytes 131104 | tf_op jit(solution)/shard_map/ppermute | solution.py:129
  45.7 3.1 %collective-permute-done.7 = f32[64,512]{1,0:T(8,128)S(1)} collective-permute-done((f32[64,512]{1,0:T(8,128)S(1)}, f32[64,512]{1,0:T(8,128)S(1)}, u32[]{:S(2)}, u32[]{:S(2)}) %collective-permute-start.7) | collective-permute-done | bytes 131104 | tf_op jit(solution)/shard_map/ppermute | solution.py:129
  48.9 0.6 %gather_fusion.1 = f32[4,64,512]{2,1,0:T(8,128)S(1)} fusion(f32[4,64,512]{2,1,0:T(8,128)S(1)} %pad_maximum_fusion, s32[1024]{0:T(1024)S(1)} %pad_clamp_fusion), kind=kCustom, calls=%fused_computation.1 | custom fusion | bytes 1048592 | tf_op jit(solution)/shard_map/jit(_take)/gather | solution.py:134
  50.1 1.1 %copy.74 = f32[64,16,128]{2,1,0:T(8,128)} copy(f32[64,16,128]{0,2,1:T(8,128)S(1)} %bitcast.134) | data formatting | bytes 1048576 | tf_op jit(solution)/shard_map/reshape | solution.py:135
  (66 shorter events, 4.3 us)
Async XLA Ops:
  5.6 3.3 %copy-start = (s32[16]{0:T(128)S(1)}, s32[16]{0:T(128)}, u32[]{:S(2)}) copy-start(s32[16]{0:T(128)} %param.6) | copy-start | bytes 196
  12.6 5.4 %collective-permute-start.2 = (bf16[16,512]{1,0:T(8,128)(2,1)S(1)}, bf16[16,512]{1,0:T(8,128)(2,1)S(1)}, u32[]{:S(2)}, u32[]{:S(2)}) collective-permute-start(bf16[16,512]{1,0:T(8,128)(2,1)S(1)} %get-tuple-element.40), channel_id=1, source_target_pairs={{0,24},{8,0},{16,8},{24,16},{1,25},{9,1},{17,9},{25,17},{2,26},{10... | collective-permute-start | bytes 49160 | tf_op jit(solution)/shard_map/ppermute | solution.py:104
  16.5 3.7 %collective-permute-start.1 = (bf16[16,512]{1,0:T(8,128)(2,1)S(1)}, bf16[16,512]{1,0:T(8,128)(2,1)S(1)}, u32[]{:S(2)}, u32[]{:S(2)}) collective-permute-start(bf16[16,512]{1,0:T(8,128)(2,1)S(1)} %get-tuple-element.41), channel_id=1, source_target_pairs={{0,16},{8,24},{16,0},{24,8},{1,17},{9,25},{17,1},{25,9},{2,18},{10... | collective-permute-start | bytes 49160 | tf_op jit(solution)/shard_map/ppermute | solution.py:104
  17.0 4.6 %collective-permute-start = (bf16[16,512]{1,0:T(8,128)(2,1)S(1)}, bf16[16,512]{1,0:T(8,128)(2,1)S(1)}, u32[]{:S(2)}, u32[]{:S(2)}) collective-permute-start(bf16[16,512]{1,0:T(8,128)(2,1)S(1)} %get-tuple-element.42), channel_id=1, source_target_pairs={{0,8},{8,16},{16,24},{24,0},{1,9},{9,17},{17,25},{25,1},{2,10},{10... | collective-permute-start | bytes 49160 | tf_op jit(solution)/shard_map/ppermute | solution.py:104
  21.7 8.1 %collective-permute-start.5 = (bf16[16,2048]{1,0:T(8,128)(2,1)S(1)}, bf16[16,2048]{1,0:T(8,128)(2,1)S(1)}, u32[]{:S(2)}, u32[]{:S(2)}) collective-permute-start(bf16[16,2048]{1,0:T(8,128)(2,1)S(1)} %get-tuple-element.37), channel_id=1, source_target_pairs={{6,0},{7,1},{14,8},{15,9},{22,16},{23,17},{30,24},{31,25}} | collective-permute-start | bytes 196616 | tf_op jit(solution)/shard_map/ppermute | solution.py:73
  23.0 8.2 %collective-permute-start.4 = (bf16[16,2048]{1,0:T(8,128)(2,1)S(1)}, bf16[16,2048]{1,0:T(8,128)(2,1)S(1)}, u32[]{:S(2)}, u32[]{:S(2)}) collective-permute-start(bf16[16,2048]{1,0:T(8,128)(2,1)S(1)} %get-tuple-element.37), channel_id=1, source_target_pairs={{4,0},{5,1},{6,2},{7,3},{12,8},{13,9},{14,10},{15,11},{20,16},{21,... | collective-permute-start | bytes 196616 | tf_op jit(solution)/shard_map/ppermute | solution.py:73
  24.3 7.0 %collective-permute-start.3 = (bf16[16,2048]{1,0:T(8,128)(2,1)S(1)}, bf16[16,2048]{1,0:T(8,128)(2,1)S(1)}, u32[]{:S(2)}, u32[]{:S(2)}) collective-permute-start(bf16[16,2048]{1,0:T(8,128)(2,1)S(1)} %get-tuple-element.37), channel_id=1, source_target_pairs={{2,0},{3,1},{4,2},{5,3},{6,4},{7,5},{10,8},{11,9},{12,10},{13,11},... | collective-permute-start | bytes 196616 | tf_op jit(solution)/shard_map/ppermute | solution.py:73
  31.2 1.6 %collective-permute-start.6 = (bf16[64,2048]{1,0:T(8,128)(2,1)S(1)}, bf16[64,2048]{1,0:T(8,128)(2,1)S(1)}, u32[]{:S(2)}, u32[]{:S(2)}) collective-permute-start(bf16[64,2048]{1,0:T(8,128)(2,1)S(1)} %pad_maximum_fusion.1), channel_id=1, source_target_pairs={{0,1},{1,0},{2,3},{3,2},{4,5},{5,4},{6,7},{7,6},{8,9},{9,8},{10,11... | collective-permute-start | bytes 786440 | tf_op jit(solution)/shard_map/ppermute | solution.py:74
  37.0 7.4 %collective-permute-start.9 = (f32[64,512]{1,0:T(8,128)S(1)}, f32[64,512]{1,0:T(8,128)S(1)}, u32[]{:S(2)}, u32[]{:S(2)}) collective-permute-start(f32[64,512]{1,0:T(8,128)S(1)} %get-tuple-element.10), channel_id=1, source_target_pairs={{8,0},{16,8},{9,1},{17,9},{10,2},{18,10},{11,3},{19,11},{12,4},{20... | collective-permute-start | bytes 393224 | tf_op jit(solution)/shard_map/ppermute | solution.py:129
  38.3 7.4 %collective-permute-start.8 = (f32[64,512]{1,0:T(8,128)S(1)}, f32[64,512]{1,0:T(8,128)S(1)}, u32[]{:S(2)}, u32[]{:S(2)}) collective-permute-start(f32[64,512]{1,0:T(8,128)S(1)} %get-tuple-element.11), channel_id=1, source_target_pairs={{16,0},{24,8},{17,1},{25,9},{18,2},{26,10},{19,3},{27,11},{20,4},{... | collective-permute-start | bytes 393224 | tf_op jit(solution)/shard_map/ppermute | solution.py:129
  39.6 9.2 %collective-permute-start.7 = (f32[64,512]{1,0:T(8,128)S(1)}, f32[64,512]{1,0:T(8,128)S(1)}, u32[]{:S(2)}, u32[]{:S(2)}) collective-permute-start(f32[64,512]{1,0:T(8,128)S(1)} %get-tuple-element.12), channel_id=1, source_target_pairs={{0,8},{24,0},{1,9},{25,1},{2,10},{26,2},{3,11},{27,3},{4,12},{28,4... | collective-permute-start | bytes 393224 | tf_op jit(solution)/shard_map/ppermute | solution.py:129

commit v4 on v3

--- a/solution.py
+++ b/solution.py
@@ -5,6 +5,8 @@
 import ml_dtypes
 import numpy as np
 from jax import lax
+from jax.experimental import pallas as pl
+from jax.experimental.pallas import tpu as pltpu
 from jax.sharding import PartitionSpec as P
 
 NF = 64
@@ -24,39 +26,59 @@
     return table.astype(ml_dtypes.bfloat16)
 
 
-def window_spectra(record_rows, starts):
-    channels, length = record_rows.shape
-    blocks = length // LANES
-    per_window = NT // LANES
-    by_block = record_rows.reshape(channels, blocks, LANES).transpose(1, 0, 2)
-    by_block = jnp.concatenate([by_block, jnp.zeros((1, channels, LANES), by_block.dtype)], axis=0)
-    first_block = starts // LANES
-    shift = starts % LANES
-    chunks = jax.vmap(lambda q: lax.dynamic_slice_in_dim(by_block, q, per_window + 1, axis=0))(first_block)
-    pairs = jnp.concatenate([chunks[:, :per_window], chunks[:, 1:]], axis=-1)
+def whiten_kernel(starts_ref, record_hbm, table_ref, near_ref, count_ref, live_ref, out_ref, chunks, moved_rows, sems):
+    windows, channels, span = chunks.shape
+    blocks = NT // LANES
+    last = record_hbm.shape[1] - span
+    shifts = []
+    for w in range(windows):
+        first = starts_ref[w]
+        base = pl.multiple_of(jnp.minimum(first - first % LANES, last), LANES)
+        pltpu.make_async_copy(record_hbm.at[:, pl.ds(base, span)], chunks.at[w], sems.at[w]).start()
+        shifts.append(first - base)
     src = lax.broadcasted_iota(jnp.int32, (2 * LANES, LANES), 0)
     dst = lax.broadcasted_iota(jnp.int32, (2 * LANES, LANES), 1)
-    pick = (src[None] == dst[None] + shift[:, None, None]).astype(jnp.bfloat16)
-    windows = jnp.einsum(
-        "wbcm,wmi->wcbi", pairs, pick, preferred_element_type=jnp.float32
-    ).astype(jnp.bfloat16)
-    table = jnp.asarray(spectral_table()).reshape(per_window, LANES, 2 * NF)
-    return jnp.einsum("wcbi,bif->wcf", windows, table, preferred_element_type=jnp.float32)
+    for w in range(windows):
+        pltpu.make_async_copy(record_hbm.at[:, pl.ds(0, span)], chunks.at[w], sems.at[w]).wait()
+        pick = (src == dst + shifts[w]).astype(jnp.bfloat16)
+        pairs = jnp.concatenate([chunks[w, :, pl.ds(b * LANES, 2 * LANES)] for b in range(blocks)], axis=0)
+        moved = jnp.dot(pairs, pick, preferred_element_type=jnp.float32).astype(jnp.bfloat16)
+        for b in range(blocks):
+            moved_rows[b, pl.ds(w * channels, channels), :] = moved[b * channels : (b + 1) * channels]
+    spectra = jnp.zeros(out_ref.shape, jnp.float32)
+    for b in range(blocks):
+        spectra = spectra + jnp.dot(moved_rows[b], table_ref[b], preferred_element_type=jnp.float32)
+    power = spectra * spectra
+    smooth = jnp.dot(
+        power, near_ref[...], precision=lax.Precision.HIGHEST, preferred_element_type=jnp.float32
+    ) / count_ref[...]
+    water_level = jnp.sum(power, axis=-1, keepdims=True) / NF
+    gain_of = live_ref[...] / jnp.sqrt(smooth + 0.1 * water_level + 1e-06)
+    out_ref[...] = (spectra * gain_of).astype(out_ref.dtype)
 
 
 def whiten(record_rows, starts, live_mask):
-    spectra = window_spectra(record_rows, starts)
-    real_part = spectra[..., :NF]
-    imag_part = spectra[..., NF:]
-    power_bins = real_part * real_part + imag_part * imag_part
-    bin_index = jnp.arange(NF, dtype=jnp.int32)
-    nearby = (jnp.abs(bin_index[:, None] - bin_index[None, :]) <= 4).astype(jnp.float32)
-    smooth = jnp.dot(power_bins, nearby, precision=lax.Precision.HIGHEST) / jnp.sum(nearby, axis=0)
-    water_level = jnp.mean(power_bins, axis=-1, keepdims=True)
-    gain_of = live_mask.astype(jnp.float32)[None, :, None] / jnp.sqrt(
-        smooth + 0.1 * water_level + 1e-06
-    )
-    return jnp.concatenate([real_part * gain_of, imag_part * gain_of], axis=-1).astype(jnp.bfloat16)
+    channels, _ = record_rows.shape
+    windows = starts.shape[0]
+    blocks = NT // LANES
+    table = jnp.asarray(spectral_table()).reshape(blocks, LANES, 2 * NF)
+    lane_bin = np.arange(2 * NF) % NF
+    near = (np.abs(lane_bin[:, None] - lane_bin[None, :]) <= 4).astype(np.float32)
+    count = near[:NF].sum(axis=0, keepdims=True)
+    live_rows = jnp.tile(live_mask.astype(jnp.float32), windows)[:, None]
+    vmem = pl.BlockSpec(memory_space=pltpu.VMEM)
+    out = pl.pallas_call(
+        whiten_kernel,
+        out_shape=jax.ShapeDtypeStruct((windows * channels, 2 * NF), jnp.bfloat16),
+        in_specs=[pl.BlockSpec(memory_space=pltpu.SMEM), pl.BlockSpec(memory_space=pl.ANY), vmem, vmem, vmem, vmem],
+        out_specs=vmem,
+        scratch_shapes=[
+            pltpu.VMEM((windows, channels, NT + LANES), jnp.bfloat16),
+            pltpu.VMEM((blocks, windows * channels, LANES), jnp.bfloat16),
+            pltpu.SemaphoreType.DMA((windows,)),
+        ],
+    )(starts, record_rows, table, jnp.asarray(near), jnp.asarray(count), live_rows)
+    return out.reshape(windows, channels, 2 * NF)
 
 
 def halo(mine, hops, fibre_count):

time: 51.6 us -> 52.9 us (1.025)
  Pallas kernels: 0 us -> 8.05 us
  matrix products: 4.14 us -> 0.73 us
  other arithmetic: 3.51 us -> 0.57 us
  waiting for transfers between devices: 15.8 us -> 17.4 us
  local copies, waits for them, and re-layouts: 11.2 us -> 10 us
  starting transfers between devices: 16.1 us -> 15.4 us
    pallas_call x0 -> x1, Pallas kernels: none -> 8.05 us  [whiten(): pl.pallas_call(whiten_kernel, out_shape=jax.ShapeDtypeStruct((windows * c...]
    dot_general x2 -> x0, matrix products: 3.42 us -> none  [the longest x1 3.13 us: window_spectra(): jnp.einsum('wcbi,bif->wcf', windows, table, preferred_element_type=jnp.fl...]
    another operation x1 -> x4, local copies, waits for them, and re-layouts: 0.12 us -> 2.36 us  [the longest x2 1.6 us: shards(): own_block.reshape(windows_count, block, 2, seg_count, bins_each)]
    ppermute x3, waiting for transfers between devices: 5.65 us -> 7.84 us  [halo(): own.append(lax.ppermute(mine, 'fibre', pairs))]
    ppermute x3, waiting for transfers between devices: 4.04 us -> 2.3 us  [shards(): gathered.append(lax.ppermute(sent, 'seg', pairs))]
    slice x1 -> x0, local copies, waits for them, and re-layouts: 1.72 us -> none  [window_spectra(): pairs = jnp.concatenate([chunks[:, :per_window], chunks[:, 1:]], axis=-1)]
    ppermute x3, starting transfers between devices: 7.13 us -> 5.47 us  [shards(): collected.append(lax.ppermute(sent, 'seg', pairs))]
    transpose x1 -> x0, other arithmetic: 1.38 us -> none  [shards(): own_block.reshape(windows_count, block, 2, seg_count, bins_each)]
where the time goes in v4:
time: 52.9 us; the launch traced here: 52.5 us
  waiting for transfers between devices  17.4 us (33%)
  starting transfers between devices  15.4 us (29%)
  local copies, waits for them, and re-layouts  10 us (19%)
  Pallas kernels  8.05 us (15%)
  matrix products  0.73 us (1%)
  other arithmetic  0.57 us (1%)
    pallas_call x1, Pallas kernels, whiten(): pl.pallas_call(whiten_kernel, out_shape=jax.ShapeDtypeStruct((windows * c...  8.05 us
    ppermute x3, waiting for transfers between devices, halo(): own.append(lax.ppermute(mine, 'fibre', pairs))  7.84 us
    ppermute x3, starting transfers between devices, shards(): gathered.append(lax.ppermute(sent, 'seg', pairs))  5.94 us
    ppermute x3, waiting for transfers between devices, shards(): collected.append(lax.ppermute(sent, 'seg', pairs))  5.82 us
    ppermute x3, starting transfers between devices, shards(): collected.append(lax.ppermute(sent, 'seg', pairs))  5.47 us
    ppermute x3, starting transfers between devices, halo(): own.append(lax.ppermute(mine, 'fibre', pairs))  3.88 us
    unnamed x32, local copies, waits for them, and re-layouts  2.34 us
    ppermute x3, waiting for transfers between devices, shards(): gathered.append(lax.ppermute(sent, 'seg', pairs))  2.3 us
  transfers between devices with their start and end apart: 10, of which 9 were waited for; matrix products, arithmetic and copies ran while one was open for 0% of the time, Pallas kernels for 0%

profile of v4, /device:TPU:0, one launch (start us, length us, event | category | flops | bytes accessed | tf_op | source)
XLA Modules:
  0.0 52.5 jit_solution(13191016960993380803)
XLA Ops:
  0.0 0.7 %copy-done.1 = s32[16]{0:T(128)S(1)} copy-done((s32[16]{0:T(128)S(1)}, s32[16]{0:T(128)}, u32[]{:S(2)}) %copy-start.1) | copy-done | bytes 88
  0.7 0.8 %broadcast_in_dim_tile.4.live_ref = f32[256,1]{1,0:T(8,128)} reshape(f32[16,16]{1,0:T(8,128)S(1)} %tile.2) | data formatting | bytes 2048 | tf_op jit(solution)/shard_map/broadcast_in_dim;tile | solution.py:68
  1.4 8.0 %shard_map.64 = bf16[256,128]{1,0:T(8,128)(2,1)} custom-call(s32[16]{0:T(128)} %bitcast.113, bf16[16,27648]{1,0:T(8,128)(2,1)} %bitcast.93, bf16[24,128,128]{2,1,0:T(8,128)(2,1)} %constant.111.table_ref, f32[128,128]{1,0:T(8,128)} %constant.103.clone.near_ref, f32[1,128]{1,0:T(1,128)} %constant.104.clone.count_ref, f32[256,1]{1,0:T(8,128)} %broadcast_in_dim_tile.4.live_ref), custom_call_target="tpu_custom_call" | custom-call | tf_op jit(solution)/shard_map/pallas_call | solution.py:70
  9.5 1.2 %reshape_reshape.3 = bf16[16,16,2,4,16]{4,3,2,1,0:T(4,128)(2,1)S(1)} reshape(bf16[256,128]{1,0:T(8,128)(2,1)} %shard_map.64) | data formatting | bytes 131072 | tf_op jit(solution)/shard_map/reshape;reshape | solution.py:120
  10.7 0.4 copy.101
  11.1 0.8 %reshape.78 = bf16[4,16,512]{2,1,0:T(8,128)(2,1)S(1)} reshape(bf16[4,16,16,2,16]{4,3,2,1,0:T(2,128)(2,1)S(1)} %bitcast.91) | data formatting | bytes 131072 | tf_op jit(solution)/shard_map/reshape | solution.py:121
  11.9 3.0 %collective-permute-start = (bf16[16,512]{1,0:T(8,128)(2,1)S(1)}, bf16[16,512]{1,0:T(8,128)(2,1)S(1)}, u32[]{:S(2)}, u32[]{:S(2)}) collective-permute-start(bf16[16,512]{1,0:T(8,128)(2,1)S(1)} %get-tuple-element.38), channel_id=1, source_target_pairs={{0,8},{8,16},{16,24},{24,0},{1,9},{9,17},{17,25},{25,1},{2,10},{10... | collective-permute-start | bytes 49160 | tf_op jit(solution)/shard_map/ppermute | solution.py:126
  14.9 1.5 %collective-permute-start.1 = (bf16[16,512]{1,0:T(8,128)(2,1)S(1)}, bf16[16,512]{1,0:T(8,128)(2,1)S(1)}, u32[]{:S(2)}, u32[]{:S(2)}) collective-permute-start(bf16[16,512]{1,0:T(8,128)(2,1)S(1)} %get-tuple-element.37), channel_id=1, source_target_pairs={{0,16},{8,24},{16,0},{24,8},{1,17},{9,25},{17,1},{25,9},{2,18},{10... | collective-permute-start | bytes 49160 | tf_op jit(solution)/shard_map/ppermute | solution.py:126
  16.4 1.4 %collective-permute-start.2 = (bf16[16,512]{1,0:T(8,128)(2,1)S(1)}, bf16[16,512]{1,0:T(8,128)(2,1)S(1)}, u32[]{:S(2)}, u32[]{:S(2)}) collective-permute-start(bf16[16,512]{1,0:T(8,128)(2,1)S(1)} %get-tuple-element.36), channel_id=1, source_target_pairs={{0,24},{8,0},{16,8},{24,16},{1,25},{9,1},{17,9},{25,17},{2,26},{10... | collective-permute-start | bytes 49160 | tf_op jit(solution)/shard_map/ppermute | solution.py:126
  17.8 0.8 %collective-permute-done.1 = bf16[16,512]{1,0:T(8,128)(2,1)S(1)} collective-permute-done((bf16[16,512]{1,0:T(8,128)(2,1)S(1)}, bf16[16,512]{1,0:T(8,128)(2,1)S(1)}, u32[]{:S(2)}, u32[]{:S(2)}) %collective-permute-start.1) | collective-permute-done | bytes 16416 | tf_op jit(solution)/shard_map/ppermute | solution.py:126
  18.6 1.5 %collective-permute-done.2 = bf16[16,512]{1,0:T(8,128)(2,1)S(1)} collective-permute-done((bf16[16,512]{1,0:T(8,128)(2,1)S(1)}, bf16[16,512]{1,0:T(8,128)(2,1)S(1)}, u32[]{:S(2)}, u32[]{:S(2)}) %collective-permute-start.2) | collective-permute-done | bytes 16416 | tf_op jit(solution)/shard_map/ppermute | solution.py:126
  20.2 1.3 %collective-permute-start.3 = (bf16[16,2048]{1,0:T(8,128)(2,1)S(1)}, bf16[16,2048]{1,0:T(8,128)(2,1)S(1)}, u32[]{:S(2)}, u32[]{:S(2)}) collective-permute-start(bf16[16,2048]{1,0:T(8,128)(2,1)S(1)} %get-tuple-element.33), channel_id=1, source_target_pairs={{2,0},{3,1},{4,2},{5,3},{6,4},{7,5},{10,8},{11,9},{12,10},{13,11},... | collective-permute-start | bytes 196616 | tf_op jit(solution)/shard_map/ppermute | solution.py:95
  21.5 1.3 %collective-permute-start.4 = (bf16[16,2048]{1,0:T(8,128)(2,1)S(1)}, bf16[16,2048]{1,0:T(8,128)(2,1)S(1)}, u32[]{:S(2)}, u32[]{:S(2)}) collective-permute-start(bf16[16,2048]{1,0:T(8,128)(2,1)S(1)} %get-tuple-element.33), channel_id=1, source_target_pairs={{4,0},{5,1},{6,2},{7,3},{12,8},{13,9},{14,10},{15,11},{20,16},{21,... | collective-permute-start | bytes 196616 | tf_op jit(solution)/shard_map/ppermute | solution.py:95
  22.8 1.3 %collective-permute-start.5 = (bf16[16,2048]{1,0:T(8,128)(2,1)S(1)}, bf16[16,2048]{1,0:T(8,128)(2,1)S(1)}, u32[]{:S(2)}, u32[]{:S(2)}) collective-permute-start(bf16[16,2048]{1,0:T(8,128)(2,1)S(1)} %get-tuple-element.33), channel_id=1, source_target_pairs={{6,0},{7,1},{14,8},{15,9},{22,16},{23,17},{30,24},{31,25}} | collective-permute-start | bytes 196616 | tf_op jit(solution)/shard_map/ppermute | solution.py:95
  24.1 2.7 %collective-permute-done.3 = bf16[16,2048]{1,0:T(8,128)(2,1)S(1)} collective-permute-done((bf16[16,2048]{1,0:T(8,128)(2,1)S(1)}, bf16[16,2048]{1,0:T(8,128)(2,1)S(1)}, u32[]{:S(2)}, u32[]{:S(2)}) %collective-permute-start.3) | collective-permute-done | bytes 65568 | tf_op jit(solution)/shard_map/ppermute | solution.py:95
  26.8 2.7 %collective-permute-done.4 = bf16[16,2048]{1,0:T(8,128)(2,1)S(1)} collective-permute-done((bf16[16,2048]{1,0:T(8,128)(2,1)S(1)}, bf16[16,2048]{1,0:T(8,128)(2,1)S(1)}, u32[]{:S(2)}, u32[]{:S(2)}) %collective-permute-start.4) | collective-permute-done | bytes 65568 | tf_op jit(solution)/shard_map/ppermute | solution.py:95
  29.4 2.5 %collective-permute-done.5 = bf16[16,2048]{1,0:T(8,128)(2,1)S(1)} collective-permute-done((bf16[16,2048]{1,0:T(8,128)(2,1)S(1)}, bf16[16,2048]{1,0:T(8,128)(2,1)S(1)}, u32[]{:S(2)}, u32[]{:S(2)}) %collective-permute-start.5) | collective-permute-done | bytes 65568 | tf_op jit(solution)/shard_map/ppermute | solution.py:95
  32.1 1.4 %collective-permute-done.6 = bf16[64,2048]{1,0:T(8,128)(2,1)S(1)} collective-permute-done((bf16[64,2048]{1,0:T(8,128)(2,1)S(1)}, bf16[64,2048]{1,0:T(8,128)(2,1)S(1)}, u32[]{:S(2)}, u32[]{:S(2)}) %collective-permute-start.6) | collective-permute-done | bytes 262176 | tf_op jit(solution)/shard_map/ppermute | solution.py:96
  34.0 0.5 copy-done
  35.3 0.6 %slice-done = bf16[16,2048]{1,0:T(8,128)(2,1)S(1)} async-done(((bf16[128,2048]{1,0:T(8,128)(2,1)}), bf16[16,2048]{1,0:T(8,128)(2,1)S(1)}, s32[]{:S(2)}) %slice-start) | async-done | bytes 65560 | tf_op jit(solution)/shard_map/stack | solution.py:137
  35.9 0.4 stack.33
  36.3 0.4 copy.53
  36.8 0.7 %convolution_bitcast_fusion = f32[16,2,16,144]{3,2,1,0:T(8,128)S(1)} fusion(bf16[144,64,2,16,1]{0,3,2,1,4:T(8,128)(2,1)S(1)} %bitcast.87, bf16[1,16,64,2,16]{2,1,3,0,4:T(8,128)(2,1)S(1)} %maximum_bitcast_fusion, bf16[1,16,64,2,16]{2,1,3,0,4:T(8,128)(2,1)S(1)} %copy.53), kind=kOutput, calls=%fused_computation.1 | convolution fusion | flops 18939904 | bytes 1015808 | tf_op jit(solution)/shard_map/ocspn,jspn->nocj/dot_general | solution.py:138
  37.5 0.6 %fusion.9 = (f32[16,2,1,128]{3,2,1,0:T(1,128)S(1)}, f32[16,2,1,128]{3,2,1,0:T(1,128)S(1)}, f32[16,2,1,128]{3,2,1,0:T(1,128)S(1)}, f32[16,2,1,128]{3,2,1,0:T(1,12...) fusion(f32[16,2,16,144]{3,2,1,0:T(8,128)S(1)} %convolution_bitc, ...), kind=kLoop, calls=%fused_computation.69 | loop fusion | bytes 524288 | tf_op jit(solution)/shard_map/slice | solution.py:139
  38.7 2.9 %collective-permute-start.7 = (f32[64,512]{1,0:T(8,128)S(1)}, f32[64,512]{1,0:T(8,128)S(1)}, u32[]{:S(2)}, u32[]{:S(2)}) collective-permute-start(f32[64,512]{1,0:T(8,128)S(1)} %get-tuple-element.10), channel_id=1, source_target_pairs={{0,8},{24,0},{1,9},{25,1},{2,10},{26,2},{3,11},{27,3},{4,12},{28,4... | collective-permute-start | bytes 393224 | tf_op jit(solution)/shard_map/ppermute | solution.py:151
  41.6 1.3 %collective-permute-start.8 = (f32[64,512]{1,0:T(8,128)S(1)}, f32[64,512]{1,0:T(8,128)S(1)}, u32[]{:S(2)}, u32[]{:S(2)}) collective-permute-start(f32[64,512]{1,0:T(8,128)S(1)} %get-tuple-element.9), channel_id=1, source_target_pairs={{16,0},{24,8},{17,1},{25,9},{18,2},{26,10},{19,3},{27,11},{20,4},{... | collective-permute-start | bytes 393224 | tf_op jit(solution)/shard_map/ppermute | solution.py:151
  42.9 1.3 %collective-permute-start.9 = (f32[64,512]{1,0:T(8,128)S(1)}, f32[64,512]{1,0:T(8,128)S(1)}, u32[]{:S(2)}, u32[]{:S(2)}) collective-permute-start(f32[64,512]{1,0:T(8,128)S(1)} %get-tuple-element.8), channel_id=1, source_target_pairs={{8,0},{16,8},{9,1},{17,9},{10,2},{18,10},{11,3},{19,11},{12,4},{20... | collective-permute-start | bytes 393224 | tf_op jit(solution)/shard_map/ppermute | solution.py:151
  44.2 2.9 %collective-permute-done.7 = f32[64,512]{1,0:T(8,128)S(1)} collective-permute-done((f32[64,512]{1,0:T(8,128)S(1)}, f32[64,512]{1,0:T(8,128)S(1)}, u32[]{:S(2)}, u32[]{:S(2)}) %collective-permute-start.7) | collective-permute-done | bytes 131104 | tf_op jit(solution)/shard_map/ppermute | solution.py:151
  47.1 2.7 %collective-permute-done.8 = f32[64,512]{1,0:T(8,128)S(1)} collective-permute-done((f32[64,512]{1,0:T(8,128)S(1)}, f32[64,512]{1,0:T(8,128)S(1)}, u32[]{:S(2)}, u32[]{:S(2)}) %collective-permute-start.8) | collective-permute-done | bytes 131104 | tf_op jit(solution)/shard_map/ppermute | solution.py:151
  50.1 0.6 %gather_fusion = f32[4,64,512]{2,1,0:T(8,128)S(1)} fusion(f32[4,64,512]{2,1,0:T(8,128)S(1)} %pad_maximum_fusion, s32[1024]{0:T(1024)S(1)} %pad_clamp_fusion), kind=kCustom, calls=%fused_computation | custom fusion | bytes 1048592 | tf_op jit(solution)/shard_map/jit(_take)/gather | solution.py:156
  50.7 0.3 copy.72
  51.4 1.1 %copy.74 = f32[64,16,128]{2,1,0:T(8,128)} copy(f32[64,16,128]{0,2,1:T(8,128)S(1)} %bitcast.89) | data formatting | bytes 1048576 | tf_op jit(solution)/shard_map/reshape | solution.py:157
  (57 shorter events, 2.5 us)
Async XLA Ops:
  0.0 0.7 %copy-start.1 = (s32[16]{0:T(128)S(1)}, s32[16]{0:T(128)}, u32[]{:S(2)}) copy-start(s32[16]{0:T(128)} %param.8) | copy-start | bytes 196
  11.9 5.9 %collective-permute-start = (bf16[16,512]{1,0:T(8,128)(2,1)S(1)}, bf16[16,512]{1,0:T(8,128)(2,1)S(1)}, u32[]{:S(2)}, u32[]{:S(2)}) collective-permute-start(bf16[16,512]{1,0:T(8,128)(2,1)S(1)} %get-tuple-element.38), channel_id=1, source_target_pairs={{0,8},{8,16},{16,24},{24,0},{1,9},{9,17},{17,25},{25,1},{2,10},{10... | collective-permute-start | bytes 49160 | tf_op jit(solution)/shard_map/ppermute | solution.py:126
  14.9 3.7 %collective-permute-start.1 = (bf16[16,512]{1,0:T(8,128)(2,1)S(1)}, bf16[16,512]{1,0:T(8,128)(2,1)S(1)}, u32[]{:S(2)}, u32[]{:S(2)}) collective-permute-start(bf16[16,512]{1,0:T(8,128)(2,1)S(1)} %get-tuple-element.37), channel_id=1, source_target_pairs={{0,16},{8,24},{16,0},{24,8},{1,17},{9,25},{17,1},{25,9},{2,18},{10... | collective-permute-start | bytes 49160 | tf_op jit(solution)/shard_map/ppermute | solution.py:126
  16.4 3.7 %collective-permute-start.2 = (bf16[16,512]{1,0:T(8,128)(2,1)S(1)}, bf16[16,512]{1,0:T(8,128)(2,1)S(1)}, u32[]{:S(2)}, u32[]{:S(2)}) collective-permute-start(bf16[16,512]{1,0:T(8,128)(2,1)S(1)} %get-tuple-element.36), channel_id=1, source_target_pairs={{0,24},{8,0},{16,8},{24,16},{1,25},{9,1},{17,9},{25,17},{2,26},{10... | collective-permute-start | bytes 49160 | tf_op jit(solution)/shard_map/ppermute | solution.py:126
  20.2 6.6 %collective-permute-start.3 = (bf16[16,2048]{1,0:T(8,128)(2,1)S(1)}, bf16[16,2048]{1,0:T(8,128)(2,1)S(1)}, u32[]{:S(2)}, u32[]{:S(2)}) collective-permute-start(bf16[16,2048]{1,0:T(8,128)(2,1)S(1)} %get-tuple-element.33), channel_id=1, source_target_pairs={{2,0},{3,1},{4,2},{5,3},{6,4},{7,5},{10,8},{11,9},{12,10},{13,11},... | collective-permute-start | bytes 196616 | tf_op jit(solution)/shard_map/ppermute | solution.py:95
  21.5 8.0 %collective-permute-start.4 = (bf16[16,2048]{1,0:T(8,128)(2,1)S(1)}, bf16[16,2048]{1,0:T(8,128)(2,1)S(1)}, u32[]{:S(2)}, u32[]{:S(2)}) collective-permute-start(bf16[16,2048]{1,0:T(8,128)(2,1)S(1)} %get-tuple-element.33), channel_id=1, source_target_pairs={{4,0},{5,1},{6,2},{7,3},{12,8},{13,9},{14,10},{15,11},{20,16},{21,... | collective-permute-start | bytes 196616 | tf_op jit(solution)/shard_map/ppermute | solution.py:95
  22.8 9.1 %collective-permute-start.5 = (bf16[16,2048]{1,0:T(8,128)(2,1)S(1)}, bf16[16,2048]{1,0:T(8,128)(2,1)S(1)}, u32[]{:S(2)}, u32[]{:S(2)}) collective-permute-start(bf16[16,2048]{1,0:T(8,128)(2,1)S(1)} %get-tuple-element.33), channel_id=1, source_target_pairs={{6,0},{7,1},{14,8},{15,9},{22,16},{23,17},{30,24},{31,25}} | collective-permute-start | bytes 196616 | tf_op jit(solution)/shard_map/ppermute | solution.py:95
  31.9 1.6 %collective-permute-start.6 = (bf16[64,2048]{1,0:T(8,128)(2,1)S(1)}, bf16[64,2048]{1,0:T(8,128)(2,1)S(1)}, u32[]{:S(2)}, u32[]{:S(2)}) collective-permute-start(bf16[64,2048]{1,0:T(8,128)(2,1)S(1)} %pad_maximum_fusion.1), channel_id=1, source_target_pairs={{0,1},{1,0},{2,3},{3,2},{4,5},{5,4},{6,7},{7,6},{8,9},{9,8},{10,11... | collective-permute-start | bytes 786440 | tf_op jit(solution)/shard_map/ppermute | solution.py:96
  33.7 0.8 %copy-start = (bf16[128,2048]{1,0:T(8,128)(2,1)}, bf16[128,2048]{1,0:T(8,128)(2,1)S(1)}, u32[]{:S(2)}) copy-start(bf16[128,2048]{1,0:T(8,128)(2,1)S(1)} %broadcast_select_fusion) | copy-start | bytes 1572868
  35.0 0.8 %slice-start = ((bf16[128,2048]{1,0:T(8,128)(2,1)}), bf16[16,2048]{1,0:T(8,128)(2,1)S(1)}, s32[]{:S(2)}) async-start(bf16[128,2048]{1,0:T(8,128)(2,1)} %copy-done), calls=%async_computation | async-start | bytes 131072 | tf_op jit(solution)/shard_map/stack | solution.py:137
  38.7 8.4 %collective-permute-start.7 = (f32[64,512]{1,0:T(8,128)S(1)}, f32[64,512]{1,0:T(8,128)S(1)}, u32[]{:S(2)}, u32[]{:S(2)}) collective-permute-start(f32[64,512]{1,0:T(8,128)S(1)} %get-tuple-element.10), channel_id=1, source_target_pairs={{0,8},{24,0},{1,9},{25,1},{2,10},{26,2},{3,11},{27,3},{4,12},{28,4... | collective-permute-start | bytes 393224 | tf_op jit(solution)/shard_map/ppermute | solution.py:151
  41.6 8.2 %collective-permute-start.8 = (f32[64,512]{1,0:T(8,128)S(1)}, f32[64,512]{1,0:T(8,128)S(1)}, u32[]{:S(2)}, u32[]{:S(2)}) collective-permute-start(f32[64,512]{1,0:T(8,128)S(1)} %get-tuple-element.9), channel_id=1, source_target_pairs={{16,0},{24,8},{17,1},{25,9},{18,2},{26,10},{19,3},{27,11},{20,4},{... | collective-permute-start | bytes 393224 | tf_op jit(solution)/shard_map/ppermute | solution.py:151
  42.9 7.2 %collective-permute-start.9 = (f32[64,512]{1,0:T(8,128)S(1)}, f32[64,512]{1,0:T(8,128)S(1)}, u32[]{:S(2)}, u32[]{:S(2)}) collective-permute-start(f32[64,512]{1,0:T(8,128)S(1)} %get-tuple-element.8), channel_id=1, source_target_pairs={{8,0},{16,8},{9,1},{17,9},{10,2},{18,10},{11,3},{19,11},{12,4},{20... | collective-permute-start | bytes 393224 | tf_op jit(solution)/shard_map/ppermute | solution.py:151

commit v5 on v4

--- a/solution.py
+++ b/solution.py
@@ -36,18 +36,20 @@
         base = pl.multiple_of(jnp.minimum(first - first % LANES, last), LANES)
         pltpu.make_async_copy(record_hbm.at[:, pl.ds(base, span)], chunks.at[w], sems.at[w]).start()
         shifts.append(first - base)
-    src = lax.broadcasted_iota(jnp.int32, (2 * LANES, LANES), 0)
-    dst = lax.broadcasted_iota(jnp.int32, (2 * LANES, LANES), 1)
+    lane = lax.broadcasted_iota(jnp.int32, (channels, LANES), 1)
     for w in range(windows):
         pltpu.make_async_copy(record_hbm.at[:, pl.ds(0, span)], chunks.at[w], sems.at[w]).wait()
-        pick = (src == dst + shifts[w]).astype(jnp.bfloat16)
-        pairs = jnp.concatenate([chunks[w, :, pl.ds(b * LANES, 2 * LANES)] for b in range(blocks)], axis=0)
-        moved = jnp.dot(pairs, pick, preferred_element_type=jnp.float32).astype(jnp.bfloat16)
+        shift = shifts[w]
+        low = lane < LANES - shift
+        rolled = [
+            pltpu.roll(chunks[w, :, pl.ds(b * LANES, LANES)].astype(jnp.float32), (LANES - shift) % LANES, 1)
+            for b in range(blocks + 1)
+        ]
         for b in range(blocks):
-            moved_rows[b, pl.ds(w * channels, channels), :] = moved[b * channels : (b + 1) * channels]
-    spectra = jnp.zeros(out_ref.shape, jnp.float32)
-    for b in range(blocks):
-        spectra = spectra + jnp.dot(moved_rows[b], table_ref[b], preferred_element_type=jnp.float32)
+            moved_rows[pl.ds(w * channels, channels), pl.ds(b * LANES, LANES)] = jnp.where(
+                low, rolled[b], rolled[b + 1]
+            ).astype(jnp.bfloat16)
+    spectra = jnp.dot(moved_rows[...], table_ref[...], preferred_element_type=jnp.float32)
     power = spectra * spectra
     smooth = jnp.dot(
         power, near_ref[...], precision=lax.Precision.HIGHEST, preferred_element_type=jnp.float32
@@ -61,7 +63,7 @@
     channels, _ = record_rows.shape
     windows = starts.shape[0]
     blocks = NT // LANES
-    table = jnp.asarray(spectral_table()).reshape(blocks, LANES, 2 * NF)
+    table = jnp.asarray(spectral_table())
     lane_bin = np.arange(2 * NF) % NF
     near = (np.abs(lane_bin[:, None] - lane_bin[None, :]) <= 4).astype(np.float32)
     count = near[:NF].sum(axis=0, keepdims=True)
@@ -74,7 +76,7 @@
         out_specs=vmem,
         scratch_shapes=[
             pltpu.VMEM((windows, channels, NT + LANES), jnp.bfloat16),
-            pltpu.VMEM((blocks, windows * channels, LANES), jnp.bfloat16),
+            pltpu.VMEM((windows * channels, NT), jnp.bfloat16),
             pltpu.SemaphoreType.DMA((windows,)),
         ],
     )(starts, record_rows, table, jnp.asarray(near), jnp.asarray(count), live_rows)

time: 52.9 us -> 50.3 us (0.951)
  Pallas kernels: 8.05 us -> 5.46 us
    pallas_call x1, Pallas kernels: 8.05 us -> 5.46 us  [whiten(): pl.pallas_call(whiten_kernel, out_shape=jax.ShapeDtypeStruct((windows * c...]
where the time goes in v5:
time: 50.3 us; the launch traced here: 49.9 us
  waiting for transfers between devices  17.4 us (35%)
  starting transfers between devices  15.4 us (31%)
  local copies, waits for them, and re-layouts  10 us (20%)
  Pallas kernels  5.46 us (11%)
  matrix products  0.73 us (1%)
  other arithmetic  0.57 us (1%)
    ppermute x3, waiting for transfers between devices, halo(): own.append(lax.ppermute(mine, 'fibre', pairs))  7.84 us
    ppermute x3, starting transfers between devices, shards(): gathered.append(lax.ppermute(sent, 'seg', pairs))  5.94 us
    ppermute x3, waiting for transfers between devices, shards(): collected.append(lax.ppermute(sent, 'seg', pairs))  5.82 us
    ppermute x3, starting transfers between devices, shards(): collected.append(lax.ppermute(sent, 'seg', pairs))  5.47 us
    pallas_call x1, Pallas kernels, whiten(): pl.pallas_call(whiten_kernel, out_shape=jax.ShapeDtypeStruct((windows * c...  5.46 us
    ppermute x3, starting transfers between devices, halo(): own.append(lax.ppermute(mine, 'fibre', pairs))  3.88 us
    unnamed x32, local copies, waits for them, and re-layouts  2.34 us
    ppermute x3, waiting for transfers between devices, shards(): gathered.append(lax.ppermute(sent, 'seg', pairs))  2.3 us
  transfers between devices with their start and end apart: 10, of which 9 were waited for; matrix products, arithmetic and copies ran while one was open for 0% of the time, Pallas kernels for 0%

profile of v5, /device:TPU:0, one launch (start us, length us, event | category | flops | bytes accessed | tf_op | source)
XLA Modules:
  0.0 49.9 jit_solution(1440934695661619268)
XLA Ops:
  0.0 0.7 %copy-done.1 = s32[16]{0:T(128)S(1)} copy-done((s32[16]{0:T(128)S(1)}, s32[16]{0:T(128)}, u32[]{:S(2)}) %copy-start.1) | copy-done | bytes 88
  0.7 0.8 %broadcast_in_dim_tile.4.live_ref = f32[256,1]{1,0:T(8,128)} reshape(f32[16,16]{1,0:T(8,128)S(1)} %tile.2) | data formatting | bytes 2048 | tf_op jit(solution)/shard_map/broadcast_in_dim;tile | solution.py:70
  1.4 5.5 %shard_map.64 = bf16[256,128]{1,0:T(8,128)(2,1)} custom-call(s32[16]{0:T(128)} %bitcast.113, bf16[16,27648]{1,0:T(8,128)(2,1)} %bitcast.93, bf16[3072,128]{1,0:T(8,128)(2,1)} %constant.102.clone.table_ref, f32[128,128]{1,0:T(8,128)} %constant.103.clone.near_ref, f32[1,128]{1,0:T(1,128)} %constant.104.clone.count_ref, f32[256,1]{1,0:T(8,128)} %broadcast_in_dim_tile.4.live_ref), custom_call_target="tpu_custom_call" | custom-call | tf_op jit(solution)/shard_map/pallas_call | solution.py:72
  6.9 1.2 %reshape_reshape.3 = bf16[16,16,2,4,16]{4,3,2,1,0:T(4,128)(2,1)S(1)} reshape(bf16[256,128]{1,0:T(8,128)(2,1)} %shard_map.64) | data formatting | bytes 131072 | tf_op jit(solution)/shard_map/reshape;reshape | solution.py:122
  8.1 0.4 copy.101
  8.5 0.8 %reshape.74 = bf16[4,16,512]{2,1,0:T(8,128)(2,1)S(1)} reshape(bf16[4,16,16,2,16]{4,3,2,1,0:T(2,128)(2,1)S(1)} %bitcast.91) | data formatting | bytes 131072 | tf_op jit(solution)/shard_map/reshape | solution.py:123
  9.3 3.0 %collective-permute-start = (bf16[16,512]{1,0:T(8,128)(2,1)S(1)}, bf16[16,512]{1,0:T(8,128)(2,1)S(1)}, u32[]{:S(2)}, u32[]{:S(2)}) collective-permute-start(bf16[16,512]{1,0:T(8,128)(2,1)S(1)} %get-tuple-element.38), channel_id=1, source_target_pairs={{0,8},{8,16},{16,24},{24,0},{1,9},{9,17},{17,25},{25,1},{2,10},{10... | collective-permute-start | bytes 49160 | tf_op jit(solution)/shard_map/ppermute | solution.py:128
  12.3 1.5 %collective-permute-start.1 = (bf16[16,512]{1,0:T(8,128)(2,1)S(1)}, bf16[16,512]{1,0:T(8,128)(2,1)S(1)}, u32[]{:S(2)}, u32[]{:S(2)}) collective-permute-start(bf16[16,512]{1,0:T(8,128)(2,1)S(1)} %get-tuple-element.37), channel_id=1, source_target_pairs={{0,16},{8,24},{16,0},{24,8},{1,17},{9,25},{17,1},{25,9},{2,18},{10... | collective-permute-start | bytes 49160 | tf_op jit(solution)/shard_map/ppermute | solution.py:128
  13.8 1.4 %collective-permute-start.2 = (bf16[16,512]{1,0:T(8,128)(2,1)S(1)}, bf16[16,512]{1,0:T(8,128)(2,1)S(1)}, u32[]{:S(2)}, u32[]{:S(2)}) collective-permute-start(bf16[16,512]{1,0:T(8,128)(2,1)S(1)} %get-tuple-element.36), channel_id=1, source_target_pairs={{0,24},{8,0},{16,8},{24,16},{1,25},{9,1},{17,9},{25,17},{2,26},{10... | collective-permute-start | bytes 49160 | tf_op jit(solution)/shard_map/ppermute | solution.py:128
  15.2 0.8 %collective-permute-done.1 = bf16[16,512]{1,0:T(8,128)(2,1)S(1)} collective-permute-done((bf16[16,512]{1,0:T(8,128)(2,1)S(1)}, bf16[16,512]{1,0:T(8,128)(2,1)S(1)}, u32[]{:S(2)}, u32[]{:S(2)}) %collective-permute-start.1) | collective-permute-done | bytes 16416 | tf_op jit(solution)/shard_map/ppermute | solution.py:128
  16.0 1.5 %collective-permute-done.2 = bf16[16,512]{1,0:T(8,128)(2,1)S(1)} collective-permute-done((bf16[16,512]{1,0:T(8,128)(2,1)S(1)}, bf16[16,512]{1,0:T(8,128)(2,1)S(1)}, u32[]{:S(2)}, u32[]{:S(2)}) %collective-permute-start.2) | collective-permute-done | bytes 16416 | tf_op jit(solution)/shard_map/ppermute | solution.py:128
  17.6 1.3 %collective-permute-start.3 = (bf16[16,2048]{1,0:T(8,128)(2,1)S(1)}, bf16[16,2048]{1,0:T(8,128)(2,1)S(1)}, u32[]{:S(2)}, u32[]{:S(2)}) collective-permute-start(bf16[16,2048]{1,0:T(8,128)(2,1)S(1)} %get-tuple-element.33), channel_id=1, source_target_pairs={{2,0},{3,1},{4,2},{5,3},{6,4},{7,5},{10,8},{11,9},{12,10},{13,11},... | collective-permute-start | bytes 196616 | tf_op jit(solution)/shard_map/ppermute | solution.py:97
  18.9 1.3 %collective-permute-start.4 = (bf16[16,2048]{1,0:T(8,128)(2,1)S(1)}, bf16[16,2048]{1,0:T(8,128)(2,1)S(1)}, u32[]{:S(2)}, u32[]{:S(2)}) collective-permute-start(bf16[16,2048]{1,0:T(8,128)(2,1)S(1)} %get-tuple-element.33), channel_id=1, source_target_pairs={{4,0},{5,1},{6,2},{7,3},{12,8},{13,9},{14,10},{15,11},{20,16},{21,... | collective-permute-start | bytes 196616 | tf_op jit(solution)/shard_map/ppermute | solution.py:97
  20.2 1.3 %collective-permute-start.5 = (bf16[16,2048]{1,0:T(8,128)(2,1)S(1)}, bf16[16,2048]{1,0:T(8,128)(2,1)S(1)}, u32[]{:S(2)}, u32[]{:S(2)}) collective-permute-start(bf16[16,2048]{1,0:T(8,128)(2,1)S(1)} %get-tuple-element.33), channel_id=1, source_target_pairs={{6,0},{7,1},{14,8},{15,9},{22,16},{23,17},{30,24},{31,25}} | collective-permute-start | bytes 196616 | tf_op jit(solution)/shard_map/ppermute | solution.py:97
  21.5 2.7 %collective-permute-done.3 = bf16[16,2048]{1,0:T(8,128)(2,1)S(1)} collective-permute-done((bf16[16,2048]{1,0:T(8,128)(2,1)S(1)}, bf16[16,2048]{1,0:T(8,128)(2,1)S(1)}, u32[]{:S(2)}, u32[]{:S(2)}) %collective-permute-start.3) | collective-permute-done | bytes 65568 | tf_op jit(solution)/shard_map/ppermute | solution.py:97
  24.2 2.6 %collective-permute-done.4 = bf16[16,2048]{1,0:T(8,128)(2,1)S(1)} collective-permute-done((bf16[16,2048]{1,0:T(8,128)(2,1)S(1)}, bf16[16,2048]{1,0:T(8,128)(2,1)S(1)}, u32[]{:S(2)}, u32[]{:S(2)}) %collective-permute-start.4) | collective-permute-done | bytes 65568 | tf_op jit(solution)/shard_map/ppermute | solution.py:97
  26.8 2.5 %collective-permute-done.5 = bf16[16,2048]{1,0:T(8,128)(2,1)S(1)} collective-permute-done((bf16[16,2048]{1,0:T(8,128)(2,1)S(1)}, bf16[16,2048]{1,0:T(8,128)(2,1)S(1)}, u32[]{:S(2)}, u32[]{:S(2)}) %collective-permute-start.5) | collective-permute-done | bytes 65568 | tf_op jit(solution)/shard_map/ppermute | solution.py:97
  29.5 1.4 %collective-permute-done.6 = bf16[64,2048]{1,0:T(8,128)(2,1)S(1)} collective-permute-done((bf16[64,2048]{1,0:T(8,128)(2,1)S(1)}, bf16[64,2048]{1,0:T(8,128)(2,1)S(1)}, u32[]{:S(2)}, u32[]{:S(2)}) %collective-permute-start.6) | collective-permute-done | bytes 262176 | tf_op jit(solution)/shard_map/ppermute | solution.py:98
  31.4 0.5 %copy-done = bf16[128,2048]{1,0:T(8,128)(2,1)} copy-done((bf16[128,2048]{1,0:T(8,128)(2,1)}, bf16[128,2048]{1,0:T(8,128)(2,1)S(1)}, u32[]{:S(2)}) %copy-start) | copy-done | bytes 524312
  32.7 0.6 %slice-done = bf16[16,2048]{1,0:T(8,128)(2,1)S(1)} async-done(((bf16[128,2048]{1,0:T(8,128)(2,1)}), bf16[16,2048]{1,0:T(8,128)(2,1)S(1)}, s32[]{:S(2)}) %slice-start) | async-done | bytes 65560 | tf_op jit(solution)/shard_map/stack | solution.py:139
  33.3 0.4 stack.33
  33.7 0.4 copy.53
  34.2 0.7 %convolution_bitcast_fusion = f32[16,2,16,144]{3,2,1,0:T(8,128)S(1)} fusion(bf16[144,64,2,16,1]{0,3,2,1,4:T(8,128)(2,1)S(1)} %bitcast.87, bf16[1,16,64,2,16]{2,1,3,0,4:T(8,128)(2,1)S(1)} %maximum_bitcast_fusion, bf16[1,16,64,2,16]{2,1,3,0,4:T(8,128)(2,1)S(1)} %copy.53), kind=kOutput, calls=%fused_computation.1 | convolution fusion | flops 18939904 | bytes 1015808 | tf_op jit(solution)/shard_map/ocspn,jspn->nocj/dot_general | solution.py:140
  34.9 0.6 %fusion.9 = (f32[16,2,1,128]{3,2,1,0:T(1,128)S(1)}, f32[16,2,1,128]{3,2,1,0:T(1,128)S(1)}, f32[16,2,1,128]{3,2,1,0:T(1,128)S(1)}, f32[16,2,1,128]{3,2,1,0:T(1,12...) fusion(f32[16,2,16,144]{3,2,1,0:T(8,128)S(1)} %convolution_bitc, ...), kind=kLoop, calls=%fused_computation.69 | loop fusion | bytes 524288 | tf_op jit(solution)/shard_map/slice | solution.py:141
  36.1 2.9 %collective-permute-start.7 = (f32[64,512]{1,0:T(8,128)S(1)}, f32[64,512]{1,0:T(8,128)S(1)}, u32[]{:S(2)}, u32[]{:S(2)}) collective-permute-start(f32[64,512]{1,0:T(8,128)S(1)} %get-tuple-element.10), channel_id=1, source_target_pairs={{0,8},{24,0},{1,9},{25,1},{2,10},{26,2},{3,11},{27,3},{4,12},{28,4... | collective-permute-start | bytes 393224 | tf_op jit(solution)/shard_map/ppermute | solution.py:153
  39.0 1.3 %collective-permute-start.8 = (f32[64,512]{1,0:T(8,128)S(1)}, f32[64,512]{1,0:T(8,128)S(1)}, u32[]{:S(2)}, u32[]{:S(2)}) collective-permute-start(f32[64,512]{1,0:T(8,128)S(1)} %get-tuple-element.9), channel_id=1, source_target_pairs={{16,0},{24,8},{17,1},{25,9},{18,2},{26,10},{19,3},{27,11},{20,4},{... | collective-permute-start | bytes 393224 | tf_op jit(solution)/shard_map/ppermute | solution.py:153
  40.3 1.3 %collective-permute-start.9 = (f32[64,512]{1,0:T(8,128)S(1)}, f32[64,512]{1,0:T(8,128)S(1)}, u32[]{:S(2)}, u32[]{:S(2)}) collective-permute-start(f32[64,512]{1,0:T(8,128)S(1)} %get-tuple-element.8), channel_id=1, source_target_pairs={{8,0},{16,8},{9,1},{17,9},{10,2},{18,10},{11,3},{19,11},{12,4},{20... | collective-permute-start | bytes 393224 | tf_op jit(solution)/shard_map/ppermute | solution.py:153
  41.6 2.9 %collective-permute-done.7 = f32[64,512]{1,0:T(8,128)S(1)} collective-permute-done((f32[64,512]{1,0:T(8,128)S(1)}, f32[64,512]{1,0:T(8,128)S(1)}, u32[]{:S(2)}, u32[]{:S(2)}) %collective-permute-start.7) | collective-permute-done | bytes 131104 | tf_op jit(solution)/shard_map/ppermute | solution.py:153
  44.6 2.7 %collective-permute-done.8 = f32[64,512]{1,0:T(8,128)S(1)} collective-permute-done((f32[64,512]{1,0:T(8,128)S(1)}, f32[64,512]{1,0:T(8,128)S(1)}, u32[]{:S(2)}, u32[]{:S(2)}) %collective-permute-start.8) | collective-permute-done | bytes 131104 | tf_op jit(solution)/shard_map/ppermute | solution.py:153
  47.5 0.6 %gather_fusion = f32[4,64,512]{2,1,0:T(8,128)S(1)} fusion(f32[4,64,512]{2,1,0:T(8,128)S(1)} %pad_maximum_fusion, s32[1024]{0:T(1024)S(1)} %pad_clamp_fusion), kind=kCustom, calls=%fused_computation | custom fusion | bytes 1048592 | tf_op jit(solution)/shard_map/jit(_take)/gather | solution.py:158
  48.1 0.3 copy.72
  48.8 1.1 %copy.74 = f32[64,16,128]{2,1,0:T(8,128)} copy(f32[64,16,128]{0,2,1:T(8,128)S(1)} %bitcast.89) | data formatting | bytes 1048576 | tf_op jit(solution)/shard_map/reshape | solution.py:159
  (57 shorter events, 2.5 us)
Async XLA Ops:
  0.0 0.7 %copy-start.1 = (s32[16]{0:T(128)S(1)}, s32[16]{0:T(128)}, u32[]{:S(2)}) copy-start(s32[16]{0:T(128)} %param.8) | copy-start | bytes 196
  9.3 5.9 %collective-permute-start = (bf16[16,512]{1,0:T(8,128)(2,1)S(1)}, bf16[16,512]{1,0:T(8,128)(2,1)S(1)}, u32[]{:S(2)}, u32[]{:S(2)}) collective-permute-start(bf16[16,512]{1,0:T(8,128)(2,1)S(1)} %get-tuple-element.38), channel_id=1, source_target_pairs={{0,8},{8,16},{16,24},{24,0},{1,9},{9,17},{17,25},{25,1},{2,10},{10... | collective-permute-start | bytes 49160 | tf_op jit(solution)/shard_map/ppermute | solution.py:128
  12.3 3.7 %collective-permute-start.1 = (bf16[16,512]{1,0:T(8,128)(2,1)S(1)}, bf16[16,512]{1,0:T(8,128)(2,1)S(1)}, u32[]{:S(2)}, u32[]{:S(2)}) collective-permute-start(bf16[16,512]{1,0:T(8,128)(2,1)S(1)} %get-tuple-element.37), channel_id=1, source_target_pairs={{0,16},{8,24},{16,0},{24,8},{1,17},{9,25},{17,1},{25,9},{2,18},{10... | collective-permute-start | bytes 49160 | tf_op jit(solution)/shard_map/ppermute | solution.py:128
  13.8 3.7 %collective-permute-start.2 = (bf16[16,512]{1,0:T(8,128)(2,1)S(1)}, bf16[16,512]{1,0:T(8,128)(2,1)S(1)}, u32[]{:S(2)}, u32[]{:S(2)}) collective-permute-start(bf16[16,512]{1,0:T(8,128)(2,1)S(1)} %get-tuple-element.36), channel_id=1, source_target_pairs={{0,24},{8,0},{16,8},{24,16},{1,25},{9,1},{17,9},{25,17},{2,26},{10... | collective-permute-start | bytes 49160 | tf_op jit(solution)/shard_map/ppermute | solution.py:128
  17.6 6.6 %collective-permute-start.3 = (bf16[16,2048]{1,0:T(8,128)(2,1)S(1)}, bf16[16,2048]{1,0:T(8,128)(2,1)S(1)}, u32[]{:S(2)}, u32[]{:S(2)}) collective-permute-start(bf16[16,2048]{1,0:T(8,128)(2,1)S(1)} %get-tuple-element.33), channel_id=1, source_target_pairs={{2,0},{3,1},{4,2},{5,3},{6,4},{7,5},{10,8},{11,9},{12,10},{13,11},... | collective-permute-start | bytes 196616 | tf_op jit(solution)/shard_map/ppermute | solution.py:97
  18.9 8.0 %collective-permute-start.4 = (bf16[16,2048]{1,0:T(8,128)(2,1)S(1)}, bf16[16,2048]{1,0:T(8,128)(2,1)S(1)}, u32[]{:S(2)}, u32[]{:S(2)}) collective-permute-start(bf16[16,2048]{1,0:T(8,128)(2,1)S(1)} %get-tuple-element.33), channel_id=1, source_target_pairs={{4,0},{5,1},{6,2},{7,3},{12,8},{13,9},{14,10},{15,11},{20,16},{21,... | collective-permute-start | bytes 196616 | tf_op jit(solution)/shard_map/ppermute | solution.py:97
  20.2 9.1 %collective-permute-start.5 = (bf16[16,2048]{1,0:T(8,128)(2,1)S(1)}, bf16[16,2048]{1,0:T(8,128)(2,1)S(1)}, u32[]{:S(2)}, u32[]{:S(2)}) collective-permute-start(bf16[16,2048]{1,0:T(8,128)(2,1)S(1)} %get-tuple-element.33), channel_id=1, source_target_pairs={{6,0},{7,1},{14,8},{15,9},{22,16},{23,17},{30,24},{31,25}} | collective-permute-start | bytes 196616 | tf_op jit(solution)/shard_map/ppermute | solution.py:97
  29.3 1.6 %collective-permute-start.6 = (bf16[64,2048]{1,0:T(8,128)(2,1)S(1)}, bf16[64,2048]{1,0:T(8,128)(2,1)S(1)}, u32[]{:S(2)}, u32[]{:S(2)}) collective-permute-start(bf16[64,2048]{1,0:T(8,128)(2,1)S(1)} %pad_maximum_fusion.1), channel_id=1, source_target_pairs={{0,1},{1,0},{2,3},{3,2},{4,5},{5,4},{6,7},{7,6},{8,9},{9,8},{10,11... | collective-permute-start | bytes 786440 | tf_op jit(solution)/shard_map/ppermute | solution.py:98
  31.1 0.8 %copy-start = (bf16[128,2048]{1,0:T(8,128)(2,1)}, bf16[128,2048]{1,0:T(8,128)(2,1)S(1)}, u32[]{:S(2)}) copy-start(bf16[128,2048]{1,0:T(8,128)(2,1)S(1)} %broadcast_select_fusion) | copy-start | bytes 1572868
  32.4 0.8 %slice-start = ((bf16[128,2048]{1,0:T(8,128)(2,1)}), bf16[16,2048]{1,0:T(8,128)(2,1)S(1)}, s32[]{:S(2)}) async-start(bf16[128,2048]{1,0:T(8,128)(2,1)} %copy-done), calls=%async_computation | async-start | bytes 131072 | tf_op jit(solution)/shard_map/stack | solution.py:139
  36.1 8.4 %collective-permute-start.7 = (f32[64,512]{1,0:T(8,128)S(1)}, f32[64,512]{1,0:T(8,128)S(1)}, u32[]{:S(2)}, u32[]{:S(2)}) collective-permute-start(f32[64,512]{1,0:T(8,128)S(1)} %get-tuple-element.10), channel_id=1, source_target_pairs={{0,8},{24,0},{1,9},{25,1},{2,10},{26,2},{3,11},{27,3},{4,12},{28,4... | collective-permute-start | bytes 393224 | tf_op jit(solution)/shard_map/ppermute | solution.py:153
  39.0 8.2 %collective-permute-start.8 = (f32[64,512]{1,0:T(8,128)S(1)}, f32[64,512]{1,0:T(8,128)S(1)}, u32[]{:S(2)}, u32[]{:S(2)}) collective-permute-start(f32[64,512]{1,0:T(8,128)S(1)} %get-tuple-element.9), channel_id=1, source_target_pairs={{16,0},{24,8},{17,1},{25,9},{18,2},{26,10},{19,3},{27,11},{20,4},{... | collective-permute-start | bytes 393224 | tf_op jit(solution)/shard_map/ppermute | solution.py:153
  40.3 7.2 %collective-permute-start.9 = (f32[64,512]{1,0:T(8,128)S(1)}, f32[64,512]{1,0:T(8,128)S(1)}, u32[]{:S(2)}, u32[]{:S(2)}) collective-permute-start(f32[64,512]{1,0:T(8,128)S(1)} %get-tuple-element.8), channel_id=1, source_target_pairs={{8,0},{16,8},{9,1},{17,9},{10,2},{18,10},{11,3},{19,11},{12,4},{20... | collective-permute-start | bytes 393224 | tf_op jit(solution)/shard_map/ppermute | solution.py:153

commit v6 on v5

--- a/solution.py
+++ b/solution.py
@@ -56,22 +56,23 @@
     ) / count_ref[...]
     water_level = jnp.sum(power, axis=-1, keepdims=True) / NF
     gain_of = live_ref[...] / jnp.sqrt(smooth + 0.1 * water_level + 1e-06)
-    out_ref[...] = (spectra * gain_of).astype(out_ref.dtype)
+    out_ref[...] = (spectra * gain_of).T.astype(out_ref.dtype)
 
 
-def whiten(record_rows, starts, live_mask):
+def whiten(record_rows, starts, live_mask, groups):
     channels, _ = record_rows.shape
     windows = starts.shape[0]
-    blocks = NT // LANES
-    table = jnp.asarray(spectral_table())
-    lane_bin = np.arange(2 * NF) % NF
+    per_group = NF // groups
+    lane_group, lane_part, lane_bin = np.unravel_index(np.arange(2 * NF), (groups, 2, per_group))
+    lane_bin = lane_group * per_group + lane_bin
+    table = jnp.asarray(spectral_table()[:, lane_part * NF + lane_bin])
     near = (np.abs(lane_bin[:, None] - lane_bin[None, :]) <= 4).astype(np.float32)
-    count = near[:NF].sum(axis=0, keepdims=True)
+    count = (np.abs(np.arange(NF)[:, None] - lane_bin[None, :]) <= 4).sum(axis=0, keepdims=True).astype(np.float32)
     live_rows = jnp.tile(live_mask.astype(jnp.float32), windows)[:, None]
     vmem = pl.BlockSpec(memory_space=pltpu.VMEM)
-    out = pl.pallas_call(
+    return pl.pallas_call(
         whiten_kernel,
-        out_shape=jax.ShapeDtypeStruct((windows * channels, 2 * NF), jnp.bfloat16),
+        out_shape=jax.ShapeDtypeStruct((2 * NF, windows * channels), jnp.bfloat16),
         in_specs=[pl.BlockSpec(memory_space=pltpu.SMEM), pl.BlockSpec(memory_space=pl.ANY), vmem, vmem, vmem, vmem],
         out_specs=vmem,
         scratch_shapes=[
@@ -80,7 +81,6 @@
             pltpu.SemaphoreType.DMA((windows,)),
         ],
     )(starts, record_rows, table, jnp.asarray(near), jnp.asarray(count), live_rows)
-    return out.reshape(windows, channels, 2 * NF)
 
 
 def halo(mine, hops, fibre_count):
@@ -106,8 +106,9 @@
 def shards(record, offsets, live_mask):
     seg_count = lax.axis_size("seg")
     fibre_count = lax.axis_size("fibre")
-    own_block = whiten(record[0], offsets[0], live_mask)
-    windows_count, block, _ = own_block.shape
+    windows_count = offsets.shape[1]
+    block = record.shape[1]
+    own_block = whiten(record[0], offsets[0], live_mask, seg_count)
     channels = block * fibre_count
     per_owner = BAND // seg_count
     bins_each = NF // seg_count
@@ -116,28 +117,31 @@
     kept = live_owners * per_owner
     span = block + kept
     hops = min(-(-span // block) - 1, fibre_count - 1)
+    needed = -(-span // block)
     me = lax.axis_index("seg")
-    rows = seg_count * windows_count
 
-    split = own_block.reshape(windows_count, block, 2, seg_count, bins_each).transpose(3, 1, 0, 2, 4)
-    split = split.reshape(seg_count, block, windows_count * 2 * bins_each)
+    split = own_block.reshape(seg_count, 2 * bins_each, windows_count * block)
     gathered = [lax.dynamic_index_in_dim(split, me, 0, keepdims=False)]
     for step in range(1, seg_count):
         sent = lax.dynamic_index_in_dim(split, (me + step) % seg_count, 0, keepdims=False)
         pairs = [(i, (i + step) % seg_count) for i in range(seg_count)]
         gathered.append(lax.ppermute(sent, "seg", pairs))
-    mine = jnp.concatenate(gathered, axis=1)
+    mine = jnp.concatenate(gathered, axis=0)
 
-    columns = halo(mine, hops, fibre_count)[:span]
-    if columns.shape[0] < span:
+    columns = halo(mine, hops, fibre_count).reshape((-1,) + mine.shape)[:needed]
+    if columns.shape[0] < needed:
         columns = jnp.concatenate(
-            [columns, jnp.zeros((span - columns.shape[0], columns.shape[1]), columns.dtype)], axis=0
+            [columns, jnp.zeros((needed - columns.shape[0],) + mine.shape, columns.dtype)], axis=0
         )
-    right = columns.reshape(span, rows, 2, bins_each)
-    re_own = right[:block, :, 0]
-    im_own = right[:block, :, 1]
-    left = jnp.stack([jnp.stack([re_own, im_own], axis=2), jnp.stack([im_own, -re_own], axis=2)])
-    cross = jnp.einsum("ocspn,jspn->nocj", left, right, preferred_element_type=jnp.float32)
+    right = columns.reshape(needed, seg_count, 2, bins_each, windows_count, block)
+    re_own = right[0, :, 0]
+    im_own = right[0, :, 1]
+    left = jnp.stack([jnp.stack([re_own, im_own], axis=1), jnp.stack([im_own, -re_own], axis=1)])
+    depth = seg_count * 2 * windows_count
+    right = right.transpose(3, 1, 2, 4, 0, 5).reshape(bins_each, depth, needed * block)
+    left = left.transpose(3, 0, 5, 1, 2, 4).reshape(bins_each, 2 * block, depth)
+    cross = jnp.einsum("nik,nkj->nij", left, right, preferred_element_type=jnp.float32)
+    cross = cross.reshape(bins_each, 2, block, needed * block)
     band = jnp.stack([cross[:, :, c, c + 1 : c + 1 + kept] for c in range(block)])
     band = band.transpose(3, 0, 2, 1) * (1.0 / math.sqrt(seg_count * windows_count))
     band = band.reshape(kept, block * 2 * bins_each)

time: 50.3 us -> 79.4 us (1.58)
  local copies, waits for them, and re-layouts: 10 us -> 37.3 us
  other arithmetic: 0.57 us -> 2.42 us
  waiting for transfers between devices: 17.4 us -> 15.6 us
  starting transfers between devices: 15.4 us -> 16.9 us
    reshape x1 -> x3, local copies, waits for them, and re-layouts: 0.75 us -> 18.2 us  [the longest x1 13 us: shards(): right.transpose(3, 1, 2, 4, 0, 5).reshape(bins_each, depth, needed * block)]
    transpose x0 -> x2, local copies, waits for them, and re-layouts: none -> 12.5 us  [the longest x1 11.6 us: shards(): right.transpose(3, 1, 2, 4, 0, 5).reshape(bins_each, depth, needed * block)]
    another operation x6 -> x1, local copies, waits for them, and re-layouts: 3 us -> 1.06 us  [shards(): jnp.stack([re_own, im_own], axis=1)]
    ppermute x3, starting transfers between devices: 5.47 us -> 7.13 us  [shards(): collected.append(lax.ppermute(sent, 'seg', pairs))]
    unnamed x32, local copies, waits for them, and re-layouts: 2.34 us -> 1.04 us
    ppermute x3, waiting for transfers between devices: 5.82 us -> 4.74 us  [shards(): collected.append(lax.ppermute(sent, 'seg', pairs))]
    neg x1, other arithmetic: 0.02 us -> 0.99 us  [shards(): -re_own]
  transfers between devices with their start and end apart: 10 -> 10, of which waited for: 9 -> 9; matrix products, arithmetic and copies ran while one was open for 0% -> 1% of each run, Pallas kernels for 0% -> 0%
where the time goes in v6:
time: 79.4 us; the launch traced here: 78.6 us
  local copies, waits for them, and re-layouts  37.3 us (47%)
  starting transfers between devices  16.9 us (21%)
  waiting for transfers between devices  15.6 us (20%)
  Pallas kernels  5.55 us (7%)
  other arithmetic  2.42 us (3%)
    reshape x1, local copies, waits for them, and re-layouts, shards(): right.transpose(3, 1, 2, 4, 0, 5).reshape(bins_each, depth, needed * block)  13 us
    transpose x1, local copies, waits for them, and re-layouts, shards(): right.transpose(3, 1, 2, 4, 0, 5).reshape(bins_each, depth, needed * block)  11.6 us
    ppermute x3, waiting for transfers between devices, halo(): own.append(lax.ppermute(mine, 'fibre', pairs))  7.79 us
    ppermute x3, starting transfers between devices, shards(): collected.append(lax.ppermute(sent, 'seg', pairs))  7.13 us
    ppermute x3, starting transfers between devices, shards(): gathered.append(lax.ppermute(sent, 'seg', pairs))  5.89 us
    pallas_call x1, Pallas kernels, whiten(): pl.pallas_call(whiten_kernel, out_shape=jax.ShapeDtypeStruct((2 * NF, win...  5.55 us
    ppermute x3, waiting for transfers between devices, shards(): collected.append(lax.ppermute(sent, 'seg', pairs))  4.74 us
    reshape x1, local copies, waits for them, and re-layouts, shards(): columns.reshape(needed, seg_count, 2, bins_each, windows_count, block)  4.49 us
  transfers between devices with their start and end apart: 10, of which 9 were waited for; matrix products, arithmetic and copies ran while one was open for 1% of the time, Pallas kernels for 0%

profile of v6, /device:TPU:0, one launch (start us, length us, event | category | flops | bytes accessed | tf_op | source)
XLA Modules:
  0.0 78.6 jit_solution(4642996163015218310)
XLA Ops:
  0.0 0.7 convert_element_type.3
  0.7 0.8 broadcast_in_dim_tile.4.live_ref
  1.4 5.6 %shard_map.64 = bf16[128,256]{1,0:T(8,128)(2,1)} custom-call(s32[16]{0:T(128)} %bitcast.127, bf16[16,27648]{1,0:T(8,128)(2,1)} %bitcast.121, bf16[3072,128]{1,0:T(8,128)(2,1)} %constant.103.clone.table_ref, f32[128,128]{1,0:T(8,128)} %constant.104.clone.near_ref, f32[1,128]{1,0:T(1,128)} %constant.105.clone.count_ref, f32[256,1]{1,0:T(8,128)} %broadcast_in_dim_tile.4.live_ref), custom_call_target="tpu_custom_call" | custom-call | tf_op jit(solution)/shard_map/pallas_call | solution.py:73
  7.0 0.8 dynamic-slice_bitcast_fusion.3
  7.7 2.9 %collective-permute-start = (bf16[32,256]{1,0:T(8,128)(2,1)S(1)}, bf16[32,256]{1,0:T(8,128)(2,1)S(1)}, u32[]{:S(2)}, u32[]{:S(2)}) collective-permute-start(bf16[32,256]{1,0:T(8,128)(2,1)S(1)} %get-tuple-element.39), channel_id=1, source_target_pairs={{0,8},{8,16},{16,24},{24,0},{1,9},{9,17},{17,25},{25,1},{2,10},{10... | collective-permute-start | bytes 49160 | tf_op jit(solution)/shard_map/ppermute | solution.py:128
  10.7 1.5 %collective-permute-start.1 = (bf16[32,256]{1,0:T(8,128)(2,1)S(1)}, bf16[32,256]{1,0:T(8,128)(2,1)S(1)}, u32[]{:S(2)}, u32[]{:S(2)}) collective-permute-start(bf16[32,256]{1,0:T(8,128)(2,1)S(1)} %get-tuple-element.38), channel_id=1, source_target_pairs={{0,16},{8,24},{16,0},{24,8},{1,17},{9,25},{17,1},{25,9},{2,18},{10... | collective-permute-start | bytes 49160 | tf_op jit(solution)/shard_map/ppermute | solution.py:128
  12.2 1.4 %collective-permute-start.2 = (bf16[32,256]{1,0:T(8,128)(2,1)S(1)}, bf16[32,256]{1,0:T(8,128)(2,1)S(1)}, u32[]{:S(2)}, u32[]{:S(2)}) collective-permute-start(bf16[32,256]{1,0:T(8,128)(2,1)S(1)} %get-tuple-element.37), channel_id=1, source_target_pairs={{0,24},{8,0},{16,8},{24,16},{1,25},{9,1},{17,9},{25,17},{2,26},{10... | collective-permute-start | bytes 49160 | tf_op jit(solution)/shard_map/ppermute | solution.py:128
  13.6 0.7 constant_dynamic-update-slice_fusion.6
  14.4 1.5 %collective-permute-done.2 = bf16[32,256]{1,0:T(8,128)(2,1)S(1)} collective-permute-done((bf16[32,256]{1,0:T(8,128)(2,1)S(1)}, bf16[32,256]{1,0:T(8,128)(2,1)S(1)}, u32[]{:S(2)}, u32[]{:S(2)}) %collective-permute-start.2) | collective-permute-done | bytes 16416 | tf_op jit(solution)/shard_map/ppermute | solution.py:128
  16.0 1.3 %collective-permute-start.3 = (bf16[128,256]{1,0:T(8,128)(2,1)S(1)}, bf16[128,256]{1,0:T(8,128)(2,1)S(1)}, u32[]{:S(2)}, u32[]{:S(2)}) collective-permute-start(bf16[128,256]{1,0:T(8,128)(2,1)S(1)} %pad_maximum_fusion.1), channel_id=1, source_target_pairs={{2,0},{3,1},{4,2},{5,3},{6,4},{7,5},{10,8},{11,9},{12,10},{13,11},... | collective-permute-start | bytes 196616 | tf_op jit(solution)/shard_map/ppermute | solution.py:97
  17.2 1.3 %collective-permute-start.4 = (bf16[128,256]{1,0:T(8,128)(2,1)S(1)}, bf16[128,256]{1,0:T(8,128)(2,1)S(1)}, u32[]{:S(2)}, u32[]{:S(2)}) collective-permute-start(bf16[128,256]{1,0:T(8,128)(2,1)S(1)} %pad_maximum_fusion.1), channel_id=1, source_target_pairs={{4,0},{5,1},{6,2},{7,3},{12,8},{13,9},{14,10},{15,11},{20,16},{21,... | collective-permute-start | bytes 196616 | tf_op jit(solution)/shard_map/ppermute | solution.py:97
  18.5 1.3 %collective-permute-start.5 = (bf16[128,256]{1,0:T(8,128)(2,1)S(1)}, bf16[128,256]{1,0:T(8,128)(2,1)S(1)}, u32[]{:S(2)}, u32[]{:S(2)}) collective-permute-start(bf16[128,256]{1,0:T(8,128)(2,1)S(1)} %pad_maximum_fusion.1), channel_id=1, source_target_pairs={{6,0},{7,1},{14,8},{15,9},{22,16},{23,17},{30,24},{31,25}} | collective-permute-start | bytes 196616 | tf_op jit(solution)/shard_map/ppermute | solution.py:97
  19.9 2.6 %collective-permute-done.3 = bf16[128,256]{1,0:T(8,128)(2,1)S(1)} collective-permute-done((bf16[128,256]{1,0:T(8,128)(2,1)S(1)}, bf16[128,256]{1,0:T(8,128)(2,1)S(1)}, u32[]{:S(2)}, u32[]{:S(2)}) %collective-permute-start.3) | collective-permute-done | bytes 65568 | tf_op jit(solution)/shard_map/ppermute | solution.py:97
  22.5 2.8 %collective-permute-done.4 = bf16[128,256]{1,0:T(8,128)(2,1)S(1)} collective-permute-done((bf16[128,256]{1,0:T(8,128)(2,1)S(1)}, bf16[128,256]{1,0:T(8,128)(2,1)S(1)}, u32[]{:S(2)}, u32[]{:S(2)}) %collective-permute-start.4) | collective-permute-done | bytes 65568 | tf_op jit(solution)/shard_map/ppermute | solution.py:97
  25.2 2.5 %collective-permute-done.5 = bf16[128,256]{1,0:T(8,128)(2,1)S(1)} collective-permute-done((bf16[128,256]{1,0:T(8,128)(2,1)S(1)}, bf16[128,256]{1,0:T(8,128)(2,1)S(1)}, u32[]{:S(2)}, u32[]{:S(2)}) %collective-permute-start.5) | collective-permute-done | bytes 65568 | tf_op jit(solution)/shard_map/ppermute | solution.py:97
  27.8 1.5 %collective-permute-done.6 = bf16[512,256]{1,0:T(8,128)(2,1)S(1)} collective-permute-done((bf16[512,256]{1,0:T(8,128)(2,1)S(1)}, bf16[512,256]{1,0:T(8,128)(2,1)S(1)}, u32[]{:S(2)}, u32[]{:S(2)}) %collective-permute-start.6) | collective-permute-done | bytes 262176 | tf_op jit(solution)/shard_map/ppermute | solution.py:98
  29.5 4.5 %reshape.97 = bf16[9,4,2,16,16,16]{5,4,3,2,1,0:T(8,128)(2,1)} reshape(bf16[9,128,256]{2,1,0:T(8,128)(2,1)S(1)} %concatenate.25) | data formatting | bytes 1179648 | tf_op jit(solution)/shard_map/reshape | solution.py:136
  34.0 1.1 %slice_bitcast_fusion.1 = (bf16[4,1,16,16,16]{4,3,2,0,1:T(8,128)(2,1)S(1)}, bf16[4,1,16,16,16]{4,3,2,0,1:T(8,128)(2,1)S(1)}) fusion(bf16[9,4,2,16,16,16]{5,4,3,2,1,0:T(8,128)(2,1)} %reshape.97), kind=kLoop, calls=%fused_computation.8 | loop fusion | bytes 131072 | tf_op jit(solution)/shard_map/stack;squeeze | solution.py:139
  35.1 1.0 %fusion.3 = bf16[4,1,16,16,16]{4,3,2,0,1:T(8,128)(2,1)S(1)} fusion(bf16[9,4,2,16,16,16]{5,4,3,2,1,0:T(8,128)(2,1)} %reshape.97), kind=kLoop, calls=%fused_computation.93 | loop fusion | flops 16384 | bytes 65536 | tf_op jit(solution)/shard_map/neg | solution.py:139
  36.5 0.8 %copy.46 = bf16[16,2,16,4,2,16]{5,4,3,2,1,0:T(2,128)(2,1)S(1)} copy(bf16[16,2,16,4,2,16]{2,5,0,3,4,1:T(8,128)(2,1)S(1)} %maximum_bitcast_fusion) | data formatting | bytes 262144 | tf_op jit(solution)/shard_map/transpose | solution.py:142
  37.3 0.7 reshape.98
  38.0 11.6 %copy.47 = bf16[16,4,2,16,9,16]{3,2,1,5,4,0:T(2,128)(2,1)} copy(bf16[16,4,2,16,9,16]{5,3,0,2,1,4:T(8,128)(2,1)} %bitcast.114) | data formatting | bytes 1179648 | tf_op jit(solution)/shard_map/transpose | solution.py:141
  49.6 13.0 %reshape.99 = bf16[16,128,144]{1,2,0:T(8,128)(2,1)S(1)} reshape(bf16[16,4,2,16,9,16]{3,2,1,5,4,0:T(2,128)(2,1)} %copy.47) | data formatting | bytes 1179648 | tf_op jit(solution)/shard_map/reshape | solution.py:141
  62.7 0.5 fusion.5
  63.1 0.6 fusion.4
  64.2 1.3 %collective-permute-start.9 = (f32[64,512]{1,0:T(8,128)S(1)}, f32[64,512]{1,0:T(8,128)S(1)}, u32[]{:S(2)}, u32[]{:S(2)}) collective-permute-start(f32[64,512]{1,0:T(8,128)S(1)} %get-tuple-element.10), channel_id=1, source_target_pairs={{8,0},{16,8},{9,1},{17,9},{10,2},{18,10},{11,3},{19,11},{12,4},{20... | collective-permute-start | bytes 393224 | tf_op jit(solution)/shard_map/ppermute | solution.py:157
  65.5 1.3 %collective-permute-start.8 = (f32[64,512]{1,0:T(8,128)S(1)}, f32[64,512]{1,0:T(8,128)S(1)}, u32[]{:S(2)}, u32[]{:S(2)}) collective-permute-start(f32[64,512]{1,0:T(8,128)S(1)} %get-tuple-element.11), channel_id=1, source_target_pairs={{16,0},{24,8},{17,1},{25,9},{18,2},{26,10},{19,3},{27,11},{20,4},{... | collective-permute-start | bytes 393224 | tf_op jit(solution)/shard_map/ppermute | solution.py:157
  66.8 4.6 %collective-permute-start.7 = (f32[64,512]{1,0:T(8,128)S(1)}, f32[64,512]{1,0:T(8,128)S(1)}, u32[]{:S(2)}, u32[]{:S(2)}) collective-permute-start(f32[64,512]{1,0:T(8,128)S(1)} %get-tuple-element.12), channel_id=1, source_target_pairs={{0,8},{24,0},{1,9},{25,1},{2,10},{26,2},{3,11},{27,3},{4,12},{28,4... | collective-permute-start | bytes 393224 | tf_op jit(solution)/shard_map/ppermute | solution.py:157
  71.7 1.7 %collective-permute-done.8 = f32[64,512]{1,0:T(8,128)S(1)} collective-permute-done((f32[64,512]{1,0:T(8,128)S(1)}, f32[64,512]{1,0:T(8,128)S(1)}, u32[]{:S(2)}, u32[]{:S(2)}) %collective-permute-start.8) | collective-permute-done | bytes 131104 | tf_op jit(solution)/shard_map/ppermute | solution.py:157
  73.4 2.8 %collective-permute-done.7 = f32[64,512]{1,0:T(8,128)S(1)} collective-permute-done((f32[64,512]{1,0:T(8,128)S(1)}, f32[64,512]{1,0:T(8,128)S(1)}, u32[]{:S(2)}, u32[]{:S(2)}) %collective-permute-start.7) | collective-permute-done | bytes 131104 | tf_op jit(solution)/shard_map/ppermute | solution.py:157
  76.2 0.6 gather_fusion
  77.5 1.1 %copy.67 = f32[64,16,128]{2,1,0:T(8,128)} copy(f32[64,16,128]{0,2,1:T(8,128)S(1)} %bitcast.116) | data formatting | bytes 1048576 | tf_op jit(solution)/shard_map/reshape | solution.py:163
  (55 shorter events, 2.0 us)
Async XLA Ops:
  7.7 6.6 %collective-permute-start = (bf16[32,256]{1,0:T(8,128)(2,1)S(1)}, bf16[32,256]{1,0:T(8,128)(2,1)S(1)}, u32[]{:S(2)}, u32[]{:S(2)}) collective-permute-start(bf16[32,256]{1,0:T(8,128)(2,1)S(1)} %get-tuple-element.39), channel_id=1, source_target_pairs={{0,8},{8,16},{16,24},{24,0},{1,9},{9,17},{17,25},{25,1},{2,10},{10... | collective-permute-start | bytes 49160 | tf_op jit(solution)/shard_map/ppermute | solution.py:128
  10.7 3.7 %collective-permute-start.1 = (bf16[32,256]{1,0:T(8,128)(2,1)S(1)}, bf16[32,256]{1,0:T(8,128)(2,1)S(1)}, u32[]{:S(2)}, u32[]{:S(2)}) collective-permute-start(bf16[32,256]{1,0:T(8,128)(2,1)S(1)} %get-tuple-element.38), channel_id=1, source_target_pairs={{0,16},{8,24},{16,0},{24,8},{1,17},{9,25},{17,1},{25,9},{2,18},{10... | collective-permute-start | bytes 49160 | tf_op jit(solution)/shard_map/ppermute | solution.py:128
  12.2 3.7 %collective-permute-start.2 = (bf16[32,256]{1,0:T(8,128)(2,1)S(1)}, bf16[32,256]{1,0:T(8,128)(2,1)S(1)}, u32[]{:S(2)}, u32[]{:S(2)}) collective-permute-start(bf16[32,256]{1,0:T(8,128)(2,1)S(1)} %get-tuple-element.37), channel_id=1, source_target_pairs={{0,24},{8,0},{16,8},{24,16},{1,25},{9,1},{17,9},{25,17},{2,26},{10... | collective-permute-start | bytes 49160 | tf_op jit(solution)/shard_map/ppermute | solution.py:128
  16.0 6.5 %collective-permute-start.3 = (bf16[128,256]{1,0:T(8,128)(2,1)S(1)}, bf16[128,256]{1,0:T(8,128)(2,1)S(1)}, u32[]{:S(2)}, u32[]{:S(2)}) collective-permute-start(bf16[128,256]{1,0:T(8,128)(2,1)S(1)} %pad_maximum_fusion.1), channel_id=1, source_target_pairs={{2,0},{3,1},{4,2},{5,3},{6,4},{7,5},{10,8},{11,9},{12,10},{13,11},... | collective-permute-start | bytes 196616 | tf_op jit(solution)/shard_map/ppermute | solution.py:97
  17.2 8.0 %collective-permute-start.4 = (bf16[128,256]{1,0:T(8,128)(2,1)S(1)}, bf16[128,256]{1,0:T(8,128)(2,1)S(1)}, u32[]{:S(2)}, u32[]{:S(2)}) collective-permute-start(bf16[128,256]{1,0:T(8,128)(2,1)S(1)} %pad_maximum_fusion.1), channel_id=1, source_target_pairs={{4,0},{5,1},{6,2},{7,3},{12,8},{13,9},{14,10},{15,11},{20,16},{21,... | collective-permute-start | bytes 196616 | tf_op jit(solution)/shard_map/ppermute | solution.py:97
  18.5 9.1 %collective-permute-start.5 = (bf16[128,256]{1,0:T(8,128)(2,1)S(1)}, bf16[128,256]{1,0:T(8,128)(2,1)S(1)}, u32[]{:S(2)}, u32[]{:S(2)}) collective-permute-start(bf16[128,256]{1,0:T(8,128)(2,1)S(1)} %pad_maximum_fusion.1), channel_id=1, source_target_pairs={{6,0},{7,1},{14,8},{15,9},{22,16},{23,17},{30,24},{31,25}} | collective-permute-start | bytes 196616 | tf_op jit(solution)/shard_map/ppermute | solution.py:97
  27.7 1.5 %collective-permute-start.6 = (bf16[512,256]{1,0:T(8,128)(2,1)S(1)}, bf16[512,256]{1,0:T(8,128)(2,1)S(1)}, u32[]{:S(2)}, u32[]{:S(2)}) collective-permute-start(bf16[512,256]{1,0:T(8,128)(2,1)S(1)} %constant_dynamic-update-slice_fusion), channel_id=1, source_target_pairs={{0,1},{1,0},{2,3},{3,2},{4,5},{5,4},{6,7},{7,6},{8,9},{9,8},{10,11... | collective-permute-start | bytes 786440 | tf_op jit(solution)/shard_map/ppermute | solution.py:98
  64.2 7.4 %collective-permute-start.9 = (f32[64,512]{1,0:T(8,128)S(1)}, f32[64,512]{1,0:T(8,128)S(1)}, u32[]{:S(2)}, u32[]{:S(2)}) collective-permute-start(f32[64,512]{1,0:T(8,128)S(1)} %get-tuple-element.10), channel_id=1, source_target_pairs={{8,0},{16,8},{9,1},{17,9},{10,2},{18,10},{11,3},{19,11},{12,4},{20... | collective-permute-start | bytes 393224 | tf_op jit(solution)/shard_map/ppermute | solution.py:157
  65.5 7.8 %collective-permute-start.8 = (f32[64,512]{1,0:T(8,128)S(1)}, f32[64,512]{1,0:T(8,128)S(1)}, u32[]{:S(2)}, u32[]{:S(2)}) collective-permute-start(f32[64,512]{1,0:T(8,128)S(1)} %get-tuple-element.11), channel_id=1, source_target_pairs={{16,0},{24,8},{17,1},{25,9},{18,2},{26,10},{19,3},{27,11},{20,4},{... | collective-permute-start | bytes 393224 | tf_op jit(solution)/shard_map/ppermute | solution.py:157
  66.8 9.3 %collective-permute-start.7 = (f32[64,512]{1,0:T(8,128)S(1)}, f32[64,512]{1,0:T(8,128)S(1)}, u32[]{:S(2)}, u32[]{:S(2)}) collective-permute-start(f32[64,512]{1,0:T(8,128)S(1)} %get-tuple-element.12), channel_id=1, source_target_pairs={{0,8},{24,0},{1,9},{25,1},{2,10},{26,2},{3,11},{27,3},{4,12},{28,4... | collective-permute-start | bytes 393224 | tf_op jit(solution)/shard_map/ppermute | solution.py:157

commit v7 on v5

--- a/solution.py
+++ b/solution.py
@@ -56,22 +56,37 @@
     ) / count_ref[...]
     water_level = jnp.sum(power, axis=-1, keepdims=True) / NF
     gain_of = live_ref[...] / jnp.sqrt(smooth + 0.1 * water_level + 1e-06)
-    out_ref[...] = (spectra * gain_of).astype(out_ref.dtype)
+    whitened = spectra * gain_of
+    groups, _, lanes_out = out_ref.shape
+    width = 2 * LANES // (2 * groups)
+    per_vreg = LANES // width
+    lane = lax.broadcasted_iota(jnp.int32, (channels, LANES), 1)
+    for g in range(groups):
+        for v in range(lanes_out // LANES):
+            gathered = jnp.zeros((channels, LANES), jnp.float32)
+            for slot in range(per_vreg):
+                w = v * per_vreg + slot
+                piece = whitened[w * channels : (w + 1) * channels]
+                piece = pltpu.roll(piece, (slot - g) * width % LANES, 1)
+                inside = (lane >= slot * width) & (lane < (slot + 1) * width)
+                gathered = jnp.where(inside, piece, gathered)
+            out_ref[g, :, pl.ds(v * LANES, LANES)] = gathered.astype(out_ref.dtype)
 
 
-def whiten(record_rows, starts, live_mask):
+def whiten(record_rows, starts, live_mask, groups):
     channels, _ = record_rows.shape
     windows = starts.shape[0]
-    blocks = NT // LANES
-    table = jnp.asarray(spectral_table())
-    lane_bin = np.arange(2 * NF) % NF
+    per_group = NF // groups
+    lane_group, lane_part, lane_bin = np.unravel_index(np.arange(2 * NF), (groups, 2, per_group))
+    lane_bin = lane_group * per_group + lane_bin
+    table = jnp.asarray(spectral_table()[:, lane_part * NF + lane_bin])
     near = (np.abs(lane_bin[:, None] - lane_bin[None, :]) <= 4).astype(np.float32)
-    count = near[:NF].sum(axis=0, keepdims=True)
+    count = (np.abs(np.arange(NF)[:, None] - lane_bin[None, :]) <= 4).sum(axis=0, keepdims=True).astype(np.float32)
     live_rows = jnp.tile(live_mask.astype(jnp.float32), windows)[:, None]
     vmem = pl.BlockSpec(memory_space=pltpu.VMEM)
-    out = pl.pallas_call(
+    return pl.pallas_call(
         whiten_kernel,
-        out_shape=jax.ShapeDtypeStruct((windows * channels, 2 * NF), jnp.bfloat16),
+        out_shape=jax.ShapeDtypeStruct((groups, channels, windows * 2 * per_group), jnp.bfloat16),
         in_specs=[pl.BlockSpec(memory_space=pltpu.SMEM), pl.BlockSpec(memory_space=pl.ANY), vmem, vmem, vmem, vmem],
         out_specs=vmem,
         scratch_shapes=[
@@ -80,7 +95,6 @@
             pltpu.SemaphoreType.DMA((windows,)),
         ],
     )(starts, record_rows, table, jnp.asarray(near), jnp.asarray(count), live_rows)
-    return out.reshape(windows, channels, 2 * NF)
 
 
 def halo(mine, hops, fibre_count):
@@ -106,8 +120,9 @@
 def shards(record, offsets, live_mask):
     seg_count = lax.axis_size("seg")
     fibre_count = lax.axis_size("fibre")
-    own_block = whiten(record[0], offsets[0], live_mask)
-    windows_count, block, _ = own_block.shape
+    windows_count = offsets.shape[1]
+    block = record.shape[1]
+    split = whiten(record[0], offsets[0], live_mask, seg_count)
     channels = block * fibre_count
     per_owner = BAND // seg_count
     bins_each = NF // seg_count
@@ -119,8 +134,6 @@
     me = lax.axis_index("seg")
     rows = seg_count * windows_count
 
-    split = own_block.reshape(windows_count, block, 2, seg_count, bins_each).transpose(3, 1, 0, 2, 4)
-    split = split.reshape(seg_count, block, windows_count * 2 * bins_each)
     gathered = [lax.dynamic_index_in_dim(split, me, 0, keepdims=False)]
     for step in range(1, seg_count):
         sent = lax.dynamic_index_in_dim(split, (me + step) % seg_count, 0, keepdims=False)

time: 50.3 us -> 48.8 us (0.970)
  local copies, waits for them, and re-layouts: 10 us -> 8.41 us
    another operation x2 -> x0, local copies, waits for them, and re-layouts: 1.6 us -> none  [shards(): own_block.reshape(windows_count, block, 2, seg_count, bins_each)]
    squeeze x1, local copies, waits for them, and re-layouts: 0.02 us -> 0.79 us  [shards(): gathered = [lax.dynamic_index_in_dim(split, me, 0, keepdims=False)]]
    reshape x1 -> x0, local copies, waits for them, and re-layouts: 0.75 us -> none  [shards(): split = split.reshape(seg_count, block, windows_count * 2 * bins_each)]
where the time goes in v7:
time: 48.8 us; the launch traced here: 48.4 us
  waiting for transfers between devices  17.4 us (36%)
  starting transfers between devices  15.3 us (31%)
  local copies, waits for them, and re-layouts  8.41 us (17%)
  Pallas kernels  5.54 us (11%)
  matrix products  0.73 us (1%)
  other arithmetic  0.57 us (1%)
    ppermute x3, waiting for transfers between devices, halo(): own.append(lax.ppermute(mine, 'fibre', pairs))  7.84 us
    ppermute x3, starting transfers between devices, shards(): gathered.append(lax.ppermute(sent, 'seg', pairs))  5.89 us
    ppermute x3, waiting for transfers between devices, shards(): collected.append(lax.ppermute(sent, 'seg', pairs))  5.82 us
    pallas_call x1, Pallas kernels, whiten(): pl.pallas_call(whiten_kernel, out_shape=jax.ShapeDtypeStruct((groups, cha...  5.54 us
    ppermute x3, starting transfers between devices, shards(): collected.append(lax.ppermute(sent, 'seg', pairs))  5.46 us
    ppermute x3, starting transfers between devices, halo(): own.append(lax.ppermute(mine, 'fibre', pairs))  3.88 us
    unnamed x32, local copies, waits for them, and re-layouts  2.34 us
    ppermute x3, waiting for transfers between devices, shards(): gathered.append(lax.ppermute(sent, 'seg', pairs))  2.31 us
  transfers between devices with their start and end apart: 10, of which 9 were waited for; matrix products, arithmetic and copies ran while one was open for 0% of the time, Pallas kernels for 0%

profile of v7, /device:TPU:0, one launch (start us, length us, event | category | flops | bytes accessed | tf_op | source)
XLA Modules:
  0.0 48.4 jit_solution(9294276897127133017)
XLA Ops:
  0.0 0.7 %copy-done.1 = s32[16]{0:T(128)S(1)} copy-done((s32[16]{0:T(128)S(1)}, s32[16]{0:T(128)}, u32[]{:S(2)}) %copy-start.1) | copy-done | bytes 88
  0.7 0.8 %broadcast_in_dim_tile.4.live_ref = f32[256,1]{1,0:T(8,128)} reshape(f32[16,16]{1,0:T(8,128)S(1)} %tile.2) | data formatting | bytes 2048 | tf_op jit(solution)/shard_map/broadcast_in_dim;tile | solution.py:85
  1.4 5.5 %shard_map.64 = bf16[4,16,512]{2,1,0:T(8,128)(2,1)} custom-call(s32[16]{0:T(128)} %bitcast.109, bf16[16,27648]{1,0:T(8,128)(2,1)} %bitcast.89, bf16[3072,128]{1,0:T(8,128)(2,1)} %constant.102.clone.table_ref, f32[128,128]{1,0:T(8,128)} %constant.103.clone.near_ref, f32[1,128]{1,0:T(1,128)} %constant.104.clone.count_ref, f32[256,1]{1,0:T(8,128)} %broadcast_in_dim_tile.4.live_ref), custom_call_target="tpu_custom_call" | custom-call | tf_op jit(solution)/shard_map/pallas_call | solution.py:87
  7.0 0.8 %dynamic-slice_bitcast_fusion.6 = (bf16[16,512]{1,0:T(8,128)(2,1)S(1)}, bf16[16,512]{1,0:T(8,128)(2,1)S(1)}, bf16[16,512]{1,0:T(8,128)(2,1)S(1)}, bf16[16,512]{1,0:T(8,128)(2,1)S(1)}) fusion(bf16[4,16,512]{2,1,0:T(8,128)(2,1)} %shard_map.64, s32[]{:T(128)S(6)} %select_n.93, s32[]{:T(128)S(6)} %select_n.99, s32[]{:T(128)S(6)} %select_n.97, s32[]{:T(128)S(6)} %select_n.95), kind=kLoop, calls=%fused_computation.51 | loop fusion | bytes 131088 | tf_op jit(solution)/shard_map/jit(dynamic_index_in_dim)/squeeze | solution.py:137
  7.8 2.9 %collective-permute-start = (bf16[16,512]{1,0:T(8,128)(2,1)S(1)}, bf16[16,512]{1,0:T(8,128)(2,1)S(1)}, u32[]{:S(2)}, u32[]{:S(2)}) collective-permute-start(bf16[16,512]{1,0:T(8,128)(2,1)S(1)} %get-tuple-element.38), channel_id=1, source_target_pairs={{0,8},{8,16},{16,24},{24,0},{1,9},{9,17},{17,25},{25,1},{2,10},{10... | collective-permute-start | bytes 49160 | tf_op jit(solution)/shard_map/ppermute | solution.py:141
  10.7 1.5 %collective-permute-start.1 = (bf16[16,512]{1,0:T(8,128)(2,1)S(1)}, bf16[16,512]{1,0:T(8,128)(2,1)S(1)}, u32[]{:S(2)}, u32[]{:S(2)}) collective-permute-start(bf16[16,512]{1,0:T(8,128)(2,1)S(1)} %get-tuple-element.37), channel_id=1, source_target_pairs={{0,16},{8,24},{16,0},{24,8},{1,17},{9,25},{17,1},{25,9},{2,18},{10... | collective-permute-start | bytes 49160 | tf_op jit(solution)/shard_map/ppermute | solution.py:141
  12.2 1.4 %collective-permute-start.2 = (bf16[16,512]{1,0:T(8,128)(2,1)S(1)}, bf16[16,512]{1,0:T(8,128)(2,1)S(1)}, u32[]{:S(2)}, u32[]{:S(2)}) collective-permute-start(bf16[16,512]{1,0:T(8,128)(2,1)S(1)} %get-tuple-element.36), channel_id=1, source_target_pairs={{0,24},{8,0},{16,8},{24,16},{1,25},{9,1},{17,9},{25,17},{2,26},{10... | collective-permute-start | bytes 49160 | tf_op jit(solution)/shard_map/ppermute | solution.py:141
  13.7 0.8 %collective-permute-done.1 = bf16[16,512]{1,0:T(8,128)(2,1)S(1)} collective-permute-done((bf16[16,512]{1,0:T(8,128)(2,1)S(1)}, bf16[16,512]{1,0:T(8,128)(2,1)S(1)}, u32[]{:S(2)}, u32[]{:S(2)}) %collective-permute-start.1) | collective-permute-done | bytes 16416 | tf_op jit(solution)/shard_map/ppermute | solution.py:141
  14.4 1.5 %collective-permute-done.2 = bf16[16,512]{1,0:T(8,128)(2,1)S(1)} collective-permute-done((bf16[16,512]{1,0:T(8,128)(2,1)S(1)}, bf16[16,512]{1,0:T(8,128)(2,1)S(1)}, u32[]{:S(2)}, u32[]{:S(2)}) %collective-permute-start.2) | collective-permute-done | bytes 16416 | tf_op jit(solution)/shard_map/ppermute | solution.py:141
  16.0 1.3 %collective-permute-start.3 = (bf16[16,2048]{1,0:T(8,128)(2,1)S(1)}, bf16[16,2048]{1,0:T(8,128)(2,1)S(1)}, u32[]{:S(2)}, u32[]{:S(2)}) collective-permute-start(bf16[16,2048]{1,0:T(8,128)(2,1)S(1)} %get-tuple-element.33), channel_id=1, source_target_pairs={{2,0},{3,1},{4,2},{5,3},{6,4},{7,5},{10,8},{11,9},{12,10},{13,11},... | collective-permute-start | bytes 196616 | tf_op jit(solution)/shard_map/ppermute | solution.py:111
  17.3 1.3 %collective-permute-start.4 = (bf16[16,2048]{1,0:T(8,128)(2,1)S(1)}, bf16[16,2048]{1,0:T(8,128)(2,1)S(1)}, u32[]{:S(2)}, u32[]{:S(2)}) collective-permute-start(bf16[16,2048]{1,0:T(8,128)(2,1)S(1)} %get-tuple-element.33), channel_id=1, source_target_pairs={{4,0},{5,1},{6,2},{7,3},{12,8},{13,9},{14,10},{15,11},{20,16},{21,... | collective-permute-start | bytes 196616 | tf_op jit(solution)/shard_map/ppermute | solution.py:111
  18.6 1.3 %collective-permute-start.5 = (bf16[16,2048]{1,0:T(8,128)(2,1)S(1)}, bf16[16,2048]{1,0:T(8,128)(2,1)S(1)}, u32[]{:S(2)}, u32[]{:S(2)}) collective-permute-start(bf16[16,2048]{1,0:T(8,128)(2,1)S(1)} %get-tuple-element.33), channel_id=1, source_target_pairs={{6,0},{7,1},{14,8},{15,9},{22,16},{23,17},{30,24},{31,25}} | collective-permute-start | bytes 196616 | tf_op jit(solution)/shard_map/ppermute | solution.py:111
  19.9 2.7 %collective-permute-done.3 = bf16[16,2048]{1,0:T(8,128)(2,1)S(1)} collective-permute-done((bf16[16,2048]{1,0:T(8,128)(2,1)S(1)}, bf16[16,2048]{1,0:T(8,128)(2,1)S(1)}, u32[]{:S(2)}, u32[]{:S(2)}) %collective-permute-start.3) | collective-permute-done | bytes 65568 | tf_op jit(solution)/shard_map/ppermute | solution.py:111
  22.6 2.6 %collective-permute-done.4 = bf16[16,2048]{1,0:T(8,128)(2,1)S(1)} collective-permute-done((bf16[16,2048]{1,0:T(8,128)(2,1)S(1)}, bf16[16,2048]{1,0:T(8,128)(2,1)S(1)}, u32[]{:S(2)}, u32[]{:S(2)}) %collective-permute-start.4) | collective-permute-done | bytes 65568 | tf_op jit(solution)/shard_map/ppermute | solution.py:111
  25.3 2.5 %collective-permute-done.5 = bf16[16,2048]{1,0:T(8,128)(2,1)S(1)} collective-permute-done((bf16[16,2048]{1,0:T(8,128)(2,1)S(1)}, bf16[16,2048]{1,0:T(8,128)(2,1)S(1)}, u32[]{:S(2)}, u32[]{:S(2)}) %collective-permute-start.5) | collective-permute-done | bytes 65568 | tf_op jit(solution)/shard_map/ppermute | solution.py:111
  27.9 1.4 %collective-permute-done.6 = bf16[64,2048]{1,0:T(8,128)(2,1)S(1)} collective-permute-done((bf16[64,2048]{1,0:T(8,128)(2,1)S(1)}, bf16[64,2048]{1,0:T(8,128)(2,1)S(1)}, u32[]{:S(2)}, u32[]{:S(2)}) %collective-permute-start.6) | collective-permute-done | bytes 262176 | tf_op jit(solution)/shard_map/ppermute | solution.py:112
  29.6 0.3 copy.94
  29.8 0.5 %copy-done = bf16[128,2048]{1,0:T(8,128)(2,1)} copy-done((bf16[128,2048]{1,0:T(8,128)(2,1)}, bf16[128,2048]{1,0:T(8,128)(2,1)S(1)}, u32[]{:S(2)}) %copy-start) | copy-done | bytes 524312
  30.9 0.3 copy.77
  31.1 0.6 %slice-done = bf16[16,2048]{1,0:T(8,128)(2,1)S(1)} async-done(((bf16[128,2048]{1,0:T(8,128)(2,1)}), bf16[16,2048]{1,0:T(8,128)(2,1)S(1)}, s32[]{:S(2)}) %slice-start) | async-done | bytes 65560 | tf_op jit(solution)/shard_map/stack | solution.py:152
  31.7 0.4 stack.33
  32.1 0.4 copy.51
  32.6 0.7 %convolution_bitcast_fusion = f32[16,2,16,144]{3,2,1,0:T(8,128)S(1)} fusion(bf16[144,64,2,16,1]{0,3,2,1,4:T(8,128)(2,1)S(1)} %bitcast.84, bf16[1,16,64,2,16]{2,1,3,0,4:T(8,128)(2,1)S(1)} %maximum_bitcast_fusion, bf16[1,16,64,2,16]{2,1,3,0,4:T(8,128)(2,1)S(1)} %copy.51), kind=kOutput, calls=%fused_computation.1 | convolution fusion | flops 18939904 | bytes 1015808 | tf_op jit(solution)/shard_map/ocspn,jspn->nocj/dot_general | solution.py:153
  33.3 0.6 %fusion.9 = (f32[16,2,1,128]{3,2,1,0:T(1,128)S(1)}, f32[16,2,1,128]{3,2,1,0:T(1,128)S(1)}, f32[16,2,1,128]{3,2,1,0:T(1,128)S(1)}, f32[16,2,1,128]{3,2,1,0:T(1,12...) fusion(f32[16,2,16,144]{3,2,1,0:T(8,128)S(1)} %convolution_bitc, ...), kind=kLoop, calls=%fused_computation.68 | loop fusion | bytes 524288 | tf_op jit(solution)/shard_map/slice | solution.py:154
  34.5 2.9 %collective-permute-start.7 = (f32[64,512]{1,0:T(8,128)S(1)}, f32[64,512]{1,0:T(8,128)S(1)}, u32[]{:S(2)}, u32[]{:S(2)}) collective-permute-start(f32[64,512]{1,0:T(8,128)S(1)} %get-tuple-element.10), channel_id=1, source_target_pairs={{0,8},{24,0},{1,9},{25,1},{2,10},{26,2},{3,11},{27,3},{4,12},{28,4... | collective-permute-start | bytes 393224 | tf_op jit(solution)/shard_map/ppermute | solution.py:166
  37.4 1.3 %collective-permute-start.8 = (f32[64,512]{1,0:T(8,128)S(1)}, f32[64,512]{1,0:T(8,128)S(1)}, u32[]{:S(2)}, u32[]{:S(2)}) collective-permute-start(f32[64,512]{1,0:T(8,128)S(1)} %get-tuple-element.9), channel_id=1, source_target_pairs={{16,0},{24,8},{17,1},{25,9},{18,2},{26,10},{19,3},{27,11},{20,4},{... | collective-permute-start | bytes 393224 | tf_op jit(solution)/shard_map/ppermute | solution.py:166
  38.7 1.3 %collective-permute-start.9 = (f32[64,512]{1,0:T(8,128)S(1)}, f32[64,512]{1,0:T(8,128)S(1)}, u32[]{:S(2)}, u32[]{:S(2)}) collective-permute-start(f32[64,512]{1,0:T(8,128)S(1)} %get-tuple-element.8), channel_id=1, source_target_pairs={{8,0},{16,8},{9,1},{17,9},{10,2},{18,10},{11,3},{19,11},{12,4},{20... | collective-permute-start | bytes 393224 | tf_op jit(solution)/shard_map/ppermute | solution.py:166
  40.1 2.9 %collective-permute-done.7 = f32[64,512]{1,0:T(8,128)S(1)} collective-permute-done((f32[64,512]{1,0:T(8,128)S(1)}, f32[64,512]{1,0:T(8,128)S(1)}, u32[]{:S(2)}, u32[]{:S(2)}) %collective-permute-start.7) | collective-permute-done | bytes 131104 | tf_op jit(solution)/shard_map/ppermute | solution.py:166
  43.0 2.7 %collective-permute-done.8 = f32[64,512]{1,0:T(8,128)S(1)} collective-permute-done((f32[64,512]{1,0:T(8,128)S(1)}, f32[64,512]{1,0:T(8,128)S(1)}, u32[]{:S(2)}, u32[]{:S(2)}) %collective-permute-start.8) | collective-permute-done | bytes 131104 | tf_op jit(solution)/shard_map/ppermute | solution.py:166
  45.9 0.6 %gather_fusion = f32[4,64,512]{2,1,0:T(8,128)S(1)} fusion(f32[4,64,512]{2,1,0:T(8,128)S(1)} %pad_maximum_fusion, s32[1024]{0:T(1024)S(1)} %pad_clamp_fusion), kind=kCustom, calls=%fused_computation | custom fusion | bytes 1048592 | tf_op jit(solution)/shard_map/jit(_take)/gather | solution.py:171
  46.5 0.3 copy.70
  47.2 1.1 %copy.72 = f32[64,16,128]{2,1,0:T(8,128)} copy(f32[64,16,128]{0,2,1:T(8,128)S(1)} %bitcast.86) | data formatting | bytes 1048576 | tf_op jit(solution)/shard_map/reshape | solution.py:172
  (54 shorter events, 2.0 us)
Async XLA Ops:
  0.0 0.7 %copy-start.1 = (s32[16]{0:T(128)S(1)}, s32[16]{0:T(128)}, u32[]{:S(2)}) copy-start(s32[16]{0:T(128)} %param.8) | copy-start | bytes 196
  7.8 5.9 %collective-permute-start = (bf16[16,512]{1,0:T(8,128)(2,1)S(1)}, bf16[16,512]{1,0:T(8,128)(2,1)S(1)}, u32[]{:S(2)}, u32[]{:S(2)}) collective-permute-start(bf16[16,512]{1,0:T(8,128)(2,1)S(1)} %get-tuple-element.38), channel_id=1, source_target_pairs={{0,8},{8,16},{16,24},{24,0},{1,9},{9,17},{17,25},{25,1},{2,10},{10... | collective-permute-start | bytes 49160 | tf_op jit(solution)/shard_map/ppermute | solution.py:141
  10.7 3.7 %collective-permute-start.1 = (bf16[16,512]{1,0:T(8,128)(2,1)S(1)}, bf16[16,512]{1,0:T(8,128)(2,1)S(1)}, u32[]{:S(2)}, u32[]{:S(2)}) collective-permute-start(bf16[16,512]{1,0:T(8,128)(2,1)S(1)} %get-tuple-element.37), channel_id=1, source_target_pairs={{0,16},{8,24},{16,0},{24,8},{1,17},{9,25},{17,1},{25,9},{2,18},{10... | collective-permute-start | bytes 49160 | tf_op jit(solution)/shard_map/ppermute | solution.py:141
  12.2 3.7 %collective-permute-start.2 = (bf16[16,512]{1,0:T(8,128)(2,1)S(1)}, bf16[16,512]{1,0:T(8,128)(2,1)S(1)}, u32[]{:S(2)}, u32[]{:S(2)}) collective-permute-start(bf16[16,512]{1,0:T(8,128)(2,1)S(1)} %get-tuple-element.36), channel_id=1, source_target_pairs={{0,24},{8,0},{16,8},{24,16},{1,25},{9,1},{17,9},{25,17},{2,26},{10... | collective-permute-start | bytes 49160 | tf_op jit(solution)/shard_map/ppermute | solution.py:141
  16.0 6.6 %collective-permute-start.3 = (bf16[16,2048]{1,0:T(8,128)(2,1)S(1)}, bf16[16,2048]{1,0:T(8,128)(2,1)S(1)}, u32[]{:S(2)}, u32[]{:S(2)}) collective-permute-start(bf16[16,2048]{1,0:T(8,128)(2,1)S(1)} %get-tuple-element.33), channel_id=1, source_target_pairs={{2,0},{3,1},{4,2},{5,3},{6,4},{7,5},{10,8},{11,9},{12,10},{13,11},... | collective-permute-start | bytes 196616 | tf_op jit(solution)/shard_map/ppermute | solution.py:111
  17.3 8.0 %collective-permute-start.4 = (bf16[16,2048]{1,0:T(8,128)(2,1)S(1)}, bf16[16,2048]{1,0:T(8,128)(2,1)S(1)}, u32[]{:S(2)}, u32[]{:S(2)}) collective-permute-start(bf16[16,2048]{1,0:T(8,128)(2,1)S(1)} %get-tuple-element.33), channel_id=1, source_target_pairs={{4,0},{5,1},{6,2},{7,3},{12,8},{13,9},{14,10},{15,11},{20,16},{21,... | collective-permute-start | bytes 196616 | tf_op jit(solution)/shard_map/ppermute | solution.py:111
  18.6 9.1 %collective-permute-start.5 = (bf16[16,2048]{1,0:T(8,128)(2,1)S(1)}, bf16[16,2048]{1,0:T(8,128)(2,1)S(1)}, u32[]{:S(2)}, u32[]{:S(2)}) collective-permute-start(bf16[16,2048]{1,0:T(8,128)(2,1)S(1)} %get-tuple-element.33), channel_id=1, source_target_pairs={{6,0},{7,1},{14,8},{15,9},{22,16},{23,17},{30,24},{31,25}} | collective-permute-start | bytes 196616 | tf_op jit(solution)/shard_map/ppermute | solution.py:111
  27.7 1.6 %collective-permute-start.6 = (bf16[64,2048]{1,0:T(8,128)(2,1)S(1)}, bf16[64,2048]{1,0:T(8,128)(2,1)S(1)}, u32[]{:S(2)}, u32[]{:S(2)}) collective-permute-start(bf16[64,2048]{1,0:T(8,128)(2,1)S(1)} %pad_maximum_fusion.1), channel_id=1, source_target_pairs={{0,1},{1,0},{2,3},{3,2},{4,5},{5,4},{6,7},{7,6},{8,9},{9,8},{10,11... | collective-permute-start | bytes 786440 | tf_op jit(solution)/shard_map/ppermute | solution.py:112
  29.6 0.8 %copy-start = (bf16[128,2048]{1,0:T(8,128)(2,1)}, bf16[128,2048]{1,0:T(8,128)(2,1)S(1)}, u32[]{:S(2)}) copy-start(bf16[128,2048]{1,0:T(8,128)(2,1)S(1)} %broadcast_select_fusion) | copy-start | bytes 1572868
  30.8 0.8 %slice-start = ((bf16[128,2048]{1,0:T(8,128)(2,1)}), bf16[16,2048]{1,0:T(8,128)(2,1)S(1)}, s32[]{:S(2)}) async-start(bf16[128,2048]{1,0:T(8,128)(2,1)} %copy-done), calls=%async_computation | async-start | bytes 131072 | tf_op jit(solution)/shard_map/stack | solution.py:152
  34.5 8.4 %collective-permute-start.7 = (f32[64,512]{1,0:T(8,128)S(1)}, f32[64,512]{1,0:T(8,128)S(1)}, u32[]{:S(2)}, u32[]{:S(2)}) collective-permute-start(f32[64,512]{1,0:T(8,128)S(1)} %get-tuple-element.10), channel_id=1, source_target_pairs={{0,8},{24,0},{1,9},{25,1},{2,10},{26,2},{3,11},{27,3},{4,12},{28,4... | collective-permute-start | bytes 393224 | tf_op jit(solution)/shard_map/ppermute | solution.py:166
  37.4 8.3 %collective-permute-start.8 = (f32[64,512]{1,0:T(8,128)S(1)}, f32[64,512]{1,0:T(8,128)S(1)}, u32[]{:S(2)}, u32[]{:S(2)}) collective-permute-start(f32[64,512]{1,0:T(8,128)S(1)} %get-tuple-element.9), channel_id=1, source_target_pairs={{16,0},{24,8},{17,1},{25,9},{18,2},{26,10},{19,3},{27,11},{20,4},{... | collective-permute-start | bytes 393224 | tf_op jit(solution)/shard_map/ppermute | solution.py:166
  38.7 7.2 %collective-permute-start.9 = (f32[64,512]{1,0:T(8,128)S(1)}, f32[64,512]{1,0:T(8,128)S(1)}, u32[]{:S(2)}, u32[]{:S(2)}) collective-permute-start(f32[64,512]{1,0:T(8,128)S(1)} %get-tuple-element.8), channel_id=1, source_target_pairs={{8,0},{16,8},{9,1},{17,9},{10,2},{18,10},{11,3},{19,11},{12,4},{20... | collective-permute-start | bytes 393224 | tf_op jit(solution)/shard_map/ppermute | solution.py:166

commit v8 on v7

--- a/solution.py
+++ b/solution.py
@@ -97,24 +97,29 @@
     )(starts, record_rows, table, jnp.asarray(near), jnp.asarray(count), live_rows)
 
 
-def halo(mine, hops, fibre_count):
-    if fibre_count % 2:
-        columns = [mine]
-        for step in range(1, hops + 1):
-            pairs = [(i, i - step) for i in range(step, fibre_count)]
-            columns.append(lax.ppermute(mine, "fibre", pairs))
-        return jnp.concatenate(columns, axis=0)
-    strides = min(-(-hops // 2), (fibre_count - 1) // 2)
-    own = [mine]
-    for step in range(1, strides + 1):
-        pairs = [(i, i - 2 * step) for i in range(2 * step, fibre_count)]
-        own.append(lax.ppermute(mine, "fibre", pairs))
-    swapped = lax.ppermute(jnp.concatenate(own, axis=0), "fibre", [(i, i ^ 1) for i in range(fibre_count)])
-    swapped = jnp.split(swapped, strides + 1, axis=0)
-    even = [part for pair in zip(own, swapped) for part in pair]
-    odd = [part for pair in zip(own, swapped[1:] + [jnp.zeros_like(mine)]) for part in pair]
-    odd_side = lax.axis_index("fibre") % 2 == 1
-    return jnp.where(odd_side, jnp.concatenate(odd, axis=0), jnp.concatenate(even, axis=0))
+def window_plan(owners, fibre_count, block, per_owner, width):
+    strides, lowest = [], []
+    for owner in range(owners):
+        low = (owner * per_owner + 1) // block
+        offsets = range(low, low + width)
+        wanted = {q // 2 for q in offsets} | {(q + 1) // 2 for q in offsets}
+        strides.append(sorted(k for k in wanted if 0 < 2 * k < fibre_count))
+        lowest.append(low)
+    rounds = max(len(s) for s in strides)
+    zero = 2 * rounds + 2
+    plan = np.full((owners * 2, width), zero, np.int32)
+    for owner in range(owners):
+        for parity in range(2):
+            for i in range(width):
+                q = lowest[owner] + i
+                k, odd = divmod(q + parity, 2)
+                if q == 0:
+                    plan[owner * 2 + parity, i] = 0
+                elif k == 0:
+                    plan[owner * 2 + parity, i] = 1
+                elif k in strides[owner]:
+                    plan[owner * 2 + parity, i] = 2 + 2 * strides[owner].index(k) + (odd if parity == 0 else 1 - odd)
+    return strides, lowest, rounds, plan
 
 
 def shards(record, offsets, live_mask):
@@ -122,54 +127,65 @@
     fibre_count = lax.axis_size("fibre")
     windows_count = offsets.shape[1]
     block = record.shape[1]
-    split = whiten(record[0], offsets[0], live_mask, seg_count)
     channels = block * fibre_count
     per_owner = BAND // seg_count
-    bins_each = NF // seg_count
     live_offsets = min(BAND, channels - 1)
-    live_owners = -(-live_offsets // per_owner)
-    kept = live_owners * per_owner
-    span = block + kept
-    hops = min(-(-span // block) - 1, fibre_count - 1)
+    owners = -(-live_offsets // per_owner)
+    helpers = seg_count // owners if seg_count % owners == 0 else 1
+    owners = seg_count // helpers
+    bins_each = NF // helpers
+    width = max((o * per_owner + per_owner + block - 1) // block - (o * per_owner + 1) // block + 1 for o in range(owners))
     me = lax.axis_index("seg")
-    rows = seg_count * windows_count
+    fibre_me = lax.axis_index("fibre")
+    my_owner = me % owners
+    split = whiten(record[0], offsets[0], live_mask, helpers)
 
-    gathered = [lax.dynamic_index_in_dim(split, me, 0, keepdims=False)]
+    gathered = [lax.dynamic_index_in_dim(split, me // owners, 0, keepdims=False)]
     for step in range(1, seg_count):
-        sent = lax.dynamic_index_in_dim(split, (me + step) % seg_count, 0, keepdims=False)
+        target = (me + step) % seg_count
+        sent = lax.dynamic_index_in_dim(split, target // owners, 0, keepdims=False)
         pairs = [(i, (i + step) % seg_count) for i in range(seg_count)]
         gathered.append(lax.ppermute(sent, "seg", pairs))
     mine = jnp.concatenate(gathered, axis=1)
 
-    columns = halo(mine, hops, fibre_count)[:span]
-    if columns.shape[0] < span:
-        columns = jnp.concatenate(
-            [columns, jnp.zeros((span - columns.shape[0], columns.shape[1]), columns.dtype)], axis=0
-        )
-    right = columns.reshape(span, rows, 2, bins_each)
-    re_own = right[:block, :, 0]
-    im_own = right[:block, :, 1]
+    strides, lowest, rounds, plan = window_plan(owners, fibre_count, block, per_owner, width)
+    fetched = []
+    for r in range(rounds):
+        pairs = []
+        for s in range(seg_count):
+            if r < len(strides[s % owners]):
+                step = 2 * strides[s % owners][r]
+                pairs += [(s * fibre_count + f, s * fibre_count + f - step) for f in range(step, fibre_count)]
+        fetched.append(lax.ppermute(mine, ("seg", "fibre"), pairs) if pairs else jnp.zeros_like(mine))
+    held = jnp.stack([mine] + fetched)
+    if fibre_count % 2 == 0:
+        swapped = lax.ppermute(held, "fibre", [(i, i ^ 1) for i in range(fibre_count)])
+    else:
+        swapped = jnp.zeros_like(held)
+    pool = jnp.stack([held, swapped], axis=1).reshape((-1,) + mine.shape)
+    pool = jnp.concatenate([pool, jnp.zeros((1,) + mine.shape, mine.dtype)], axis=0)
+    pick = jnp.asarray(plan)[my_owner * 2 + fibre_me % 2]
+    right = jnp.take(pool, pick, axis=0).reshape(width * block, seg_count * windows_count, 2, bins_each)
+    re_own = mine.reshape(block, seg_count * windows_count, 2, bins_each)[:, :, 0]
+    im_own = mine.reshape(block, seg_count * windows_count, 2, bins_each)[:, :, 1]
     left = jnp.stack([jnp.stack([re_own, im_own], axis=2), jnp.stack([im_own, -re_own], axis=2)])
     cross = jnp.einsum("ocspn,jspn->nocj", left, right, preferred_element_type=jnp.float32)
-    band = jnp.stack([cross[:, :, c, c + 1 : c + 1 + kept] for c in range(block)])
+    shifts = [o * per_owner - lowest[o] * block for o in range(owners)]
+    if len(set(shifts)) > 1:
+        cross = lax.dynamic_slice_in_dim(cross, jnp.asarray(shifts, jnp.int32)[my_owner], cross.shape[3] - max(shifts), 3)
+    else:
+        cross = cross[..., shifts[0]:]
+    band = jnp.stack([cross[:, :, c, c + 1 : c + 1 + per_owner] for c in range(block)])
     band = band.transpose(3, 0, 2, 1) * (1.0 / math.sqrt(seg_count * windows_count))
-    band = band.reshape(kept, block * 2 * bins_each)
-    if kept < BAND:
-        band = jnp.concatenate([band, jnp.zeros((BAND - kept, band.shape[1]), band.dtype)], axis=0)
-    band = band.reshape(seg_count, per_owner, band.shape[1])
 
-    collected = [lax.dynamic_index_in_dim(band, me, 0, keepdims=False)]
-    for step in range(1, seg_count):
-        sent = lax.dynamic_index_in_dim(band, (me + step) % seg_count, 0, keepdims=False)
-        pairs = [(i, (i + step) % seg_count) for i in range(seg_count) if (i + step) % seg_count < live_owners]
-        if pairs:
-            collected.append(lax.ppermute(sent, "seg", pairs))
-        else:
-            collected.append(jnp.zeros_like(sent))
-    collected = jnp.stack(collected)
-    holder = (me - jnp.arange(seg_count, dtype=jnp.int32)) % seg_count
-    by_bins = jnp.take(collected, holder, axis=0).reshape(seg_count, per_owner, block, 2, bins_each)
-    return by_bins.transpose(1, 2, 3, 0, 4).reshape(per_owner, block, 2 * NF)
+    band = band.reshape(per_owner, block * 2 * bins_each)
+    parts = [band]
+    for helper in range(1, helpers):
+        pairs = [(o + owners * helper, o) for o in range(owners)]
+        parts.append(lax.ppermute(band, "seg", pairs))
+    parts = jnp.stack(parts).reshape(helpers, per_owner, block, 2, bins_each)
+    stacked = parts.transpose(1, 2, 3, 0, 4).reshape(per_owner, block, 2 * NF)
+    return jnp.where(me < owners, stacked, jnp.zeros_like(stacked))
 
 
 def solution(mesh):

time: 48.8 us -> 64.5 us (1.32)
  local copies, waits for them, and re-layouts: 8.41 us -> 15.9 us
  waiting for transfers between devices: 17.4 us -> 24.7 us
  other arithmetic: 0.57 us -> 7.22 us
  starting transfers between devices: 15.3 us -> 9.89 us
    select_n x0 -> x3, local copies, waits for them, and re-layouts: none -> 7.28 us  [the longest x1 6 us: shards(): jnp.take(pool, pick, axis=0)]
    ppermute x7 -> x4, waiting for transfers between devices: 15.1 us -> 22.2 us  [the longest x1 14.6 us: shards(): parts.append(lax.ppermute(band, 'seg', pairs))]
    ppermute x7 -> x4, starting transfers between devices: 9.41 us -> 3.95 us  [the longest x2 2.58 us: shards(): lax.ppermute(mine, ('seg', 'fibre'), pairs)]
    select_n x2 -> x3, other arithmetic: 0.07 us -> 4.63 us  [the longest x2 3.94 us: shards(): jnp.take(pool, pick, axis=0)]
    concatenate x4 -> x9, local copies, waits for them, and re-layouts: 0.17 us -> 2.41 us  [the longest x8 2.34 us: shards(): mine = jnp.concatenate(gathered, axis=1)]
    unnamed x32 -> x19, local copies, waits for them, and re-layouts: 2.34 us -> 0.16 us
    gather x2, local copies, waits for them, and re-layouts: 0.91 us -> 2.67 us  [shards(): jnp.take(pool, pick, axis=0)]
    reshape x1 -> x0, local copies, waits for them, and re-layouts: 1.15 us -> none  [shards(): return by_bins.transpose(1, 2, 3, 0, 4).reshape(per_owner, block, 2 * NF)]
  transfers between devices with their start and end apart: 10 -> 7, of which waited for: 9 -> 6; matrix products, arithmetic and copies ran while one was open for 0% -> 6% of each run, Pallas kernels for 0% -> 0%
where the time goes in v8:
time: 64.5 us; the launch traced here: 64.1 us
  waiting for transfers between devices  24.7 us (38%)
  local copies, waits for them, and re-layouts  15.9 us (25%)
  starting transfers between devices  9.89 us (15%)
  other arithmetic  7.22 us (11%)
  Pallas kernels  5.53 us (9%)
    ppermute x1, waiting for transfers between devices, shards(): parts.append(lax.ppermute(band, 'seg', pairs))  14.6 us
    ppermute x2, waiting for transfers between devices, shards(): lax.ppermute(mine, ('seg', 'fibre'), pairs)  7.14 us
    select_n x1, local copies, waits for them, and re-layouts, shards(): jnp.take(pool, pick, axis=0)  6 us
    ppermute x3, starting transfers between devices, shards(): gathered.append(lax.ppermute(sent, 'seg', pairs))  5.94 us
    pallas_call x1, Pallas kernels, whiten(): pl.pallas_call(whiten_kernel, out_shape=jax.ShapeDtypeStruct((groups, cha...  5.53 us
    select_n x2, other arithmetic, shards(): jnp.take(pool, pick, axis=0)  3.94 us
    gather x2, local copies, waits for them, and re-layouts, shards(): jnp.take(pool, pick, axis=0)  2.67 us
    ppermute x2, starting transfers between devices, shards(): lax.ppermute(mine, ('seg', 'fibre'), pairs)  2.58 us
  transfers between devices with their start and end apart: 7, of which 6 were waited for; matrix products, arithmetic and copies ran while one was open for 6% of the time, Pallas kernels for 0%

profile of v8, /device:TPU:0, one launch (start us, length us, event | category | flops | bytes accessed | tf_op | source)
XLA Modules:
  0.0 64.1 jit_solution(2323625246420446182)
XLA Ops:
  0.0 0.7 %convert_element_type.3 = f32[16]{0:T(128)S(1)} convert(s32[16]{0:T(128)} %param.9) | non-fusion elementwise | flops 16 | bytes 128 | tf_op jit(solution)/shard_map/convert_element_type | solution.py:85
  0.7 0.8 %broadcast_in_dim_tile.4.live_ref = f32[256,1]{1,0:T(8,128)} reshape(f32[16,16]{1,0:T(8,128)S(1)} %tile.2) | data formatting | bytes 2048 | tf_op jit(solution)/shard_map/broadcast_in_dim;tile | solution.py:85
  1.4 5.5 %shard_map.73 = bf16[2,16,1024]{2,1,0:T(8,128)(2,1)} custom-call(s32[16]{0:T(128)} %bitcast.118, bf16[16,27648]{1,0:T(8,128)(2,1)} %bitcast.95, bf16[3072,128]{1,0:T(8,128)(2,1)} %constant.117.clone.table_ref, f32[128,128]{1,0:T(8,128)} %constant.118.clone.near_ref, f32[1,128]{1,0:T(1,128)} %constant.119.clone.count_ref, f32[256,1]{1,0:T(8,128)} %broadcast_in_dim_tile.4.live_ref), custom_call_target="tpu_custom_call" | custom-call | tf_op jit(solution)/shard_map/pallas_call | solution.py:87
  7.0 0.9 %constant_dynamic-slice_fusion.1 = (bf16[1,16,1024]{2,1,0:T(8,128)(2,1)S(1)}, bf16[16,1024]{1,0:T(8,128)(2,1)S(1)}, bf16[16,1024]{1,0:T(8,128)(2,1)S(1)}, bf16[16,1024]{1,0:T(8,128)(2,1)S(1)}) fusion(bf16[2,16,1024]{2,1,0:T(8,128)(2,1)} %shard_map.73, s32[]{:T(128)S(6)} %select_n.89, s32[]{:T(128)S(6)} %select_n.98, s32[]{:T(128)S(6)} %select_n.95, ...), kind=kLoop, calls=%fused_computation.41 | loop fusion | bytes 262160 | tf_op jit(solution)/shard_map/jit(dynamic_index_in_dim)/dynamic_slice | solution.py:143
  7.8 3.0 %collective-permute-start = (bf16[16,1024]{1,0:T(8,128)(2,1)S(1)}, bf16[16,1024]{1,0:T(8,128)(2,1)S(1)}, u32[]{:S(2)}, u32[]{:S(2)}) collective-permute-start(bf16[16,1024]{1,0:T(8,128)(2,1)S(1)} %get-tuple-element.32), channel_id=1, source_target_pairs={{0,8},{8,16},{16,24},{24,0},{1,9},{9,17},{17,25},{25,1},{2,10},{10... | collective-permute-start | bytes 98312 | tf_op jit(solution)/shard_map/ppermute | solution.py:148
  10.8 1.5 %collective-permute-start.1 = (bf16[16,1024]{1,0:T(8,128)(2,1)S(1)}, bf16[16,1024]{1,0:T(8,128)(2,1)S(1)}, u32[]{:S(2)}, u32[]{:S(2)}) collective-permute-start(bf16[16,1024]{1,0:T(8,128)(2,1)S(1)} %get-tuple-element.31), channel_id=1, source_target_pairs={{0,16},{8,24},{16,0},{24,8},{1,17},{9,25},{17,1},{25,9},{2,18},{10... | collective-permute-start | bytes 98312 | tf_op jit(solution)/shard_map/ppermute | solution.py:148
  12.4 1.4 %collective-permute-start.2 = (bf16[16,1024]{1,0:T(8,128)(2,1)S(1)}, bf16[16,1024]{1,0:T(8,128)(2,1)S(1)}, u32[]{:S(2)}, u32[]{:S(2)}) collective-permute-start(bf16[16,1024]{1,0:T(8,128)(2,1)S(1)} %get-tuple-element.30), channel_id=1, source_target_pairs={{0,24},{8,0},{16,8},{24,16},{1,25},{9,1},{17,9},{25,17},{2,26},{10... | collective-permute-start | bytes 98312 | tf_op jit(solution)/shard_map/ppermute | solution.py:148
  13.8 0.9 %collective-permute-done.1 = bf16[16,1024]{1,0:T(8,128)(2,1)S(1)} collective-permute-done((bf16[16,1024]{1,0:T(8,128)(2,1)S(1)}, bf16[16,1024]{1,0:T(8,128)(2,1)S(1)}, u32[]{:S(2)}, u32[]{:S(2)}) %collective-permute-start.1) | collective-permute-done | bytes 32800 | tf_op jit(solution)/shard_map/ppermute | solution.py:148
  14.7 1.5 %collective-permute-done.2 = bf16[16,1024]{1,0:T(8,128)(2,1)S(1)} collective-permute-done((bf16[16,1024]{1,0:T(8,128)(2,1)S(1)}, bf16[16,1024]{1,0:T(8,128)(2,1)S(1)}, u32[]{:S(2)}, u32[]{:S(2)}) %collective-permute-start.2) | collective-permute-done | bytes 32800 | tf_op jit(solution)/shard_map/ppermute | solution.py:148
  16.3 1.3 %collective-permute-start.3 = (bf16[16,4096]{1,0:T(8,128)(2,1)S(1)}, bf16[16,4096]{1,0:T(8,128)(2,1)S(1)}, u32[]{:S(2)}, u32[]{:S(2)}) collective-permute-start(bf16[16,4096]{1,0:T(8,128)(2,1)S(1)} %get-tuple-element.28), channel_id=1, source_target_pairs={{2,0},{3,1},{4,2},{5,3},{6,4},{7,5},{12,8},{13,9},{14,10},{15,11},... | collective-permute-start | bytes 393224 | tf_op jit(solution)/shard_map/ppermute | solution.py:159
  17.6 1.3 %collective-permute-start.4 = (bf16[16,4096]{1,0:T(8,128)(2,1)S(1)}, bf16[16,4096]{1,0:T(8,128)(2,1)S(1)}, u32[]{:S(2)}, u32[]{:S(2)}) collective-permute-start(bf16[16,4096]{1,0:T(8,128)(2,1)S(1)} %get-tuple-element.28), channel_id=1, source_target_pairs={{4,0},{5,1},{6,2},{7,3},{14,8},{15,9},{20,16},{21,17},{22,18},{23,... | collective-permute-start | bytes 393224 | tf_op jit(solution)/shard_map/ppermute | solution.py:159
  19.2 0.4 copy.25
  19.8 0.4 copy.26
  20.4 0.4 copy.27
  21.0 0.4 copy.28
  21.5 2.9 %collective-permute-done.3 = bf16[16,4096]{1,0:T(8,128)(2,1)S(1)} collective-permute-done((bf16[16,4096]{1,0:T(8,128)(2,1)S(1)}, bf16[16,4096]{1,0:T(8,128)(2,1)S(1)}, u32[]{:S(2)}, u32[]{:S(2)}) %collective-permute-start.3) | collective-permute-done | bytes 131104 | tf_op jit(solution)/shard_map/ppermute | solution.py:159
  24.4 4.2 %collective-permute-done.4 = bf16[16,4096]{1,0:T(8,128)(2,1)S(1)} collective-permute-done((bf16[16,4096]{1,0:T(8,128)(2,1)S(1)}, bf16[16,4096]{1,0:T(8,128)(2,1)S(1)}, u32[]{:S(2)}, u32[]{:S(2)}) %collective-permute-start.4) | collective-permute-done | bytes 131104 | tf_op jit(solution)/shard_map/ppermute | solution.py:159
  28.8 0.4 pad_maximum_fusion.2
  29.2 0.8 %maximum_bitcast_fusion = bf16[1,16,64,2,32]{2,1,3,0,4:T(8,128)(2,1)} fusion(bf16[16,64,1,32]{1,0,2,3:T(8,128)(2,1)S(1)} %get-tuple-element.26, bf16[16,64,1,32]{1,0,2,3:T(8,128)(2,1)S(1)} %get-tuple-element.25), kind=kLoop, calls=%fused_computation.14 | loop fusion | flops 65536 | bytes 262144 | tf_op jit(solution)/shard_map/stack | solution.py:171
  29.9 0.6 collective-permute-done.5
  30.6 0.6 gather_fusion
  31.2 2.1 %gather.7 = bf16[80,64,2,32]{3,2,1,0:T(2,128)(2,1)S(1)} reshape(bf16[5,16,4096]{2,1,0:T(8,128)(2,1)S(1)} %gather_fusion) | data formatting | bytes 1310720 | tf_op jit(solution)/shard_map/jit(_take)/gather | solution.py:168
  33.3 3.9 %fusion = bf16[80,64,2,32,1]{3,2,1,0,4:T(2,128)(2,1)} fusion(bf16[80,64,2,32]{3,2,1,0:T(2,128)(2,1)S(1)} %gather.7, pred[80]{0:T(512)(128)(4,1)S(1)} %broadcast_in_dim.19), kind=kLoop, calls=%fused_computation.2 | loop fusion | flops 327680 | bytes 1310800 | tf_op jit(solution)/shard_map/jit(_take)/select_n | solution.py:168
  37.3 6.0 %copy.51 = bf16[80,64,2,32,1]{0,1,2,4,3:T(8,128)(2,1)S(1)} copy(bf16[80,64,2,32,1]{3,2,1,0,4:T(2,128)(2,1)} %fusion) | data formatting | bytes 1310720 | tf_op jit(solution)/shard_map/jit(_take)/select_n | solution.py:168
  43.3 0.4 convolution_bitcast_fusion
  43.7 1.1 %fusion.9 = (f32[32,2,1,64]{3,2,1,0:T(1,128)S(1)}, f32[32,2,1,64]{3,2,1,0:T(1,128)S(1)}, f32[32,2,1,64]{3,2,1,0:T(1,128)S(1)}, f32[32,2,1,64]{3,2,1,0:T(1,128)S(...) fusion(f32[32,2,16,80]{3,2,1,0:T(8,128)S(1)} %convolution_bitca, ...), kind=kLoop, calls=%fused_computation.46 | loop fusion | bytes 524288 | tf_op jit(solution)/shard_map/slice | solution.py:178
  45.1 0.6 multiply_bitcast_fusion
  45.8 1.3 %collective-permute-start.6 = (f32[64,1024]{0,1:T(8,128)S(1)}, f32[64,1024]{0,1:T(8,128)S(1)}, u32[]{:S(2)}, u32[]{:S(2)}) collective-permute-start(f32[64,1024]{0,1:T(8,128)S(1)} %bitcast.96), channel_id=1, source_target_pairs={{16,0},{24,8},{17,1},{25,9},{18,2},{26,10},{19,3},{27,11},{20,4},{... | collective-permute-start | bytes 786440 | tf_op jit(solution)/shard_map/ppermute | solution.py:185
  47.1 14.6 %collective-permute-done.6 = f32[64,1024]{0,1:T(8,128)S(1)} collective-permute-done((f32[64,1024]{0,1:T(8,128)S(1)}, f32[64,1024]{0,1:T(8,128)S(1)}, u32[]{:S(2)}, u32[]{:S(2)}) %collective-permute-start.6) | collective-permute-done | bytes 262176 | tf_op jit(solution)/shard_map/ppermute | solution.py:185
  61.7 0.4 copy.48
  62.1 0.7 %fusion.1 = f32[64,16,2,2,32]{0,2,4,1,3:T(2,128)S(1)} fusion(f32[1,64,16,2,32]{1,3,4,2,0:T(2,128)S(1)} %copy.48, f32[1,64,16,2,32]{1,3,4,2,0:T(2,128)S(1)} %get-tuple-element.5, pred[]{:T(512)S(6)} %lt.56), kind=kLoop, calls=%fused_computation.5 | loop fusion | flops 262144 | bytes 1048577 | tf_op jit(solution)/shard_map/jit(_where)/select_n | solution.py:188
  62.9 1.1 %copy.50 = f32[64,16,128]{2,1,0:T(8,128)} copy(f32[64,16,128]{0,2,1:T(8,128)S(1)} %bitcast.92) | data formatting | bytes 1048576 | tf_op jit(solution)/shard_map/jit(_where)/select_n | solution.py:188
  (39 shorter events, 1.5 us)
Async XLA Ops:
  0.0 13.8 %copy-start.1 = (s32[4,5]{1,0:T(4,128)S(1)}, s32[4,5]{1,0:T(4,128)}, u32[]{:S(2)}) copy-start(s32[4,5]{1,0:T(4,128)} %constant.120.clone) | copy-start | bytes 244
  7.8 6.0 %collective-permute-start = (bf16[16,1024]{1,0:T(8,128)(2,1)S(1)}, bf16[16,1024]{1,0:T(8,128)(2,1)S(1)}, u32[]{:S(2)}, u32[]{:S(2)}) collective-permute-start(bf16[16,1024]{1,0:T(8,128)(2,1)S(1)} %get-tuple-element.32), channel_id=1, source_target_pairs={{0,8},{8,16},{16,24},{24,0},{1,9},{9,17},{17,25},{25,1},{2,10},{10... | collective-permute-start | bytes 98312 | tf_op jit(solution)/shard_map/ppermute | solution.py:148
  10.8 3.9 %collective-permute-start.1 = (bf16[16,1024]{1,0:T(8,128)(2,1)S(1)}, bf16[16,1024]{1,0:T(8,128)(2,1)S(1)}, u32[]{:S(2)}, u32[]{:S(2)}) collective-permute-start(bf16[16,1024]{1,0:T(8,128)(2,1)S(1)} %get-tuple-element.31), channel_id=1, source_target_pairs={{0,16},{8,24},{16,0},{24,8},{1,17},{9,25},{17,1},{25,9},{2,18},{10... | collective-permute-start | bytes 98312 | tf_op jit(solution)/shard_map/ppermute | solution.py:148
  12.4 3.9 %collective-permute-start.2 = (bf16[16,1024]{1,0:T(8,128)(2,1)S(1)}, bf16[16,1024]{1,0:T(8,128)(2,1)S(1)}, u32[]{:S(2)}, u32[]{:S(2)}) collective-permute-start(bf16[16,1024]{1,0:T(8,128)(2,1)S(1)} %get-tuple-element.30), channel_id=1, source_target_pairs={{0,24},{8,0},{16,8},{24,16},{1,25},{9,1},{17,9},{25,17},{2,26},{10... | collective-permute-start | bytes 98312 | tf_op jit(solution)/shard_map/ppermute | solution.py:148
  16.3 8.1 %collective-permute-start.3 = (bf16[16,4096]{1,0:T(8,128)(2,1)S(1)}, bf16[16,4096]{1,0:T(8,128)(2,1)S(1)}, u32[]{:S(2)}, u32[]{:S(2)}) collective-permute-start(bf16[16,4096]{1,0:T(8,128)(2,1)S(1)} %get-tuple-element.28), channel_id=1, source_target_pairs={{2,0},{3,1},{4,2},{5,3},{6,4},{7,5},{12,8},{13,9},{14,10},{15,11},... | collective-permute-start | bytes 393224 | tf_op jit(solution)/shard_map/ppermute | solution.py:159
  17.6 11.0 %collective-permute-start.4 = (bf16[16,4096]{1,0:T(8,128)(2,1)S(1)}, bf16[16,4096]{1,0:T(8,128)(2,1)S(1)}, u32[]{:S(2)}, u32[]{:S(2)}) collective-permute-start(bf16[16,4096]{1,0:T(8,128)(2,1)S(1)} %get-tuple-element.28), channel_id=1, source_target_pairs={{4,0},{5,1},{6,2},{7,3},{14,8},{15,9},{20,16},{21,17},{22,18},{23,... | collective-permute-start | bytes 393224 | tf_op jit(solution)/shard_map/ppermute | solution.py:159
  28.7 1.8 %collective-permute-start.5 = (bf16[3,16,4096]{2,1,0:T(8,128)(2,1)S(1)}, bf16[3,16,4096]{2,1,0:T(8,128)(2,1)S(1)}, u32[]{:S(2)}, u32[]{:S(2)}) collective-permute-start(bf16[3,16,4096]{2,1,0:T(8,128)(2,1)S(1)} %get-tuple-element.24), channel_id=1, source_target_pairs={{0,1},{1,0},{2,3},{3,2},{4,5},{5,4},{6,7},{7,6},{8,9},{9,8},{10,11... | collective-permute-start | bytes 1179656 | tf_op jit(solution)/shard_map/ppermute | solution.py:162
  37.3 6.0 %copy-start = (bf16[1,16,64,2,32]{2,1,3,0,4:T(8,128)(2,1)S(1)}, bf16[1,16,64,2,32]{2,1,3,0,4:T(8,128)(2,1)}, u32[]{:S(2)}) copy-start(bf16[1,16,64,2,32]{2,1,3,0,4:T(8,128)(2,1)} %maximum_bitcast_fusion) | copy-start | bytes 393220
  45.8 15.9 %collective-permute-start.6 = (f32[64,1024]{0,1:T(8,128)S(1)}, f32[64,1024]{0,1:T(8,128)S(1)}, u32[]{:S(2)}, u32[]{:S(2)}) collective-permute-start(f32[64,1024]{0,1:T(8,128)S(1)} %bitcast.96), channel_id=1, source_target_pairs={{16,0},{24,8},{17,1},{25,9},{18,2},{26,10},{19,3},{27,11},{20,4},{... | collective-permute-start | bytes 786440 | tf_op jit(solution)/shard_map/ppermute | solution.py:185

commit v9 on v7

--- a/solution.py
+++ b/solution.py
@@ -26,7 +26,7 @@
     return table.astype(ml_dtypes.bfloat16)
 
 
-def whiten_kernel(starts_ref, record_hbm, table_ref, near_ref, count_ref, live_ref, out_ref, chunks, moved_rows, sems):
+def whiten_kernel(starts_ref, place_ref, live_ref, record_hbm, table_ref, near_ref, count_ref, out_ref, chunks, moved_rows, sems):
     windows, channels, span = chunks.shape
     blocks = NT // LANES
     last = record_hbm.shape[1] - span
@@ -55,13 +55,18 @@
         power, near_ref[...], precision=lax.Precision.HIGHEST, preferred_element_type=jnp.float32
     ) / count_ref[...]
     water_level = jnp.sum(power, axis=-1, keepdims=True) / NF
-    gain_of = live_ref[...] / jnp.sqrt(smooth + 0.1 * water_level + 1e-06)
+    rows_of = lax.broadcasted_iota(jnp.int32, spectra.shape, 0) % channels
+    live = jnp.zeros(spectra.shape, jnp.float32)
+    for c in range(channels):
+        live = jnp.where(rows_of == c, live_ref[c].astype(jnp.float32), live)
+    gain_of = live / jnp.sqrt(smooth + 0.1 * water_level + 1e-06)
     whitened = spectra * gain_of
     groups, _, lanes_out = out_ref.shape
     width = 2 * LANES // (2 * groups)
     per_vreg = LANES // width
     lane = lax.broadcasted_iota(jnp.int32, (channels, LANES), 1)
-    for g in range(groups):
+    for d in range(groups):
+        g = (place_ref[0] + d) % groups
         for v in range(lanes_out // LANES):
             gathered = jnp.zeros((channels, LANES), jnp.float32)
             for slot in range(per_vreg):
@@ -70,10 +75,10 @@
                 piece = pltpu.roll(piece, (slot - g) * width % LANES, 1)
                 inside = (lane >= slot * width) & (lane < (slot + 1) * width)
                 gathered = jnp.where(inside, piece, gathered)
-            out_ref[g, :, pl.ds(v * LANES, LANES)] = gathered.astype(out_ref.dtype)
+            out_ref[d, :, pl.ds(v * LANES, LANES)] = gathered.astype(out_ref.dtype)
 
 
-def whiten(record_rows, starts, live_mask, groups):
+def whiten(record_rows, starts, live_mask, groups, place):
     channels, _ = record_rows.shape
     windows = starts.shape[0]
     per_group = NF // groups
@@ -82,19 +87,19 @@
     table = jnp.asarray(spectral_table()[:, lane_part * NF + lane_bin])
     near = (np.abs(lane_bin[:, None] - lane_bin[None, :]) <= 4).astype(np.float32)
     count = (np.abs(np.arange(NF)[:, None] - lane_bin[None, :]) <= 4).sum(axis=0, keepdims=True).astype(np.float32)
-    live_rows = jnp.tile(live_mask.astype(jnp.float32), windows)[:, None]
     vmem = pl.BlockSpec(memory_space=pltpu.VMEM)
+    smem = pl.BlockSpec(memory_space=pltpu.SMEM)
     return pl.pallas_call(
         whiten_kernel,
         out_shape=jax.ShapeDtypeStruct((groups, channels, windows * 2 * per_group), jnp.bfloat16),
-        in_specs=[pl.BlockSpec(memory_space=pltpu.SMEM), pl.BlockSpec(memory_space=pl.ANY), vmem, vmem, vmem, vmem],
+        in_specs=[smem, smem, smem, pl.BlockSpec(memory_space=pl.ANY), vmem, vmem, vmem],
         out_specs=vmem,
         scratch_shapes=[
             pltpu.VMEM((windows, channels, NT + LANES), jnp.bfloat16),
             pltpu.VMEM((windows * channels, NT), jnp.bfloat16),
             pltpu.SemaphoreType.DMA((windows,)),
         ],
-    )(starts, record_rows, table, jnp.asarray(near), jnp.asarray(count), live_rows)
+    )(starts, place.reshape(1), live_mask, record_rows, table, jnp.asarray(near), jnp.asarray(count))
 
 
 def halo(mine, hops, fibre_count):
@@ -122,7 +127,6 @@
     fibre_count = lax.axis_size("fibre")
     windows_count = offsets.shape[1]
     block = record.shape[1]
-    split = whiten(record[0], offsets[0], live_mask, seg_count)
     channels = block * fibre_count
     per_owner = BAND // seg_count
     bins_each = NF // seg_count
@@ -133,12 +137,12 @@
     hops = min(-(-span // block) - 1, fibre_count - 1)
     me = lax.axis_index("seg")
     rows = seg_count * windows_count
+    split = whiten(record[0], offsets[0], live_mask, seg_count, me.astype(jnp.int32))
 
-    gathered = [lax.dynamic_index_in_dim(split, me, 0, keepdims=False)]
+    gathered = [split[0]]
     for step in range(1, seg_count):
-        sent = lax.dynamic_index_in_dim(split, (me + step) % seg_count, 0, keepdims=False)
         pairs = [(i, (i + step) % seg_count) for i in range(seg_count)]
-        gathered.append(lax.ppermute(sent, "seg", pairs))
+        gathered.append(lax.ppermute(split[step], "seg", pairs))
     mine = jnp.concatenate(gathered, axis=1)
 
     columns = halo(mine, hops, fibre_count)[:span]

time: 48.8 us -> 47.3 us (0.969)
  local copies, waits for them, and re-layouts: 8.41 us -> 6.99 us
    another operation x2 -> x0, local copies, waits for them, and re-layouts: 0.76 us -> none  [whiten(): live_rows = jnp.tile(live_mask.astype(jnp.float32), windows)[:, None]]
    unnamed x32 -> x30, local copies, waits for them, and re-layouts: 2.34 us -> 1.68 us
where the time goes in v9:
time: 47.3 us; the launch traced here: 46.9 us
  waiting for transfers between devices  17.4 us (37%)
  starting transfers between devices  15.3 us (32%)
  local copies, waits for them, and re-layouts  6.99 us (15%)
  Pallas kernels  5.55 us (12%)
  matrix products  0.73 us (2%)
  other arithmetic  0.56 us (1%)
    ppermute x3, waiting for transfers between devices, halo(): own.append(lax.ppermute(mine, 'fibre', pairs))  7.84 us
    ppermute x3, starting transfers between devices, shards(): gathered.append(lax.ppermute(split[step], 'seg', pairs))  5.89 us
    ppermute x3, waiting for transfers between devices, shards(): collected.append(lax.ppermute(sent, 'seg', pairs))  5.82 us
    pallas_call x1, Pallas kernels, whiten(): pl.pallas_call(whiten_kernel, out_shape=jax.ShapeDtypeStruct((groups, cha...  5.55 us
    ppermute x3, starting transfers between devices, shards(): collected.append(lax.ppermute(sent, 'seg', pairs))  5.46 us
    ppermute x3, starting transfers between devices, halo(): own.append(lax.ppermute(mine, 'fibre', pairs))  3.88 us
    ppermute x3, waiting for transfers between devices, shards(): gathered.append(lax.ppermute(split[step], 'seg', pairs))  2.31 us
    unnamed x30, local copies, waits for them, and re-layouts  1.68 us
  transfers between devices with their start and end apart: 10, of which 9 were waited for; matrix products, arithmetic and copies ran while one was open for 0% of the time, Pallas kernels for 0%

profile of v9, /device:TPU:0, one launch (start us, length us, event | category | flops | bytes accessed | tf_op | source)
XLA Modules:
  0.0 46.9 jit_solution(6817697287987399527)
XLA Ops:
  0.0 5.5 %shard_map.64 = bf16[4,16,512]{2,1,0:T(8,128)(2,1)} custom-call(s32[16]{0:T(128)} %bitcast.110, s32[1]{0:T(128)} %bitcast.1.place_ref, s32[16]{0:T(128)} %live_ref.1, bf16[16,27648]{1,0:T(8,128)(2,1)} %bitcast.90, bf16[3072,128]{1,0:T(8,128)(2,1)} %constant.86.clone.table_ref, f32[128,128]{1,0:T(8,128)} %constant.87.clone.near_ref, ...), custom_call_target="tpu_custom_call" | custom-call | tf_op jit(solution)/shard_map/pallas_call | solution.py:92
  5.6 0.8 %slice_bitcast_fusion.3 = (bf16[16,512]{1,0:T(8,128)(2,1)S(1)}, bf16[16,512]{1,0:T(8,128)(2,1)S(1)}, bf16[16,512]{1,0:T(8,128)(2,1)S(1)}, bf16[16,512]{1,0:T(8,128)(2,1)S(1)}) fusion(bf16[4,16,512]{2,1,0:T(8,128)(2,1)} %shard_map.64), kind=kLoop, calls=%fused_computation.51 | loop fusion | bytes 131072 | tf_op jit(solution)/shard_map/squeeze | solution.py:142
  6.3 2.9 %collective-permute-start = (bf16[16,512]{1,0:T(8,128)(2,1)S(1)}, bf16[16,512]{1,0:T(8,128)(2,1)S(1)}, u32[]{:S(2)}, u32[]{:S(2)}) collective-permute-start(bf16[16,512]{1,0:T(8,128)(2,1)S(1)} %get-tuple-element.38), channel_id=1, source_target_pairs={{0,8},{8,16},{16,24},{24,0},{1,9},{9,17},{17,25},{25,1},{2,10},{10... | collective-permute-start | bytes 49160 | tf_op jit(solution)/shard_map/ppermute | solution.py:145
  9.3 1.5 %collective-permute-start.1 = (bf16[16,512]{1,0:T(8,128)(2,1)S(1)}, bf16[16,512]{1,0:T(8,128)(2,1)S(1)}, u32[]{:S(2)}, u32[]{:S(2)}) collective-permute-start(bf16[16,512]{1,0:T(8,128)(2,1)S(1)} %get-tuple-element.37), channel_id=1, source_target_pairs={{0,16},{8,24},{16,0},{24,8},{1,17},{9,25},{17,1},{25,9},{2,18},{10... | collective-permute-start | bytes 49160 | tf_op jit(solution)/shard_map/ppermute | solution.py:145
  10.8 1.4 %collective-permute-start.2 = (bf16[16,512]{1,0:T(8,128)(2,1)S(1)}, bf16[16,512]{1,0:T(8,128)(2,1)S(1)}, u32[]{:S(2)}, u32[]{:S(2)}) collective-permute-start(bf16[16,512]{1,0:T(8,128)(2,1)S(1)} %get-tuple-element.36), channel_id=1, source_target_pairs={{0,24},{8,0},{16,8},{24,16},{1,25},{9,1},{17,9},{25,17},{2,26},{10... | collective-permute-start | bytes 49160 | tf_op jit(solution)/shard_map/ppermute | solution.py:145
  12.2 0.8 %collective-permute-done.1 = bf16[16,512]{1,0:T(8,128)(2,1)S(1)} collective-permute-done((bf16[16,512]{1,0:T(8,128)(2,1)S(1)}, bf16[16,512]{1,0:T(8,128)(2,1)S(1)}, u32[]{:S(2)}, u32[]{:S(2)}) %collective-permute-start.1) | collective-permute-done | bytes 16416 | tf_op jit(solution)/shard_map/ppermute | solution.py:145
  13.0 1.5 %collective-permute-done.2 = bf16[16,512]{1,0:T(8,128)(2,1)S(1)} collective-permute-done((bf16[16,512]{1,0:T(8,128)(2,1)S(1)}, bf16[16,512]{1,0:T(8,128)(2,1)S(1)}, u32[]{:S(2)}, u32[]{:S(2)}) %collective-permute-start.2) | collective-permute-done | bytes 16416 | tf_op jit(solution)/shard_map/ppermute | solution.py:145
  14.6 1.3 %collective-permute-start.3 = (bf16[16,2048]{1,0:T(8,128)(2,1)S(1)}, bf16[16,2048]{1,0:T(8,128)(2,1)S(1)}, u32[]{:S(2)}, u32[]{:S(2)}) collective-permute-start(bf16[16,2048]{1,0:T(8,128)(2,1)S(1)} %get-tuple-element.33), channel_id=1, source_target_pairs={{2,0},{3,1},{4,2},{5,3},{6,4},{7,5},{10,8},{11,9},{12,10},{13,11},... | collective-permute-start | bytes 196616 | tf_op jit(solution)/shard_map/ppermute | solution.py:116
  15.9 1.3 %collective-permute-start.4 = (bf16[16,2048]{1,0:T(8,128)(2,1)S(1)}, bf16[16,2048]{1,0:T(8,128)(2,1)S(1)}, u32[]{:S(2)}, u32[]{:S(2)}) collective-permute-start(bf16[16,2048]{1,0:T(8,128)(2,1)S(1)} %get-tuple-element.33), channel_id=1, source_target_pairs={{4,0},{5,1},{6,2},{7,3},{12,8},{13,9},{14,10},{15,11},{20,16},{21,... | collective-permute-start | bytes 196616 | tf_op jit(solution)/shard_map/ppermute | solution.py:116
  17.2 1.3 %collective-permute-start.5 = (bf16[16,2048]{1,0:T(8,128)(2,1)S(1)}, bf16[16,2048]{1,0:T(8,128)(2,1)S(1)}, u32[]{:S(2)}, u32[]{:S(2)}) collective-permute-start(bf16[16,2048]{1,0:T(8,128)(2,1)S(1)} %get-tuple-element.33), channel_id=1, source_target_pairs={{6,0},{7,1},{14,8},{15,9},{22,16},{23,17},{30,24},{31,25}} | collective-permute-start | bytes 196616 | tf_op jit(solution)/shard_map/ppermute | solution.py:116
  18.5 2.7 %collective-permute-done.3 = bf16[16,2048]{1,0:T(8,128)(2,1)S(1)} collective-permute-done((bf16[16,2048]{1,0:T(8,128)(2,1)S(1)}, bf16[16,2048]{1,0:T(8,128)(2,1)S(1)}, u32[]{:S(2)}, u32[]{:S(2)}) %collective-permute-start.3) | collective-permute-done | bytes 65568 | tf_op jit(solution)/shard_map/ppermute | solution.py:116
  21.2 2.7 %collective-permute-done.4 = bf16[16,2048]{1,0:T(8,128)(2,1)S(1)} collective-permute-done((bf16[16,2048]{1,0:T(8,128)(2,1)S(1)}, bf16[16,2048]{1,0:T(8,128)(2,1)S(1)}, u32[]{:S(2)}, u32[]{:S(2)}) %collective-permute-start.4) | collective-permute-done | bytes 65568 | tf_op jit(solution)/shard_map/ppermute | solution.py:116
  23.8 2.5 %collective-permute-done.5 = bf16[16,2048]{1,0:T(8,128)(2,1)S(1)} collective-permute-done((bf16[16,2048]{1,0:T(8,128)(2,1)S(1)}, bf16[16,2048]{1,0:T(8,128)(2,1)S(1)}, u32[]{:S(2)}, u32[]{:S(2)}) %collective-permute-start.5) | collective-permute-done | bytes 65568 | tf_op jit(solution)/shard_map/ppermute | solution.py:116
  26.5 1.4 %collective-permute-done.6 = bf16[64,2048]{1,0:T(8,128)(2,1)S(1)} collective-permute-done((bf16[64,2048]{1,0:T(8,128)(2,1)S(1)}, bf16[64,2048]{1,0:T(8,128)(2,1)S(1)}, u32[]{:S(2)}, u32[]{:S(2)}) %collective-permute-start.6) | collective-permute-done | bytes 262176 | tf_op jit(solution)/shard_map/ppermute | solution.py:117
  28.1 0.3 copy.95
  28.4 0.5 %copy-done = bf16[128,2048]{1,0:T(8,128)(2,1)} copy-done((bf16[128,2048]{1,0:T(8,128)(2,1)}, bf16[128,2048]{1,0:T(8,128)(2,1)S(1)}, u32[]{:S(2)}) %copy-start) | copy-done | bytes 524312
  29.1 0.3 copy.79
  29.4 0.3 copy.78
  29.7 0.6 %slice-done = bf16[16,2048]{1,0:T(8,128)(2,1)S(1)} async-done(((bf16[128,2048]{1,0:T(8,128)(2,1)}), bf16[16,2048]{1,0:T(8,128)(2,1)S(1)}, s32[]{:S(2)}) %slice-start) | async-done | bytes 65560 | tf_op jit(solution)/shard_map/stack | solution.py:156
  30.3 0.4 stack.33
  30.7 0.4 copy.52
  31.1 0.7 %convolution_bitcast_fusion = f32[16,2,16,144]{3,2,1,0:T(8,128)S(1)} fusion(bf16[144,64,2,16,1]{0,3,2,1,4:T(8,128)(2,1)S(1)} %bitcast.85, bf16[1,16,64,2,16]{2,1,3,0,4:T(8,128)(2,1)S(1)} %maximum_bitcast_fusion, bf16[1,16,64,2,16]{2,1,3,0,4:T(8,128)(2,1)S(1)} %copy.52), kind=kOutput, calls=%fused_computation.1 | convolution fusion | flops 18939904 | bytes 1015808 | tf_op jit(solution)/shard_map/ocspn,jspn->nocj/dot_general | solution.py:157
  31.9 0.6 %fusion.9 = (f32[16,2,1,128]{3,2,1,0:T(1,128)S(1)}, f32[16,2,1,128]{3,2,1,0:T(1,128)S(1)}, f32[16,2,1,128]{3,2,1,0:T(1,128)S(1)}, f32[16,2,1,128]{3,2,1,0:T(1,12...) fusion(f32[16,2,16,144]{3,2,1,0:T(8,128)S(1)} %convolution_bitc, ...), kind=kLoop, calls=%fused_computation.68 | loop fusion | bytes 524288 | tf_op jit(solution)/shard_map/slice | solution.py:158
  33.1 2.9 %collective-permute-start.7 = (f32[64,512]{1,0:T(8,128)S(1)}, f32[64,512]{1,0:T(8,128)S(1)}, u32[]{:S(2)}, u32[]{:S(2)}) collective-permute-start(f32[64,512]{1,0:T(8,128)S(1)} %get-tuple-element.10), channel_id=1, source_target_pairs={{0,8},{24,0},{1,9},{25,1},{2,10},{26,2},{3,11},{27,3},{4,12},{28,4... | collective-permute-start | bytes 393224 | tf_op jit(solution)/shard_map/ppermute | solution.py:170
  36.0 1.3 %collective-permute-start.8 = (f32[64,512]{1,0:T(8,128)S(1)}, f32[64,512]{1,0:T(8,128)S(1)}, u32[]{:S(2)}, u32[]{:S(2)}) collective-permute-start(f32[64,512]{1,0:T(8,128)S(1)} %get-tuple-element.9), channel_id=1, source_target_pairs={{16,0},{24,8},{17,1},{25,9},{18,2},{26,10},{19,3},{27,11},{20,4},{... | collective-permute-start | bytes 393224 | tf_op jit(solution)/shard_map/ppermute | solution.py:170
  37.3 1.3 %collective-permute-start.9 = (f32[64,512]{1,0:T(8,128)S(1)}, f32[64,512]{1,0:T(8,128)S(1)}, u32[]{:S(2)}, u32[]{:S(2)}) collective-permute-start(f32[64,512]{1,0:T(8,128)S(1)} %get-tuple-element.8), channel_id=1, source_target_pairs={{8,0},{16,8},{9,1},{17,9},{10,2},{18,10},{11,3},{19,11},{12,4},{20... | collective-permute-start | bytes 393224 | tf_op jit(solution)/shard_map/ppermute | solution.py:170
  38.6 2.9 %collective-permute-done.7 = f32[64,512]{1,0:T(8,128)S(1)} collective-permute-done((f32[64,512]{1,0:T(8,128)S(1)}, f32[64,512]{1,0:T(8,128)S(1)}, u32[]{:S(2)}, u32[]{:S(2)}) %collective-permute-start.7) | collective-permute-done | bytes 131104 | tf_op jit(solution)/shard_map/ppermute | solution.py:170
  41.5 2.7 %collective-permute-done.8 = f32[64,512]{1,0:T(8,128)S(1)} collective-permute-done((f32[64,512]{1,0:T(8,128)S(1)}, f32[64,512]{1,0:T(8,128)S(1)}, u32[]{:S(2)}, u32[]{:S(2)}) %collective-permute-start.8) | collective-permute-done | bytes 131104 | tf_op jit(solution)/shard_map/ppermute | solution.py:170
  44.5 0.6 %gather_fusion = f32[4,64,512]{2,1,0:T(8,128)S(1)} fusion(f32[4,64,512]{2,1,0:T(8,128)S(1)} %pad_maximum_fusion, s32[1024]{0:T(1024)S(1)} %pad_clamp_fusion), kind=kCustom, calls=%fused_computation | custom fusion | bytes 1048592 | tf_op jit(solution)/shard_map/jit(_take)/gather | solution.py:175
  45.1 0.3 copy.71
  45.4 0.2 select_bitcast_fusion
  45.8 1.1 %copy.73 = f32[64,16,128]{2,1,0:T(8,128)} copy(f32[64,16,128]{0,2,1:T(8,128)S(1)} %bitcast.87) | data formatting | bytes 1048576 | tf_op jit(solution)/shard_map/reshape | solution.py:176
  (49 shorter events, 1.5 us)
Async XLA Ops:
  6.3 5.9 %collective-permute-start = (bf16[16,512]{1,0:T(8,128)(2,1)S(1)}, bf16[16,512]{1,0:T(8,128)(2,1)S(1)}, u32[]{:S(2)}, u32[]{:S(2)}) collective-permute-start(bf16[16,512]{1,0:T(8,128)(2,1)S(1)} %get-tuple-element.38), channel_id=1, source_target_pairs={{0,8},{8,16},{16,24},{24,0},{1,9},{9,17},{17,25},{25,1},{2,10},{10... | collective-permute-start | bytes 49160 | tf_op jit(solution)/shard_map/ppermute | solution.py:145
  9.3 3.7 %collective-permute-start.1 = (bf16[16,512]{1,0:T(8,128)(2,1)S(1)}, bf16[16,512]{1,0:T(8,128)(2,1)S(1)}, u32[]{:S(2)}, u32[]{:S(2)}) collective-permute-start(bf16[16,512]{1,0:T(8,128)(2,1)S(1)} %get-tuple-element.37), channel_id=1, source_target_pairs={{0,16},{8,24},{16,0},{24,8},{1,17},{9,25},{17,1},{25,9},{2,18},{10... | collective-permute-start | bytes 49160 | tf_op jit(solution)/shard_map/ppermute | solution.py:145
  10.8 3.7 %collective-permute-start.2 = (bf16[16,512]{1,0:T(8,128)(2,1)S(1)}, bf16[16,512]{1,0:T(8,128)(2,1)S(1)}, u32[]{:S(2)}, u32[]{:S(2)}) collective-permute-start(bf16[16,512]{1,0:T(8,128)(2,1)S(1)} %get-tuple-element.36), channel_id=1, source_target_pairs={{0,24},{8,0},{16,8},{24,16},{1,25},{9,1},{17,9},{25,17},{2,26},{10... | collective-permute-start | bytes 49160 | tf_op jit(solution)/shard_map/ppermute | solution.py:145
  14.6 6.6 %collective-permute-start.3 = (bf16[16,2048]{1,0:T(8,128)(2,1)S(1)}, bf16[16,2048]{1,0:T(8,128)(2,1)S(1)}, u32[]{:S(2)}, u32[]{:S(2)}) collective-permute-start(bf16[16,2048]{1,0:T(8,128)(2,1)S(1)} %get-tuple-element.33), channel_id=1, source_target_pairs={{2,0},{3,1},{4,2},{5,3},{6,4},{7,5},{10,8},{11,9},{12,10},{13,11},... | collective-permute-start | bytes 196616 | tf_op jit(solution)/shard_map/ppermute | solution.py:116
  15.9 8.0 %collective-permute-start.4 = (bf16[16,2048]{1,0:T(8,128)(2,1)S(1)}, bf16[16,2048]{1,0:T(8,128)(2,1)S(1)}, u32[]{:S(2)}, u32[]{:S(2)}) collective-permute-start(bf16[16,2048]{1,0:T(8,128)(2,1)S(1)} %get-tuple-element.33), channel_id=1, source_target_pairs={{4,0},{5,1},{6,2},{7,3},{12,8},{13,9},{14,10},{15,11},{20,16},{21,... | collective-permute-start | bytes 196616 | tf_op jit(solution)/shard_map/ppermute | solution.py:116
  17.2 9.1 %collective-permute-start.5 = (bf16[16,2048]{1,0:T(8,128)(2,1)S(1)}, bf16[16,2048]{1,0:T(8,128)(2,1)S(1)}, u32[]{:S(2)}, u32[]{:S(2)}) collective-permute-start(bf16[16,2048]{1,0:T(8,128)(2,1)S(1)} %get-tuple-element.33), channel_id=1, source_target_pairs={{6,0},{7,1},{14,8},{15,9},{22,16},{23,17},{30,24},{31,25}} | collective-permute-start | bytes 196616 | tf_op jit(solution)/shard_map/ppermute | solution.py:116
  26.3 1.6 %collective-permute-start.6 = (bf16[64,2048]{1,0:T(8,128)(2,1)S(1)}, bf16[64,2048]{1,0:T(8,128)(2,1)S(1)}, u32[]{:S(2)}, u32[]{:S(2)}) collective-permute-start(bf16[64,2048]{1,0:T(8,128)(2,1)S(1)} %pad_maximum_fusion.1), channel_id=1, source_target_pairs={{0,1},{1,0},{2,3},{3,2},{4,5},{5,4},{6,7},{7,6},{8,9},{9,8},{10,11... | collective-permute-start | bytes 786440 | tf_op jit(solution)/shard_map/ppermute | solution.py:117
  28.1 0.8 %copy-start = (bf16[128,2048]{1,0:T(8,128)(2,1)}, bf16[128,2048]{1,0:T(8,128)(2,1)S(1)}, u32[]{:S(2)}) copy-start(bf16[128,2048]{1,0:T(8,128)(2,1)S(1)} %broadcast_select_fusion) | copy-start | bytes 1572868
  29.4 0.8 %slice-start = ((bf16[128,2048]{1,0:T(8,128)(2,1)}), bf16[16,2048]{1,0:T(8,128)(2,1)S(1)}, s32[]{:S(2)}) async-start(bf16[128,2048]{1,0:T(8,128)(2,1)} %copy-done), calls=%async_computation | async-start | bytes 131072 | tf_op jit(solution)/shard_map/stack | solution.py:156
  33.1 8.4 %collective-permute-start.7 = (f32[64,512]{1,0:T(8,128)S(1)}, f32[64,512]{1,0:T(8,128)S(1)}, u32[]{:S(2)}, u32[]{:S(2)}) collective-permute-start(f32[64,512]{1,0:T(8,128)S(1)} %get-tuple-element.10), channel_id=1, source_target_pairs={{0,8},{24,0},{1,9},{25,1},{2,10},{26,2},{3,11},{27,3},{4,12},{28,4... | collective-permute-start | bytes 393224 | tf_op jit(solution)/shard_map/ppermute | solution.py:170
  36.0 8.3 %collective-permute-start.8 = (f32[64,512]{1,0:T(8,128)S(1)}, f32[64,512]{1,0:T(8,128)S(1)}, u32[]{:S(2)}, u32[]{:S(2)}) collective-permute-start(f32[64,512]{1,0:T(8,128)S(1)} %get-tuple-element.9), channel_id=1, source_target_pairs={{16,0},{24,8},{17,1},{25,9},{18,2},{26,10},{19,3},{27,11},{20,4},{... | collective-permute-start | bytes 393224 | tf_op jit(solution)/shard_map/ppermute | solution.py:170
  37.3 7.2 %collective-permute-start.9 = (f32[64,512]{1,0:T(8,128)S(1)}, f32[64,512]{1,0:T(8,128)S(1)}, u32[]{:S(2)}, u32[]{:S(2)}) collective-permute-start(f32[64,512]{1,0:T(8,128)S(1)} %get-tuple-element.8), channel_id=1, source_target_pairs={{8,0},{16,8},{9,1},{17,9},{10,2},{18,10},{11,3},{19,11},{12,4},{20... | collective-permute-start | bytes 393224 | tf_op jit(solution)/shard_map/ppermute | solution.py:170

commit v10 on v9

--- a/solution.py
+++ b/solution.py
@@ -26,7 +26,8 @@
     return table.astype(ml_dtypes.bfloat16)
 
 
-def whiten_kernel(starts_ref, place_ref, live_ref, record_hbm, table_ref, near_ref, count_ref, out_ref, chunks, moved_rows, sems):
+def whiten_kernel(starts_ref, place_ref, live_ref, record_hbm, table_ref, near_ref, count_ref, *refs):
+    *out_refs, chunks, moved_rows, sems = refs
     windows, channels, span = chunks.shape
     blocks = NT // LANES
     last = record_hbm.shape[1] - span
@@ -61,7 +62,8 @@
         live = jnp.where(rows_of == c, live_ref[c].astype(jnp.float32), live)
     gain_of = live / jnp.sqrt(smooth + 0.1 * water_level + 1e-06)
     whitened = spectra * gain_of
-    groups, _, lanes_out = out_ref.shape
+    groups = len(out_refs)
+    _, lanes_out = out_refs[0].shape
     width = 2 * LANES // (2 * groups)
     per_vreg = LANES // width
     lane = lax.broadcasted_iota(jnp.int32, (channels, LANES), 1)
@@ -75,7 +77,7 @@
                 piece = pltpu.roll(piece, (slot - g) * width % LANES, 1)
                 inside = (lane >= slot * width) & (lane < (slot + 1) * width)
                 gathered = jnp.where(inside, piece, gathered)
-            out_ref[d, :, pl.ds(v * LANES, LANES)] = gathered.astype(out_ref.dtype)
+            out_refs[d][:, pl.ds(v * LANES, LANES)] = gathered.astype(out_refs[d].dtype)
 
 
 def whiten(record_rows, starts, live_mask, groups, place):
@@ -91,9 +93,9 @@
     smem = pl.BlockSpec(memory_space=pltpu.SMEM)
     return pl.pallas_call(
         whiten_kernel,
-        out_shape=jax.ShapeDtypeStruct((groups, channels, windows * 2 * per_group), jnp.bfloat16),
+        out_shape=[jax.ShapeDtypeStruct((channels, windows * 2 * per_group), jnp.bfloat16)] * groups,
         in_specs=[smem, smem, smem, pl.BlockSpec(memory_space=pl.ANY), vmem, vmem, vmem],
-        out_specs=vmem,
+        out_specs=[vmem] * groups,
         scratch_shapes=[
             pltpu.VMEM((windows, channels, NT + LANES), jnp.bfloat16),
             pltpu.VMEM((windows * channels, NT), jnp.bfloat16),

time: 47.3 us -> 46.8 us (0.989)
  waiting for transfers between devices: 17.4 us -> 16.8 us
    squeeze x1 -> x0, local copies, waits for them, and re-layouts: 0.78 us -> none  [shards(): gathered = [split[0]]]
    unnamed x30 -> x33, local copies, waits for them, and re-layouts: 1.68 us -> 2.41 us
    ppermute x3, waiting for transfers between devices: 2.31 us -> 1.79 us  [shards(): gathered.append(lax.ppermute(split[step], 'seg', pairs))]
  transfers between devices with their start and end apart: 10 -> 10, of which waited for: 9 -> 9; matrix products, arithmetic and copies ran while one was open for 0% -> 2% of each run, Pallas kernels for 0% -> 0%
where the time goes in v10:
time: 46.8 us; the launch traced here: 46.4 us
  waiting for transfers between devices  16.8 us (36%)
  starting transfers between devices  15.3 us (33%)
  local copies, waits for them, and re-layouts  6.94 us (15%)
  Pallas kernels  5.53 us (12%)
  matrix products  0.73 us (2%)
  other arithmetic  0.55 us (1%)
    ppermute x3, waiting for transfers between devices, halo(): own.append(lax.ppermute(mine, 'fibre', pairs))  7.84 us
    ppermute x3, starting transfers between devices, shards(): gathered.append(lax.ppermute(split[step], 'seg', pairs))  5.94 us
    ppermute x3, waiting for transfers between devices, shards(): collected.append(lax.ppermute(sent, 'seg', pairs))  5.82 us
    pallas_call x1, Pallas kernels, whiten(): pl.pallas_call(whiten_kernel, out_shape=[jax.ShapeDtypeStruct((channels,...  5.53 us
    ppermute x3, starting transfers between devices, shards(): collected.append(lax.ppermute(sent, 'seg', pairs))  5.47 us
    ppermute x3, starting transfers between devices, halo(): own.append(lax.ppermute(mine, 'fibre', pairs))  3.86 us
    unnamed x33, local copies, waits for them, and re-layouts  2.41 us
    ppermute x3, waiting for transfers between devices, shards(): gathered.append(lax.ppermute(split[step], 'seg', pairs))  1.79 us
  transfers between devices with their start and end apart: 10, of which 9 were waited for; matrix products, arithmetic and copies ran while one was open for 2% of the time, Pallas kernels for 0%

profile of v10, /device:TPU:0, one launch (start us, length us, event | category | flops | bytes accessed | tf_op | source)
XLA Modules:
  0.0 46.4 jit_solution(8430926930573409586)
XLA Ops:
  0.0 5.5 %shard_map.64 = (bf16[16,512]{1,0:T(8,128)(2,1)}, bf16[16,512]{1,0:T(8,128)(2,1)}, bf16[16,512]{1,0:T(8,128)(2,1)}, bf16[16,512]{1,0:T(8,128)(2,1)}) custom-call(s32[16]{0:T(128)} %bitcast.102, s32[1]{0:T(128)} %bitcast.1.place_ref, s32[16]{0:T(128)} %live_ref.1, bf16[16,27648]{1,0:T(8,128)(2,1)} %bitcast.82, bf16[3072,128]{1,0:T(8,128)(2,1)} %constant.86.clone.table_ref, ...), custom_call_target="tpu_custom_call" | custom-call | tf_op jit(solution)/shard_map/pallas_call | solution.py:94
  5.5 3.0 %collective-permute-start = (bf16[16,512]{1,0:T(8,128)(2,1)}, bf16[16,512]{1,0:T(8,128)(2,1)S(1)}, u32[]{:S(2)}, u32[]{:S(2)}) collective-permute-start(bf16[16,512]{1,0:T(8,128)(2,1)} %get-tuple-element.10), channel_id=1, source_target_pairs={{0,8},{8,16},{16,24},{24,0},{1,9},{9,17},{17,25},{25,1},{2,10},{10... | collective-permute-start | bytes 49160 | tf_op jit(solution)/shard_map/ppermute | solution.py:147
  8.5 1.5 %collective-permute-start.1 = (bf16[16,512]{1,0:T(8,128)(2,1)}, bf16[16,512]{1,0:T(8,128)(2,1)S(1)}, u32[]{:S(2)}, u32[]{:S(2)}) collective-permute-start(bf16[16,512]{1,0:T(8,128)(2,1)} %get-tuple-element.11), channel_id=1, source_target_pairs={{0,16},{8,24},{16,0},{24,8},{1,17},{9,25},{17,1},{25,9},{2,18},{10... | collective-permute-start | bytes 49160 | tf_op jit(solution)/shard_map/ppermute | solution.py:147
  10.1 1.4 %collective-permute-start.2 = (bf16[16,512]{1,0:T(8,128)(2,1)}, bf16[16,512]{1,0:T(8,128)(2,1)S(1)}, u32[]{:S(2)}, u32[]{:S(2)}) collective-permute-start(bf16[16,512]{1,0:T(8,128)(2,1)} %get-tuple-element.12), channel_id=1, source_target_pairs={{0,24},{8,0},{16,8},{24,16},{1,25},{9,1},{17,9},{25,17},{2,26},{10... | collective-permute-start | bytes 49160 | tf_op jit(solution)/shard_map/ppermute | solution.py:147
  11.5 0.7 %constant_dynamic-update-slice_fusion.3 = (bf16[16,2048]{1,0:T(8,128)(2,1)S(1)}, bf16[128,2048]{1,0:T(8,128)(2,1)S(1)}) fusion(bf16[16,512]{1,0:T(8,128)(2,1)} %get-tuple-element.9), kind=kLoop, calls=%fused_computation.18 | loop fusion | bytes 49152
  12.2 0.3 collective-permute-done.1
  12.5 1.5 %collective-permute-done.2 = bf16[16,512]{1,0:T(8,128)(2,1)S(1)} collective-permute-done((bf16[16,512]{1,0:T(8,128)(2,1)}, bf16[16,512]{1,0:T(8,128)(2,1)S(1)}, u32[]{:S(2)}, u32[]{:S(2)}) %collective-permute-start.2) | collective-permute-done | bytes 16416 | tf_op jit(solution)/shard_map/ppermute | solution.py:147
  14.0 1.3 %collective-permute-start.3 = (bf16[16,2048]{1,0:T(8,128)(2,1)S(1)}, bf16[16,2048]{1,0:T(8,128)(2,1)S(1)}, u32[]{:S(2)}, u32[]{:S(2)}) collective-permute-start(bf16[16,2048]{1,0:T(8,128)(2,1)S(1)} %get-tuple-element.41), channel_id=1, source_target_pairs={{2,0},{3,1},{4,2},{5,3},{6,4},{7,5},{10,8},{11,9},{12,10},{13,11},... | collective-permute-start | bytes 196616 | tf_op jit(solution)/shard_map/ppermute | solution.py:118
  15.3 1.3 %collective-permute-start.4 = (bf16[16,2048]{1,0:T(8,128)(2,1)S(1)}, bf16[16,2048]{1,0:T(8,128)(2,1)S(1)}, u32[]{:S(2)}, u32[]{:S(2)}) collective-permute-start(bf16[16,2048]{1,0:T(8,128)(2,1)S(1)} %get-tuple-element.41), channel_id=1, source_target_pairs={{4,0},{5,1},{6,2},{7,3},{12,8},{13,9},{14,10},{15,11},{20,16},{21,... | collective-permute-start | bytes 196616 | tf_op jit(solution)/shard_map/ppermute | solution.py:118
  16.6 1.3 %collective-permute-start.5 = (bf16[16,2048]{1,0:T(8,128)(2,1)S(1)}, bf16[16,2048]{1,0:T(8,128)(2,1)S(1)}, u32[]{:S(2)}, u32[]{:S(2)}) collective-permute-start(bf16[16,2048]{1,0:T(8,128)(2,1)S(1)} %get-tuple-element.41), channel_id=1, source_target_pairs={{6,0},{7,1},{14,8},{15,9},{22,16},{23,17},{30,24},{31,25}} | collective-permute-start | bytes 196616 | tf_op jit(solution)/shard_map/ppermute | solution.py:118
  17.9 2.7 %collective-permute-done.3 = bf16[16,2048]{1,0:T(8,128)(2,1)S(1)} collective-permute-done((bf16[16,2048]{1,0:T(8,128)(2,1)S(1)}, bf16[16,2048]{1,0:T(8,128)(2,1)S(1)}, u32[]{:S(2)}, u32[]{:S(2)}) %collective-permute-start.3) | collective-permute-done | bytes 65568 | tf_op jit(solution)/shard_map/ppermute | solution.py:118
  20.6 2.7 %collective-permute-done.4 = bf16[16,2048]{1,0:T(8,128)(2,1)S(1)} collective-permute-done((bf16[16,2048]{1,0:T(8,128)(2,1)S(1)}, bf16[16,2048]{1,0:T(8,128)(2,1)S(1)}, u32[]{:S(2)}, u32[]{:S(2)}) %collective-permute-start.4) | collective-permute-done | bytes 65568 | tf_op jit(solution)/shard_map/ppermute | solution.py:118
  23.3 2.5 %collective-permute-done.5 = bf16[16,2048]{1,0:T(8,128)(2,1)S(1)} collective-permute-done((bf16[16,2048]{1,0:T(8,128)(2,1)S(1)}, bf16[16,2048]{1,0:T(8,128)(2,1)S(1)}, u32[]{:S(2)}, u32[]{:S(2)}) %collective-permute-start.5) | collective-permute-done | bytes 65568 | tf_op jit(solution)/shard_map/ppermute | solution.py:118
  26.0 1.4 %collective-permute-done.6 = bf16[64,2048]{1,0:T(8,128)(2,1)S(1)} collective-permute-done((bf16[64,2048]{1,0:T(8,128)(2,1)S(1)}, bf16[64,2048]{1,0:T(8,128)(2,1)S(1)}, u32[]{:S(2)}, u32[]{:S(2)}) %collective-permute-start.6) | collective-permute-done | bytes 262176 | tf_op jit(solution)/shard_map/ppermute | solution.py:119
  27.6 0.3 copy.95
  27.9 0.5 %copy-done = bf16[128,2048]{1,0:T(8,128)(2,1)} copy-done((bf16[128,2048]{1,0:T(8,128)(2,1)}, bf16[128,2048]{1,0:T(8,128)(2,1)S(1)}, u32[]{:S(2)}) %copy-start) | copy-done | bytes 524312
  28.6 0.3 copy.79
  28.9 0.3 copy.78
  29.1 0.6 %slice-done = bf16[16,2048]{1,0:T(8,128)(2,1)S(1)} async-done(((bf16[128,2048]{1,0:T(8,128)(2,1)}), bf16[16,2048]{1,0:T(8,128)(2,1)S(1)}, s32[]{:S(2)}) %slice-start) | async-done | bytes 65560 | tf_op jit(solution)/shard_map/stack | solution.py:158
  29.7 0.4 stack.33
  30.1 0.4 copy.52
  30.6 0.7 %convolution_bitcast_fusion = f32[16,2,16,144]{3,2,1,0:T(8,128)S(1)} fusion(bf16[144,64,2,16,1]{0,3,2,1,4:T(8,128)(2,1)S(1)} %bitcast.77, bf16[1,16,64,2,16]{2,1,3,0,4:T(8,128)(2,1)S(1)} %maximum_bitcast_fusion, bf16[1,16,64,2,16]{2,1,3,0,4:T(8,128)(2,1)S(1)} %copy.52), kind=kOutput, calls=%fused_computation.1 | convolution fusion | flops 18939904 | bytes 1015808 | tf_op jit(solution)/shard_map/ocspn,jspn->nocj/dot_general | solution.py:159
  31.3 0.6 %fusion.9 = (f32[16,2,1,128]{3,2,1,0:T(1,128)S(1)}, f32[16,2,1,128]{3,2,1,0:T(1,128)S(1)}, f32[16,2,1,128]{3,2,1,0:T(1,128)S(1)}, f32[16,2,1,128]{3,2,1,0:T(1,12...) fusion(f32[16,2,16,144]{3,2,1,0:T(8,128)S(1)} %convolution_bitc, ...), kind=kLoop, calls=%fused_computation.73 | loop fusion | bytes 524288 | tf_op jit(solution)/shard_map/slice | solution.py:160
  32.6 2.9 %collective-permute-start.7 = (f32[64,512]{1,0:T(8,128)S(1)}, f32[64,512]{1,0:T(8,128)S(1)}, u32[]{:S(2)}, u32[]{:S(2)}) collective-permute-start(f32[64,512]{1,0:T(8,128)S(1)} %get-tuple-element.18), channel_id=1, source_target_pairs={{0,8},{24,0},{1,9},{25,1},{2,10},{26,2},{3,11},{27,3},{4,12},{28,4... | collective-permute-start | bytes 393224 | tf_op jit(solution)/shard_map/ppermute | solution.py:172
  35.4 1.3 %collective-permute-start.8 = (f32[64,512]{1,0:T(8,128)S(1)}, f32[64,512]{1,0:T(8,128)S(1)}, u32[]{:S(2)}, u32[]{:S(2)}) collective-permute-start(f32[64,512]{1,0:T(8,128)S(1)} %get-tuple-element.17), channel_id=1, source_target_pairs={{16,0},{24,8},{17,1},{25,9},{18,2},{26,10},{19,3},{27,11},{20,4},{... | collective-permute-start | bytes 393224 | tf_op jit(solution)/shard_map/ppermute | solution.py:172
  36.7 1.3 %collective-permute-start.9 = (f32[64,512]{1,0:T(8,128)S(1)}, f32[64,512]{1,0:T(8,128)S(1)}, u32[]{:S(2)}, u32[]{:S(2)}) collective-permute-start(f32[64,512]{1,0:T(8,128)S(1)} %get-tuple-element.16), channel_id=1, source_target_pairs={{8,0},{16,8},{9,1},{17,9},{10,2},{18,10},{11,3},{19,11},{12,4},{20... | collective-permute-start | bytes 393224 | tf_op jit(solution)/shard_map/ppermute | solution.py:172
  38.1 2.9 %collective-permute-done.7 = f32[64,512]{1,0:T(8,128)S(1)} collective-permute-done((f32[64,512]{1,0:T(8,128)S(1)}, f32[64,512]{1,0:T(8,128)S(1)}, u32[]{:S(2)}, u32[]{:S(2)}) %collective-permute-start.7) | collective-permute-done | bytes 131104 | tf_op jit(solution)/shard_map/ppermute | solution.py:172
  41.0 2.7 %collective-permute-done.8 = f32[64,512]{1,0:T(8,128)S(1)} collective-permute-done((f32[64,512]{1,0:T(8,128)S(1)}, f32[64,512]{1,0:T(8,128)S(1)}, u32[]{:S(2)}, u32[]{:S(2)}) %collective-permute-start.8) | collective-permute-done | bytes 131104 | tf_op jit(solution)/shard_map/ppermute | solution.py:172
  43.9 0.6 %gather_fusion = f32[4,64,512]{2,1,0:T(8,128)S(1)} fusion(f32[4,64,512]{2,1,0:T(8,128)S(1)} %pad_maximum_fusion, s32[1024]{0:T(1024)S(1)} %pad_clamp_fusion), kind=kCustom, calls=%fused_computation | custom fusion | bytes 1048592 | tf_op jit(solution)/shard_map/jit(_take)/gather | solution.py:177
  44.5 0.3 copy.71
  44.9 0.2 select_bitcast_fusion
  45.2 1.1 %copy.73 = f32[64,16,128]{2,1,0:T(8,128)} copy(f32[64,16,128]{0,2,1:T(8,128)S(1)} %bitcast.79) | data formatting | bytes 1048576 | tf_op jit(solution)/shard_map/reshape | solution.py:178
  (51 shorter events, 1.5 us)
Async XLA Ops:
  5.5 6.7 %collective-permute-start = (bf16[16,512]{1,0:T(8,128)(2,1)}, bf16[16,512]{1,0:T(8,128)(2,1)S(1)}, u32[]{:S(2)}, u32[]{:S(2)}) collective-permute-start(bf16[16,512]{1,0:T(8,128)(2,1)} %get-tuple-element.10), channel_id=1, source_target_pairs={{0,8},{8,16},{16,24},{24,0},{1,9},{9,17},{17,25},{25,1},{2,10},{10... | collective-permute-start | bytes 49160 | tf_op jit(solution)/shard_map/ppermute | solution.py:147
  8.5 3.9 %collective-permute-start.1 = (bf16[16,512]{1,0:T(8,128)(2,1)}, bf16[16,512]{1,0:T(8,128)(2,1)S(1)}, u32[]{:S(2)}, u32[]{:S(2)}) collective-permute-start(bf16[16,512]{1,0:T(8,128)(2,1)} %get-tuple-element.11), channel_id=1, source_target_pairs={{0,16},{8,24},{16,0},{24,8},{1,17},{9,25},{17,1},{25,9},{2,18},{10... | collective-permute-start | bytes 49160 | tf_op jit(solution)/shard_map/ppermute | solution.py:147
  10.1 3.9 %collective-permute-start.2 = (bf16[16,512]{1,0:T(8,128)(2,1)}, bf16[16,512]{1,0:T(8,128)(2,1)S(1)}, u32[]{:S(2)}, u32[]{:S(2)}) collective-permute-start(bf16[16,512]{1,0:T(8,128)(2,1)} %get-tuple-element.12), channel_id=1, source_target_pairs={{0,24},{8,0},{16,8},{24,16},{1,25},{9,1},{17,9},{25,17},{2,26},{10... | collective-permute-start | bytes 49160 | tf_op jit(solution)/shard_map/ppermute | solution.py:147
  14.0 6.6 %collective-permute-start.3 = (bf16[16,2048]{1,0:T(8,128)(2,1)S(1)}, bf16[16,2048]{1,0:T(8,128)(2,1)S(1)}, u32[]{:S(2)}, u32[]{:S(2)}) collective-permute-start(bf16[16,2048]{1,0:T(8,128)(2,1)S(1)} %get-tuple-element.41), channel_id=1, source_target_pairs={{2,0},{3,1},{4,2},{5,3},{6,4},{7,5},{10,8},{11,9},{12,10},{13,11},... | collective-permute-start | bytes 196616 | tf_op jit(solution)/shard_map/ppermute | solution.py:118
  15.3 8.0 %collective-permute-start.4 = (bf16[16,2048]{1,0:T(8,128)(2,1)S(1)}, bf16[16,2048]{1,0:T(8,128)(2,1)S(1)}, u32[]{:S(2)}, u32[]{:S(2)}) collective-permute-start(bf16[16,2048]{1,0:T(8,128)(2,1)S(1)} %get-tuple-element.41), channel_id=1, source_target_pairs={{4,0},{5,1},{6,2},{7,3},{12,8},{13,9},{14,10},{15,11},{20,16},{21,... | collective-permute-start | bytes 196616 | tf_op jit(solution)/shard_map/ppermute | solution.py:118
  16.6 9.1 %collective-permute-start.5 = (bf16[16,2048]{1,0:T(8,128)(2,1)S(1)}, bf16[16,2048]{1,0:T(8,128)(2,1)S(1)}, u32[]{:S(2)}, u32[]{:S(2)}) collective-permute-start(bf16[16,2048]{1,0:T(8,128)(2,1)S(1)} %get-tuple-element.41), channel_id=1, source_target_pairs={{6,0},{7,1},{14,8},{15,9},{22,16},{23,17},{30,24},{31,25}} | collective-permute-start | bytes 196616 | tf_op jit(solution)/shard_map/ppermute | solution.py:118
  25.8 1.6 %collective-permute-start.6 = (bf16[64,2048]{1,0:T(8,128)(2,1)S(1)}, bf16[64,2048]{1,0:T(8,128)(2,1)S(1)}, u32[]{:S(2)}, u32[]{:S(2)}) collective-permute-start(bf16[64,2048]{1,0:T(8,128)(2,1)S(1)} %pad_maximum_fusion.1), channel_id=1, source_target_pairs={{0,1},{1,0},{2,3},{3,2},{4,5},{5,4},{6,7},{7,6},{8,9},{9,8},{10,11... | collective-permute-start | bytes 786440 | tf_op jit(solution)/shard_map/ppermute | solution.py:119
  27.6 0.8 %copy-start = (bf16[128,2048]{1,0:T(8,128)(2,1)}, bf16[128,2048]{1,0:T(8,128)(2,1)S(1)}, u32[]{:S(2)}) copy-start(bf16[128,2048]{1,0:T(8,128)(2,1)S(1)} %broadcast_select_fusion) | copy-start | bytes 1572868
  28.9 0.8 %slice-start = ((bf16[128,2048]{1,0:T(8,128)(2,1)}), bf16[16,2048]{1,0:T(8,128)(2,1)S(1)}, s32[]{:S(2)}) async-start(bf16[128,2048]{1,0:T(8,128)(2,1)} %copy-done), calls=%async_computation | async-start | bytes 131072 | tf_op jit(solution)/shard_map/stack | solution.py:158
  32.6 8.4 %collective-permute-start.7 = (f32[64,512]{1,0:T(8,128)S(1)}, f32[64,512]{1,0:T(8,128)S(1)}, u32[]{:S(2)}, u32[]{:S(2)}) collective-permute-start(f32[64,512]{1,0:T(8,128)S(1)} %get-tuple-element.18), channel_id=1, source_target_pairs={{0,8},{24,0},{1,9},{25,1},{2,10},{26,2},{3,11},{27,3},{4,12},{28,4... | collective-permute-start | bytes 393224 | tf_op jit(solution)/shard_map/ppermute | solution.py:172
  35.4 8.2 %collective-permute-start.8 = (f32[64,512]{1,0:T(8,128)S(1)}, f32[64,512]{1,0:T(8,128)S(1)}, u32[]{:S(2)}, u32[]{:S(2)}) collective-permute-start(f32[64,512]{1,0:T(8,128)S(1)} %get-tuple-element.17), channel_id=1, source_target_pairs={{16,0},{24,8},{17,1},{25,9},{18,2},{26,10},{19,3},{27,11},{20,4},{... | collective-permute-start | bytes 393224 | tf_op jit(solution)/shard_map/ppermute | solution.py:172
  36.7 7.2 %collective-permute-start.9 = (f32[64,512]{1,0:T(8,128)S(1)}, f32[64,512]{1,0:T(8,128)S(1)}, u32[]{:S(2)}, u32[]{:S(2)}) collective-permute-start(f32[64,512]{1,0:T(8,128)S(1)} %get-tuple-element.16), channel_id=1, source_target_pairs={{8,0},{16,8},{9,1},{17,9},{10,2},{18,10},{11,3},{19,11},{12,4},{20... | collective-permute-start | bytes 393224 | tf_op jit(solution)/shard_map/ppermute | solution.py:172

commit v11 on v10

--- a/solution.py
+++ b/solution.py
@@ -104,6 +104,67 @@
     )(starts, place.reshape(1), live_mask, record_rows, table, jnp.asarray(near), jnp.asarray(count))
 
 
+def band_kernel(place_ref, own_ref, right_ref, *refs):
+    *slot_refs, left, staged = refs
+    block, lanes = own_ref.shape
+    groups = len(slot_refs)
+    per_owner, slot_lanes = slot_refs[0].shape
+    width = slot_lanes // block
+    bins_each = width // 2
+    kept = staged.shape[0]
+    scale = 1.0 / math.sqrt(lanes // width)
+    lane = lax.broadcasted_iota(jnp.int32, (bins_each, lanes), 1)
+    row = lax.broadcasted_iota(jnp.int32, (bins_each, lanes), 0)
+    keep = lane % bins_each == row
+    own = own_ref[...].astype(jnp.float32)
+    turned = jnp.where(
+        (lax.broadcasted_iota(jnp.int32, own.shape, 1) // bins_each) % 2 == 0,
+        pltpu.roll(own, lanes - bins_each, 1),
+        -pltpu.roll(own, bins_each, 1),
+    )
+    for c in range(block):
+        for o, source in enumerate((own, turned)):
+            rows = jnp.where(keep, jnp.broadcast_to(source[c : c + 1], (bins_each, lanes)), 0.0)
+            left[pl.ds((2 * c + o) * bins_each, bins_each), :] = rows.astype(left.dtype)
+    cross = lax.dot_general(
+        left[...], right_ref[...], (((1,), (1,)), ((), ())), preferred_element_type=jnp.float32
+    )
+    span = cross.shape[1]
+    per_vreg = LANES // width
+    out_lane = lax.broadcasted_iota(jnp.int32, (kept, LANES), 1)
+    columns = [jnp.zeros((kept, LANES), jnp.float32) for _ in range(slot_lanes // LANES)]
+    for c in range(block):
+        part = cross[c * width : (c + 1) * width]
+        part = pltpu.roll(part, span - (c + 1), 1)[:, :kept]
+        part = jnp.concatenate([part, jnp.zeros((LANES - width, kept), jnp.float32)], axis=0).T
+        slot = c % per_vreg
+        part = pltpu.roll(part, slot * width, 1)
+        inside = (out_lane >= slot * width) & (out_lane < (slot + 1) * width)
+        columns[c // per_vreg] = jnp.where(inside, part, columns[c // per_vreg])
+    staged[...] = jnp.concatenate(columns, axis=1) * scale
+    for d in range(groups):
+        owner = (place_ref[0] + d) % groups
+        start = pl.multiple_of(jnp.minimum(owner * per_owner, kept - per_owner), per_owner)
+        block_rows = staged[pl.ds(start, per_owner), :]
+        slot_refs[d][...] = jnp.where(owner * per_owner < kept, block_rows, jnp.zeros_like(block_rows))
+
+
+def band(place, own, right, groups, per_owner, kept):
+    block, lanes = own.shape
+    width = 2 * NF // groups
+    vmem = pl.BlockSpec(memory_space=pltpu.VMEM)
+    return pl.pallas_call(
+        band_kernel,
+        out_shape=[jax.ShapeDtypeStruct((per_owner, block * width), jnp.float32)] * groups,
+        in_specs=[pl.BlockSpec(memory_space=pltpu.SMEM), vmem, vmem],
+        out_specs=[vmem] * groups,
+        scratch_shapes=[
+            pltpu.VMEM((block * width, lanes), jnp.bfloat16),
+            pltpu.VMEM((kept, block * width), jnp.float32),
+        ],
+    )(place.reshape(1), own, right)
+
+
 def halo(mine, hops, fibre_count):
     if fibre_count % 2:
         columns = [mine]
@@ -152,26 +213,19 @@
         columns = jnp.concatenate(
             [columns, jnp.zeros((span - columns.shape[0], columns.shape[1]), columns.dtype)], axis=0
         )
-    right = columns.reshape(span, rows, 2, bins_each)
-    re_own = right[:block, :, 0]
-    im_own = right[:block, :, 1]
-    left = jnp.stack([jnp.stack([re_own, im_own], axis=2), jnp.stack([im_own, -re_own], axis=2)])
-    cross = jnp.einsum("ocspn,jspn->nocj", left, right, preferred_element_type=jnp.float32)
-    band = jnp.stack([cross[:, :, c, c + 1 : c + 1 + kept] for c in range(block)])
-    band = band.transpose(3, 0, 2, 1) * (1.0 / math.sqrt(seg_count * windows_count))
-    band = band.reshape(kept, block * 2 * bins_each)
-    if kept < BAND:
-        band = jnp.concatenate([band, jnp.zeros((BAND - kept, band.shape[1]), band.dtype)], axis=0)
-    band = band.reshape(seg_count, per_owner, band.shape[1])
-
-    collected = [lax.dynamic_index_in_dim(band, me, 0, keepdims=False)]
+    padded = -(-span // LANES) * LANES
+    columns = jnp.concatenate(
+        [columns, jnp.zeros((padded - columns.shape[0], columns.shape[1]), columns.dtype)], axis=0
+    )
+    slots = band(me.astype(jnp.int32), mine, columns, seg_count, per_owner, kept)
+
+    collected = [slots[0]]
     for step in range(1, seg_count):
-        sent = lax.dynamic_index_in_dim(band, (me + step) % seg_count, 0, keepdims=False)
         pairs = [(i, (i + step) % seg_count) for i in range(seg_count) if (i + step) % seg_count < live_owners]
         if pairs:
-            collected.append(lax.ppermute(sent, "seg", pairs))
+            collected.append(lax.ppermute(slots[step], "seg", pairs))
         else:
-            collected.append(jnp.zeros_like(sent))
+            collected.append(jnp.zeros_like(slots[step]))
     collected = jnp.stack(collected)
     holder = (me - jnp.arange(seg_count, dtype=jnp.int32)) % seg_count
     by_bins = jnp.take(collected, holder, axis=0).reshape(seg_count, per_owner, block, 2, bins_each)

time: 46.8 us -> 47.8 us (1.021)
  local copies, waits for them, and re-layouts: 6.94 us -> 3.12 us
  Pallas kernels: 5.53 us -> 9.2 us
  other arithmetic: 0.55 us -> 2.46 us
  matrix products: 0.73 us -> 0 us
    pallas_call x0 -> x1, Pallas kernels: none -> 3.67 us  [band(): pl.pallas_call(band_kernel, out_shape=[jax.ShapeDtypeStruct((per_owner, b...]
    unnamed x33 -> x15, local copies, waits for them, and re-layouts: 2.41 us -> 0.83 us
    another operation x5 -> x1, local copies, waits for them, and re-layouts: 1.41 us -> 0.01 us  [the longest x2 0.83 us: shards(): jnp.stack([jnp.stack([re_own, im_own], axis=2), jnp.stack([im_own, -re_ow...]
    concatenate x0 -> x1, other arithmetic: none -> 1.19 us  [shards(): jnp.concatenate([columns, jnp.zeros((padded - columns.shape[0], columns.s...]
    another operation x1, other arithmetic: 0.03 us -> 0.94 us  [shards(): collected = jnp.stack(collected)]
    dot_general x1 -> x0, matrix products: 0.73 us -> none  [shards(): jnp.einsum('ocspn,jspn->nocj', left, right, preferred_element_type=jnp.fl...]
    slice x2 -> x0, local copies, waits for them, and re-layouts: 0.7 us -> none  [the longest x1 0.61 us: shards(): band = jnp.stack([cross[:, :, c, c + 1:c + 1 + kept] for c in range(block)])]
where the time goes in v11:
time: 47.8 us; the launch traced here: 47.4 us
  waiting for transfers between devices  17 us (36%)
  starting transfers between devices  15.3 us (32%)
  Pallas kernels  9.2 us (19%)
  local copies, waits for them, and re-layouts  3.12 us (7%)
  other arithmetic  2.46 us (5%)
    ppermute x3, waiting for transfers between devices, halo(): own.append(lax.ppermute(mine, 'fibre', pairs))  7.84 us
    ppermute x3, waiting for transfers between devices, shards(): collected.append(lax.ppermute(slots[step], 'seg', pairs))  6.03 us
    ppermute x3, starting transfers between devices, shards(): gathered.append(lax.ppermute(split[step], 'seg', pairs))  5.94 us
    pallas_call x1, Pallas kernels, whiten(): pl.pallas_call(whiten_kernel, out_shape=[jax.ShapeDtypeStruct((channels,...  5.53 us
    ppermute x3, starting transfers between devices, shards(): collected.append(lax.ppermute(slots[step], 'seg', pairs))  5.46 us
    ppermute x3, starting transfers between devices, halo(): own.append(lax.ppermute(mine, 'fibre', pairs))  3.86 us
    pallas_call x1, Pallas kernels, band(): pl.pallas_call(band_kernel, out_shape=[jax.ShapeDtypeStruct((per_owner, b...  3.67 us
    ppermute x3, waiting for transfers between devices, shards(): gathered.append(lax.ppermute(split[step], 'seg', pairs))  1.79 us
  transfers between devices with their start and end apart: 10, of which 9 were waited for; matrix products, arithmetic and copies ran while one was open for 2% of the time, Pallas kernels for 0%

profile of v11, /device:TPU:0, one launch (start us, length us, event | category | flops | bytes accessed | tf_op | source)
XLA Modules:
  0.0 47.4 jit_solution(14590300691616280680)
XLA Ops:
  0.0 5.5 %shard_map.64 = (bf16[16,512]{1,0:T(8,128)(2,1)}, bf16[16,512]{1,0:T(8,128)(2,1)}, bf16[16,512]{1,0:T(8,128)(2,1)}, bf16[16,512]{1,0:T(8,128)(2,1)}) custom-call(s32[16]{0:T(128)} %bitcast.20, s32[1]{0:T(128)} %bitcast.place_ref, s32[16]{0:T(128)} %live_ref.1, bf16[16,27648]{1,0:T(8,128)(2,1)} %bitcast.15, bf16[3072,128]{1,0:T(8,128)(2,1)} %constant.60.clone.table_ref, ...), custom_call_target="tpu_custom_call" | custom-call | tf_op jit(solution)/shard_map/pallas_call | solution.py:94
  5.5 3.0 %collective-permute-start = (bf16[16,512]{1,0:T(8,128)(2,1)}, bf16[16,512]{1,0:T(8,128)(2,1)S(1)}, u32[]{:S(2)}, u32[]{:S(2)}) collective-permute-start(bf16[16,512]{1,0:T(8,128)(2,1)} %get-tuple-element.14), channel_id=1, source_target_pairs={{0,8},{8,16},{16,24},{24,0},{1,9},{9,17},{17,25},{25,1},{2,10},{10... | collective-permute-start | bytes 49160 | tf_op jit(solution)/shard_map/ppermute | solution.py:208
  8.5 1.5 %collective-permute-start.1 = (bf16[16,512]{1,0:T(8,128)(2,1)}, bf16[16,512]{1,0:T(8,128)(2,1)S(1)}, u32[]{:S(2)}, u32[]{:S(2)}) collective-permute-start(bf16[16,512]{1,0:T(8,128)(2,1)} %get-tuple-element.15), channel_id=1, source_target_pairs={{0,16},{8,24},{16,0},{24,8},{1,17},{9,25},{17,1},{25,9},{2,18},{10... | collective-permute-start | bytes 49160 | tf_op jit(solution)/shard_map/ppermute | solution.py:208
  10.1 1.4 %collective-permute-start.2 = (bf16[16,512]{1,0:T(8,128)(2,1)}, bf16[16,512]{1,0:T(8,128)(2,1)S(1)}, u32[]{:S(2)}, u32[]{:S(2)}) collective-permute-start(bf16[16,512]{1,0:T(8,128)(2,1)} %get-tuple-element.16), channel_id=1, source_target_pairs={{0,24},{8,0},{16,8},{24,16},{1,25},{9,1},{17,9},{25,17},{2,26},{10... | collective-permute-start | bytes 49160 | tf_op jit(solution)/shard_map/ppermute | solution.py:208
  11.5 0.7 %constant_dynamic-update-slice_fusion.11 = (bf16[128,2048]{1,0:T(8,128)(2,1)S(1)}, bf16[16,2048]{1,0:T(8,128)(2,1)S(1)}) fusion(bf16[16,512]{1,0:T(8,128)(2,1)} %get-tuple-element.13), kind=kLoop, calls=%fused_computation.24 | loop fusion | bytes 49152
  12.2 0.0 collective-permute-done
  12.2 0.3 collective-permute-done.1
  12.5 1.5 %collective-permute-done.2 = bf16[16,512]{1,0:T(8,128)(2,1)S(1)} collective-permute-done((bf16[16,512]{1,0:T(8,128)(2,1)}, bf16[16,512]{1,0:T(8,128)(2,1)S(1)}, u32[]{:S(2)}, u32[]{:S(2)}) %collective-permute-start.2) | collective-permute-done | bytes 16416 | tf_op jit(solution)/shard_map/ppermute | solution.py:208
  14.0 1.3 %collective-permute-start.3 = (bf16[16,2048]{1,0:T(8,128)(2,1)S(1)}, bf16[16,2048]{1,0:T(8,128)(2,1)S(1)}, u32[]{:S(2)}, u32[]{:S(2)}) collective-permute-start(bf16[16,2048]{1,0:T(8,128)(2,1)S(1)} %get-tuple-element.28.own_ref), channel_id=1, source_target_pairs={{2,0},{3,1},{4,2},{5,3},{6,4},{7,5},{10,8},{11,9},{12,10},{13,11},... | collective-permute-start | bytes 196616 | tf_op jit(solution)/shard_map/ppermute | solution.py:179
  15.3 1.3 %collective-permute-start.4 = (bf16[16,2048]{1,0:T(8,128)(2,1)S(1)}, bf16[16,2048]{1,0:T(8,128)(2,1)S(1)}, u32[]{:S(2)}, u32[]{:S(2)}) collective-permute-start(bf16[16,2048]{1,0:T(8,128)(2,1)S(1)} %get-tuple-element.28.own_ref), channel_id=1, source_target_pairs={{4,0},{5,1},{6,2},{7,3},{12,8},{13,9},{14,10},{15,11},{20,16},{21,... | collective-permute-start | bytes 196616 | tf_op jit(solution)/shard_map/ppermute | solution.py:179
  16.6 1.3 %collective-permute-start.5 = (bf16[16,2048]{1,0:T(8,128)(2,1)S(1)}, bf16[16,2048]{1,0:T(8,128)(2,1)S(1)}, u32[]{:S(2)}, u32[]{:S(2)}) collective-permute-start(bf16[16,2048]{1,0:T(8,128)(2,1)S(1)} %get-tuple-element.28.own_ref), channel_id=1, source_target_pairs={{6,0},{7,1},{14,8},{15,9},{22,16},{23,17},{30,24},{31,25}} | collective-permute-start | bytes 196616 | tf_op jit(solution)/shard_map/ppermute | solution.py:179
  17.9 2.7 %collective-permute-done.3 = bf16[16,2048]{1,0:T(8,128)(2,1)S(1)} collective-permute-done((bf16[16,2048]{1,0:T(8,128)(2,1)S(1)}, bf16[16,2048]{1,0:T(8,128)(2,1)S(1)}, u32[]{:S(2)}, u32[]{:S(2)}) %collective-permute-start.3) | collective-permute-done | bytes 65568 | tf_op jit(solution)/shard_map/ppermute | solution.py:179
  20.6 2.7 %collective-permute-done.4 = bf16[16,2048]{1,0:T(8,128)(2,1)S(1)} collective-permute-done((bf16[16,2048]{1,0:T(8,128)(2,1)S(1)}, bf16[16,2048]{1,0:T(8,128)(2,1)S(1)}, u32[]{:S(2)}, u32[]{:S(2)}) %collective-permute-start.4) | collective-permute-done | bytes 65568 | tf_op jit(solution)/shard_map/ppermute | solution.py:179
  23.3 2.5 %collective-permute-done.5 = bf16[16,2048]{1,0:T(8,128)(2,1)S(1)} collective-permute-done((bf16[16,2048]{1,0:T(8,128)(2,1)S(1)}, bf16[16,2048]{1,0:T(8,128)(2,1)S(1)}, u32[]{:S(2)}, u32[]{:S(2)}) %collective-permute-start.5) | collective-permute-done | bytes 65568 | tf_op jit(solution)/shard_map/ppermute | solution.py:179
  25.8 0.1 collective-permute-start.6
  25.9 0.1 pad.6.clone
  26.0 1.4 %collective-permute-done.6 = bf16[64,2048]{1,0:T(8,128)(2,1)S(1)} collective-permute-done((bf16[64,2048]{1,0:T(8,128)(2,1)S(1)}, bf16[64,2048]{1,0:T(8,128)(2,1)S(1)}, u32[]{:S(2)}, u32[]{:S(2)}) %collective-permute-start.6) | collective-permute-done | bytes 262176 | tf_op jit(solution)/shard_map/ppermute | solution.py:180
  27.5 0.1 broadcast_select_fusion
  27.6 1.2 %maximum_maximum_fusion.right_ref = bf16[256,2048]{1,0:T(8,128)(2,1)} fusion(bf16[16,2048]{1,0:T(8,128)(2,1)S(1)} %broadcast.100, bf16[128,2048]{1,0:T(8,128)(2,1)S(1)} %broadcast_select_fusion, bf16[256]{0:T(256)(128)(2,1)S(1)} %pad.6.clone), kind=kLoop, calls=%fused_computation.1 | loop fusion | flops 3145728 | bytes 1638912 | tf_op jit(solution)/shard_map/concatenate | solution.py:217
  28.8 3.7 %shard_map.65 = (f32[64,512]{1,0:T(8,128)}, f32[64,512]{1,0:T(8,128)}, f32[64,512]{1,0:T(8,128)}, f32[64,512]{1,0:T(8,128)}) custom-call(s32[1]{0:T(128)} %bitcast.place_ref, bf16[16,2048]{1,0:T(8,128)(2,1)} %copy-done, bf16[256,2048]{1,0:T(8,128)(2,1)} %maximum_maximum_fusion.right_ref), custom_call_target="tpu_custom_call" | custom-call | tf_op jit(solution)/shard_map/pallas_call | solution.py:156
  32.5 2.9 %collective-permute-start.7 = (f32[64,512]{1,0:T(8,128)}, f32[64,512]{1,0:T(8,128)S(1)}, u32[]{:S(2)}, u32[]{:S(2)}) collective-permute-start(f32[64,512]{1,0:T(8,128)} %get-tuple-element.18), channel_id=1, source_target_pairs={{0,8},{24,0},{1,9},{25,1},{2,10},{26,2},{3,11},{27,3},{4,12},{28,4... | collective-permute-start | bytes 393224 | tf_op jit(solution)/shard_map/ppermute | solution.py:226
  35.3 1.3 %collective-permute-start.8 = (f32[64,512]{1,0:T(8,128)}, f32[64,512]{1,0:T(8,128)S(1)}, u32[]{:S(2)}, u32[]{:S(2)}) collective-permute-start(f32[64,512]{1,0:T(8,128)} %get-tuple-element.19), channel_id=1, source_target_pairs={{16,0},{24,8},{17,1},{25,9},{18,2},{26,10},{19,3},{27,11},{20,4},{... | collective-permute-start | bytes 393224 | tf_op jit(solution)/shard_map/ppermute | solution.py:226
  36.6 1.3 %collective-permute-start.9 = (f32[64,512]{1,0:T(8,128)}, f32[64,512]{1,0:T(8,128)S(1)}, u32[]{:S(2)}, u32[]{:S(2)}) collective-permute-start(f32[64,512]{1,0:T(8,128)} %get-tuple-element.20), channel_id=1, source_target_pairs={{8,0},{16,8},{9,1},{17,9},{10,2},{18,10},{11,3},{19,11},{12,4},{20... | collective-permute-start | bytes 393224 | tf_op jit(solution)/shard_map/ppermute | solution.py:226
  38.0 3.1 %collective-permute-done.7 = f32[64,512]{1,0:T(8,128)S(1)} collective-permute-done((f32[64,512]{1,0:T(8,128)}, f32[64,512]{1,0:T(8,128)S(1)}, u32[]{:S(2)}, u32[]{:S(2)}) %collective-permute-start.7) | collective-permute-done | bytes 131104 | tf_op jit(solution)/shard_map/ppermute | solution.py:226
  41.1 2.7 %collective-permute-done.8 = f32[64,512]{1,0:T(8,128)S(1)} collective-permute-done((f32[64,512]{1,0:T(8,128)}, f32[64,512]{1,0:T(8,128)S(1)}, u32[]{:S(2)}, u32[]{:S(2)}) %collective-permute-start.8) | collective-permute-done | bytes 131104 | tf_op jit(solution)/shard_map/ppermute | solution.py:226
  43.8 0.2 collective-permute-done.9
  44.0 0.9 %pad_maximum_fusion = f32[4,64,512]{2,1,0:T(8,128)S(1)} fusion(f32[1,64,512]{2,1,0:T(8,128)S(1)} %bitcast.19, f32[1,64,512]{2,1,0:T(8,128)S(1)} %bitcast.18, f32[1,64,512]{2,1,0:T(8,128)S(1)} %bitcast.17, f32[1,64,512]{2,1,0:T(8,128)} %bitcast.16), kind=kLoop, calls=%fused_computation.3 | loop fusion | flops 393216 | bytes 1048576 | tf_op jit(solution)/shard_map/stack | solution.py:229
  44.9 0.6 %gather_fusion = f32[4,64,512]{2,1,0:T(8,128)S(1)} fusion(f32[4,64,512]{2,1,0:T(8,128)S(1)} %pad_maximum_fusion, s32[1024]{0:T(1024)S(1)} %pad_clamp_fusion), kind=kCustom, calls=%fused_computation | custom fusion | bytes 1048592 | tf_op jit(solution)/shard_map/jit(_take)/gather | solution.py:231
  45.5 0.3 copy.8
  45.9 0.2 select_bitcast_fusion
  46.1 0.1 copy.9
  46.2 1.1 %copy.10 = f32[64,16,128]{2,1,0:T(8,128)} copy(f32[64,16,128]{0,2,1:T(8,128)S(1)} %bitcast.14) | data formatting | bytes 1048576 | tf_op jit(solution)/shard_map/reshape | solution.py:232
  (22 shorter events, 0.2 us)
Async XLA Ops:
  5.5 6.7 %collective-permute-start = (bf16[16,512]{1,0:T(8,128)(2,1)}, bf16[16,512]{1,0:T(8,128)(2,1)S(1)}, u32[]{:S(2)}, u32[]{:S(2)}) collective-permute-start(bf16[16,512]{1,0:T(8,128)(2,1)} %get-tuple-element.14), channel_id=1, source_target_pairs={{0,8},{8,16},{16,24},{24,0},{1,9},{9,17},{17,25},{25,1},{2,10},{10... | collective-permute-start | bytes 49160 | tf_op jit(solution)/shard_map/ppermute | solution.py:208
  8.5 3.9 %collective-permute-start.1 = (bf16[16,512]{1,0:T(8,128)(2,1)}, bf16[16,512]{1,0:T(8,128)(2,1)S(1)}, u32[]{:S(2)}, u32[]{:S(2)}) collective-permute-start(bf16[16,512]{1,0:T(8,128)(2,1)} %get-tuple-element.15), channel_id=1, source_target_pairs={{0,16},{8,24},{16,0},{24,8},{1,17},{9,25},{17,1},{25,9},{2,18},{10... | collective-permute-start | bytes 49160 | tf_op jit(solution)/shard_map/ppermute | solution.py:208
  10.1 3.9 %collective-permute-start.2 = (bf16[16,512]{1,0:T(8,128)(2,1)}, bf16[16,512]{1,0:T(8,128)(2,1)S(1)}, u32[]{:S(2)}, u32[]{:S(2)}) collective-permute-start(bf16[16,512]{1,0:T(8,128)(2,1)} %get-tuple-element.16), channel_id=1, source_target_pairs={{0,24},{8,0},{16,8},{24,16},{1,25},{9,1},{17,9},{25,17},{2,26},{10... | collective-permute-start | bytes 49160 | tf_op jit(solution)/shard_map/ppermute | solution.py:208
  14.0 13.4 %copy-start = (bf16[16,2048]{1,0:T(8,128)(2,1)}, bf16[16,2048]{1,0:T(8,128)(2,1)S(1)}, u32[]{:S(2)}) copy-start(bf16[16,2048]{1,0:T(8,128)(2,1)S(1)} %get-tuple-element.28.own_ref) | copy-start | bytes 196612
  14.0 6.6 %collective-permute-start.3 = (bf16[16,2048]{1,0:T(8,128)(2,1)S(1)}, bf16[16,2048]{1,0:T(8,128)(2,1)S(1)}, u32[]{:S(2)}, u32[]{:S(2)}) collective-permute-start(bf16[16,2048]{1,0:T(8,128)(2,1)S(1)} %get-tuple-element.28.own_ref), channel_id=1, source_target_pairs={{2,0},{3,1},{4,2},{5,3},{6,4},{7,5},{10,8},{11,9},{12,10},{13,11},... | collective-permute-start | bytes 196616 | tf_op jit(solution)/shard_map/ppermute | solution.py:179
  15.3 8.0 %collective-permute-start.4 = (bf16[16,2048]{1,0:T(8,128)(2,1)S(1)}, bf16[16,2048]{1,0:T(8,128)(2,1)S(1)}, u32[]{:S(2)}, u32[]{:S(2)}) collective-permute-start(bf16[16,2048]{1,0:T(8,128)(2,1)S(1)} %get-tuple-element.28.own_ref), channel_id=1, source_target_pairs={{4,0},{5,1},{6,2},{7,3},{12,8},{13,9},{14,10},{15,11},{20,16},{21,... | collective-permute-start | bytes 196616 | tf_op jit(solution)/shard_map/ppermute | solution.py:179
  16.6 9.1 %collective-permute-start.5 = (bf16[16,2048]{1,0:T(8,128)(2,1)S(1)}, bf16[16,2048]{1,0:T(8,128)(2,1)S(1)}, u32[]{:S(2)}, u32[]{:S(2)}) collective-permute-start(bf16[16,2048]{1,0:T(8,128)(2,1)S(1)} %get-tuple-element.28.own_ref), channel_id=1, source_target_pairs={{6,0},{7,1},{14,8},{15,9},{22,16},{23,17},{30,24},{31,25}} | collective-permute-start | bytes 196616 | tf_op jit(solution)/shard_map/ppermute | solution.py:179
  25.8 1.6 %collective-permute-start.6 = (bf16[64,2048]{1,0:T(8,128)(2,1)S(1)}, bf16[64,2048]{1,0:T(8,128)(2,1)S(1)}, u32[]{:S(2)}, u32[]{:S(2)}) collective-permute-start(bf16[64,2048]{1,0:T(8,128)(2,1)S(1)} %pad_maximum_fusion.1), channel_id=1, source_target_pairs={{0,1},{1,0},{2,3},{3,2},{4,5},{5,4},{6,7},{7,6},{8,9},{9,8},{10,11... | collective-permute-start | bytes 786440 | tf_op jit(solution)/shard_map/ppermute | solution.py:180
  32.5 8.6 %collective-permute-start.7 = (f32[64,512]{1,0:T(8,128)}, f32[64,512]{1,0:T(8,128)S(1)}, u32[]{:S(2)}, u32[]{:S(2)}) collective-permute-start(f32[64,512]{1,0:T(8,128)} %get-tuple-element.18), channel_id=1, source_target_pairs={{0,8},{24,0},{1,9},{25,1},{2,10},{26,2},{3,11},{27,3},{4,12},{28,4... | collective-permute-start | bytes 393224 | tf_op jit(solution)/shard_map/ppermute | solution.py:226
  35.3 8.5 %collective-permute-start.8 = (f32[64,512]{1,0:T(8,128)}, f32[64,512]{1,0:T(8,128)S(1)}, u32[]{:S(2)}, u32[]{:S(2)}) collective-permute-start(f32[64,512]{1,0:T(8,128)} %get-tuple-element.19), channel_id=1, source_target_pairs={{16,0},{24,8},{17,1},{25,9},{18,2},{26,10},{19,3},{27,11},{20,4},{... | collective-permute-start | bytes 393224 | tf_op jit(solution)/shard_map/ppermute | solution.py:226
  36.6 7.4 %collective-permute-start.9 = (f32[64,512]{1,0:T(8,128)}, f32[64,512]{1,0:T(8,128)S(1)}, u32[]{:S(2)}, u32[]{:S(2)}) collective-permute-start(f32[64,512]{1,0:T(8,128)} %get-tuple-element.20), channel_id=1, source_target_pairs={{8,0},{16,8},{9,1},{17,9},{10,2},{18,10},{11,3},{19,11},{12,4},{20... | collective-permute-start | bytes 393224 | tf_op jit(solution)/shard_map/ppermute | solution.py:226

commit v12 on v10

--- a/solution.py
+++ b/solution.py
@@ -26,7 +26,7 @@
     return table.astype(ml_dtypes.bfloat16)
 
 
-def whiten_kernel(starts_ref, place_ref, live_ref, record_hbm, table_ref, near_ref, count_ref, *refs):
+def whiten_kernel(starts_ref, place_ref, live_ref, record_hbm, table_ref, count_ref, *refs):
     *out_refs, chunks, moved_rows, sems = refs
     windows, channels, span = chunks.shape
     blocks = NT // LANES
@@ -51,11 +51,16 @@
                 low, rolled[b], rolled[b + 1]
             ).astype(jnp.bfloat16)
     spectra = jnp.dot(moved_rows[...], table_ref[...], preferred_element_type=jnp.float32)
-    power = spectra * spectra
-    smooth = jnp.dot(
-        power, near_ref[...], precision=lax.Precision.HIGHEST, preferred_element_type=jnp.float32
-    ) / count_ref[...]
-    water_level = jnp.sum(power, axis=-1, keepdims=True) / NF
+    squares = spectra * spectra
+    power = squares + pltpu.roll(squares, NF, 1)
+    bin_of = lax.broadcasted_iota(jnp.int32, power.shape, 1) % NF
+    smooth = power
+    for step in range(1, 5):
+        above = pltpu.roll(power, 2 * NF - step, 1)
+        below = pltpu.roll(power, step, 1)
+        smooth = smooth + jnp.where(bin_of + step < NF, above, 0.0) + jnp.where(bin_of >= step, below, 0.0)
+    smooth = smooth / count_ref[...]
+    water_level = jnp.sum(squares, axis=-1, keepdims=True) / NF
     rows_of = lax.broadcasted_iota(jnp.int32, spectra.shape, 0) % channels
     live = jnp.zeros(spectra.shape, jnp.float32)
     for c in range(channels):
@@ -74,9 +79,11 @@
             for slot in range(per_vreg):
                 w = v * per_vreg + slot
                 piece = whitened[w * channels : (w + 1) * channels]
-                piece = pltpu.roll(piece, (slot - g) * width % LANES, 1)
-                inside = (lane >= slot * width) & (lane < (slot + 1) * width)
-                gathered = jnp.where(inside, piece, gathered)
+                half = width // 2
+                for part in range(2):
+                    moved = pltpu.roll(piece, (slot * width + part * half - part * NF - g * half) % LANES, 1)
+                    inside = (lane >= slot * width + part * half) & (lane < slot * width + (part + 1) * half)
+                    gathered = jnp.where(inside, moved, gathered)
             out_refs[d][:, pl.ds(v * LANES, LANES)] = gathered.astype(out_refs[d].dtype)
 
 
@@ -84,24 +91,22 @@
     channels, _ = record_rows.shape
     windows = starts.shape[0]
     per_group = NF // groups
-    lane_group, lane_part, lane_bin = np.unravel_index(np.arange(2 * NF), (groups, 2, per_group))
-    lane_bin = lane_group * per_group + lane_bin
-    table = jnp.asarray(spectral_table()[:, lane_part * NF + lane_bin])
-    near = (np.abs(lane_bin[:, None] - lane_bin[None, :]) <= 4).astype(np.float32)
+    table = jnp.asarray(spectral_table())
+    lane_bin = np.arange(2 * NF) % NF
     count = (np.abs(np.arange(NF)[:, None] - lane_bin[None, :]) <= 4).sum(axis=0, keepdims=True).astype(np.float32)
     vmem = pl.BlockSpec(memory_space=pltpu.VMEM)
     smem = pl.BlockSpec(memory_space=pltpu.SMEM)
     return pl.pallas_call(
         whiten_kernel,
         out_shape=[jax.ShapeDtypeStruct((channels, windows * 2 * per_group), jnp.bfloat16)] * groups,
-        in_specs=[smem, smem, smem, pl.BlockSpec(memory_space=pl.ANY), vmem, vmem, vmem],
+        in_specs=[smem, smem, smem, pl.BlockSpec(memory_space=pl.ANY), vmem, vmem],
         out_specs=[vmem] * groups,
         scratch_shapes=[
             pltpu.VMEM((windows, channels, NT + LANES), jnp.bfloat16),
             pltpu.VMEM((windows * channels, NT), jnp.bfloat16),
             pltpu.SemaphoreType.DMA((windows,)),
         ],
-    )(starts, place.reshape(1), live_mask, record_rows, table, jnp.asarray(near), jnp.asarray(count))
+    )(starts, place.reshape(1), live_mask, record_rows, table, jnp.asarray(count))
 
 
 def halo(mine, hops, fibre_count):

time: 46.8 us -> 47.1 us (level)
  no operation moved by 1% of the time
where the time goes in v12:
time: 47.1 us; the launch traced here: 46.7 us
  waiting for transfers between devices  16.8 us (36%)
  starting transfers between devices  15.3 us (32%)
  local copies, waits for them, and re-layouts  6.94 us (15%)
  Pallas kernels  5.82 us (12%)
  matrix products  0.73 us (2%)
  other arithmetic  0.55 us (1%)
    ppermute x3, waiting for transfers between devices, halo(): own.append(lax.ppermute(mine, 'fibre', pairs))  7.84 us
    ppermute x3, starting transfers between devices, shards(): gathered.append(lax.ppermute(split[step], 'seg', pairs))  5.94 us
    pallas_call x1, Pallas kernels, whiten(): pl.pallas_call(whiten_kernel, out_shape=[jax.ShapeDtypeStruct((channels,...  5.82 us
    ppermute x3, waiting for transfers between devices, shards(): collected.append(lax.ppermute(sent, 'seg', pairs))  5.82 us
    ppermute x3, starting transfers between devices, shards(): collected.append(lax.ppermute(sent, 'seg', pairs))  5.47 us
    ppermute x3, starting transfers between devices, halo(): own.append(lax.ppermute(mine, 'fibre', pairs))  3.86 us
    unnamed x33, local copies, waits for them, and re-layouts  2.41 us
    ppermute x3, waiting for transfers between devices, shards(): gathered.append(lax.ppermute(split[step], 'seg', pairs))  1.8 us
  transfers between devices with their start and end apart: 10, of which 9 were waited for; matrix products, arithmetic and copies ran while one was open for 2% of the time, Pallas kernels for 0%

profile of v12, /device:TPU:0, one launch (start us, length us, event | category | flops | bytes accessed | tf_op | source)
XLA Modules:
  0.0 46.7 jit_solution(10666670632270847668)
XLA Ops:
  0.0 5.8 %shard_map.55 = (bf16[16,512]{1,0:T(8,128)(2,1)}, bf16[16,512]{1,0:T(8,128)(2,1)}, bf16[16,512]{1,0:T(8,128)(2,1)}, bf16[16,512]{1,0:T(8,128)(2,1)}) custom-call(s32[16]{0:T(128)} %bitcast.102, s32[1]{0:T(128)} %bitcast.1.place_ref, s32[16]{0:T(128)} %live_ref.1, bf16[16,27648]{1,0:T(8,128)(2,1)} %bitcast.82, bf16[3072,128]{1,0:T(8,128)(2,1)} %constant.84.clone.table_ref, ...), custom_call_target="tpu_custom_call" | custom-call | tf_op jit(solution)/shard_map/pallas_call | solution.py:99
  5.8 3.0 %collective-permute-start = (bf16[16,512]{1,0:T(8,128)(2,1)}, bf16[16,512]{1,0:T(8,128)(2,1)S(1)}, u32[]{:S(2)}, u32[]{:S(2)}) collective-permute-start(bf16[16,512]{1,0:T(8,128)(2,1)} %get-tuple-element.10), channel_id=1, source_target_pairs={{0,8},{8,16},{16,24},{24,0},{1,9},{9,17},{17,25},{25,1},{2,10},{10... | collective-permute-start | bytes 49160 | tf_op jit(solution)/shard_map/ppermute | solution.py:152
  8.8 1.5 %collective-permute-start.1 = (bf16[16,512]{1,0:T(8,128)(2,1)}, bf16[16,512]{1,0:T(8,128)(2,1)S(1)}, u32[]{:S(2)}, u32[]{:S(2)}) collective-permute-start(bf16[16,512]{1,0:T(8,128)(2,1)} %get-tuple-element.11), channel_id=1, source_target_pairs={{0,16},{8,24},{16,0},{24,8},{1,17},{9,25},{17,1},{25,9},{2,18},{10... | collective-permute-start | bytes 49160 | tf_op jit(solution)/shard_map/ppermute | solution.py:152
  10.4 1.4 %collective-permute-start.2 = (bf16[16,512]{1,0:T(8,128)(2,1)}, bf16[16,512]{1,0:T(8,128)(2,1)S(1)}, u32[]{:S(2)}, u32[]{:S(2)}) collective-permute-start(bf16[16,512]{1,0:T(8,128)(2,1)} %get-tuple-element.12), channel_id=1, source_target_pairs={{0,24},{8,0},{16,8},{24,16},{1,25},{9,1},{17,9},{25,17},{2,26},{10... | collective-permute-start | bytes 49160 | tf_op jit(solution)/shard_map/ppermute | solution.py:152
  11.8 0.7 %constant_dynamic-update-slice_fusion.3 = (bf16[16,2048]{1,0:T(8,128)(2,1)S(1)}, bf16[128,2048]{1,0:T(8,128)(2,1)S(1)}) fusion(bf16[16,512]{1,0:T(8,128)(2,1)} %get-tuple-element.9), kind=kLoop, calls=%fused_computation.18 | loop fusion | bytes 49152
  12.5 0.3 collective-permute-done.1
  12.8 1.5 %collective-permute-done.2 = bf16[16,512]{1,0:T(8,128)(2,1)S(1)} collective-permute-done((bf16[16,512]{1,0:T(8,128)(2,1)}, bf16[16,512]{1,0:T(8,128)(2,1)S(1)}, u32[]{:S(2)}, u32[]{:S(2)}) %collective-permute-start.2) | collective-permute-done | bytes 16416 | tf_op jit(solution)/shard_map/ppermute | solution.py:152
  14.3 1.3 %collective-permute-start.3 = (bf16[16,2048]{1,0:T(8,128)(2,1)S(1)}, bf16[16,2048]{1,0:T(8,128)(2,1)S(1)}, u32[]{:S(2)}, u32[]{:S(2)}) collective-permute-start(bf16[16,2048]{1,0:T(8,128)(2,1)S(1)} %get-tuple-element.41), channel_id=1, source_target_pairs={{2,0},{3,1},{4,2},{5,3},{6,4},{7,5},{10,8},{11,9},{12,10},{13,11},... | collective-permute-start | bytes 196616 | tf_op jit(solution)/shard_map/ppermute | solution.py:123
  15.6 1.3 %collective-permute-start.4 = (bf16[16,2048]{1,0:T(8,128)(2,1)S(1)}, bf16[16,2048]{1,0:T(8,128)(2,1)S(1)}, u32[]{:S(2)}, u32[]{:S(2)}) collective-permute-start(bf16[16,2048]{1,0:T(8,128)(2,1)S(1)} %get-tuple-element.41), channel_id=1, source_target_pairs={{4,0},{5,1},{6,2},{7,3},{12,8},{13,9},{14,10},{15,11},{20,16},{21,... | collective-permute-start | bytes 196616 | tf_op jit(solution)/shard_map/ppermute | solution.py:123
  16.9 1.3 %collective-permute-start.5 = (bf16[16,2048]{1,0:T(8,128)(2,1)S(1)}, bf16[16,2048]{1,0:T(8,128)(2,1)S(1)}, u32[]{:S(2)}, u32[]{:S(2)}) collective-permute-start(bf16[16,2048]{1,0:T(8,128)(2,1)S(1)} %get-tuple-element.41), channel_id=1, source_target_pairs={{6,0},{7,1},{14,8},{15,9},{22,16},{23,17},{30,24},{31,25}} | collective-permute-start | bytes 196616 | tf_op jit(solution)/shard_map/ppermute | solution.py:123
  18.2 2.7 %collective-permute-done.3 = bf16[16,2048]{1,0:T(8,128)(2,1)S(1)} collective-permute-done((bf16[16,2048]{1,0:T(8,128)(2,1)S(1)}, bf16[16,2048]{1,0:T(8,128)(2,1)S(1)}, u32[]{:S(2)}, u32[]{:S(2)}) %collective-permute-start.3) | collective-permute-done | bytes 65568 | tf_op jit(solution)/shard_map/ppermute | solution.py:123
  20.9 2.7 %collective-permute-done.4 = bf16[16,2048]{1,0:T(8,128)(2,1)S(1)} collective-permute-done((bf16[16,2048]{1,0:T(8,128)(2,1)S(1)}, bf16[16,2048]{1,0:T(8,128)(2,1)S(1)}, u32[]{:S(2)}, u32[]{:S(2)}) %collective-permute-start.4) | collective-permute-done | bytes 65568 | tf_op jit(solution)/shard_map/ppermute | solution.py:123
  23.6 2.5 %collective-permute-done.5 = bf16[16,2048]{1,0:T(8,128)(2,1)S(1)} collective-permute-done((bf16[16,2048]{1,0:T(8,128)(2,1)S(1)}, bf16[16,2048]{1,0:T(8,128)(2,1)S(1)}, u32[]{:S(2)}, u32[]{:S(2)}) %collective-permute-start.5) | collective-permute-done | bytes 65568 | tf_op jit(solution)/shard_map/ppermute | solution.py:123
  26.3 1.4 %collective-permute-done.6 = bf16[64,2048]{1,0:T(8,128)(2,1)S(1)} collective-permute-done((bf16[64,2048]{1,0:T(8,128)(2,1)S(1)}, bf16[64,2048]{1,0:T(8,128)(2,1)S(1)}, u32[]{:S(2)}, u32[]{:S(2)}) %collective-permute-start.6) | collective-permute-done | bytes 262176 | tf_op jit(solution)/shard_map/ppermute | solution.py:124
  27.9 0.3 copy.94
  28.2 0.5 %copy-done = bf16[128,2048]{1,0:T(8,128)(2,1)} copy-done((bf16[128,2048]{1,0:T(8,128)(2,1)}, bf16[128,2048]{1,0:T(8,128)(2,1)S(1)}, u32[]{:S(2)}) %copy-start) | copy-done | bytes 524312
  28.9 0.3 copy.78
  29.2 0.3 copy.77
  29.4 0.6 %slice-done = bf16[16,2048]{1,0:T(8,128)(2,1)S(1)} async-done(((bf16[128,2048]{1,0:T(8,128)(2,1)}), bf16[16,2048]{1,0:T(8,128)(2,1)S(1)}, s32[]{:S(2)}) %slice-start) | async-done | bytes 65560 | tf_op jit(solution)/shard_map/stack | solution.py:163
  30.0 0.4 stack.33
  30.4 0.4 copy.51
  30.9 0.7 %convolution_bitcast_fusion = f32[16,2,16,144]{3,2,1,0:T(8,128)S(1)} fusion(bf16[144,64,2,16,1]{0,3,2,1,4:T(8,128)(2,1)S(1)} %bitcast.77, bf16[1,16,64,2,16]{2,1,3,0,4:T(8,128)(2,1)S(1)} %maximum_bitcast_fusion, bf16[1,16,64,2,16]{2,1,3,0,4:T(8,128)(2,1)S(1)} %copy.51), kind=kOutput, calls=%fused_computation.1 | convolution fusion | flops 18939904 | bytes 1015808 | tf_op jit(solution)/shard_map/ocspn,jspn->nocj/dot_general | solution.py:164
  31.6 0.6 %fusion.9 = (f32[16,2,1,128]{3,2,1,0:T(1,128)S(1)}, f32[16,2,1,128]{3,2,1,0:T(1,128)S(1)}, f32[16,2,1,128]{3,2,1,0:T(1,128)S(1)}, f32[16,2,1,128]{3,2,1,0:T(1,12...) fusion(f32[16,2,16,144]{3,2,1,0:T(8,128)S(1)} %convolution_bitc, ...), kind=kLoop, calls=%fused_computation.73 | loop fusion | bytes 524288 | tf_op jit(solution)/shard_map/slice | solution.py:165
  32.9 2.9 %collective-permute-start.7 = (f32[64,512]{1,0:T(8,128)S(1)}, f32[64,512]{1,0:T(8,128)S(1)}, u32[]{:S(2)}, u32[]{:S(2)}) collective-permute-start(f32[64,512]{1,0:T(8,128)S(1)} %get-tuple-element.18), channel_id=1, source_target_pairs={{0,8},{24,0},{1,9},{25,1},{2,10},{26,2},{3,11},{27,3},{4,12},{28,4... | collective-permute-start | bytes 393224 | tf_op jit(solution)/shard_map/ppermute | solution.py:177
  35.7 1.3 %collective-permute-start.8 = (f32[64,512]{1,0:T(8,128)S(1)}, f32[64,512]{1,0:T(8,128)S(1)}, u32[]{:S(2)}, u32[]{:S(2)}) collective-permute-start(f32[64,512]{1,0:T(8,128)S(1)} %get-tuple-element.17), channel_id=1, source_target_pairs={{16,0},{24,8},{17,1},{25,9},{18,2},{26,10},{19,3},{27,11},{20,4},{... | collective-permute-start | bytes 393224 | tf_op jit(solution)/shard_map/ppermute | solution.py:177
  37.0 1.3 %collective-permute-start.9 = (f32[64,512]{1,0:T(8,128)S(1)}, f32[64,512]{1,0:T(8,128)S(1)}, u32[]{:S(2)}, u32[]{:S(2)}) collective-permute-start(f32[64,512]{1,0:T(8,128)S(1)} %get-tuple-element.16), channel_id=1, source_target_pairs={{8,0},{16,8},{9,1},{17,9},{10,2},{18,10},{11,3},{19,11},{12,4},{20... | collective-permute-start | bytes 393224 | tf_op jit(solution)/shard_map/ppermute | solution.py:177
  38.4 2.9 %collective-permute-done.7 = f32[64,512]{1,0:T(8,128)S(1)} collective-permute-done((f32[64,512]{1,0:T(8,128)S(1)}, f32[64,512]{1,0:T(8,128)S(1)}, u32[]{:S(2)}, u32[]{:S(2)}) %collective-permute-start.7) | collective-permute-done | bytes 131104 | tf_op jit(solution)/shard_map/ppermute | solution.py:177
  41.3 2.7 %collective-permute-done.8 = f32[64,512]{1,0:T(8,128)S(1)} collective-permute-done((f32[64,512]{1,0:T(8,128)S(1)}, f32[64,512]{1,0:T(8,128)S(1)}, u32[]{:S(2)}, u32[]{:S(2)}) %collective-permute-start.8) | collective-permute-done | bytes 131104 | tf_op jit(solution)/shard_map/ppermute | solution.py:177
  44.2 0.6 %gather_fusion = f32[4,64,512]{2,1,0:T(8,128)S(1)} fusion(f32[4,64,512]{2,1,0:T(8,128)S(1)} %pad_maximum_fusion, s32[1024]{0:T(1024)S(1)} %pad_clamp_fusion), kind=kCustom, calls=%fused_computation | custom fusion | bytes 1048592 | tf_op jit(solution)/shard_map/jit(_take)/gather | solution.py:182
  44.8 0.3 copy.70
  45.2 0.2 select_bitcast_fusion
  45.5 1.1 %copy.72 = f32[64,16,128]{2,1,0:T(8,128)} copy(f32[64,16,128]{0,2,1:T(8,128)S(1)} %bitcast.79) | data formatting | bytes 1048576 | tf_op jit(solution)/shard_map/reshape | solution.py:183
  (51 shorter events, 1.5 us)
Async XLA Ops:
  5.8 6.7 %collective-permute-start = (bf16[16,512]{1,0:T(8,128)(2,1)}, bf16[16,512]{1,0:T(8,128)(2,1)S(1)}, u32[]{:S(2)}, u32[]{:S(2)}) collective-permute-start(bf16[16,512]{1,0:T(8,128)(2,1)} %get-tuple-element.10), channel_id=1, source_target_pairs={{0,8},{8,16},{16,24},{24,0},{1,9},{9,17},{17,25},{25,1},{2,10},{10... | collective-permute-start | bytes 49160 | tf_op jit(solution)/shard_map/ppermute | solution.py:152
  8.8 3.9 %collective-permute-start.1 = (bf16[16,512]{1,0:T(8,128)(2,1)}, bf16[16,512]{1,0:T(8,128)(2,1)S(1)}, u32[]{:S(2)}, u32[]{:S(2)}) collective-permute-start(bf16[16,512]{1,0:T(8,128)(2,1)} %get-tuple-element.11), channel_id=1, source_target_pairs={{0,16},{8,24},{16,0},{24,8},{1,17},{9,25},{17,1},{25,9},{2,18},{10... | collective-permute-start | bytes 49160 | tf_op jit(solution)/shard_map/ppermute | solution.py:152
  10.4 3.9 %collective-permute-start.2 = (bf16[16,512]{1,0:T(8,128)(2,1)}, bf16[16,512]{1,0:T(8,128)(2,1)S(1)}, u32[]{:S(2)}, u32[]{:S(2)}) collective-permute-start(bf16[16,512]{1,0:T(8,128)(2,1)} %get-tuple-element.12), channel_id=1, source_target_pairs={{0,24},{8,0},{16,8},{24,16},{1,25},{9,1},{17,9},{25,17},{2,26},{10... | collective-permute-start | bytes 49160 | tf_op jit(solution)/shard_map/ppermute | solution.py:152
  14.3 6.6 %collective-permute-start.3 = (bf16[16,2048]{1,0:T(8,128)(2,1)S(1)}, bf16[16,2048]{1,0:T(8,128)(2,1)S(1)}, u32[]{:S(2)}, u32[]{:S(2)}) collective-permute-start(bf16[16,2048]{1,0:T(8,128)(2,1)S(1)} %get-tuple-element.41), channel_id=1, source_target_pairs={{2,0},{3,1},{4,2},{5,3},{6,4},{7,5},{10,8},{11,9},{12,10},{13,11},... | collective-permute-start | bytes 196616 | tf_op jit(solution)/shard_map/ppermute | solution.py:123
  15.6 8.0 %collective-permute-start.4 = (bf16[16,2048]{1,0:T(8,128)(2,1)S(1)}, bf16[16,2048]{1,0:T(8,128)(2,1)S(1)}, u32[]{:S(2)}, u32[]{:S(2)}) collective-permute-start(bf16[16,2048]{1,0:T(8,128)(2,1)S(1)} %get-tuple-element.41), channel_id=1, source_target_pairs={{4,0},{5,1},{6,2},{7,3},{12,8},{13,9},{14,10},{15,11},{20,16},{21,... | collective-permute-start | bytes 196616 | tf_op jit(solution)/shard_map/ppermute | solution.py:123
  16.9 9.1 %collective-permute-start.5 = (bf16[16,2048]{1,0:T(8,128)(2,1)S(1)}, bf16[16,2048]{1,0:T(8,128)(2,1)S(1)}, u32[]{:S(2)}, u32[]{:S(2)}) collective-permute-start(bf16[16,2048]{1,0:T(8,128)(2,1)S(1)} %get-tuple-element.41), channel_id=1, source_target_pairs={{6,0},{7,1},{14,8},{15,9},{22,16},{23,17},{30,24},{31,25}} | collective-permute-start | bytes 196616 | tf_op jit(solution)/shard_map/ppermute | solution.py:123
  26.1 1.6 %collective-permute-start.6 = (bf16[64,2048]{1,0:T(8,128)(2,1)S(1)}, bf16[64,2048]{1,0:T(8,128)(2,1)S(1)}, u32[]{:S(2)}, u32[]{:S(2)}) collective-permute-start(bf16[64,2048]{1,0:T(8,128)(2,1)S(1)} %pad_maximum_fusion.1), channel_id=1, source_target_pairs={{0,1},{1,0},{2,3},{3,2},{4,5},{5,4},{6,7},{7,6},{8,9},{9,8},{10,11... | collective-permute-start | bytes 786440 | tf_op jit(solution)/shard_map/ppermute | solution.py:124
  27.9 0.8 %copy-start = (bf16[128,2048]{1,0:T(8,128)(2,1)}, bf16[128,2048]{1,0:T(8,128)(2,1)S(1)}, u32[]{:S(2)}) copy-start(bf16[128,2048]{1,0:T(8,128)(2,1)S(1)} %broadcast_select_fusion) | copy-start | bytes 1572868
  29.2 0.8 %slice-start = ((bf16[128,2048]{1,0:T(8,128)(2,1)}), bf16[16,2048]{1,0:T(8,128)(2,1)S(1)}, s32[]{:S(2)}) async-start(bf16[128,2048]{1,0:T(8,128)(2,1)} %copy-done), calls=%async_computation | async-start | bytes 131072 | tf_op jit(solution)/shard_map/stack | solution.py:163
  32.9 8.4 %collective-permute-start.7 = (f32[64,512]{1,0:T(8,128)S(1)}, f32[64,512]{1,0:T(8,128)S(1)}, u32[]{:S(2)}, u32[]{:S(2)}) collective-permute-start(f32[64,512]{1,0:T(8,128)S(1)} %get-tuple-element.18), channel_id=1, source_target_pairs={{0,8},{24,0},{1,9},{25,1},{2,10},{26,2},{3,11},{27,3},{4,12},{28,4... | collective-permute-start | bytes 393224 | tf_op jit(solution)/shard_map/ppermute | solution.py:177
  35.7 8.2 %collective-permute-start.8 = (f32[64,512]{1,0:T(8,128)S(1)}, f32[64,512]{1,0:T(8,128)S(1)}, u32[]{:S(2)}, u32[]{:S(2)}) collective-permute-start(f32[64,512]{1,0:T(8,128)S(1)} %get-tuple-element.17), channel_id=1, source_target_pairs={{16,0},{24,8},{17,1},{25,9},{18,2},{26,10},{19,3},{27,11},{20,4},{... | collective-permute-start | bytes 393224 | tf_op jit(solution)/shard_map/ppermute | solution.py:177
  37.0 7.2 %collective-permute-start.9 = (f32[64,512]{1,0:T(8,128)S(1)}, f32[64,512]{1,0:T(8,128)S(1)}, u32[]{:S(2)}, u32[]{:S(2)}) collective-permute-start(f32[64,512]{1,0:T(8,128)S(1)} %get-tuple-element.16), channel_id=1, source_target_pairs={{8,0},{16,8},{9,1},{17,9},{10,2},{18,10},{11,3},{19,11},{12,4},{20... | collective-permute-start | bytes 393224 | tf_op jit(solution)/shard_map/ppermute | solution.py:177

commit v13 on v10

--- a/solution.py
+++ b/solution.py
@@ -43,13 +43,13 @@
         shift = shifts[w]
         low = lane < LANES - shift
         rolled = [
-            pltpu.roll(chunks[w, :, pl.ds(b * LANES, LANES)].astype(jnp.float32), (LANES - shift) % LANES, 1)
+            pltpu.roll(chunks[w, :, pl.ds(b * LANES, LANES)], (LANES - shift) % LANES, 1)
             for b in range(blocks + 1)
         ]
         for b in range(blocks):
             moved_rows[pl.ds(w * channels, channels), pl.ds(b * LANES, LANES)] = jnp.where(
                 low, rolled[b], rolled[b + 1]
-            ).astype(jnp.bfloat16)
+            )
     spectra = jnp.dot(moved_rows[...], table_ref[...], preferred_element_type=jnp.float32)
     power = spectra * spectra
     smooth = jnp.dot(

time: 46.8 us -> 46.7 us (level)
  no operation moved by 1% of the time
where the time goes in v13:
time: 46.7 us; the launch traced here: 46.3 us
  waiting for transfers between devices  16.8 us (36%)
  starting transfers between devices  15.3 us (33%)
  local copies, waits for them, and re-layouts  6.94 us (15%)
  Pallas kernels  5.49 us (12%)
  matrix products  0.73 us (2%)
  other arithmetic  0.55 us (1%)
    ppermute x3, waiting for transfers between devices, halo(): own.append(lax.ppermute(mine, 'fibre', pairs))  7.84 us
    ppermute x3, starting transfers between devices, shards(): gathered.append(lax.ppermute(split[step], 'seg', pairs))  5.94 us
    ppermute x3, waiting for transfers between devices, shards(): collected.append(lax.ppermute(sent, 'seg', pairs))  5.82 us
    pallas_call x1, Pallas kernels, whiten(): pl.pallas_call(whiten_kernel, out_shape=[jax.ShapeDtypeStruct((channels,...  5.49 us
    ppermute x3, starting transfers between devices, shards(): collected.append(lax.ppermute(sent, 'seg', pairs))  5.47 us
    ppermute x3, starting transfers between devices, halo(): own.append(lax.ppermute(mine, 'fibre', pairs))  3.86 us
    unnamed x33, local copies, waits for them, and re-layouts  2.41 us
    ppermute x3, waiting for transfers between devices, shards(): gathered.append(lax.ppermute(split[step], 'seg', pairs))  1.79 us
  transfers between devices with their start and end apart: 10, of which 9 were waited for; matrix products, arithmetic and copies ran while one was open for 2% of the time, Pallas kernels for 0%

profile of v13, /device:TPU:0, one launch (start us, length us, event | category | flops | bytes accessed | tf_op | source)
XLA Modules:
  0.0 46.3 jit_solution(1343034258512254669)
XLA Ops:
  0.0 5.5 %shard_map.64 = (bf16[16,512]{1,0:T(8,128)(2,1)}, bf16[16,512]{1,0:T(8,128)(2,1)}, bf16[16,512]{1,0:T(8,128)(2,1)}, bf16[16,512]{1,0:T(8,128)(2,1)}) custom-call(s32[16]{0:T(128)} %bitcast.102, s32[1]{0:T(128)} %bitcast.1.place_ref, s32[16]{0:T(128)} %live_ref.1, bf16[16,27648]{1,0:T(8,128)(2,1)} %bitcast.82, bf16[3072,128]{1,0:T(8,128)(2,1)} %constant.86.clone.table_ref, ...), custom_call_target="tpu_custom_call" | custom-call | tf_op jit(solution)/shard_map/pallas_call | solution.py:94
  5.5 3.0 %collective-permute-start = (bf16[16,512]{1,0:T(8,128)(2,1)}, bf16[16,512]{1,0:T(8,128)(2,1)S(1)}, u32[]{:S(2)}, u32[]{:S(2)}) collective-permute-start(bf16[16,512]{1,0:T(8,128)(2,1)} %get-tuple-element.10), channel_id=1, source_target_pairs={{0,8},{8,16},{16,24},{24,0},{1,9},{9,17},{17,25},{25,1},{2,10},{10... | collective-permute-start | bytes 49160 | tf_op jit(solution)/shard_map/ppermute | solution.py:147
  8.5 1.5 %collective-permute-start.1 = (bf16[16,512]{1,0:T(8,128)(2,1)}, bf16[16,512]{1,0:T(8,128)(2,1)S(1)}, u32[]{:S(2)}, u32[]{:S(2)}) collective-permute-start(bf16[16,512]{1,0:T(8,128)(2,1)} %get-tuple-element.11), channel_id=1, source_target_pairs={{0,16},{8,24},{16,0},{24,8},{1,17},{9,25},{17,1},{25,9},{2,18},{10... | collective-permute-start | bytes 49160 | tf_op jit(solution)/shard_map/ppermute | solution.py:147
  10.0 1.4 %collective-permute-start.2 = (bf16[16,512]{1,0:T(8,128)(2,1)}, bf16[16,512]{1,0:T(8,128)(2,1)S(1)}, u32[]{:S(2)}, u32[]{:S(2)}) collective-permute-start(bf16[16,512]{1,0:T(8,128)(2,1)} %get-tuple-element.12), channel_id=1, source_target_pairs={{0,24},{8,0},{16,8},{24,16},{1,25},{9,1},{17,9},{25,17},{2,26},{10... | collective-permute-start | bytes 49160 | tf_op jit(solution)/shard_map/ppermute | solution.py:147
  11.4 0.7 %constant_dynamic-update-slice_fusion.3 = (bf16[16,2048]{1,0:T(8,128)(2,1)S(1)}, bf16[128,2048]{1,0:T(8,128)(2,1)S(1)}) fusion(bf16[16,512]{1,0:T(8,128)(2,1)} %get-tuple-element.9), kind=kLoop, calls=%fused_computation.18 | loop fusion | bytes 49152
  12.2 0.3 collective-permute-done.1
  12.4 1.5 %collective-permute-done.2 = bf16[16,512]{1,0:T(8,128)(2,1)S(1)} collective-permute-done((bf16[16,512]{1,0:T(8,128)(2,1)}, bf16[16,512]{1,0:T(8,128)(2,1)S(1)}, u32[]{:S(2)}, u32[]{:S(2)}) %collective-permute-start.2) | collective-permute-done | bytes 16416 | tf_op jit(solution)/shard_map/ppermute | solution.py:147
  14.0 1.3 %collective-permute-start.3 = (bf16[16,2048]{1,0:T(8,128)(2,1)S(1)}, bf16[16,2048]{1,0:T(8,128)(2,1)S(1)}, u32[]{:S(2)}, u32[]{:S(2)}) collective-permute-start(bf16[16,2048]{1,0:T(8,128)(2,1)S(1)} %get-tuple-element.41), channel_id=1, source_target_pairs={{2,0},{3,1},{4,2},{5,3},{6,4},{7,5},{10,8},{11,9},{12,10},{13,11},... | collective-permute-start | bytes 196616 | tf_op jit(solution)/shard_map/ppermute | solution.py:118
  15.3 1.3 %collective-permute-start.4 = (bf16[16,2048]{1,0:T(8,128)(2,1)S(1)}, bf16[16,2048]{1,0:T(8,128)(2,1)S(1)}, u32[]{:S(2)}, u32[]{:S(2)}) collective-permute-start(bf16[16,2048]{1,0:T(8,128)(2,1)S(1)} %get-tuple-element.41), channel_id=1, source_target_pairs={{4,0},{5,1},{6,2},{7,3},{12,8},{13,9},{14,10},{15,11},{20,16},{21,... | collective-permute-start | bytes 196616 | tf_op jit(solution)/shard_map/ppermute | solution.py:118
  16.6 1.3 %collective-permute-start.5 = (bf16[16,2048]{1,0:T(8,128)(2,1)S(1)}, bf16[16,2048]{1,0:T(8,128)(2,1)S(1)}, u32[]{:S(2)}, u32[]{:S(2)}) collective-permute-start(bf16[16,2048]{1,0:T(8,128)(2,1)S(1)} %get-tuple-element.41), channel_id=1, source_target_pairs={{6,0},{7,1},{14,8},{15,9},{22,16},{23,17},{30,24},{31,25}} | collective-permute-start | bytes 196616 | tf_op jit(solution)/shard_map/ppermute | solution.py:118
  17.9 2.7 %collective-permute-done.3 = bf16[16,2048]{1,0:T(8,128)(2,1)S(1)} collective-permute-done((bf16[16,2048]{1,0:T(8,128)(2,1)S(1)}, bf16[16,2048]{1,0:T(8,128)(2,1)S(1)}, u32[]{:S(2)}, u32[]{:S(2)}) %collective-permute-start.3) | collective-permute-done | bytes 65568 | tf_op jit(solution)/shard_map/ppermute | solution.py:118
  20.6 2.7 %collective-permute-done.4 = bf16[16,2048]{1,0:T(8,128)(2,1)S(1)} collective-permute-done((bf16[16,2048]{1,0:T(8,128)(2,1)S(1)}, bf16[16,2048]{1,0:T(8,128)(2,1)S(1)}, u32[]{:S(2)}, u32[]{:S(2)}) %collective-permute-start.4) | collective-permute-done | bytes 65568 | tf_op jit(solution)/shard_map/ppermute | solution.py:118
  23.2 2.5 %collective-permute-done.5 = bf16[16,2048]{1,0:T(8,128)(2,1)S(1)} collective-permute-done((bf16[16,2048]{1,0:T(8,128)(2,1)S(1)}, bf16[16,2048]{1,0:T(8,128)(2,1)S(1)}, u32[]{:S(2)}, u32[]{:S(2)}) %collective-permute-start.5) | collective-permute-done | bytes 65568 | tf_op jit(solution)/shard_map/ppermute | solution.py:118
  25.9 1.4 %collective-permute-done.6 = bf16[64,2048]{1,0:T(8,128)(2,1)S(1)} collective-permute-done((bf16[64,2048]{1,0:T(8,128)(2,1)S(1)}, bf16[64,2048]{1,0:T(8,128)(2,1)S(1)}, u32[]{:S(2)}, u32[]{:S(2)}) %collective-permute-start.6) | collective-permute-done | bytes 262176 | tf_op jit(solution)/shard_map/ppermute | solution.py:119
  27.5 0.3 copy.95
  27.8 0.5 %copy-done = bf16[128,2048]{1,0:T(8,128)(2,1)} copy-done((bf16[128,2048]{1,0:T(8,128)(2,1)}, bf16[128,2048]{1,0:T(8,128)(2,1)S(1)}, u32[]{:S(2)}) %copy-start) | copy-done | bytes 524312
  28.5 0.3 copy.79
  28.8 0.3 copy.78
  29.1 0.6 %slice-done = bf16[16,2048]{1,0:T(8,128)(2,1)S(1)} async-done(((bf16[128,2048]{1,0:T(8,128)(2,1)}), bf16[16,2048]{1,0:T(8,128)(2,1)S(1)}, s32[]{:S(2)}) %slice-start) | async-done | bytes 65560 | tf_op jit(solution)/shard_map/stack | solution.py:158
  29.7 0.4 stack.33
  30.1 0.4 copy.52
  30.6 0.7 %convolution_bitcast_fusion = f32[16,2,16,144]{3,2,1,0:T(8,128)S(1)} fusion(bf16[144,64,2,16,1]{0,3,2,1,4:T(8,128)(2,1)S(1)} %bitcast.77, bf16[1,16,64,2,16]{2,1,3,0,4:T(8,128)(2,1)S(1)} %maximum_bitcast_fusion, bf16[1,16,64,2,16]{2,1,3,0,4:T(8,128)(2,1)S(1)} %copy.52), kind=kOutput, calls=%fused_computation.1 | convolution fusion | flops 18939904 | bytes 1015808 | tf_op jit(solution)/shard_map/ocspn,jspn->nocj/dot_general | solution.py:159
  31.3 0.6 %fusion.9 = (f32[16,2,1,128]{3,2,1,0:T(1,128)S(1)}, f32[16,2,1,128]{3,2,1,0:T(1,128)S(1)}, f32[16,2,1,128]{3,2,1,0:T(1,128)S(1)}, f32[16,2,1,128]{3,2,1,0:T(1,12...) fusion(f32[16,2,16,144]{3,2,1,0:T(8,128)S(1)} %convolution_bitc, ...), kind=kLoop, calls=%fused_computation.73 | loop fusion | bytes 524288 | tf_op jit(solution)/shard_map/slice | solution.py:160
  32.5 2.9 %collective-permute-start.7 = (f32[64,512]{1,0:T(8,128)S(1)}, f32[64,512]{1,0:T(8,128)S(1)}, u32[]{:S(2)}, u32[]{:S(2)}) collective-permute-start(f32[64,512]{1,0:T(8,128)S(1)} %get-tuple-element.18), channel_id=1, source_target_pairs={{0,8},{24,0},{1,9},{25,1},{2,10},{26,2},{3,11},{27,3},{4,12},{28,4... | collective-permute-start | bytes 393224 | tf_op jit(solution)/shard_map/ppermute | solution.py:172
  35.4 1.3 %collective-permute-start.8 = (f32[64,512]{1,0:T(8,128)S(1)}, f32[64,512]{1,0:T(8,128)S(1)}, u32[]{:S(2)}, u32[]{:S(2)}) collective-permute-start(f32[64,512]{1,0:T(8,128)S(1)} %get-tuple-element.17), channel_id=1, source_target_pairs={{16,0},{24,8},{17,1},{25,9},{18,2},{26,10},{19,3},{27,11},{20,4},{... | collective-permute-start | bytes 393224 | tf_op jit(solution)/shard_map/ppermute | solution.py:172
  36.7 1.3 %collective-permute-start.9 = (f32[64,512]{1,0:T(8,128)S(1)}, f32[64,512]{1,0:T(8,128)S(1)}, u32[]{:S(2)}, u32[]{:S(2)}) collective-permute-start(f32[64,512]{1,0:T(8,128)S(1)} %get-tuple-element.16), channel_id=1, source_target_pairs={{8,0},{16,8},{9,1},{17,9},{10,2},{18,10},{11,3},{19,11},{12,4},{20... | collective-permute-start | bytes 393224 | tf_op jit(solution)/shard_map/ppermute | solution.py:172
  38.0 2.9 %collective-permute-done.7 = f32[64,512]{1,0:T(8,128)S(1)} collective-permute-done((f32[64,512]{1,0:T(8,128)S(1)}, f32[64,512]{1,0:T(8,128)S(1)}, u32[]{:S(2)}, u32[]{:S(2)}) %collective-permute-start.7) | collective-permute-done | bytes 131104 | tf_op jit(solution)/shard_map/ppermute | solution.py:172
  40.9 2.7 %collective-permute-done.8 = f32[64,512]{1,0:T(8,128)S(1)} collective-permute-done((f32[64,512]{1,0:T(8,128)S(1)}, f32[64,512]{1,0:T(8,128)S(1)}, u32[]{:S(2)}, u32[]{:S(2)}) %collective-permute-start.8) | collective-permute-done | bytes 131104 | tf_op jit(solution)/shard_map/ppermute | solution.py:172
  43.9 0.6 %gather_fusion = f32[4,64,512]{2,1,0:T(8,128)S(1)} fusion(f32[4,64,512]{2,1,0:T(8,128)S(1)} %pad_maximum_fusion, s32[1024]{0:T(1024)S(1)} %pad_clamp_fusion), kind=kCustom, calls=%fused_computation | custom fusion | bytes 1048592 | tf_op jit(solution)/shard_map/jit(_take)/gather | solution.py:177
  44.5 0.3 copy.71
  44.8 0.2 select_bitcast_fusion
  45.2 1.1 %copy.73 = f32[64,16,128]{2,1,0:T(8,128)} copy(f32[64,16,128]{0,2,1:T(8,128)S(1)} %bitcast.79) | data formatting | bytes 1048576 | tf_op jit(solution)/shard_map/reshape | solution.py:178
  (51 shorter events, 1.5 us)
Async XLA Ops:
  5.5 6.7 %collective-permute-start = (bf16[16,512]{1,0:T(8,128)(2,1)}, bf16[16,512]{1,0:T(8,128)(2,1)S(1)}, u32[]{:S(2)}, u32[]{:S(2)}) collective-permute-start(bf16[16,512]{1,0:T(8,128)(2,1)} %get-tuple-element.10), channel_id=1, source_target_pairs={{0,8},{8,16},{16,24},{24,0},{1,9},{9,17},{17,25},{25,1},{2,10},{10... | collective-permute-start | bytes 49160 | tf_op jit(solution)/shard_map/ppermute | solution.py:147
  8.5 3.9 %collective-permute-start.1 = (bf16[16,512]{1,0:T(8,128)(2,1)}, bf16[16,512]{1,0:T(8,128)(2,1)S(1)}, u32[]{:S(2)}, u32[]{:S(2)}) collective-permute-start(bf16[16,512]{1,0:T(8,128)(2,1)} %get-tuple-element.11), channel_id=1, source_target_pairs={{0,16},{8,24},{16,0},{24,8},{1,17},{9,25},{17,1},{25,9},{2,18},{10... | collective-permute-start | bytes 49160 | tf_op jit(solution)/shard_map/ppermute | solution.py:147
  10.0 3.9 %collective-permute-start.2 = (bf16[16,512]{1,0:T(8,128)(2,1)}, bf16[16,512]{1,0:T(8,128)(2,1)S(1)}, u32[]{:S(2)}, u32[]{:S(2)}) collective-permute-start(bf16[16,512]{1,0:T(8,128)(2,1)} %get-tuple-element.12), channel_id=1, source_target_pairs={{0,24},{8,0},{16,8},{24,16},{1,25},{9,1},{17,9},{25,17},{2,26},{10... | collective-permute-start | bytes 49160 | tf_op jit(solution)/shard_map/ppermute | solution.py:147
  14.0 6.6 %collective-permute-start.3 = (bf16[16,2048]{1,0:T(8,128)(2,1)S(1)}, bf16[16,2048]{1,0:T(8,128)(2,1)S(1)}, u32[]{:S(2)}, u32[]{:S(2)}) collective-permute-start(bf16[16,2048]{1,0:T(8,128)(2,1)S(1)} %get-tuple-element.41), channel_id=1, source_target_pairs={{2,0},{3,1},{4,2},{5,3},{6,4},{7,5},{10,8},{11,9},{12,10},{13,11},... | collective-permute-start | bytes 196616 | tf_op jit(solution)/shard_map/ppermute | solution.py:118
  15.3 8.0 %collective-permute-start.4 = (bf16[16,2048]{1,0:T(8,128)(2,1)S(1)}, bf16[16,2048]{1,0:T(8,128)(2,1)S(1)}, u32[]{:S(2)}, u32[]{:S(2)}) collective-permute-start(bf16[16,2048]{1,0:T(8,128)(2,1)S(1)} %get-tuple-element.41), channel_id=1, source_target_pairs={{4,0},{5,1},{6,2},{7,3},{12,8},{13,9},{14,10},{15,11},{20,16},{21,... | collective-permute-start | bytes 196616 | tf_op jit(solution)/shard_map/ppermute | solution.py:118
  16.6 9.1 %collective-permute-start.5 = (bf16[16,2048]{1,0:T(8,128)(2,1)S(1)}, bf16[16,2048]{1,0:T(8,128)(2,1)S(1)}, u32[]{:S(2)}, u32[]{:S(2)}) collective-permute-start(bf16[16,2048]{1,0:T(8,128)(2,1)S(1)} %get-tuple-element.41), channel_id=1, source_target_pairs={{6,0},{7,1},{14,8},{15,9},{22,16},{23,17},{30,24},{31,25}} | collective-permute-start | bytes 196616 | tf_op jit(solution)/shard_map/ppermute | solution.py:118
  25.7 1.6 %collective-permute-start.6 = (bf16[64,2048]{1,0:T(8,128)(2,1)S(1)}, bf16[64,2048]{1,0:T(8,128)(2,1)S(1)}, u32[]{:S(2)}, u32[]{:S(2)}) collective-permute-start(bf16[64,2048]{1,0:T(8,128)(2,1)S(1)} %pad_maximum_fusion.1), channel_id=1, source_target_pairs={{0,1},{1,0},{2,3},{3,2},{4,5},{5,4},{6,7},{7,6},{8,9},{9,8},{10,11... | collective-permute-start | bytes 786440 | tf_op jit(solution)/shard_map/ppermute | solution.py:119
  27.5 0.8 %copy-start = (bf16[128,2048]{1,0:T(8,128)(2,1)}, bf16[128,2048]{1,0:T(8,128)(2,1)S(1)}, u32[]{:S(2)}) copy-start(bf16[128,2048]{1,0:T(8,128)(2,1)S(1)} %broadcast_select_fusion) | copy-start | bytes 1572868
  28.8 0.8 %slice-start = ((bf16[128,2048]{1,0:T(8,128)(2,1)}), bf16[16,2048]{1,0:T(8,128)(2,1)S(1)}, s32[]{:S(2)}) async-start(bf16[128,2048]{1,0:T(8,128)(2,1)} %copy-done), calls=%async_computation | async-start | bytes 131072 | tf_op jit(solution)/shard_map/stack | solution.py:158
  32.5 8.4 %collective-permute-start.7 = (f32[64,512]{1,0:T(8,128)S(1)}, f32[64,512]{1,0:T(8,128)S(1)}, u32[]{:S(2)}, u32[]{:S(2)}) collective-permute-start(f32[64,512]{1,0:T(8,128)S(1)} %get-tuple-element.18), channel_id=1, source_target_pairs={{0,8},{24,0},{1,9},{25,1},{2,10},{26,2},{3,11},{27,3},{4,12},{28,4... | collective-permute-start | bytes 393224 | tf_op jit(solution)/shard_map/ppermute | solution.py:172
  35.4 8.2 %collective-permute-start.8 = (f32[64,512]{1,0:T(8,128)S(1)}, f32[64,512]{1,0:T(8,128)S(1)}, u32[]{:S(2)}, u32[]{:S(2)}) collective-permute-start(f32[64,512]{1,0:T(8,128)S(1)} %get-tuple-element.17), channel_id=1, source_target_pairs={{16,0},{24,8},{17,1},{25,9},{18,2},{26,10},{19,3},{27,11},{20,4},{... | collective-permute-start | bytes 393224 | tf_op jit(solution)/shard_map/ppermute | solution.py:172
  36.7 7.2 %collective-permute-start.9 = (f32[64,512]{1,0:T(8,128)S(1)}, f32[64,512]{1,0:T(8,128)S(1)}, u32[]{:S(2)}, u32[]{:S(2)}) collective-permute-start(f32[64,512]{1,0:T(8,128)S(1)} %get-tuple-element.16), channel_id=1, source_target_pairs={{8,0},{16,8},{9,1},{17,9},{10,2},{18,10},{11,3},{19,11},{12,4},{20... | collective-permute-start | bytes 393224 | tf_op jit(solution)/shard_map/ppermute | solution.py:172

commit v14 on v10

--- a/solution.py
+++ b/solution.py
@@ -139,13 +139,10 @@
     hops = min(-(-span // block) - 1, fibre_count - 1)
     me = lax.axis_index("seg")
     rows = seg_count * windows_count
-    split = whiten(record[0], offsets[0], live_mask, seg_count, me.astype(jnp.int32))
+    split = whiten(record[0], offsets[0], live_mask, seg_count, jnp.zeros((), jnp.int32))
 
-    gathered = [split[0]]
-    for step in range(1, seg_count):
-        pairs = [(i, (i + step) % seg_count) for i in range(seg_count)]
-        gathered.append(lax.ppermute(split[step], "seg", pairs))
-    mine = jnp.concatenate(gathered, axis=1)
+    arrived = lax.all_to_all(jnp.stack(split), "seg", 0, 0, tiled=False)
+    mine = arrived.transpose(1, 0, 2).reshape(block, -1)
 
     columns = halo(mine, hops, fibre_count)[:span]
     if columns.shape[0] < span:

time: 46.8 us -> 48.7 us (1.041)
  blocking collectives: 0 us -> 9.81 us
  starting transfers between devices: 15.3 us -> 9.17 us
  waiting for transfers between devices: 16.8 us -> 15.1 us
  other arithmetic: 0.55 us -> 1.34 us
  local copies, waits for them, and re-layouts: 6.94 us -> 6.22 us
    all_to_all x0 -> x1, blocking collectives: none -> 9.81 us  [shards(): arrived = lax.all_to_all(jnp.stack(split), 'seg', 0, 0, tiled=False)]
    ppermute x3 -> x0, starting transfers between devices: 5.94 us -> none  [shards(): gathered.append(lax.ppermute(split[step], 'seg', pairs))]
    ppermute x3 -> x0, waiting for transfers between devices: 1.79 us -> none  [shards(): gathered.append(lax.ppermute(split[step], 'seg', pairs))]
    another operation x0 -> x1, other arithmetic: none -> 0.78 us  [shards(): arrived = lax.all_to_all(jnp.stack(split), 'seg', 0, 0, tiled=False)]
    unnamed x33 -> x31, local copies, waits for them, and re-layouts: 2.41 us -> 1.69 us
  transfers between devices with their start and end apart: 10 -> 7, of which waited for: 9 -> 6; matrix products, arithmetic and copies ran while one was open for 2% -> 0% of each run, Pallas kernels for 0% -> 0%
where the time goes in v14:
time: 48.7 us; the launch traced here: 48.3 us
  waiting for transfers between devices  15.1 us (31%)
  blocking collectives  9.81 us (20%)
  starting transfers between devices  9.17 us (19%)
  local copies, waits for them, and re-layouts  6.22 us (13%)
  Pallas kernels  5.53 us (11%)
  other arithmetic  1.34 us (3%)
  matrix products  0.73 us (1%)
    all_to_all x1, blocking collectives, shards(): arrived = lax.all_to_all(jnp.stack(split), 'seg', 0, 0, tiled=False)  9.81 us
    ppermute x3, waiting for transfers between devices, halo(): own.append(lax.ppermute(mine, 'fibre', pairs))  7.83 us
    ppermute x3, waiting for transfers between devices, shards(): collected.append(lax.ppermute(sent, 'seg', pairs))  5.85 us
    pallas_call x1, Pallas kernels, whiten(): pl.pallas_call(whiten_kernel, out_shape=[jax.ShapeDtypeStruct((channels,...  5.53 us
    ppermute x3, starting transfers between devices, shards(): collected.append(lax.ppermute(sent, 'seg', pairs))  5.23 us
    ppermute x3, starting transfers between devices, halo(): own.append(lax.ppermute(mine, 'fibre', pairs))  3.86 us
    unnamed x31, local copies, waits for them, and re-layouts  1.69 us
    ppermute x1, waiting for transfers between devices, halo(): lax.ppermute(jnp.concatenate(own, axis=0), 'fibre', [(i, i ^ 1) for i in...  1.38 us
  transfers between devices with their start and end apart: 7, of which 6 were waited for; matrix products, arithmetic and copies ran while one was open for 0% of the time, Pallas kernels for 0%

profile of v14, /device:TPU:0, one launch (start us, length us, event | category | flops | bytes accessed | tf_op | source)
XLA Modules:
  0.0 48.3 jit_solution(3882828926304235790)
XLA Ops:
  0.0 5.5 %shard_map.64 = (bf16[16,512]{1,0:T(8,128)(2,1)}, bf16[16,512]{1,0:T(8,128)(2,1)}, bf16[16,512]{1,0:T(8,128)(2,1)}, bf16[16,512]{1,0:T(8,128)(2,1)}) custom-call(s32[16]{0:T(128)} %bitcast.118, s32[1]{0:T(128)} %constant.83.clone.1.place_ref, s32[16]{0:T(128)} %live_ref.1, bf16[16,27648]{1,0:T(8,128)(2,1)} %bitcast.88, ...), custom_call_target="tpu_custom_call" | custom-call | tf_op jit(solution)/shard_map/pallas_call | solution.py:94
  5.5 0.8 %pad_maximum_fusion.2 = bf16[4,16,512]{2,1,0:T(8,128)(2,1)S(1)} fusion(bf16[1,16,512]{2,1,0:T(8,128)(2,1)} %bitcast.117, bf16[1,16,512]{2,1,0:T(8,128)(2,1)} %bitcast.116, bf16[1,16,512]{2,1,0:T(8,128)(2,1)} %bitcast.115, bf16[1,16,512]{2,1,0:T(8,128)(2,1)} %bitcast.114), kind=kLoop, calls=%fused_computation.16 | loop fusion | flops 98304 | bytes 131072 | tf_op jit(solution)/shard_map/stack | solution.py:144
  6.3 9.8 %all_to_all.5 = bf16[4,16,512]{2,1,0:T(8,128)(2,1)S(1)} all-to-all(bf16[4,16,512]{2,1,0:T(8,128)(2,1)S(1)} %pad_maximum_fusion.2), channel_id=1, replica_groups=mesh['seg'=4,'fibre'=8] {'seg'}, dimensions={0} | all-to-all | bytes 131072 | tf_op jit(solution)/shard_map/all_to_all | solution.py:144
  16.1 1.3 %collective-permute-start = (bf16[16,2048]{1,0:T(8,128)(2,1)S(1)}, bf16[16,2048]{1,0:T(8,128)(2,1)S(1)}, u32[]{:S(2)}, u32[]{:S(2)}) collective-permute-start(bf16[16,2048]{1,0:T(8,128)(2,1)S(1)} %bitcast.89), channel_id=1, source_target_pairs={{2,0},{3,1},{4,2},{5,3},{6,4},{7,5},{10,8},{11,9},{12,10},{13,11},... | collective-permute-start | bytes 196616 | tf_op jit(solution)/shard_map/ppermute | solution.py:118
  17.4 1.3 %collective-permute-start.1 = (bf16[16,2048]{1,0:T(8,128)(2,1)S(1)}, bf16[16,2048]{1,0:T(8,128)(2,1)S(1)}, u32[]{:S(2)}, u32[]{:S(2)}) collective-permute-start(bf16[16,2048]{1,0:T(8,128)(2,1)S(1)} %bitcast.90), channel_id=1, source_target_pairs={{4,0},{5,1},{6,2},{7,3},{12,8},{13,9},{14,10},{15,11},{20,16},{21,... | collective-permute-start | bytes 196616 | tf_op jit(solution)/shard_map/ppermute | solution.py:118
  18.7 1.3 %collective-permute-start.2 = (bf16[16,2048]{1,0:T(8,128)(2,1)S(1)}, bf16[16,2048]{1,0:T(8,128)(2,1)S(1)}, u32[]{:S(2)}, u32[]{:S(2)}) collective-permute-start(bf16[16,2048]{1,0:T(8,128)(2,1)S(1)} %bitcast.91), channel_id=1, source_target_pairs={{6,0},{7,1},{14,8},{15,9},{22,16},{23,17},{30,24},{31,25}} | collective-permute-start | bytes 196616 | tf_op jit(solution)/shard_map/ppermute | solution.py:118
  20.0 2.7 %collective-permute-done = bf16[16,2048]{1,0:T(8,128)(2,1)S(1)} collective-permute-done((bf16[16,2048]{1,0:T(8,128)(2,1)S(1)}, bf16[16,2048]{1,0:T(8,128)(2,1)S(1)}, u32[]{:S(2)}, u32[]{:S(2)}) %collective-permute-start) | collective-permute-done | bytes 65568 | tf_op jit(solution)/shard_map/ppermute | solution.py:118
  22.7 2.7 %collective-permute-done.1 = bf16[16,2048]{1,0:T(8,128)(2,1)S(1)} collective-permute-done((bf16[16,2048]{1,0:T(8,128)(2,1)S(1)}, bf16[16,2048]{1,0:T(8,128)(2,1)S(1)}, u32[]{:S(2)}, u32[]{:S(2)}) %collective-permute-start.1) | collective-permute-done | bytes 65568 | tf_op jit(solution)/shard_map/ppermute | solution.py:118
  25.4 2.5 %collective-permute-done.2 = bf16[16,2048]{1,0:T(8,128)(2,1)S(1)} collective-permute-done((bf16[16,2048]{1,0:T(8,128)(2,1)S(1)}, bf16[16,2048]{1,0:T(8,128)(2,1)S(1)}, u32[]{:S(2)}, u32[]{:S(2)}) %collective-permute-start.2) | collective-permute-done | bytes 65568 | tf_op jit(solution)/shard_map/ppermute | solution.py:118
  28.1 1.4 %collective-permute-done.3 = bf16[64,2048]{1,0:T(8,128)(2,1)S(1)} collective-permute-done((bf16[64,2048]{1,0:T(8,128)(2,1)S(1)}, bf16[64,2048]{1,0:T(8,128)(2,1)S(1)}, u32[]{:S(2)}, u32[]{:S(2)}) %collective-permute-start.3) | collective-permute-done | bytes 262176 | tf_op jit(solution)/shard_map/ppermute | solution.py:119
  29.7 0.3 copy.94
  30.0 0.5 %copy-done = bf16[128,2048]{1,0:T(8,128)(2,1)} copy-done((bf16[128,2048]{1,0:T(8,128)(2,1)}, bf16[128,2048]{1,0:T(8,128)(2,1)S(1)}, u32[]{:S(2)}) %copy-start) | copy-done | bytes 524312
  30.5 0.1 concatenate.18.clone
  30.7 0.3 copy.78
  31.0 0.3 copy.77
  31.3 0.6 %slice-done = bf16[16,2048]{1,0:T(8,128)(2,1)S(1)} async-done(((bf16[128,2048]{1,0:T(8,128)(2,1)}), bf16[16,2048]{1,0:T(8,128)(2,1)S(1)}, s32[]{:S(2)}) %slice-start) | async-done | bytes 65560 | tf_op jit(solution)/shard_map/stack | solution.py:155
  31.8 0.4 stack.53
  32.2 0.4 copy.51
  32.7 0.7 %convolution_bitcast_fusion = f32[16,2,16,144]{3,2,1,0:T(8,128)S(1)} fusion(bf16[144,64,2,16,1]{0,3,2,1,4:T(8,128)(2,1)S(1)} %bitcast.83, bf16[1,16,64,2,16]{2,1,3,0,4:T(8,128)(2,1)S(1)} %maximum_bitcast_fusion, bf16[1,16,64,2,16]{2,1,3,0,4:T(8,128)(2,1)S(1)} %copy.51), kind=kOutput, calls=%fused_computation.1 | convolution fusion | flops 18939904 | bytes 1015808 | tf_op jit(solution)/shard_map/ocspn,jspn->nocj/dot_general | solution.py:156
  33.5 0.6 %fusion.9 = (f32[16,2,1,128]{3,2,1,0:T(1,128)S(1)}, f32[16,2,1,128]{3,2,1,0:T(1,128)S(1)}, f32[16,2,1,128]{3,2,1,0:T(1,128)S(1)}, f32[16,2,1,128]{3,2,1,0:T(1,12...) fusion(f32[16,2,16,144]{3,2,1,0:T(8,128)S(1)} %convolution_bitc, ...), kind=kLoop, calls=%fused_computation.64 | loop fusion | bytes 524288 | tf_op jit(solution)/shard_map/slice | solution.py:157
  34.3 0.1 multiply_bitcast_fusion
  34.4 0.1 copy.95
  34.7 2.6 %collective-permute-start.4 = (f32[64,512]{1,0:T(8,128)S(1)}, f32[64,512]{1,0:T(8,128)S(1)}, u32[]{:S(2)}, u32[]{:S(2)}) collective-permute-start(f32[64,512]{1,0:T(8,128)S(1)} %get-tuple-element.18), channel_id=1, source_target_pairs={{0,8},{24,0},{1,9},{25,1},{2,10},{26,2},{3,11},{27,3},{4,12},{28,4... | collective-permute-start | bytes 393224 | tf_op jit(solution)/shard_map/ppermute | solution.py:169
  37.3 1.3 %collective-permute-start.5 = (f32[64,512]{1,0:T(8,128)S(1)}, f32[64,512]{1,0:T(8,128)S(1)}, u32[]{:S(2)}, u32[]{:S(2)}) collective-permute-start(f32[64,512]{1,0:T(8,128)S(1)} %get-tuple-element.17), channel_id=1, source_target_pairs={{16,0},{24,8},{17,1},{25,9},{18,2},{26,10},{19,3},{27,11},{20,4},{... | collective-permute-start | bytes 393224 | tf_op jit(solution)/shard_map/ppermute | solution.py:169
  38.6 1.3 %collective-permute-start.6 = (f32[64,512]{1,0:T(8,128)S(1)}, f32[64,512]{1,0:T(8,128)S(1)}, u32[]{:S(2)}, u32[]{:S(2)}) collective-permute-start(f32[64,512]{1,0:T(8,128)S(1)} %get-tuple-element.16), channel_id=1, source_target_pairs={{8,0},{16,8},{9,1},{17,9},{10,2},{18,10},{11,3},{19,11},{12,4},{20... | collective-permute-start | bytes 393224 | tf_op jit(solution)/shard_map/ppermute | solution.py:169
  40.0 3.1 %collective-permute-done.4 = f32[64,512]{1,0:T(8,128)S(1)} collective-permute-done((f32[64,512]{1,0:T(8,128)S(1)}, f32[64,512]{1,0:T(8,128)S(1)}, u32[]{:S(2)}, u32[]{:S(2)}) %collective-permute-start.4) | collective-permute-done | bytes 131104 | tf_op jit(solution)/shard_map/ppermute | solution.py:169
  43.1 2.7 %collective-permute-done.5 = f32[64,512]{1,0:T(8,128)S(1)} collective-permute-done((f32[64,512]{1,0:T(8,128)S(1)}, f32[64,512]{1,0:T(8,128)S(1)}, u32[]{:S(2)}, u32[]{:S(2)}) %collective-permute-start.5) | collective-permute-done | bytes 131104 | tf_op jit(solution)/shard_map/ppermute | solution.py:169
  45.9 0.6 %gather_fusion = f32[4,64,512]{2,1,0:T(8,128)S(1)} fusion(f32[4,64,512]{2,1,0:T(8,128)S(1)} %pad_maximum_fusion, s32[1024]{0:T(1024)S(1)} %pad_clamp_fusion), kind=kCustom, calls=%fused_computation | custom fusion | bytes 1048592 | tf_op jit(solution)/shard_map/jit(_take)/gather | solution.py:174
  46.5 0.3 copy.70
  46.8 0.2 select_bitcast_fusion
  47.0 0.1 copy.71
  47.2 1.1 %copy.72 = f32[64,16,128]{2,1,0:T(8,128)} copy(f32[64,16,128]{0,2,1:T(8,128)S(1)} %bitcast.85) | data formatting | bytes 1048576 | tf_op jit(solution)/shard_map/reshape | solution.py:175
  (45 shorter events, 0.8 us)
Async XLA Ops:
  16.1 6.6 %collective-permute-start = (bf16[16,2048]{1,0:T(8,128)(2,1)S(1)}, bf16[16,2048]{1,0:T(8,128)(2,1)S(1)}, u32[]{:S(2)}, u32[]{:S(2)}) collective-permute-start(bf16[16,2048]{1,0:T(8,128)(2,1)S(1)} %bitcast.89), channel_id=1, source_target_pairs={{2,0},{3,1},{4,2},{5,3},{6,4},{7,5},{10,8},{11,9},{12,10},{13,11},... | collective-permute-start | bytes 196616 | tf_op jit(solution)/shard_map/ppermute | solution.py:118
  17.4 8.0 %collective-permute-start.1 = (bf16[16,2048]{1,0:T(8,128)(2,1)S(1)}, bf16[16,2048]{1,0:T(8,128)(2,1)S(1)}, u32[]{:S(2)}, u32[]{:S(2)}) collective-permute-start(bf16[16,2048]{1,0:T(8,128)(2,1)S(1)} %bitcast.90), channel_id=1, source_target_pairs={{4,0},{5,1},{6,2},{7,3},{12,8},{13,9},{14,10},{15,11},{20,16},{21,... | collective-permute-start | bytes 196616 | tf_op jit(solution)/shard_map/ppermute | solution.py:118
  18.7 9.1 %collective-permute-start.2 = (bf16[16,2048]{1,0:T(8,128)(2,1)S(1)}, bf16[16,2048]{1,0:T(8,128)(2,1)S(1)}, u32[]{:S(2)}, u32[]{:S(2)}) collective-permute-start(bf16[16,2048]{1,0:T(8,128)(2,1)S(1)} %bitcast.91), channel_id=1, source_target_pairs={{6,0},{7,1},{14,8},{15,9},{22,16},{23,17},{30,24},{31,25}} | collective-permute-start | bytes 196616 | tf_op jit(solution)/shard_map/ppermute | solution.py:118
  27.9 1.6 %collective-permute-start.3 = (bf16[64,2048]{1,0:T(8,128)(2,1)S(1)}, bf16[64,2048]{1,0:T(8,128)(2,1)S(1)}, u32[]{:S(2)}, u32[]{:S(2)}) collective-permute-start(bf16[64,2048]{1,0:T(8,128)(2,1)S(1)} %pad_maximum_fusion.1), channel_id=1, source_target_pairs={{0,1},{1,0},{2,3},{3,2},{4,5},{5,4},{6,7},{7,6},{8,9},{9,8},{10,11... | collective-permute-start | bytes 786440 | tf_op jit(solution)/shard_map/ppermute | solution.py:119
  29.7 0.8 %copy-start = (bf16[128,2048]{1,0:T(8,128)(2,1)}, bf16[128,2048]{1,0:T(8,128)(2,1)S(1)}, u32[]{:S(2)}) copy-start(bf16[128,2048]{1,0:T(8,128)(2,1)S(1)} %broadcast_select_fusion) | copy-start | bytes 1572868
  31.0 0.8 %slice-start = ((bf16[128,2048]{1,0:T(8,128)(2,1)}), bf16[16,2048]{1,0:T(8,128)(2,1)S(1)}, s32[]{:S(2)}) async-start(bf16[128,2048]{1,0:T(8,128)(2,1)} %copy-done), calls=%async_computation.1 | async-start | bytes 131072 | tf_op jit(solution)/shard_map/stack | solution.py:155
  34.7 8.4 %collective-permute-start.4 = (f32[64,512]{1,0:T(8,128)S(1)}, f32[64,512]{1,0:T(8,128)S(1)}, u32[]{:S(2)}, u32[]{:S(2)}) collective-permute-start(f32[64,512]{1,0:T(8,128)S(1)} %get-tuple-element.18), channel_id=1, source_target_pairs={{0,8},{24,0},{1,9},{25,1},{2,10},{26,2},{3,11},{27,3},{4,12},{28,4... | collective-permute-start | bytes 393224 | tf_op jit(solution)/shard_map/ppermute | solution.py:169
  37.3 8.5 %collective-permute-start.5 = (f32[64,512]{1,0:T(8,128)S(1)}, f32[64,512]{1,0:T(8,128)S(1)}, u32[]{:S(2)}, u32[]{:S(2)}) collective-permute-start(f32[64,512]{1,0:T(8,128)S(1)} %get-tuple-element.17), channel_id=1, source_target_pairs={{16,0},{24,8},{17,1},{25,9},{18,2},{26,10},{19,3},{27,11},{20,4},{... | collective-permute-start | bytes 393224 | tf_op jit(solution)/shard_map/ppermute | solution.py:169
  38.6 7.2 %collective-permute-start.6 = (f32[64,512]{1,0:T(8,128)S(1)}, f32[64,512]{1,0:T(8,128)S(1)}, u32[]{:S(2)}, u32[]{:S(2)}) collective-permute-start(f32[64,512]{1,0:T(8,128)S(1)} %get-tuple-element.16), channel_id=1, source_target_pairs={{8,0},{16,8},{9,1},{17,9},{10,2},{18,10},{11,3},{19,11},{12,4},{20... | collective-permute-start | bytes 393224 | tf_op jit(solution)/shard_map/ppermute | solution.py:169

commit v15 on v10

--- a/solution.py
+++ b/solution.py
@@ -153,8 +153,9 @@
             [columns, jnp.zeros((span - columns.shape[0], columns.shape[1]), columns.dtype)], axis=0
         )
     right = columns.reshape(span, rows, 2, bins_each)
-    re_own = right[:block, :, 0]
-    im_own = right[:block, :, 1]
+    own = mine.reshape(block, rows, 2, bins_each)
+    re_own = own[:, :, 0]
+    im_own = own[:, :, 1]
     left = jnp.stack([jnp.stack([re_own, im_own], axis=2), jnp.stack([im_own, -re_own], axis=2)])
     cross = jnp.einsum("ocspn,jspn->nocj", left, right, preferred_element_type=jnp.float32)
     band = jnp.stack([cross[:, :, c, c + 1 : c + 1 + kept] for c in range(block)])

time: 46.8 us -> 49.5 us (1.058)
  local copies, waits for them, and re-layouts: 6.94 us -> 10.8 us
  waiting for transfers between devices: 16.8 us -> 14.9 us
  other arithmetic: 0.55 us -> 1.26 us
    unnamed x33 -> x31, local copies, waits for them, and re-layouts: 2.41 us -> 4.6 us
    ppermute x1, waiting for transfers between devices: 1.4 us -> 0.01 us  [halo(): lax.ppermute(jnp.concatenate(own, axis=0), 'fibre', [(i, i ^ 1) for i in...]
    slice x1, local copies, waits for them, and re-layouts: 0.09 us -> 1.12 us  [shards(): im_own = own[:, :, 1]]
    ppermute x3, waiting for transfers between devices: 7.84 us -> 6.97 us  [halo(): own.append(lax.ppermute(mine, 'fibre', pairs))]
    concatenate x1, local copies, waits for them, and re-layouts: 0.01 us -> 0.85 us  [halo(): jnp.concatenate(even, axis=0)]
    concatenate x1, other arithmetic: 0.02 us -> 0.72 us  [halo(): jnp.concatenate(own, axis=0)]
    another operation x2 -> x0, local copies, waits for them, and re-layouts: 0.57 us -> none  [shards(): jnp.stack([re_own, im_own], axis=2)]
  transfers between devices with their start and end apart: 10 -> 10, of which waited for: 9 -> 8; matrix products, arithmetic and copies ran while one was open for 2% -> 8% of each run, Pallas kernels for 0% -> 0%
where the time goes in v15:
time: 49.5 us; the launch traced here: 48.9 us
  starting transfers between devices  15.3 us (31%)
  waiting for transfers between devices  14.9 us (30%)
  local copies, waits for them, and re-layouts  10.8 us (22%)
  Pallas kernels  5.53 us (11%)
  other arithmetic  1.26 us (3%)
  matrix products  0.73 us (1%)
    ppermute x3, waiting for transfers between devices, halo(): own.append(lax.ppermute(mine, 'fibre', pairs))  6.97 us
    ppermute x3, waiting for transfers between devices, shards(): collected.append(lax.ppermute(sent, 'seg', pairs))  6.19 us
    ppermute x3, starting transfers between devices, shards(): gathered.append(lax.ppermute(split[step], 'seg', pairs))  5.94 us
    pallas_call x1, Pallas kernels, whiten(): pl.pallas_call(whiten_kernel, out_shape=[jax.ShapeDtypeStruct((channels,...  5.53 us
    ppermute x3, starting transfers between devices, shards(): collected.append(lax.ppermute(sent, 'seg', pairs))  5.47 us
    unnamed x31, local copies, waits for them, and re-layouts  4.6 us
    ppermute x3, starting transfers between devices, halo(): own.append(lax.ppermute(mine, 'fibre', pairs))  3.86 us
    ppermute x3, waiting for transfers between devices, shards(): gathered.append(lax.ppermute(split[step], 'seg', pairs))  1.79 us
  transfers between devices with their start and end apart: 10, of which 8 were waited for; matrix products, arithmetic and copies ran while one was open for 8% of the time, Pallas kernels for 0%

profile of v15, /device:TPU:0, one launch (start us, length us, event | category | flops | bytes accessed | tf_op | source)
XLA Modules:
  0.0 48.9 jit_solution(18211641114312152741)
XLA Ops:
  0.0 5.5 %shard_map.64 = (bf16[16,512]{1,0:T(8,128)(2,1)}, bf16[16,512]{1,0:T(8,128)(2,1)}, bf16[16,512]{1,0:T(8,128)(2,1)}, bf16[16,512]{1,0:T(8,128)(2,1)}) custom-call(s32[16]{0:T(128)} %bitcast.101, s32[1]{0:T(128)} %bitcast.1.place_ref, s32[16]{0:T(128)} %live_ref.1, bf16[16,27648]{1,0:T(8,128)(2,1)} %bitcast.81, bf16[3072,128]{1,0:T(8,128)(2,1)} %constant.86.clone.table_ref, ...), custom_call_target="tpu_custom_call" | custom-call | tf_op jit(solution)/shard_map/pallas_call | solution.py:94
  5.5 3.0 %collective-permute-start = (bf16[16,512]{1,0:T(8,128)(2,1)}, bf16[16,512]{1,0:T(8,128)(2,1)S(1)}, u32[]{:S(2)}, u32[]{:S(2)}) collective-permute-start(bf16[16,512]{1,0:T(8,128)(2,1)} %get-tuple-element.10), channel_id=1, source_target_pairs={{0,8},{8,16},{16,24},{24,0},{1,9},{9,17},{17,25},{25,1},{2,10},{10... | collective-permute-start | bytes 49160 | tf_op jit(solution)/shard_map/ppermute | solution.py:147
  8.5 1.5 %collective-permute-start.1 = (bf16[16,512]{1,0:T(8,128)(2,1)}, bf16[16,512]{1,0:T(8,128)(2,1)S(1)}, u32[]{:S(2)}, u32[]{:S(2)}) collective-permute-start(bf16[16,512]{1,0:T(8,128)(2,1)} %get-tuple-element.11), channel_id=1, source_target_pairs={{0,16},{8,24},{16,0},{24,8},{1,17},{9,25},{17,1},{25,9},{2,18},{10... | collective-permute-start | bytes 49160 | tf_op jit(solution)/shard_map/ppermute | solution.py:147
  10.1 1.4 %collective-permute-start.2 = (bf16[16,512]{1,0:T(8,128)(2,1)}, bf16[16,512]{1,0:T(8,128)(2,1)S(1)}, u32[]{:S(2)}, u32[]{:S(2)}) collective-permute-start(bf16[16,512]{1,0:T(8,128)(2,1)} %get-tuple-element.12), channel_id=1, source_target_pairs={{0,24},{8,0},{16,8},{24,16},{1,25},{9,1},{17,9},{25,17},{2,26},{10... | collective-permute-start | bytes 49160 | tf_op jit(solution)/shard_map/ppermute | solution.py:147
  11.5 0.7 %constant_dynamic-update-slice_fusion.3 = (bf16[16,2048]{1,0:T(8,128)(2,1)S(1)}, bf16[128,2048]{1,0:T(8,128)(2,1)S(1)}) fusion(bf16[16,512]{1,0:T(8,128)(2,1)} %get-tuple-element.9), kind=kLoop, calls=%fused_computation.18 | loop fusion | bytes 49152
  12.5 1.5 %collective-permute-done.2 = bf16[16,512]{1,0:T(8,128)(2,1)S(1)} collective-permute-done((bf16[16,512]{1,0:T(8,128)(2,1)}, bf16[16,512]{1,0:T(8,128)(2,1)S(1)}, u32[]{:S(2)}, u32[]{:S(2)}) %collective-permute-start.2) | collective-permute-done | bytes 16416 | tf_op jit(solution)/shard_map/ppermute | solution.py:147
  14.0 1.3 %collective-permute-start.3 = (bf16[16,2048]{1,0:T(8,128)(2,1)S(1)}, bf16[16,2048]{1,0:T(8,128)(2,1)S(1)}, u32[]{:S(2)}, u32[]{:S(2)}) collective-permute-start(bf16[16,2048]{1,0:T(8,128)(2,1)S(1)} %get-tuple-element.41), channel_id=1, source_target_pairs={{2,0},{3,1},{4,2},{5,3},{6,4},{7,5},{10,8},{11,9},{12,10},{13,11},... | collective-permute-start | bytes 196616 | tf_op jit(solution)/shard_map/ppermute | solution.py:118
  15.3 1.3 %collective-permute-start.4 = (bf16[16,2048]{1,0:T(8,128)(2,1)S(1)}, bf16[16,2048]{1,0:T(8,128)(2,1)S(1)}, u32[]{:S(2)}, u32[]{:S(2)}) collective-permute-start(bf16[16,2048]{1,0:T(8,128)(2,1)S(1)} %get-tuple-element.41), channel_id=1, source_target_pairs={{4,0},{5,1},{6,2},{7,3},{12,8},{13,9},{14,10},{15,11},{20,16},{21,... | collective-permute-start | bytes 196616 | tf_op jit(solution)/shard_map/ppermute | solution.py:118
  16.6 1.3 %collective-permute-start.5 = (bf16[16,2048]{1,0:T(8,128)(2,1)S(1)}, bf16[16,2048]{1,0:T(8,128)(2,1)S(1)}, u32[]{:S(2)}, u32[]{:S(2)}) collective-permute-start(bf16[16,2048]{1,0:T(8,128)(2,1)S(1)} %get-tuple-element.41), channel_id=1, source_target_pairs={{6,0},{7,1},{14,8},{15,9},{22,16},{23,17},{30,24},{31,25}} | collective-permute-start | bytes 196616 | tf_op jit(solution)/shard_map/ppermute | solution.py:118
  17.9 0.4 reshape.76
  18.3 0.4 stack.30
  18.8 1.9 %collective-permute-done.3 = bf16[16,2048]{1,0:T(8,128)(2,1)S(1)} collective-permute-done((bf16[16,2048]{1,0:T(8,128)(2,1)S(1)}, bf16[16,2048]{1,0:T(8,128)(2,1)S(1)}, u32[]{:S(2)}, u32[]{:S(2)}) %collective-permute-start.3) | collective-permute-done | bytes 65568 | tf_op jit(solution)/shard_map/ppermute | solution.py:118
  20.6 2.7 %collective-permute-done.4 = bf16[16,2048]{1,0:T(8,128)(2,1)S(1)} collective-permute-done((bf16[16,2048]{1,0:T(8,128)(2,1)S(1)}, bf16[16,2048]{1,0:T(8,128)(2,1)S(1)}, u32[]{:S(2)}, u32[]{:S(2)}) %collective-permute-start.4) | collective-permute-done | bytes 65568 | tf_op jit(solution)/shard_map/ppermute | solution.py:118
  23.3 2.5 %collective-permute-done.5 = bf16[16,2048]{1,0:T(8,128)(2,1)S(1)} collective-permute-done((bf16[16,2048]{1,0:T(8,128)(2,1)S(1)}, bf16[16,2048]{1,0:T(8,128)(2,1)S(1)}, u32[]{:S(2)}, u32[]{:S(2)}) %collective-permute-start.5) | collective-permute-done | bytes 65568 | tf_op jit(solution)/shard_map/ppermute | solution.py:118
  25.7 0.7 %pad_maximum_fusion.1 = bf16[64,2048]{1,0:T(8,128)(2,1)} fusion(bf16[16,2048]{1,0:T(8,128)(2,1)S(1)} %collective-permute-done.5, bf16[16,2048]{1,0:T(8,128)(2,1)S(1)} %collective-permute-done.4, bf16[16,2048]{1,0:T(8,128)(2,1)S(1)} %collective-permute-done.3, bf16[16,2048]{1,0:T(8,128)(2,1)S(1)} %get-tuple-element.41), kind=kLoop, calls=%fused_computation.9 | loop fusion | flops 1048576 | bytes 524288 | tf_op jit(solution)/shard_map/concatenate | solution.py:119
  26.5 1.1 %fusion.9 = (bf16[16,64,1,16]{3,2,1,0:T(2,128)(2,1)S(1)}, bf16[16,64,1,16]{3,2,1,0:T(2,128)(2,1)S(1)}) fusion(bf16[16,64,2,16]{3,2,1,0:T(2,128)(2,1)S(1)} %reshape.76), kind=kLoop, calls=%fused_computation.73 | loop fusion | bytes 131072 | tf_op jit(solution)/shard_map/slice | solution.py:158
  27.6 0.4 copy.79
  28.0 0.4 copy.78
  28.3 0.4 copy.51
  28.8 0.8 %constant_dynamic-update-slice_fusion.21 = bf16[128,2048]{1,0:T(8,128)(2,1)S(1)} fusion(bf16[128,2048]{1,0:T(8,128)(2,1)S(1)} %get-tuple-element.42, bf16[64,2048]{1,0:T(8,128)(2,1)} %collective-permute-done.6), kind=kLoop, calls=%fused_computation.36 | loop fusion | bytes 131072
  29.7 0.9 %constant_dynamic-update-slice_fusion.19 = (bf16[128,2048]{1,0:T(8,128)(2,1)S(1)}, bf16[128,2048]{1,0:T(8,128)(2,1)S(1)}) fusion(bf16[128,2048]{1,0:T(8,128)(2,1)S(1)} %constant_dynamic-update-slice_fusion.20, bf16[64,2048]{1,0:T(8,128)(2,1)} %collective-permute-done.6, bf16[128,2048]{1,0:T(8,128)(2,1)S(1)} %copy.108), kind=kLoop, calls=%fused_computation.34 | loop fusion | bytes 196608
  30.6 0.9 %constant_dynamic-update-slice_fusion.17 = (bf16[128,2048]{1,0:T(8,128)(2,1)S(1)}, bf16[128,2048]{1,0:T(8,128)(2,1)S(1)}) fusion(bf16[128,2048]{1,0:T(8,128)(2,1)S(1)} %get-tuple-element.50, bf16[64,2048]{1,0:T(8,128)(2,1)} %collective-permute-done.6, bf16[128,2048]{1,0:T(8,128)(2,1)S(1)} %get-tuple-element.49), kind=kLoop, calls=%fused_computation.32 | loop fusion | bytes 196608
  31.5 0.9 %constant_dynamic-update-slice_fusion.15 = (bf16[128,2048]{1,0:T(8,128)(2,1)S(1)}, bf16[128,2048]{1,0:T(8,128)(2,1)S(1)}) fusion(bf16[128,2048]{1,0:T(8,128)(2,1)S(1)} %constant_dynamic-update-slice_fusion.16, bf16[64,2048]{1,0:T(8,128)(2,1)} %collective-permute-done.6, bf16[128,2048]{1,0:T(8,128)(2,1)S(1)} %constant_dynamic-update-slice_fusion.7), kind=kLoop, calls=%fused_computation.30 | loop fusion | bytes 196608 | tf_op jit(solution)/shard_map/concatenate | solution.py:124
  32.8 0.7 %convolution_bitcast_fusion = f32[16,2,16,144]{3,2,1,0:T(8,128)S(1)} fusion(bf16[144,64,2,16,1]{0,3,2,1,4:T(8,128)(2,1)S(1)} %bitcast.77, bf16[1,16,64,2,16]{2,1,3,0,4:T(8,128)(2,1)S(1)} %maximum_bitcast_fusion, bf16[1,16,64,2,16]{2,1,3,0,4:T(8,128)(2,1)S(1)} %copy.51), kind=kOutput, calls=%fused_computation.1 | convolution fusion | flops 18939904 | bytes 1015808 | tf_op jit(solution)/shard_map/ocspn,jspn->nocj/dot_general | solution.py:160
  33.5 0.6 %fusion.8 = (f32[16,2,1,128]{3,2,1,0:T(1,128)S(1)}, f32[16,2,1,128]{3,2,1,0:T(1,128)S(1)}, f32[16,2,1,128]{3,2,1,0:T(1,128)S(1)}, f32[16,2,1,128]{3,2,1,0:T(1,12...) fusion(f32[16,2,16,144]{3,2,1,0:T(8,128)S(1)} %convolution_bitc, ...), kind=kLoop, calls=%fused_computation.72 | loop fusion | bytes 524288 | tf_op jit(solution)/shard_map/slice | solution.py:161
  34.7 2.9 %collective-permute-start.7 = (f32[64,512]{1,0:T(8,128)S(1)}, f32[64,512]{1,0:T(8,128)S(1)}, u32[]{:S(2)}, u32[]{:S(2)}) collective-permute-start(f32[64,512]{1,0:T(8,128)S(1)} %get-tuple-element.16), channel_id=1, source_target_pairs={{0,8},{24,0},{1,9},{25,1},{2,10},{26,2},{3,11},{27,3},{4,12},{28,4... | collective-permute-start | bytes 393224 | tf_op jit(solution)/shard_map/ppermute | solution.py:173
  37.6 1.3 %collective-permute-start.8 = (f32[64,512]{1,0:T(8,128)S(1)}, f32[64,512]{1,0:T(8,128)S(1)}, u32[]{:S(2)}, u32[]{:S(2)}) collective-permute-start(f32[64,512]{1,0:T(8,128)S(1)} %get-tuple-element.15), channel_id=1, source_target_pairs={{16,0},{24,8},{17,1},{25,9},{18,2},{26,10},{19,3},{27,11},{20,4},{... | collective-permute-start | bytes 393224 | tf_op jit(solution)/shard_map/ppermute | solution.py:173
  38.9 1.3 %collective-permute-start.9 = (f32[64,512]{1,0:T(8,128)S(1)}, f32[64,512]{1,0:T(8,128)S(1)}, u32[]{:S(2)}, u32[]{:S(2)}) collective-permute-start(f32[64,512]{1,0:T(8,128)S(1)} %get-tuple-element.14), channel_id=1, source_target_pairs={{8,0},{16,8},{9,1},{17,9},{10,2},{18,10},{11,3},{19,11},{12,4},{20... | collective-permute-start | bytes 393224 | tf_op jit(solution)/shard_map/ppermute | solution.py:173
  40.3 3.3 %collective-permute-done.7 = f32[64,512]{1,0:T(8,128)S(1)} collective-permute-done((f32[64,512]{1,0:T(8,128)S(1)}, f32[64,512]{1,0:T(8,128)S(1)}, u32[]{:S(2)}, u32[]{:S(2)}) %collective-permute-start.7) | collective-permute-done | bytes 131104 | tf_op jit(solution)/shard_map/ppermute | solution.py:173
  43.6 2.7 %collective-permute-done.8 = f32[64,512]{1,0:T(8,128)S(1)} collective-permute-done((f32[64,512]{1,0:T(8,128)S(1)}, f32[64,512]{1,0:T(8,128)S(1)}, u32[]{:S(2)}, u32[]{:S(2)}) %collective-permute-start.8) | collective-permute-done | bytes 131104 | tf_op jit(solution)/shard_map/ppermute | solution.py:173
  46.5 0.6 %gather_fusion = f32[4,64,512]{2,1,0:T(8,128)S(1)} fusion(f32[4,64,512]{2,1,0:T(8,128)S(1)} %pad_maximum_fusion, s32[1024]{0:T(1024)S(1)} %pad_clamp_fusion), kind=kCustom, calls=%fused_computation | custom fusion | bytes 1048592 | tf_op jit(solution)/shard_map/jit(_take)/gather | solution.py:178
  47.8 1.1 %copy.73 = f32[64,16,128]{2,1,0:T(8,128)} copy(f32[64,16,128]{0,2,1:T(8,128)S(1)} %bitcast.78) | data formatting | bytes 1048576 | tf_op jit(solution)/shard_map/reshape | solution.py:179
  (48 shorter events, 2.3 us)
Async XLA Ops:
  5.5 6.7 %collective-permute-start = (bf16[16,512]{1,0:T(8,128)(2,1)}, bf16[16,512]{1,0:T(8,128)(2,1)S(1)}, u32[]{:S(2)}, u32[]{:S(2)}) collective-permute-start(bf16[16,512]{1,0:T(8,128)(2,1)} %get-tuple-element.10), channel_id=1, source_target_pairs={{0,8},{8,16},{16,24},{24,0},{1,9},{9,17},{17,25},{25,1},{2,10},{10... | collective-permute-start | bytes 49160 | tf_op jit(solution)/shard_map/ppermute | solution.py:147
  8.5 3.9 %collective-permute-start.1 = (bf16[16,512]{1,0:T(8,128)(2,1)}, bf16[16,512]{1,0:T(8,128)(2,1)S(1)}, u32[]{:S(2)}, u32[]{:S(2)}) collective-permute-start(bf16[16,512]{1,0:T(8,128)(2,1)} %get-tuple-element.11), channel_id=1, source_target_pairs={{0,16},{8,24},{16,0},{24,8},{1,17},{9,25},{17,1},{25,9},{2,18},{10... | collective-permute-start | bytes 49160 | tf_op jit(solution)/shard_map/ppermute | solution.py:147
  10.1 3.9 %collective-permute-start.2 = (bf16[16,512]{1,0:T(8,128)(2,1)}, bf16[16,512]{1,0:T(8,128)(2,1)S(1)}, u32[]{:S(2)}, u32[]{:S(2)}) collective-permute-start(bf16[16,512]{1,0:T(8,128)(2,1)} %get-tuple-element.12), channel_id=1, source_target_pairs={{0,24},{8,0},{16,8},{24,16},{1,25},{9,1},{17,9},{25,17},{2,26},{10... | collective-permute-start | bytes 49160 | tf_op jit(solution)/shard_map/ppermute | solution.py:147
  14.0 6.6 %collective-permute-start.3 = (bf16[16,2048]{1,0:T(8,128)(2,1)S(1)}, bf16[16,2048]{1,0:T(8,128)(2,1)S(1)}, u32[]{:S(2)}, u32[]{:S(2)}) collective-permute-start(bf16[16,2048]{1,0:T(8,128)(2,1)S(1)} %get-tuple-element.41), channel_id=1, source_target_pairs={{2,0},{3,1},{4,2},{5,3},{6,4},{7,5},{10,8},{11,9},{12,10},{13,11},... | collective-permute-start | bytes 196616 | tf_op jit(solution)/shard_map/ppermute | solution.py:118
  15.3 8.0 %collective-permute-start.4 = (bf16[16,2048]{1,0:T(8,128)(2,1)S(1)}, bf16[16,2048]{1,0:T(8,128)(2,1)S(1)}, u32[]{:S(2)}, u32[]{:S(2)}) collective-permute-start(bf16[16,2048]{1,0:T(8,128)(2,1)S(1)} %get-tuple-element.41), channel_id=1, source_target_pairs={{4,0},{5,1},{6,2},{7,3},{12,8},{13,9},{14,10},{15,11},{20,16},{21,... | collective-permute-start | bytes 196616 | tf_op jit(solution)/shard_map/ppermute | solution.py:118
  16.6 9.1 %collective-permute-start.5 = (bf16[16,2048]{1,0:T(8,128)(2,1)S(1)}, bf16[16,2048]{1,0:T(8,128)(2,1)S(1)}, u32[]{:S(2)}, u32[]{:S(2)}) collective-permute-start(bf16[16,2048]{1,0:T(8,128)(2,1)S(1)} %get-tuple-element.41), channel_id=1, source_target_pairs={{6,0},{7,1},{14,8},{15,9},{22,16},{23,17},{30,24},{31,25}} | collective-permute-start | bytes 196616 | tf_op jit(solution)/shard_map/ppermute | solution.py:118
  26.5 2.4 %collective-permute-start.6 = (bf16[64,2048]{1,0:T(8,128)(2,1)}, bf16[64,2048]{1,0:T(8,128)(2,1)}, u32[]{:S(2)}, u32[]{:S(2)}) collective-permute-start(bf16[64,2048]{1,0:T(8,128)(2,1)} %pad_maximum_fusion.1), channel_id=1, source_target_pairs={{0,1},{1,0},{2,3},{3,2},{4,5},{5,4},{6,7},{7,6},{8,9},{9,8},{10,11... | collective-permute-start | bytes 786440 | tf_op jit(solution)/shard_map/ppermute | solution.py:119
  34.7 8.8 %collective-permute-start.7 = (f32[64,512]{1,0:T(8,128)S(1)}, f32[64,512]{1,0:T(8,128)S(1)}, u32[]{:S(2)}, u32[]{:S(2)}) collective-permute-start(f32[64,512]{1,0:T(8,128)S(1)} %get-tuple-element.16), channel_id=1, source_target_pairs={{0,8},{24,0},{1,9},{25,1},{2,10},{26,2},{3,11},{27,3},{4,12},{28,4... | collective-permute-start | bytes 393224 | tf_op jit(solution)/shard_map/ppermute | solution.py:173
  37.6 8.6 %collective-permute-start.8 = (f32[64,512]{1,0:T(8,128)S(1)}, f32[64,512]{1,0:T(8,128)S(1)}, u32[]{:S(2)}, u32[]{:S(2)}) collective-permute-start(f32[64,512]{1,0:T(8,128)S(1)} %get-tuple-element.15), channel_id=1, source_target_pairs={{16,0},{24,8},{17,1},{25,9},{18,2},{26,10},{19,3},{27,11},{20,4},{... | collective-permute-start | bytes 393224 | tf_op jit(solution)/shard_map/ppermute | solution.py:173
  38.9 7.5 %collective-permute-start.9 = (f32[64,512]{1,0:T(8,128)S(1)}, f32[64,512]{1,0:T(8,128)S(1)}, u32[]{:S(2)}, u32[]{:S(2)}) collective-permute-start(f32[64,512]{1,0:T(8,128)S(1)} %get-tuple-element.14), channel_id=1, source_target_pairs={{8,0},{16,8},{9,1},{17,9},{10,2},{18,10},{11,3},{19,11},{12,4},{20... | collective-permute-start | bytes 393224 | tf_op jit(solution)/shard_map/ppermute | solution.py:173

commit v16 on v10

--- a/solution.py
+++ b/solution.py
@@ -153,9 +153,10 @@
             [columns, jnp.zeros((span - columns.shape[0], columns.shape[1]), columns.dtype)], axis=0
         )
     right = columns.reshape(span, rows, 2, bins_each)
-    re_own = right[:block, :, 0]
-    im_own = right[:block, :, 1]
-    left = jnp.stack([jnp.stack([re_own, im_own], axis=2), jnp.stack([im_own, -re_own], axis=2)])
+    own = right[:block]
+    sign = jnp.asarray([1.0, -1.0], own.dtype)[None, None, :, None]
+    turned = jnp.flip(own, axis=2) * sign
+    left = jnp.stack([own, turned])
     cross = jnp.einsum("ocspn,jspn->nocj", left, right, preferred_element_type=jnp.float32)
     band = jnp.stack([cross[:, :, c, c + 1 : c + 1 + kept] for c in range(block)])
     band = band.transpose(3, 0, 2, 1) * (1.0 / math.sqrt(seg_count * windows_count))

time: 46.8 us -> 46.4 us (level)
    slice x1 -> x3, local copies, waits for them, and re-layouts: 0.09 us -> 0.84 us  [shards(): own = right[:block]]
    another operation x4 -> x2, local copies, waits for them, and re-layouts: 1.4 us -> 0.83 us  [shards(): left = jnp.stack([own, turned])]
    unnamed x33 -> x31, local copies, waits for them, and re-layouts: 2.41 us -> 1.9 us
where the time goes in v16:
time: 46.4 us; the launch traced here: 46.1 us
  waiting for transfers between devices  16.8 us (36%)
  starting transfers between devices  15.3 us (33%)
  local copies, waits for them, and re-layouts  6.62 us (14%)
  Pallas kernels  5.53 us (12%)
  matrix products  0.73 us (2%)
  other arithmetic  0.6 us (1%)
    ppermute x3, waiting for transfers between devices, halo(): own.append(lax.ppermute(mine, 'fibre', pairs))  7.84 us
    ppermute x3, starting transfers between devices, shards(): gathered.append(lax.ppermute(split[step], 'seg', pairs))  5.94 us
    ppermute x3, waiting for transfers between devices, shards(): collected.append(lax.ppermute(sent, 'seg', pairs))  5.82 us
    pallas_call x1, Pallas kernels, whiten(): pl.pallas_call(whiten_kernel, out_shape=[jax.ShapeDtypeStruct((channels,...  5.53 us
    ppermute x3, starting transfers between devices, shards(): collected.append(lax.ppermute(sent, 'seg', pairs))  5.47 us
    ppermute x3, starting transfers between devices, halo(): own.append(lax.ppermute(mine, 'fibre', pairs))  3.86 us
    unnamed x31, local copies, waits for them, and re-layouts  1.9 us
    ppermute x3, waiting for transfers between devices, shards(): gathered.append(lax.ppermute(split[step], 'seg', pairs))  1.79 us
  transfers between devices with their start and end apart: 10, of which 9 were waited for; matrix products, arithmetic and copies ran while one was open for 2% of the time, Pallas kernels for 0%

profile of v16, /device:TPU:0, one launch (start us, length us, event | category | flops | bytes accessed | tf_op | source)
XLA Modules:
  0.0 46.1 jit_solution(5913549787635282914)
XLA Ops:
  0.0 5.5 %shard_map.73 = (bf16[16,512]{1,0:T(8,128)(2,1)}, bf16[16,512]{1,0:T(8,128)(2,1)}, bf16[16,512]{1,0:T(8,128)(2,1)}, bf16[16,512]{1,0:T(8,128)(2,1)}) custom-call(s32[16]{0:T(128)} %bitcast.101, s32[1]{0:T(128)} %bitcast.1.place_ref, s32[16]{0:T(128)} %live_ref.1, bf16[16,27648]{1,0:T(8,128)(2,1)} %bitcast.81, bf16[3072,128]{1,0:T(8,128)(2,1)} %constant.88.clone.table_ref, ...), custom_call_target="tpu_custom_call" | custom-call | tf_op jit(solution)/shard_map/pallas_call | solution.py:94
  5.5 3.0 %collective-permute-start = (bf16[16,512]{1,0:T(8,128)(2,1)}, bf16[16,512]{1,0:T(8,128)(2,1)S(1)}, u32[]{:S(2)}, u32[]{:S(2)}) collective-permute-start(bf16[16,512]{1,0:T(8,128)(2,1)} %get-tuple-element.10), channel_id=1, source_target_pairs={{0,8},{8,16},{16,24},{24,0},{1,9},{9,17},{17,25},{25,1},{2,10},{10... | collective-permute-start | bytes 49160 | tf_op jit(solution)/shard_map/ppermute | solution.py:147
  8.5 1.5 %collective-permute-start.1 = (bf16[16,512]{1,0:T(8,128)(2,1)}, bf16[16,512]{1,0:T(8,128)(2,1)S(1)}, u32[]{:S(2)}, u32[]{:S(2)}) collective-permute-start(bf16[16,512]{1,0:T(8,128)(2,1)} %get-tuple-element.11), channel_id=1, source_target_pairs={{0,16},{8,24},{16,0},{24,8},{1,17},{9,25},{17,1},{25,9},{2,18},{10... | collective-permute-start | bytes 49160 | tf_op jit(solution)/shard_map/ppermute | solution.py:147
  10.1 1.4 %collective-permute-start.2 = (bf16[16,512]{1,0:T(8,128)(2,1)}, bf16[16,512]{1,0:T(8,128)(2,1)S(1)}, u32[]{:S(2)}, u32[]{:S(2)}) collective-permute-start(bf16[16,512]{1,0:T(8,128)(2,1)} %get-tuple-element.12), channel_id=1, source_target_pairs={{0,24},{8,0},{16,8},{24,16},{1,25},{9,1},{17,9},{25,17},{2,26},{10... | collective-permute-start | bytes 49160 | tf_op jit(solution)/shard_map/ppermute | solution.py:147
  11.5 0.7 %constant_dynamic-update-slice_fusion.3 = (bf16[16,2048]{1,0:T(8,128)(2,1)S(1)}, bf16[128,2048]{1,0:T(8,128)(2,1)S(1)}) fusion(bf16[16,512]{1,0:T(8,128)(2,1)} %get-tuple-element.9), kind=kLoop, calls=%fused_computation.18 | loop fusion | bytes 49152
  12.2 0.3 collective-permute-done.1
  12.5 1.5 %collective-permute-done.2 = bf16[16,512]{1,0:T(8,128)(2,1)S(1)} collective-permute-done((bf16[16,512]{1,0:T(8,128)(2,1)}, bf16[16,512]{1,0:T(8,128)(2,1)S(1)}, u32[]{:S(2)}, u32[]{:S(2)}) %collective-permute-start.2) | collective-permute-done | bytes 16416 | tf_op jit(solution)/shard_map/ppermute | solution.py:147
  14.0 1.3 %collective-permute-start.3 = (bf16[16,2048]{1,0:T(8,128)(2,1)S(1)}, bf16[16,2048]{1,0:T(8,128)(2,1)S(1)}, u32[]{:S(2)}, u32[]{:S(2)}) collective-permute-start(bf16[16,2048]{1,0:T(8,128)(2,1)S(1)} %get-tuple-element.39), channel_id=1, source_target_pairs={{2,0},{3,1},{4,2},{5,3},{6,4},{7,5},{10,8},{11,9},{12,10},{13,11},... | collective-permute-start | bytes 196616 | tf_op jit(solution)/shard_map/ppermute | solution.py:118
  15.3 1.3 %collective-permute-start.4 = (bf16[16,2048]{1,0:T(8,128)(2,1)S(1)}, bf16[16,2048]{1,0:T(8,128)(2,1)S(1)}, u32[]{:S(2)}, u32[]{:S(2)}) collective-permute-start(bf16[16,2048]{1,0:T(8,128)(2,1)S(1)} %get-tuple-element.39), channel_id=1, source_target_pairs={{4,0},{5,1},{6,2},{7,3},{12,8},{13,9},{14,10},{15,11},{20,16},{21,... | collective-permute-start | bytes 196616 | tf_op jit(solution)/shard_map/ppermute | solution.py:118
  16.6 1.3 %collective-permute-start.5 = (bf16[16,2048]{1,0:T(8,128)(2,1)S(1)}, bf16[16,2048]{1,0:T(8,128)(2,1)S(1)}, u32[]{:S(2)}, u32[]{:S(2)}) collective-permute-start(bf16[16,2048]{1,0:T(8,128)(2,1)S(1)} %get-tuple-element.39), channel_id=1, source_target_pairs={{6,0},{7,1},{14,8},{15,9},{22,16},{23,17},{30,24},{31,25}} | collective-permute-start | bytes 196616 | tf_op jit(solution)/shard_map/ppermute | solution.py:118
  17.9 2.7 %collective-permute-done.3 = bf16[16,2048]{1,0:T(8,128)(2,1)S(1)} collective-permute-done((bf16[16,2048]{1,0:T(8,128)(2,1)S(1)}, bf16[16,2048]{1,0:T(8,128)(2,1)S(1)}, u32[]{:S(2)}, u32[]{:S(2)}) %collective-permute-start.3) | collective-permute-done | bytes 65568 | tf_op jit(solution)/shard_map/ppermute | solution.py:118
  20.6 2.7 %collective-permute-done.4 = bf16[16,2048]{1,0:T(8,128)(2,1)S(1)} collective-permute-done((bf16[16,2048]{1,0:T(8,128)(2,1)S(1)}, bf16[16,2048]{1,0:T(8,128)(2,1)S(1)}, u32[]{:S(2)}, u32[]{:S(2)}) %collective-permute-start.4) | collective-permute-done | bytes 65568 | tf_op jit(solution)/shard_map/ppermute | solution.py:118
  23.3 2.5 %collective-permute-done.5 = bf16[16,2048]{1,0:T(8,128)(2,1)S(1)} collective-permute-done((bf16[16,2048]{1,0:T(8,128)(2,1)S(1)}, bf16[16,2048]{1,0:T(8,128)(2,1)S(1)}, u32[]{:S(2)}, u32[]{:S(2)}) %collective-permute-start.5) | collective-permute-done | bytes 65568 | tf_op jit(solution)/shard_map/ppermute | solution.py:118
  26.0 1.4 %collective-permute-done.6 = bf16[64,2048]{1,0:T(8,128)(2,1)S(1)} collective-permute-done((bf16[64,2048]{1,0:T(8,128)(2,1)S(1)}, bf16[64,2048]{1,0:T(8,128)(2,1)S(1)}, u32[]{:S(2)}, u32[]{:S(2)}) %collective-permute-start.6) | collective-permute-done | bytes 262176 | tf_op jit(solution)/shard_map/ppermute | solution.py:119
  27.6 0.3 copy.91
  27.9 0.4 slice.56
  28.3 0.4 stack.25
  28.7 0.4 copy.48
  29.1 0.4 copy.49
  29.7 0.5 %copy-done = bf16[2]{0:T(256)(128)(2,1)S(1)} copy-done((bf16[2]{0:T(256)(128)(2,1)S(1)}, bf16[2]{0:T(256)(128)(2,1)}, u32[]{:S(2)}) %copy-start) | copy-done | bytes 28
  30.3 0.7 %convolution_bitcast_fusion = f32[16,2,16,144]{3,2,1,0:T(8,128)S(1)} fusion(bf16[144,64,2,16,1]{0,3,2,1,4:T(8,128)(2,1)S(1)} %bitcast.77, bf16[1,16,64,2,16]{2,1,3,0,4:T(8,128)(2,1)S(1)} %multiply_bitcast_fusion.1, bf16[1,16,64,2,16]{2,1,3,0,4:T(8,128)(2,1)S(1)} %copy.49), kind=kOutput, calls=%fused_computation.1 | convolution fusion | flops 18939904 | bytes 1015808 | tf_op jit(solution)/shard_map/ocspn,jspn->nocj/dot_general | solution.py:160
  31.0 0.6 %fusion.8 = (f32[16,2,1,128]{3,2,1,0:T(1,128)S(1)}, f32[16,2,1,128]{3,2,1,0:T(1,128)S(1)}, f32[16,2,1,128]{3,2,1,0:T(1,128)S(1)}, f32[16,2,1,128]{3,2,1,0:T(1,12...) fusion(f32[16,2,16,144]{3,2,1,0:T(8,128)S(1)} %convolution_bitc, ...), kind=kLoop, calls=%fused_computation.72 | loop fusion | bytes 524288 | tf_op jit(solution)/shard_map/slice | solution.py:161
  32.3 2.9 %collective-permute-start.7 = (f32[64,512]{1,0:T(8,128)S(1)}, f32[64,512]{1,0:T(8,128)S(1)}, u32[]{:S(2)}, u32[]{:S(2)}) collective-permute-start(f32[64,512]{1,0:T(8,128)S(1)} %get-tuple-element.16), channel_id=1, source_target_pairs={{0,8},{24,0},{1,9},{25,1},{2,10},{26,2},{3,11},{27,3},{4,12},{28,4... | collective-permute-start | bytes 393224 | tf_op jit(solution)/shard_map/ppermute | solution.py:173
  35.2 1.3 %collective-permute-start.8 = (f32[64,512]{1,0:T(8,128)S(1)}, f32[64,512]{1,0:T(8,128)S(1)}, u32[]{:S(2)}, u32[]{:S(2)}) collective-permute-start(f32[64,512]{1,0:T(8,128)S(1)} %get-tuple-element.15), channel_id=1, source_target_pairs={{16,0},{24,8},{17,1},{25,9},{18,2},{26,10},{19,3},{27,11},{20,4},{... | collective-permute-start | bytes 393224 | tf_op jit(solution)/shard_map/ppermute | solution.py:173
  36.5 1.3 %collective-permute-start.9 = (f32[64,512]{1,0:T(8,128)S(1)}, f32[64,512]{1,0:T(8,128)S(1)}, u32[]{:S(2)}, u32[]{:S(2)}) collective-permute-start(f32[64,512]{1,0:T(8,128)S(1)} %get-tuple-element.14), channel_id=1, source_target_pairs={{8,0},{16,8},{9,1},{17,9},{10,2},{18,10},{11,3},{19,11},{12,4},{20... | collective-permute-start | bytes 393224 | tf_op jit(solution)/shard_map/ppermute | solution.py:173
  37.8 2.9 %collective-permute-done.7 = f32[64,512]{1,0:T(8,128)S(1)} collective-permute-done((f32[64,512]{1,0:T(8,128)S(1)}, f32[64,512]{1,0:T(8,128)S(1)}, u32[]{:S(2)}, u32[]{:S(2)}) %collective-permute-start.7) | collective-permute-done | bytes 131104 | tf_op jit(solution)/shard_map/ppermute | solution.py:173
  40.7 2.7 %collective-permute-done.8 = f32[64,512]{1,0:T(8,128)S(1)} collective-permute-done((f32[64,512]{1,0:T(8,128)S(1)}, f32[64,512]{1,0:T(8,128)S(1)}, u32[]{:S(2)}, u32[]{:S(2)}) %collective-permute-start.8) | collective-permute-done | bytes 131104 | tf_op jit(solution)/shard_map/ppermute | solution.py:173
  43.4 0.2 collective-permute-done.9
  43.7 0.6 %gather_fusion = f32[4,64,512]{2,1,0:T(8,128)S(1)} fusion(f32[4,64,512]{2,1,0:T(8,128)S(1)} %pad_maximum_fusion, s32[1024]{0:T(1024)S(1)} %pad_clamp_fusion), kind=kCustom, calls=%fused_computation | custom fusion | bytes 1048592 | tf_op jit(solution)/shard_map/jit(_take)/gather | solution.py:178
  44.3 0.3 copy.69
  44.6 0.2 select_bitcast_fusion
  45.0 1.1 %copy.71 = f32[64,16,128]{2,1,0:T(8,128)} copy(f32[64,16,128]{0,2,1:T(8,128)S(1)} %bitcast.78) | data formatting | bytes 1048576 | tf_op jit(solution)/shard_map/reshape | solution.py:179
  (48 shorter events, 1.2 us)
Async XLA Ops:
  5.5 6.7 %collective-permute-start = (bf16[16,512]{1,0:T(8,128)(2,1)}, bf16[16,512]{1,0:T(8,128)(2,1)S(1)}, u32[]{:S(2)}, u32[]{:S(2)}) collective-permute-start(bf16[16,512]{1,0:T(8,128)(2,1)} %get-tuple-element.10), channel_id=1, source_target_pairs={{0,8},{8,16},{16,24},{24,0},{1,9},{9,17},{17,25},{25,1},{2,10},{10... | collective-permute-start | bytes 49160 | tf_op jit(solution)/shard_map/ppermute | solution.py:147
  8.5 3.9 %collective-permute-start.1 = (bf16[16,512]{1,0:T(8,128)(2,1)}, bf16[16,512]{1,0:T(8,128)(2,1)S(1)}, u32[]{:S(2)}, u32[]{:S(2)}) collective-permute-start(bf16[16,512]{1,0:T(8,128)(2,1)} %get-tuple-element.11), channel_id=1, source_target_pairs={{0,16},{8,24},{16,0},{24,8},{1,17},{9,25},{17,1},{25,9},{2,18},{10... | collective-permute-start | bytes 49160 | tf_op jit(solution)/shard_map/ppermute | solution.py:147
  10.1 3.9 %collective-permute-start.2 = (bf16[16,512]{1,0:T(8,128)(2,1)}, bf16[16,512]{1,0:T(8,128)(2,1)S(1)}, u32[]{:S(2)}, u32[]{:S(2)}) collective-permute-start(bf16[16,512]{1,0:T(8,128)(2,1)} %get-tuple-element.12), channel_id=1, source_target_pairs={{0,24},{8,0},{16,8},{24,16},{1,25},{9,1},{17,9},{25,17},{2,26},{10... | collective-permute-start | bytes 49160 | tf_op jit(solution)/shard_map/ppermute | solution.py:147
  14.0 6.6 %collective-permute-start.3 = (bf16[16,2048]{1,0:T(8,128)(2,1)S(1)}, bf16[16,2048]{1,0:T(8,128)(2,1)S(1)}, u32[]{:S(2)}, u32[]{:S(2)}) collective-permute-start(bf16[16,2048]{1,0:T(8,128)(2,1)S(1)} %get-tuple-element.39), channel_id=1, source_target_pairs={{2,0},{3,1},{4,2},{5,3},{6,4},{7,5},{10,8},{11,9},{12,10},{13,11},... | collective-permute-start | bytes 196616 | tf_op jit(solution)/shard_map/ppermute | solution.py:118
  15.3 8.0 %collective-permute-start.4 = (bf16[16,2048]{1,0:T(8,128)(2,1)S(1)}, bf16[16,2048]{1,0:T(8,128)(2,1)S(1)}, u32[]{:S(2)}, u32[]{:S(2)}) collective-permute-start(bf16[16,2048]{1,0:T(8,128)(2,1)S(1)} %get-tuple-element.39), channel_id=1, source_target_pairs={{4,0},{5,1},{6,2},{7,3},{12,8},{13,9},{14,10},{15,11},{20,16},{21,... | collective-permute-start | bytes 196616 | tf_op jit(solution)/shard_map/ppermute | solution.py:118
  16.6 9.1 %collective-permute-start.5 = (bf16[16,2048]{1,0:T(8,128)(2,1)S(1)}, bf16[16,2048]{1,0:T(8,128)(2,1)S(1)}, u32[]{:S(2)}, u32[]{:S(2)}) collective-permute-start(bf16[16,2048]{1,0:T(8,128)(2,1)S(1)} %get-tuple-element.39), channel_id=1, source_target_pairs={{6,0},{7,1},{14,8},{15,9},{22,16},{23,17},{30,24},{31,25}} | collective-permute-start | bytes 196616 | tf_op jit(solution)/shard_map/ppermute | solution.py:118
  25.8 1.6 %collective-permute-start.6 = (bf16[64,2048]{1,0:T(8,128)(2,1)S(1)}, bf16[64,2048]{1,0:T(8,128)(2,1)S(1)}, u32[]{:S(2)}, u32[]{:S(2)}) collective-permute-start(bf16[64,2048]{1,0:T(8,128)(2,1)S(1)} %pad_maximum_fusion.1), channel_id=1, source_target_pairs={{0,1},{1,0},{2,3},{3,2},{4,5},{5,4},{6,7},{7,6},{8,9},{9,8},{10,11... | collective-permute-start | bytes 786440 | tf_op jit(solution)/shard_map/ppermute | solution.py:119
  29.6 0.7 %copy-start = (bf16[2]{0:T(256)(128)(2,1)S(1)}, bf16[2]{0:T(256)(128)(2,1)}, u32[]{:S(2)}) copy-start(bf16[2]{0:T(256)(128)(2,1)} %constant.91.clone) | copy-start | bytes 16
  32.3 8.4 %collective-permute-start.7 = (f32[64,512]{1,0:T(8,128)S(1)}, f32[64,512]{1,0:T(8,128)S(1)}, u32[]{:S(2)}, u32[]{:S(2)}) collective-permute-start(f32[64,512]{1,0:T(8,128)S(1)} %get-tuple-element.16), channel_id=1, source_target_pairs={{0,8},{24,0},{1,9},{25,1},{2,10},{26,2},{3,11},{27,3},{4,12},{28,4... | collective-permute-start | bytes 393224 | tf_op jit(solution)/shard_map/ppermute | solution.py:173
  35.2 8.2 %collective-permute-start.8 = (f32[64,512]{1,0:T(8,128)S(1)}, f32[64,512]{1,0:T(8,128)S(1)}, u32[]{:S(2)}, u32[]{:S(2)}) collective-permute-start(f32[64,512]{1,0:T(8,128)S(1)} %get-tuple-element.15), channel_id=1, source_target_pairs={{16,0},{24,8},{17,1},{25,9},{18,2},{26,10},{19,3},{27,11},{20,4},{... | collective-permute-start | bytes 393224 | tf_op jit(solution)/shard_map/ppermute | solution.py:173
  36.5 7.2 %collective-permute-start.9 = (f32[64,512]{1,0:T(8,128)S(1)}, f32[64,512]{1,0:T(8,128)S(1)}, u32[]{:S(2)}, u32[]{:S(2)}) collective-permute-start(f32[64,512]{1,0:T(8,128)S(1)} %get-tuple-element.14), channel_id=1, source_target_pairs={{8,0},{16,8},{9,1},{17,9},{10,2},{18,10},{11,3},{19,11},{12,4},{20... | collective-permute-start | bytes 393224 | tf_op jit(solution)/shard_map/ppermute | solution.py:173

commit v17 on v16

--- a/solution.py
+++ b/solution.py
@@ -174,8 +174,10 @@
         else:
             collected.append(jnp.zeros_like(sent))
     collected = jnp.stack(collected)
-    holder = (me - jnp.arange(seg_count, dtype=jnp.int32)) % seg_count
-    by_bins = jnp.take(collected, holder, axis=0).reshape(seg_count, per_owner, block, 2, bins_each)
+    turned_rows = jnp.concatenate([collected[:1], collected[1:][::-1]], axis=0)
+    doubled = jnp.concatenate([turned_rows, turned_rows], axis=0)
+    by_bins = lax.dynamic_slice_in_dim(doubled, (seg_count - me) % seg_count, seg_count, 0)
+    by_bins = by_bins.reshape(seg_count, per_owner, block, 2, bins_each)
     return by_bins.transpose(1, 2, 3, 0, 4).reshape(per_owner, block, 2 * NF)
 
 

time: 46.4 us -> 45.8 us (0.987)
  local copies, waits for them, and re-layouts: 6.62 us -> 6.07 us
    gather x2 -> x0, local copies, waits for them, and re-layouts: 0.91 us -> none  [shards(): jnp.take(collected, holder, axis=0)]
where the time goes in v17:
time: 45.8 us; the launch traced here: 45.5 us
  waiting for transfers between devices  16.9 us (37%)
  starting transfers between devices  15.3 us (33%)
  local copies, waits for them, and re-layouts  6.07 us (13%)
  Pallas kernels  5.53 us (12%)
  matrix products  0.73 us (2%)
  other arithmetic  0.49 us (1%)
    ppermute x3, waiting for transfers between devices, halo(): own.append(lax.ppermute(mine, 'fibre', pairs))  7.84 us
    ppermute x3, starting transfers between devices, shards(): gathered.append(lax.ppermute(split[step], 'seg', pairs))  5.94 us
    ppermute x3, waiting for transfers between devices, shards(): collected.append(lax.ppermute(sent, 'seg', pairs))  5.83 us
    pallas_call x1, Pallas kernels, whiten(): pl.pallas_call(whiten_kernel, out_shape=[jax.ShapeDtypeStruct((channels,...  5.53 us
    ppermute x3, starting transfers between devices, shards(): collected.append(lax.ppermute(sent, 'seg', pairs))  5.47 us
    ppermute x3, starting transfers between devices, halo(): own.append(lax.ppermute(mine, 'fibre', pairs))  3.86 us
    unnamed x31, local copies, waits for them, and re-layouts  1.9 us
    ppermute x3, waiting for transfers between devices, shards(): gathered.append(lax.ppermute(split[step], 'seg', pairs))  1.79 us
  transfers between devices with their start and end apart: 10, of which 9 were waited for; matrix products, arithmetic and copies ran while one was open for 2% of the time, Pallas kernels for 0%

profile of v17, /device:TPU:0, one launch (start us, length us, event | category | flops | bytes accessed | tf_op | source)
XLA Modules:
  0.0 45.5 jit_solution(4532381313212327910)
XLA Ops:
  0.0 5.5 %shard_map.73 = (bf16[16,512]{1,0:T(8,128)(2,1)}, bf16[16,512]{1,0:T(8,128)(2,1)}, bf16[16,512]{1,0:T(8,128)(2,1)}, bf16[16,512]{1,0:T(8,128)(2,1)}) custom-call(s32[16]{0:T(128)} %bitcast.99, s32[1]{0:T(128)} %bitcast.1.place_ref, s32[16]{0:T(128)} %live_ref.1, bf16[16,27648]{1,0:T(8,128)(2,1)} %bitcast.79, bf16[3072,128]{1,0:T(8,128)(2,1)} %constant.72.clone.table_ref, ...), custom_call_target="tpu_custom_call" | custom-call | tf_op jit(solution)/shard_map/pallas_call | solution.py:94
  5.5 3.0 %collective-permute-start = (bf16[16,512]{1,0:T(8,128)(2,1)}, bf16[16,512]{1,0:T(8,128)(2,1)S(1)}, u32[]{:S(2)}, u32[]{:S(2)}) collective-permute-start(bf16[16,512]{1,0:T(8,128)(2,1)} %get-tuple-element.10), channel_id=1, source_target_pairs={{0,8},{8,16},{16,24},{24,0},{1,9},{9,17},{17,25},{25,1},{2,10},{10... | collective-permute-start | bytes 49160 | tf_op jit(solution)/shard_map/ppermute | solution.py:147
  8.5 1.5 %collective-permute-start.1 = (bf16[16,512]{1,0:T(8,128)(2,1)}, bf16[16,512]{1,0:T(8,128)(2,1)S(1)}, u32[]{:S(2)}, u32[]{:S(2)}) collective-permute-start(bf16[16,512]{1,0:T(8,128)(2,1)} %get-tuple-element.11), channel_id=1, source_target_pairs={{0,16},{8,24},{16,0},{24,8},{1,17},{9,25},{17,1},{25,9},{2,18},{10... | collective-permute-start | bytes 49160 | tf_op jit(solution)/shard_map/ppermute | solution.py:147
  10.1 1.4 %collective-permute-start.2 = (bf16[16,512]{1,0:T(8,128)(2,1)}, bf16[16,512]{1,0:T(8,128)(2,1)S(1)}, u32[]{:S(2)}, u32[]{:S(2)}) collective-permute-start(bf16[16,512]{1,0:T(8,128)(2,1)} %get-tuple-element.12), channel_id=1, source_target_pairs={{0,24},{8,0},{16,8},{24,16},{1,25},{9,1},{17,9},{25,17},{2,26},{10... | collective-permute-start | bytes 49160 | tf_op jit(solution)/shard_map/ppermute | solution.py:147
  11.5 0.7 %constant_dynamic-update-slice_fusion.3 = (bf16[16,2048]{1,0:T(8,128)(2,1)S(1)}, bf16[128,2048]{1,0:T(8,128)(2,1)S(1)}) fusion(bf16[16,512]{1,0:T(8,128)(2,1)} %get-tuple-element.9), kind=kLoop, calls=%fused_computation.23 | loop fusion | bytes 49152
  12.2 0.3 collective-permute-done.1
  12.5 1.5 %collective-permute-done.2 = bf16[16,512]{1,0:T(8,128)(2,1)S(1)} collective-permute-done((bf16[16,512]{1,0:T(8,128)(2,1)}, bf16[16,512]{1,0:T(8,128)(2,1)S(1)}, u32[]{:S(2)}, u32[]{:S(2)}) %collective-permute-start.2) | collective-permute-done | bytes 16416 | tf_op jit(solution)/shard_map/ppermute | solution.py:147
  14.0 1.3 %collective-permute-start.3 = (bf16[16,2048]{1,0:T(8,128)(2,1)S(1)}, bf16[16,2048]{1,0:T(8,128)(2,1)S(1)}, u32[]{:S(2)}, u32[]{:S(2)}) collective-permute-start(bf16[16,2048]{1,0:T(8,128)(2,1)S(1)} %get-tuple-element.39), channel_id=1, source_target_pairs={{2,0},{3,1},{4,2},{5,3},{6,4},{7,5},{10,8},{11,9},{12,10},{13,11},... | collective-permute-start | bytes 196616 | tf_op jit(solution)/shard_map/ppermute | solution.py:118
  15.3 1.3 %collective-permute-start.4 = (bf16[16,2048]{1,0:T(8,128)(2,1)S(1)}, bf16[16,2048]{1,0:T(8,128)(2,1)S(1)}, u32[]{:S(2)}, u32[]{:S(2)}) collective-permute-start(bf16[16,2048]{1,0:T(8,128)(2,1)S(1)} %get-tuple-element.39), channel_id=1, source_target_pairs={{4,0},{5,1},{6,2},{7,3},{12,8},{13,9},{14,10},{15,11},{20,16},{21,... | collective-permute-start | bytes 196616 | tf_op jit(solution)/shard_map/ppermute | solution.py:118
  16.6 1.3 %collective-permute-start.5 = (bf16[16,2048]{1,0:T(8,128)(2,1)S(1)}, bf16[16,2048]{1,0:T(8,128)(2,1)S(1)}, u32[]{:S(2)}, u32[]{:S(2)}) collective-permute-start(bf16[16,2048]{1,0:T(8,128)(2,1)S(1)} %get-tuple-element.39), channel_id=1, source_target_pairs={{6,0},{7,1},{14,8},{15,9},{22,16},{23,17},{30,24},{31,25}} | collective-permute-start | bytes 196616 | tf_op jit(solution)/shard_map/ppermute | solution.py:118
  17.9 2.7 %collective-permute-done.3 = bf16[16,2048]{1,0:T(8,128)(2,1)S(1)} collective-permute-done((bf16[16,2048]{1,0:T(8,128)(2,1)S(1)}, bf16[16,2048]{1,0:T(8,128)(2,1)S(1)}, u32[]{:S(2)}, u32[]{:S(2)}) %collective-permute-start.3) | collective-permute-done | bytes 65568 | tf_op jit(solution)/shard_map/ppermute | solution.py:118
  20.6 2.7 %collective-permute-done.4 = bf16[16,2048]{1,0:T(8,128)(2,1)S(1)} collective-permute-done((bf16[16,2048]{1,0:T(8,128)(2,1)S(1)}, bf16[16,2048]{1,0:T(8,128)(2,1)S(1)}, u32[]{:S(2)}, u32[]{:S(2)}) %collective-permute-start.4) | collective-permute-done | bytes 65568 | tf_op jit(solution)/shard_map/ppermute | solution.py:118
  23.3 2.5 %collective-permute-done.5 = bf16[16,2048]{1,0:T(8,128)(2,1)S(1)} collective-permute-done((bf16[16,2048]{1,0:T(8,128)(2,1)S(1)}, bf16[16,2048]{1,0:T(8,128)(2,1)S(1)}, u32[]{:S(2)}, u32[]{:S(2)}) %collective-permute-start.5) | collective-permute-done | bytes 65568 | tf_op jit(solution)/shard_map/ppermute | solution.py:118
  25.9 1.4 %collective-permute-done.6 = bf16[64,2048]{1,0:T(8,128)(2,1)S(1)} collective-permute-done((bf16[64,2048]{1,0:T(8,128)(2,1)S(1)}, bf16[64,2048]{1,0:T(8,128)(2,1)S(1)}, u32[]{:S(2)}, u32[]{:S(2)}) %collective-permute-start.6) | collective-permute-done | bytes 262176 | tf_op jit(solution)/shard_map/ppermute | solution.py:119
  27.6 0.3 copy.117
  27.9 0.4 slice.56
  28.3 0.4 stack.25
  28.7 0.4 copy.74
  29.1 0.4 copy.75
  29.7 0.5 %copy-done = bf16[2]{0:T(256)(128)(2,1)S(1)} copy-done((bf16[2]{0:T(256)(128)(2,1)S(1)}, bf16[2]{0:T(256)(128)(2,1)}, u32[]{:S(2)}) %copy-start) | copy-done | bytes 28
  30.3 0.7 %convolution_bitcast_fusion = f32[16,2,16,144]{3,2,1,0:T(8,128)S(1)} fusion(bf16[144,64,2,16,1]{0,3,2,1,4:T(8,128)(2,1)S(1)} %bitcast.74, bf16[1,16,64,2,16]{2,1,3,0,4:T(8,128)(2,1)S(1)} %multiply_bitcast_fusion.1, bf16[1,16,64,2,16]{2,1,3,0,4:T(8,128)(2,1)S(1)} %copy.75), kind=kOutput, calls=%fused_computation | convolution fusion | flops 18939904 | bytes 1015808 | tf_op jit(solution)/shard_map/ocspn,jspn->nocj/dot_general | solution.py:160
  31.0 0.6 %fusion.8 = (f32[16,2,1,128]{3,2,1,0:T(1,128)S(1)}, f32[16,2,1,128]{3,2,1,0:T(1,128)S(1)}, f32[16,2,1,128]{3,2,1,0:T(1,128)S(1)}, f32[16,2,1,128]{3,2,1,0:T(1,12...) fusion(f32[16,2,16,144]{3,2,1,0:T(8,128)S(1)} %convolution_bitc, ...), kind=kLoop, calls=%fused_computation.64 | loop fusion | bytes 524288 | tf_op jit(solution)/shard_map/slice | solution.py:161
  31.9 0.1 multiply_bitcast_fusion
  32.3 2.9 %collective-permute-start.7 = (f32[64,512]{1,0:T(8,128)S(1)}, f32[64,512]{1,0:T(8,128)S(1)}, u32[]{:S(2)}, u32[]{:S(2)}) collective-permute-start(f32[64,512]{1,0:T(8,128)S(1)} %get-tuple-element.13), channel_id=1, source_target_pairs={{0,8},{24,0},{1,9},{25,1},{2,10},{26,2},{3,11},{27,3},{4,12},{28,4... | collective-permute-start | bytes 393224 | tf_op jit(solution)/shard_map/ppermute | solution.py:173
  35.2 1.3 %collective-permute-start.8 = (f32[64,512]{1,0:T(8,128)S(1)}, f32[64,512]{1,0:T(8,128)S(1)}, u32[]{:S(2)}, u32[]{:S(2)}) collective-permute-start(f32[64,512]{1,0:T(8,128)S(1)} %get-tuple-element.15), channel_id=1, source_target_pairs={{16,0},{24,8},{17,1},{25,9},{18,2},{26,10},{19,3},{27,11},{20,4},{... | collective-permute-start | bytes 393224 | tf_op jit(solution)/shard_map/ppermute | solution.py:173
  36.5 1.3 %collective-permute-start.9 = (f32[64,512]{1,0:T(8,128)S(1)}, f32[64,512]{1,0:T(8,128)S(1)}, u32[]{:S(2)}, u32[]{:S(2)}) collective-permute-start(f32[64,512]{1,0:T(8,128)S(1)} %get-tuple-element.14), channel_id=1, source_target_pairs={{8,0},{16,8},{9,1},{17,9},{10,2},{18,10},{11,3},{19,11},{12,4},{20... | collective-permute-start | bytes 393224 | tf_op jit(solution)/shard_map/ppermute | solution.py:173
  37.8 2.9 %collective-permute-done.7 = f32[64,512]{1,0:T(8,128)S(1)} collective-permute-done((f32[64,512]{1,0:T(8,128)S(1)}, f32[64,512]{1,0:T(8,128)S(1)}, u32[]{:S(2)}, u32[]{:S(2)}) %collective-permute-start.7) | collective-permute-done | bytes 131104 | tf_op jit(solution)/shard_map/ppermute | solution.py:173
  40.7 2.7 %collective-permute-done.8 = f32[64,512]{1,0:T(8,128)S(1)} collective-permute-done((f32[64,512]{1,0:T(8,128)S(1)}, f32[64,512]{1,0:T(8,128)S(1)}, u32[]{:S(2)}, u32[]{:S(2)}) %collective-permute-start.8) | collective-permute-done | bytes 131104 | tf_op jit(solution)/shard_map/ppermute | solution.py:173
  43.4 0.2 collective-permute-done.9
  43.7 0.2 fusion.3
  43.9 0.3 copy.95
  44.3 1.1 %copy.97 = f32[64,16,128]{2,1,0:T(8,128)} copy(f32[64,16,128]{0,2,1:T(8,128)S(1)} %bitcast.76) | data formatting | bytes 1048576 | tf_op jit(solution)/shard_map/reshape | solution.py:181
  (45 shorter events, 1.1 us)
Async XLA Ops:
  5.5 6.7 %collective-permute-start = (bf16[16,512]{1,0:T(8,128)(2,1)}, bf16[16,512]{1,0:T(8,128)(2,1)S(1)}, u32[]{:S(2)}, u32[]{:S(2)}) collective-permute-start(bf16[16,512]{1,0:T(8,128)(2,1)} %get-tuple-element.10), channel_id=1, source_target_pairs={{0,8},{8,16},{16,24},{24,0},{1,9},{9,17},{17,25},{25,1},{2,10},{10... | collective-permute-start | bytes 49160 | tf_op jit(solution)/shard_map/ppermute | solution.py:147
  8.5 3.9 %collective-permute-start.1 = (bf16[16,512]{1,0:T(8,128)(2,1)}, bf16[16,512]{1,0:T(8,128)(2,1)S(1)}, u32[]{:S(2)}, u32[]{:S(2)}) collective-permute-start(bf16[16,512]{1,0:T(8,128)(2,1)} %get-tuple-element.11), channel_id=1, source_target_pairs={{0,16},{8,24},{16,0},{24,8},{1,17},{9,25},{17,1},{25,9},{2,18},{10... | collective-permute-start | bytes 49160 | tf_op jit(solution)/shard_map/ppermute | solution.py:147
  10.1 3.9 %collective-permute-start.2 = (bf16[16,512]{1,0:T(8,128)(2,1)}, bf16[16,512]{1,0:T(8,128)(2,1)S(1)}, u32[]{:S(2)}, u32[]{:S(2)}) collective-permute-start(bf16[16,512]{1,0:T(8,128)(2,1)} %get-tuple-element.12), channel_id=1, source_target_pairs={{0,24},{8,0},{16,8},{24,16},{1,25},{9,1},{17,9},{25,17},{2,26},{10... | collective-permute-start | bytes 49160 | tf_op jit(solution)/shard_map/ppermute | solution.py:147
  14.0 6.6 %collective-permute-start.3 = (bf16[16,2048]{1,0:T(8,128)(2,1)S(1)}, bf16[16,2048]{1,0:T(8,128)(2,1)S(1)}, u32[]{:S(2)}, u32[]{:S(2)}) collective-permute-start(bf16[16,2048]{1,0:T(8,128)(2,1)S(1)} %get-tuple-element.39), channel_id=1, source_target_pairs={{2,0},{3,1},{4,2},{5,3},{6,4},{7,5},{10,8},{11,9},{12,10},{13,11},... | collective-permute-start | bytes 196616 | tf_op jit(solution)/shard_map/ppermute | solution.py:118
  15.3 8.0 %collective-permute-start.4 = (bf16[16,2048]{1,0:T(8,128)(2,1)S(1)}, bf16[16,2048]{1,0:T(8,128)(2,1)S(1)}, u32[]{:S(2)}, u32[]{:S(2)}) collective-permute-start(bf16[16,2048]{1,0:T(8,128)(2,1)S(1)} %get-tuple-element.39), channel_id=1, source_target_pairs={{4,0},{5,1},{6,2},{7,3},{12,8},{13,9},{14,10},{15,11},{20,16},{21,... | collective-permute-start | bytes 196616 | tf_op jit(solution)/shard_map/ppermute | solution.py:118
  16.6 9.1 %collective-permute-start.5 = (bf16[16,2048]{1,0:T(8,128)(2,1)S(1)}, bf16[16,2048]{1,0:T(8,128)(2,1)S(1)}, u32[]{:S(2)}, u32[]{:S(2)}) collective-permute-start(bf16[16,2048]{1,0:T(8,128)(2,1)S(1)} %get-tuple-element.39), channel_id=1, source_target_pairs={{6,0},{7,1},{14,8},{15,9},{22,16},{23,17},{30,24},{31,25}} | collective-permute-start | bytes 196616 | tf_op jit(solution)/shard_map/ppermute | solution.py:118
  25.8 1.6 %collective-permute-start.6 = (bf16[64,2048]{1,0:T(8,128)(2,1)S(1)}, bf16[64,2048]{1,0:T(8,128)(2,1)S(1)}, u32[]{:S(2)}, u32[]{:S(2)}) collective-permute-start(bf16[64,2048]{1,0:T(8,128)(2,1)S(1)} %pad_maximum_fusion.1), channel_id=1, source_target_pairs={{0,1},{1,0},{2,3},{3,2},{4,5},{5,4},{6,7},{7,6},{8,9},{9,8},{10,11... | collective-permute-start | bytes 786440 | tf_op jit(solution)/shard_map/ppermute | solution.py:119
  29.6 0.7 %copy-start = (bf16[2]{0:T(256)(128)(2,1)S(1)}, bf16[2]{0:T(256)(128)(2,1)}, u32[]{:S(2)}) copy-start(bf16[2]{0:T(256)(128)(2,1)} %constant.75.clone) | copy-start | bytes 16
  32.3 8.4 %collective-permute-start.7 = (f32[64,512]{1,0:T(8,128)S(1)}, f32[64,512]{1,0:T(8,128)S(1)}, u32[]{:S(2)}, u32[]{:S(2)}) collective-permute-start(f32[64,512]{1,0:T(8,128)S(1)} %get-tuple-element.13), channel_id=1, source_target_pairs={{0,8},{24,0},{1,9},{25,1},{2,10},{26,2},{3,11},{27,3},{4,12},{28,4... | collective-permute-start | bytes 393224 | tf_op jit(solution)/shard_map/ppermute | solution.py:173
  35.2 8.2 %collective-permute-start.8 = (f32[64,512]{1,0:T(8,128)S(1)}, f32[64,512]{1,0:T(8,128)S(1)}, u32[]{:S(2)}, u32[]{:S(2)}) collective-permute-start(f32[64,512]{1,0:T(8,128)S(1)} %get-tuple-element.15), channel_id=1, source_target_pairs={{16,0},{24,8},{17,1},{25,9},{18,2},{26,10},{19,3},{27,11},{20,4},{... | collective-permute-start | bytes 393224 | tf_op jit(solution)/shard_map/ppermute | solution.py:173
  36.5 7.2 %collective-permute-start.9 = (f32[64,512]{1,0:T(8,128)S(1)}, f32[64,512]{1,0:T(8,128)S(1)}, u32[]{:S(2)}, u32[]{:S(2)}) collective-permute-start(f32[64,512]{1,0:T(8,128)S(1)} %get-tuple-element.14), channel_id=1, source_target_pairs={{8,0},{16,8},{9,1},{17,9},{10,2},{18,10},{11,3},{19,11},{12,4},{20... | collective-permute-start | bytes 393224 | tf_op jit(solution)/shard_map/ppermute | solution.py:173

commit v18 on v17

--- a/solution.py
+++ b/solution.py
@@ -176,9 +176,10 @@
     collected = jnp.stack(collected)
     turned_rows = jnp.concatenate([collected[:1], collected[1:][::-1]], axis=0)
     doubled = jnp.concatenate([turned_rows, turned_rows], axis=0)
-    by_bins = lax.dynamic_slice_in_dim(doubled, (seg_count - me) % seg_count, seg_count, 0)
-    by_bins = by_bins.reshape(seg_count, per_owner, block, 2, bins_each)
-    return by_bins.transpose(1, 2, 3, 0, 4).reshape(per_owner, block, 2 * NF)
+    doubled = doubled.reshape(2 * seg_count, per_owner, block, 2, bins_each)
+    start = (seg_count - me) % seg_count
+    by_bins = [lax.dynamic_index_in_dim(doubled, start + b, 0, keepdims=False) for b in range(seg_count)]
+    return jnp.stack(by_bins, axis=3).reshape(per_owner, block, 2 * NF)
 
 
 def solution(mesh):

time: 45.8 us -> 44.4 us (0.969)
  waiting for transfers between devices: 16.9 us -> 14 us
  starting transfers between devices: 15.3 us -> 17 us
    ppermute x3, waiting for transfers between devices: 7.84 us -> 5.65 us  [halo(): own.append(lax.ppermute(mine, 'fibre', pairs))]
    ppermute x3, starting transfers between devices: 5.47 us -> 7.13 us  [shards(): collected.append(lax.ppermute(sent, 'seg', pairs))]
    ppermute x3, waiting for transfers between devices: 5.83 us -> 5.11 us  [shards(): collected.append(lax.ppermute(sent, 'seg', pairs))]
    concatenate x0 -> x1, local copies, waits for them, and re-layouts: none -> 0.6 us  [shards(): doubled = jnp.concatenate([turned_rows, turned_rows], axis=0)]
    unnamed x31, local copies, waits for them, and re-layouts: 1.9 us -> 1.37 us
  transfers between devices with their start and end apart: 10 -> 10, of which waited for: 9 -> 7; matrix products, arithmetic and copies ran while one was open for 2% -> 2% of each run, Pallas kernels for 0% -> 0%
where the time goes in v18:
time: 44.4 us; the launch traced here: 44 us
  starting transfers between devices  17 us (38%)
  waiting for transfers between devices  14 us (32%)
  local copies, waits for them, and re-layouts  5.76 us (13%)
  Pallas kernels  5.53 us (12%)
  matrix products  0.72 us (2%)
  other arithmetic  0.56 us (1%)
  between operations  0.48 us (1%)
    ppermute x3, starting transfers between devices, shards(): collected.append(lax.ppermute(sent, 'seg', pairs))  7.13 us
    ppermute x3, starting transfers between devices, shards(): gathered.append(lax.ppermute(split[step], 'seg', pairs))  5.94 us
    ppermute x3, waiting for transfers between devices, halo(): own.append(lax.ppermute(mine, 'fibre', pairs))  5.65 us
    pallas_call x1, Pallas kernels, whiten(): pl.pallas_call(whiten_kernel, out_shape=[jax.ShapeDtypeStruct((channels,...  5.53 us
    ppermute x3, waiting for transfers between devices, shards(): collected.append(lax.ppermute(sent, 'seg', pairs))  5.11 us
    ppermute x3, starting transfers between devices, halo(): own.append(lax.ppermute(mine, 'fibre', pairs))  3.86 us
    ppermute x3, waiting for transfers between devices, shards(): gathered.append(lax.ppermute(split[step], 'seg', pairs))  1.79 us
    ppermute x1, waiting for transfers between devices, halo(): lax.ppermute(jnp.concatenate(own, axis=0), 'fibre', [(i, i ^ 1) for i in...  1.42 us
  transfers between devices with their start and end apart: 10, of which 7 were waited for; matrix products, arithmetic and copies ran while one was open for 2% of the time, Pallas kernels for 0%

profile of v18, /device:TPU:0, one launch (start us, length us, event | category | flops | bytes accessed | tf_op | source)
XLA Modules:
  0.0 44.0 jit_solution(18075056677722109223)
XLA Ops:
  0.0 5.5 %shard_map.73 = (bf16[16,512]{1,0:T(8,128)(2,1)}, bf16[16,512]{1,0:T(8,128)(2,1)}, bf16[16,512]{1,0:T(8,128)(2,1)}, bf16[16,512]{1,0:T(8,128)(2,1)}) custom-call(s32[16]{0:T(128)} %bitcast.105, s32[1]{0:T(128)} %bitcast.1.place_ref, s32[16]{0:T(128)} %live_ref.1, bf16[16,27648]{1,0:T(8,128)(2,1)} %bitcast.85, bf16[3072,128]{1,0:T(8,128)(2,1)} %constant.86.clone.table_ref, ...), custom_call_target="tpu_custom_call" | custom-call | tf_op jit(solution)/shard_map/pallas_call | solution.py:94
  5.5 3.0 %collective-permute-start = (bf16[16,512]{1,0:T(8,128)(2,1)}, bf16[16,512]{1,0:T(8,128)(2,1)S(1)}, u32[]{:S(2)}, u32[]{:S(2)}) collective-permute-start(bf16[16,512]{1,0:T(8,128)(2,1)} %get-tuple-element.10), channel_id=1, source_target_pairs={{0,8},{8,16},{16,24},{24,0},{1,9},{9,17},{17,25},{25,1},{2,10},{10... | collective-permute-start | bytes 49160 | tf_op jit(solution)/shard_map/ppermute | solution.py:147
  8.5 1.5 %collective-permute-start.1 = (bf16[16,512]{1,0:T(8,128)(2,1)}, bf16[16,512]{1,0:T(8,128)(2,1)S(1)}, u32[]{:S(2)}, u32[]{:S(2)}) collective-permute-start(bf16[16,512]{1,0:T(8,128)(2,1)} %get-tuple-element.11), channel_id=1, source_target_pairs={{0,16},{8,24},{16,0},{24,8},{1,17},{9,25},{17,1},{25,9},{2,18},{10... | collective-permute-start | bytes 49160 | tf_op jit(solution)/shard_map/ppermute | solution.py:147
  10.1 1.4 %collective-permute-start.2 = (bf16[16,512]{1,0:T(8,128)(2,1)}, bf16[16,512]{1,0:T(8,128)(2,1)S(1)}, u32[]{:S(2)}, u32[]{:S(2)}) collective-permute-start(bf16[16,512]{1,0:T(8,128)(2,1)} %get-tuple-element.12), channel_id=1, source_target_pairs={{0,24},{8,0},{16,8},{24,16},{1,25},{9,1},{17,9},{25,17},{2,26},{10... | collective-permute-start | bytes 49160 | tf_op jit(solution)/shard_map/ppermute | solution.py:147
  11.5 0.7 %constant_dynamic-update-slice_fusion.3 = (bf16[16,2048]{1,0:T(8,128)(2,1)S(1)}, bf16[128,2048]{1,0:T(8,128)(2,1)S(1)}) fusion(bf16[16,512]{1,0:T(8,128)(2,1)} %get-tuple-element.9), kind=kLoop, calls=%fused_computation.22 | loop fusion | bytes 49152
  12.2 0.3 collective-permute-done.1
  12.5 1.5 %collective-permute-done.2 = bf16[16,512]{1,0:T(8,128)(2,1)S(1)} collective-permute-done((bf16[16,512]{1,0:T(8,128)(2,1)}, bf16[16,512]{1,0:T(8,128)(2,1)S(1)}, u32[]{:S(2)}, u32[]{:S(2)}) %collective-permute-start.2) | collective-permute-done | bytes 16416 | tf_op jit(solution)/shard_map/ppermute | solution.py:147
  14.0 1.3 %collective-permute-start.5 = (bf16[16,2048]{1,0:T(8,128)(2,1)S(1)}, bf16[16,2048]{1,0:T(8,128)(2,1)S(1)}, u32[]{:S(2)}, u32[]{:S(2)}) collective-permute-start(bf16[16,2048]{1,0:T(8,128)(2,1)S(1)} %get-tuple-element.43), channel_id=1, source_target_pairs={{6,0},{7,1},{14,8},{15,9},{22,16},{23,17},{30,24},{31,25}} | collective-permute-start | bytes 196616 | tf_op jit(solution)/shard_map/ppermute | solution.py:118
  15.3 1.3 %collective-permute-start.4 = (bf16[16,2048]{1,0:T(8,128)(2,1)S(1)}, bf16[16,2048]{1,0:T(8,128)(2,1)S(1)}, u32[]{:S(2)}, u32[]{:S(2)}) collective-permute-start(bf16[16,2048]{1,0:T(8,128)(2,1)S(1)} %get-tuple-element.43), channel_id=1, source_target_pairs={{4,0},{5,1},{6,2},{7,3},{12,8},{13,9},{14,10},{15,11},{20,16},{21,... | collective-permute-start | bytes 196616 | tf_op jit(solution)/shard_map/ppermute | solution.py:118
  16.6 1.3 %collective-permute-start.3 = (bf16[16,2048]{1,0:T(8,128)(2,1)S(1)}, bf16[16,2048]{1,0:T(8,128)(2,1)S(1)}, u32[]{:S(2)}, u32[]{:S(2)}) collective-permute-start(bf16[16,2048]{1,0:T(8,128)(2,1)S(1)} %get-tuple-element.43), channel_id=1, source_target_pairs={{2,0},{3,1},{4,2},{5,3},{6,4},{7,5},{10,8},{11,9},{12,10},{13,11},... | collective-permute-start | bytes 196616 | tf_op jit(solution)/shard_map/ppermute | solution.py:118
  17.9 4.2 %collective-permute-done.5 = bf16[16,2048]{1,0:T(8,128)(2,1)S(1)} collective-permute-done((bf16[16,2048]{1,0:T(8,128)(2,1)S(1)}, bf16[16,2048]{1,0:T(8,128)(2,1)S(1)}, u32[]{:S(2)}, u32[]{:S(2)}) %collective-permute-start.5) | collective-permute-done | bytes 65568 | tf_op jit(solution)/shard_map/ppermute | solution.py:118
  22.1 1.5 %collective-permute-done.4 = bf16[16,2048]{1,0:T(8,128)(2,1)S(1)} collective-permute-done((bf16[16,2048]{1,0:T(8,128)(2,1)S(1)}, bf16[16,2048]{1,0:T(8,128)(2,1)S(1)}, u32[]{:S(2)}, u32[]{:S(2)}) %collective-permute-start.4) | collective-permute-done | bytes 65568 | tf_op jit(solution)/shard_map/ppermute | solution.py:118
  23.7 1.4 %collective-permute-done.6 = bf16[64,2048]{1,0:T(8,128)(2,1)S(1)} collective-permute-done((bf16[64,2048]{1,0:T(8,128)(2,1)S(1)}, bf16[64,2048]{1,0:T(8,128)(2,1)S(1)}, u32[]{:S(2)}, u32[]{:S(2)}) %collective-permute-start.6) | collective-permute-done | bytes 262176 | tf_op jit(solution)/shard_map/ppermute | solution.py:119
  25.4 0.3 copy.114
  25.7 0.4 slice.56
  26.1 0.4 stack.40
  26.5 0.4 %copy.72 = bf16[16,64,2,16]{1,0,2,3:T(8,128)(2,1)S(1)} copy(bf16[16,64,2,16]{3,2,1,0:T(2,128)(2,1)S(1)} %slice.56) | data formatting | bytes 131072 | tf_op jit(solution)/shard_map/slice | solution.py:156
  26.9 0.4 %copy.73 = bf16[1,16,64,2,16]{2,1,3,0,4:T(8,128)(2,1)S(1)} copy(bf16[1,16,64,2,16]{4,3,2,1,0:T(2,128)(2,1)S(1)} %stack.40) | data formatting | bytes 131072 | tf_op jit(solution)/shard_map/stack | solution.py:159
  27.4 0.1 concatenate.27.clone
  27.6 0.7 %convolution_bitcast_fusion = f32[16,2,16,144]{3,2,1,0:T(8,128)S(1)} fusion(bf16[144,64,2,16,1]{0,3,2,1,4:T(8,128)(2,1)S(1)} %bitcast.81, bf16[1,16,64,2,16]{2,1,3,0,4:T(8,128)(2,1)S(1)} %multiply_bitcast_fusion.1, bf16[1,16,64,2,16]{2,1,3,0,4:T(8,128)(2,1)S(1)} %copy.73), kind=kOutput, calls=%fused_computation | convolution fusion | flops 18939904 | bytes 1015808 | tf_op jit(solution)/shard_map/ocspn,jspn->nocj/dot_general | solution.py:160
  28.3 0.6 %fusion.5 = (f32[16,2,1,128]{3,2,1,0:T(1,128)S(1)}, f32[16,2,1,128]{3,2,1,0:T(1,128)S(1)}, f32[16,2,1,128]{3,2,1,0:T(1,128)S(1)}, f32[16,2,1,128]{3,2,1,0:T(1,12...) fusion(f32[16,2,16,144]{3,2,1,0:T(8,128)S(1)} %convolution_bitc, ...), kind=kLoop, calls=%fused_computation.63 | loop fusion | bytes 524288 | tf_op jit(solution)/shard_map/slice | solution.py:161
  29.1 0.1 multiply_bitcast_fusion
  29.3 0.1 copy.115
  29.6 1.3 %collective-permute-start.9 = (f32[64,512]{1,0:T(8,128)S(1)}, f32[64,512]{1,0:T(8,128)S(1)}, u32[]{:S(2)}, u32[]{:S(2)}) collective-permute-start(f32[64,512]{1,0:T(8,128)S(1)} %get-tuple-element.18), channel_id=1, source_target_pairs={{8,0},{16,8},{9,1},{17,9},{10,2},{18,10},{11,3},{19,11},{12,4},{20... | collective-permute-start | bytes 393224 | tf_op jit(solution)/shard_map/ppermute | solution.py:173
  30.9 1.3 %collective-permute-start.8 = (f32[64,512]{1,0:T(8,128)S(1)}, f32[64,512]{1,0:T(8,128)S(1)}, u32[]{:S(2)}, u32[]{:S(2)}) collective-permute-start(f32[64,512]{1,0:T(8,128)S(1)} %get-tuple-element.19), channel_id=1, source_target_pairs={{16,0},{24,8},{17,1},{25,9},{18,2},{26,10},{19,3},{27,11},{20,4},{... | collective-permute-start | bytes 393224 | tf_op jit(solution)/shard_map/ppermute | solution.py:173
  32.2 4.6 %collective-permute-start.7 = (f32[64,512]{1,0:T(8,128)S(1)}, f32[64,512]{1,0:T(8,128)S(1)}, u32[]{:S(2)}, u32[]{:S(2)}) collective-permute-start(f32[64,512]{1,0:T(8,128)S(1)} %get-tuple-element.20), channel_id=1, source_target_pairs={{0,8},{24,0},{1,9},{25,1},{2,10},{26,2},{3,11},{27,3},{4,12},{28,4... | collective-permute-start | bytes 393224 | tf_op jit(solution)/shard_map/ppermute | solution.py:173
  36.8 0.2 collective-permute-done.9
  37.0 4.9 %collective-permute-done.8 = f32[64,512]{1,0:T(8,128)S(1)} collective-permute-done((f32[64,512]{1,0:T(8,128)S(1)}, f32[64,512]{1,0:T(8,128)S(1)}, u32[]{:S(2)}, u32[]{:S(2)}) %collective-permute-start.8) | collective-permute-done | bytes 131104 | tf_op jit(solution)/shard_map/ppermute | solution.py:173
  41.9 0.1 pad_maximum_fusion
  42.1 0.6 %copy.93 = f32[8,64,512]{1,2,0:T(8,128)S(1)} copy(f32[8,64,512]{2,1,0:T(8,128)S(1)} %pad_maximum_fusion) | data formatting | bytes 2097152 | tf_op jit(solution)/shard_map/concatenate | solution.py:178
  42.8 0.1 pad_maximum_fusion.1
  42.9 1.1 %copy.94 = f32[64,16,128]{2,1,0:T(8,128)} copy(f32[64,16,128]{0,2,1:T(8,128)S(1)} %bitcast.82) | data formatting | bytes 1048576 | tf_op jit(solution)/shard_map/reshape | solution.py:182
  (46 shorter events, 0.8 us)
Async XLA Ops:
  5.5 6.7 %collective-permute-start = (bf16[16,512]{1,0:T(8,128)(2,1)}, bf16[16,512]{1,0:T(8,128)(2,1)S(1)}, u32[]{:S(2)}, u32[]{:S(2)}) collective-permute-start(bf16[16,512]{1,0:T(8,128)(2,1)} %get-tuple-element.10), channel_id=1, source_target_pairs={{0,8},{8,16},{16,24},{24,0},{1,9},{9,17},{17,25},{25,1},{2,10},{10... | collective-permute-start | bytes 49160 | tf_op jit(solution)/shard_map/ppermute | solution.py:147
  8.5 3.9 %collective-permute-start.1 = (bf16[16,512]{1,0:T(8,128)(2,1)}, bf16[16,512]{1,0:T(8,128)(2,1)S(1)}, u32[]{:S(2)}, u32[]{:S(2)}) collective-permute-start(bf16[16,512]{1,0:T(8,128)(2,1)} %get-tuple-element.11), channel_id=1, source_target_pairs={{0,16},{8,24},{16,0},{24,8},{1,17},{9,25},{17,1},{25,9},{2,18},{10... | collective-permute-start | bytes 49160 | tf_op jit(solution)/shard_map/ppermute | solution.py:147
  10.1 3.9 %collective-permute-start.2 = (bf16[16,512]{1,0:T(8,128)(2,1)}, bf16[16,512]{1,0:T(8,128)(2,1)S(1)}, u32[]{:S(2)}, u32[]{:S(2)}) collective-permute-start(bf16[16,512]{1,0:T(8,128)(2,1)} %get-tuple-element.12), channel_id=1, source_target_pairs={{0,24},{8,0},{16,8},{24,16},{1,25},{9,1},{17,9},{25,17},{2,26},{10... | collective-permute-start | bytes 49160 | tf_op jit(solution)/shard_map/ppermute | solution.py:147
  14.0 8.0 %collective-permute-start.5 = (bf16[16,2048]{1,0:T(8,128)(2,1)S(1)}, bf16[16,2048]{1,0:T(8,128)(2,1)S(1)}, u32[]{:S(2)}, u32[]{:S(2)}) collective-permute-start(bf16[16,2048]{1,0:T(8,128)(2,1)S(1)} %get-tuple-element.43), channel_id=1, source_target_pairs={{6,0},{7,1},{14,8},{15,9},{22,16},{23,17},{30,24},{31,25}} | collective-permute-start | bytes 196616 | tf_op jit(solution)/shard_map/ppermute | solution.py:118
  15.3 8.2 %collective-permute-start.4 = (bf16[16,2048]{1,0:T(8,128)(2,1)S(1)}, bf16[16,2048]{1,0:T(8,128)(2,1)S(1)}, u32[]{:S(2)}, u32[]{:S(2)}) collective-permute-start(bf16[16,2048]{1,0:T(8,128)(2,1)S(1)} %get-tuple-element.43), channel_id=1, source_target_pairs={{4,0},{5,1},{6,2},{7,3},{12,8},{13,9},{14,10},{15,11},{20,16},{21,... | collective-permute-start | bytes 196616 | tf_op jit(solution)/shard_map/ppermute | solution.py:118
  16.6 7.0 %collective-permute-start.3 = (bf16[16,2048]{1,0:T(8,128)(2,1)S(1)}, bf16[16,2048]{1,0:T(8,128)(2,1)S(1)}, u32[]{:S(2)}, u32[]{:S(2)}) collective-permute-start(bf16[16,2048]{1,0:T(8,128)(2,1)S(1)} %get-tuple-element.43), channel_id=1, source_target_pairs={{2,0},{3,1},{4,2},{5,3},{6,4},{7,5},{10,8},{11,9},{12,10},{13,11},... | collective-permute-start | bytes 196616 | tf_op jit(solution)/shard_map/ppermute | solution.py:118
  23.6 1.6 %collective-permute-start.6 = (bf16[64,2048]{1,0:T(8,128)(2,1)S(1)}, bf16[64,2048]{1,0:T(8,128)(2,1)S(1)}, u32[]{:S(2)}, u32[]{:S(2)}) collective-permute-start(bf16[64,2048]{1,0:T(8,128)(2,1)S(1)} %pad_maximum_fusion.3), channel_id=1, source_target_pairs={{0,1},{1,0},{2,3},{3,2},{4,5},{5,4},{6,7},{7,6},{8,9},{9,8},{10,11... | collective-permute-start | bytes 786440 | tf_op jit(solution)/shard_map/ppermute | solution.py:119
  25.7 1.8 %copy-start = (bf16[2]{0:T(256)(128)(2,1)S(1)}, bf16[2]{0:T(256)(128)(2,1)}, u32[]{:S(2)}) copy-start(bf16[2]{0:T(256)(128)(2,1)} %constant.89.clone) | copy-start | bytes 16
  29.6 7.4 %collective-permute-start.9 = (f32[64,512]{1,0:T(8,128)S(1)}, f32[64,512]{1,0:T(8,128)S(1)}, u32[]{:S(2)}, u32[]{:S(2)}) collective-permute-start(f32[64,512]{1,0:T(8,128)S(1)} %get-tuple-element.18), channel_id=1, source_target_pairs={{8,0},{16,8},{9,1},{17,9},{10,2},{18,10},{11,3},{19,11},{12,4},{20... | collective-permute-start | bytes 393224 | tf_op jit(solution)/shard_map/ppermute | solution.py:173
  30.9 11.0 %collective-permute-start.8 = (f32[64,512]{1,0:T(8,128)S(1)}, f32[64,512]{1,0:T(8,128)S(1)}, u32[]{:S(2)}, u32[]{:S(2)}) collective-permute-start(f32[64,512]{1,0:T(8,128)S(1)} %get-tuple-element.19), channel_id=1, source_target_pairs={{16,0},{24,8},{17,1},{25,9},{18,2},{26,10},{19,3},{27,11},{20,4},{... | collective-permute-start | bytes 393224 | tf_op jit(solution)/shard_map/ppermute | solution.py:173
  32.2 9.7 %collective-permute-start.7 = (f32[64,512]{1,0:T(8,128)S(1)}, f32[64,512]{1,0:T(8,128)S(1)}, u32[]{:S(2)}, u32[]{:S(2)}) collective-permute-start(f32[64,512]{1,0:T(8,128)S(1)} %get-tuple-element.20), channel_id=1, source_target_pairs={{0,8},{24,0},{1,9},{25,1},{2,10},{26,2},{3,11},{27,3},{4,12},{28,4... | collective-permute-start | bytes 393224 | tf_op jit(solution)/shard_map/ppermute | solution.py:173

commit v19 on v18

--- a/solution.py
+++ b/solution.py
@@ -156,8 +156,10 @@
     own = right[:block]
     sign = jnp.asarray([1.0, -1.0], own.dtype)[None, None, :, None]
     turned = jnp.flip(own, axis=2) * sign
-    left = jnp.stack([own, turned])
-    cross = jnp.einsum("ocspn,jspn->nocj", left, right, preferred_element_type=jnp.float32)
+    cross = jnp.stack(
+        [jnp.einsum("cspn,jspn->ncj", part, right, preferred_element_type=jnp.float32) for part in (own, turned)],
+        axis=1,
+    )
     band = jnp.stack([cross[:, :, c, c + 1 : c + 1 + kept] for c in range(block)])
     band = band.transpose(3, 0, 2, 1) * (1.0 / math.sqrt(seg_count * windows_count))
     band = band.reshape(kept, block * 2 * bins_each)

time: 44.4 us -> 44.4 us (level)
  local copies, waits for them, and re-layouts: 5.76 us -> 4.55 us
  matrix products: 0.72 us -> 1.38 us
  other arithmetic: 0.56 us -> 1.13 us
    another operation x2 -> x0, local copies, waits for them, and re-layouts: 0.83 us -> none  [shards(): left = jnp.stack([own, turned])]
    dot_general x1 -> x2, matrix products: 0.72 us -> 1.38 us  [shards(): jnp.einsum('cspn,jspn->ncj', part, right, preferred_element_type=jnp.floa...]
    slice x1 -> x0, local copies, waits for them, and re-layouts: 0.61 us -> none  [shards(): band = jnp.stack([cross[:, :, c, c + 1:c + 1 + kept] for c in range(block)])]
    slice x3 -> x4, local copies, waits for them, and re-layouts: 0.84 us -> 1.18 us  [shards(): own = right[:block]]
    unnamed x31 -> x30, local copies, waits for them, and re-layouts: 1.37 us -> 1.16 us
where the time goes in v19:
time: 44.4 us; the launch traced here: 44.1 us
  starting transfers between devices  17 us (38%)
  waiting for transfers between devices  14 us (32%)
  Pallas kernels  5.53 us (12%)
  local copies, waits for them, and re-layouts  4.55 us (10%)
  matrix products  1.38 us (3%)
  other arithmetic  1.13 us (3%)
  between operations  0.53 us (1%)
    ppermute x3, starting transfers between devices, shards(): collected.append(lax.ppermute(sent, 'seg', pairs))  7.13 us
    ppermute x3, starting transfers between devices, shards(): gathered.append(lax.ppermute(split[step], 'seg', pairs))  5.94 us
    ppermute x3, waiting for transfers between devices, halo(): own.append(lax.ppermute(mine, 'fibre', pairs))  5.65 us
    pallas_call x1, Pallas kernels, whiten(): pl.pallas_call(whiten_kernel, out_shape=[jax.ShapeDtypeStruct((channels,...  5.53 us
    ppermute x3, waiting for transfers between devices, shards(): collected.append(lax.ppermute(sent, 'seg', pairs))  5.11 us
    ppermute x3, starting transfers between devices, halo(): own.append(lax.ppermute(mine, 'fibre', pairs))  3.86 us
    ppermute x3, waiting for transfers between devices, shards(): gathered.append(lax.ppermute(split[step], 'seg', pairs))  1.79 us
    ppermute x1, waiting for transfers between devices, halo(): lax.ppermute(jnp.concatenate(own, axis=0), 'fibre', [(i, i ^ 1) for i in...  1.42 us
  transfers between devices with their start and end apart: 10, of which 7 were waited for; matrix products, arithmetic and copies ran while one was open for 2% of the time, Pallas kernels for 0%

profile of v19, /device:TPU:0, one launch (start us, length us, event | category | flops | bytes accessed | tf_op | source)
XLA Modules:
  0.0 44.1 jit_solution(16185295898209662858)
XLA Ops:
  0.0 5.5 %shard_map.73 = (bf16[16,512]{1,0:T(8,128)(2,1)}, bf16[16,512]{1,0:T(8,128)(2,1)}, bf16[16,512]{1,0:T(8,128)(2,1)}, bf16[16,512]{1,0:T(8,128)(2,1)}) custom-call(s32[16]{0:T(128)} %bitcast.108, s32[1]{0:T(128)} %bitcast.1.place_ref, s32[16]{0:T(128)} %live_ref.1, bf16[16,27648]{1,0:T(8,128)(2,1)} %bitcast.88, bf16[3072,128]{1,0:T(8,128)(2,1)} %constant.86.clone.table_ref, ...), custom_call_target="tpu_custom_call" | custom-call | tf_op jit(solution)/shard_map/pallas_call | solution.py:94
  5.5 3.0 %collective-permute-start = (bf16[16,512]{1,0:T(8,128)(2,1)}, bf16[16,512]{1,0:T(8,128)(2,1)S(1)}, u32[]{:S(2)}, u32[]{:S(2)}) collective-permute-start(bf16[16,512]{1,0:T(8,128)(2,1)} %get-tuple-element.10), channel_id=1, source_target_pairs={{0,8},{8,16},{16,24},{24,0},{1,9},{9,17},{17,25},{25,1},{2,10},{10... | collective-permute-start | bytes 49160 | tf_op jit(solution)/shard_map/ppermute | solution.py:147
  8.5 1.5 %collective-permute-start.1 = (bf16[16,512]{1,0:T(8,128)(2,1)}, bf16[16,512]{1,0:T(8,128)(2,1)S(1)}, u32[]{:S(2)}, u32[]{:S(2)}) collective-permute-start(bf16[16,512]{1,0:T(8,128)(2,1)} %get-tuple-element.11), channel_id=1, source_target_pairs={{0,16},{8,24},{16,0},{24,8},{1,17},{9,25},{17,1},{25,9},{2,18},{10... | collective-permute-start | bytes 49160 | tf_op jit(solution)/shard_map/ppermute | solution.py:147
  10.1 1.4 %collective-permute-start.2 = (bf16[16,512]{1,0:T(8,128)(2,1)}, bf16[16,512]{1,0:T(8,128)(2,1)S(1)}, u32[]{:S(2)}, u32[]{:S(2)}) collective-permute-start(bf16[16,512]{1,0:T(8,128)(2,1)} %get-tuple-element.12), channel_id=1, source_target_pairs={{0,24},{8,0},{16,8},{24,16},{1,25},{9,1},{17,9},{25,17},{2,26},{10... | collective-permute-start | bytes 49160 | tf_op jit(solution)/shard_map/ppermute | solution.py:147
  11.5 0.7 %constant_dynamic-update-slice_fusion.3 = (bf16[16,2048]{1,0:T(8,128)(2,1)S(1)}, bf16[128,2048]{1,0:T(8,128)(2,1)S(1)}) fusion(bf16[16,512]{1,0:T(8,128)(2,1)} %get-tuple-element.9), kind=kLoop, calls=%fused_computation.22 | loop fusion | bytes 49152
  12.2 0.3 collective-permute-done.1
  12.5 1.5 %collective-permute-done.2 = bf16[16,512]{1,0:T(8,128)(2,1)S(1)} collective-permute-done((bf16[16,512]{1,0:T(8,128)(2,1)}, bf16[16,512]{1,0:T(8,128)(2,1)S(1)}, u32[]{:S(2)}, u32[]{:S(2)}) %collective-permute-start.2) | collective-permute-done | bytes 16416 | tf_op jit(solution)/shard_map/ppermute | solution.py:147
  14.0 1.3 %collective-permute-start.5 = (bf16[16,2048]{1,0:T(8,128)(2,1)S(1)}, bf16[16,2048]{1,0:T(8,128)(2,1)S(1)}, u32[]{:S(2)}, u32[]{:S(2)}) collective-permute-start(bf16[16,2048]{1,0:T(8,128)(2,1)S(1)} %get-tuple-element.43), channel_id=1, source_target_pairs={{6,0},{7,1},{14,8},{15,9},{22,16},{23,17},{30,24},{31,25}} | collective-permute-start | bytes 196616 | tf_op jit(solution)/shard_map/ppermute | solution.py:118
  15.3 1.3 %collective-permute-start.4 = (bf16[16,2048]{1,0:T(8,128)(2,1)S(1)}, bf16[16,2048]{1,0:T(8,128)(2,1)S(1)}, u32[]{:S(2)}, u32[]{:S(2)}) collective-permute-start(bf16[16,2048]{1,0:T(8,128)(2,1)S(1)} %get-tuple-element.43), channel_id=1, source_target_pairs={{4,0},{5,1},{6,2},{7,3},{12,8},{13,9},{14,10},{15,11},{20,16},{21,... | collective-permute-start | bytes 196616 | tf_op jit(solution)/shard_map/ppermute | solution.py:118
  16.6 1.3 %collective-permute-start.3 = (bf16[16,2048]{1,0:T(8,128)(2,1)S(1)}, bf16[16,2048]{1,0:T(8,128)(2,1)S(1)}, u32[]{:S(2)}, u32[]{:S(2)}) collective-permute-start(bf16[16,2048]{1,0:T(8,128)(2,1)S(1)} %get-tuple-element.43), channel_id=1, source_target_pairs={{2,0},{3,1},{4,2},{5,3},{6,4},{7,5},{10,8},{11,9},{12,10},{13,11},... | collective-permute-start | bytes 196616 | tf_op jit(solution)/shard_map/ppermute | solution.py:118
  17.9 4.2 %collective-permute-done.5 = bf16[16,2048]{1,0:T(8,128)(2,1)S(1)} collective-permute-done((bf16[16,2048]{1,0:T(8,128)(2,1)S(1)}, bf16[16,2048]{1,0:T(8,128)(2,1)S(1)}, u32[]{:S(2)}, u32[]{:S(2)}) %collective-permute-start.5) | collective-permute-done | bytes 65568 | tf_op jit(solution)/shard_map/ppermute | solution.py:118
  22.1 1.5 %collective-permute-done.4 = bf16[16,2048]{1,0:T(8,128)(2,1)S(1)} collective-permute-done((bf16[16,2048]{1,0:T(8,128)(2,1)S(1)}, bf16[16,2048]{1,0:T(8,128)(2,1)S(1)}, u32[]{:S(2)}, u32[]{:S(2)}) %collective-permute-start.4) | collective-permute-done | bytes 65568 | tf_op jit(solution)/shard_map/ppermute | solution.py:118
  23.8 1.4 %collective-permute-done.6 = bf16[64,2048]{1,0:T(8,128)(2,1)S(1)} collective-permute-done((bf16[64,2048]{1,0:T(8,128)(2,1)S(1)}, bf16[64,2048]{1,0:T(8,128)(2,1)S(1)}, u32[]{:S(2)}, u32[]{:S(2)}) %collective-permute-start.6) | collective-permute-done | bytes 262176 | tf_op jit(solution)/shard_map/ppermute | solution.py:119
  25.4 0.3 copy.95
  25.7 0.4 slice.56
  26.1 0.3 copy.57
  26.4 0.4 %copy.55 = bf16[16,64,2,16]{1,0,2,3:T(8,128)(2,1)S(1)} copy(bf16[16,64,2,16]{3,2,1,0:T(2,128)(2,1)S(1)} %slice.56) | data formatting | bytes 131072 | tf_op jit(solution)/shard_map/slice | solution.py:156
  27.0 0.1 concatenate.27.clone
  27.1 0.7 %convolution_bitcast_fusion = f32[16,1,16,144]{3,2,0,1:T(8,128)S(1)} fusion(bf16[144,64,2,16]{0,3,2,1:T(8,128)(2,1)S(1)} %bitcast.82, bf16[16,64,2,16]{1,3,2,0:T(8,128)(2,1)S(1)} %reverse_multiply_fusion), kind=kOutput, calls=%fused_computation | convolution fusion | flops 9437184 | bytes 802816 | tf_op jit(solution)/shard_map/cspn,jspn->ncj/dot_general | solution.py:160
  27.8 0.7 %convolution_bitcast_fusion.1 = f32[16,1,16,144]{3,2,0,1:T(8,128)S(1)} fusion(bf16[16,64,2,16]{1,0,2,3:T(8,128)(2,1)S(1)} %copy.55, bf16[144,64,2,16]{0,3,2,1:T(8,128)(2,1)S(1)} %bitcast.83), kind=kOutput, calls=%fused_computation.1 | convolution fusion | flops 9437184 | bytes 802816 | tf_op jit(solution)/shard_map/cspn,jspn->ncj/dot_general | solution.py:160
  28.5 0.3 pad_maximum_fusion.13
  28.8 0.4 pad_maximum_fusion.4
  29.4 0.1 copy.75
  29.6 1.3 %collective-permute-start.9 = (f32[64,512]{1,0:T(8,128)S(1)}, f32[64,512]{1,0:T(8,128)S(1)}, u32[]{:S(2)}, u32[]{:S(2)}) collective-permute-start(f32[64,512]{1,0:T(8,128)S(1)} %get-tuple-element.18), channel_id=1, source_target_pairs={{8,0},{16,8},{9,1},{17,9},{10,2},{18,10},{11,3},{19,11},{12,4},{20... | collective-permute-start | bytes 393224 | tf_op jit(solution)/shard_map/ppermute | solution.py:175
  30.9 1.3 %collective-permute-start.8 = (f32[64,512]{1,0:T(8,128)S(1)}, f32[64,512]{1,0:T(8,128)S(1)}, u32[]{:S(2)}, u32[]{:S(2)}) collective-permute-start(f32[64,512]{1,0:T(8,128)S(1)} %get-tuple-element.19), channel_id=1, source_target_pairs={{16,0},{24,8},{17,1},{25,9},{18,2},{26,10},{19,3},{27,11},{20,4},{... | collective-permute-start | bytes 393224 | tf_op jit(solution)/shard_map/ppermute | solution.py:175
  32.2 4.6 %collective-permute-start.7 = (f32[64,512]{1,0:T(8,128)S(1)}, f32[64,512]{1,0:T(8,128)S(1)}, u32[]{:S(2)}, u32[]{:S(2)}) collective-permute-start(f32[64,512]{1,0:T(8,128)S(1)} %get-tuple-element.20), channel_id=1, source_target_pairs={{0,8},{24,0},{1,9},{25,1},{2,10},{26,2},{3,11},{27,3},{4,12},{28,4... | collective-permute-start | bytes 393224 | tf_op jit(solution)/shard_map/ppermute | solution.py:175
  36.8 0.2 collective-permute-done.9
  37.1 4.9 %collective-permute-done.8 = f32[64,512]{1,0:T(8,128)S(1)} collective-permute-done((f32[64,512]{1,0:T(8,128)S(1)}, f32[64,512]{1,0:T(8,128)S(1)}, u32[]{:S(2)}, u32[]{:S(2)}) %collective-permute-start.8) | collective-permute-done | bytes 131104 | tf_op jit(solution)/shard_map/ppermute | solution.py:175
  42.0 0.1 pad_maximum_fusion
  42.1 0.6 %copy.76 = f32[8,64,512]{1,2,0:T(8,128)S(1)} copy(f32[8,64,512]{2,1,0:T(8,128)S(1)} %pad_maximum_fusion) | data formatting | bytes 2097152 | tf_op jit(solution)/shard_map/concatenate | solution.py:180
  42.8 0.1 pad_maximum_fusion.1
  43.0 1.1 %copy.77 = f32[64,16,128]{2,1,0:T(8,128)} copy(f32[64,16,128]{0,2,1:T(8,128)S(1)} %bitcast.85) | data formatting | bytes 1048576 | tf_op jit(solution)/shard_map/reshape | solution.py:184
  (46 shorter events, 0.7 us)
Async XLA Ops:
  5.5 6.7 %collective-permute-start = (bf16[16,512]{1,0:T(8,128)(2,1)}, bf16[16,512]{1,0:T(8,128)(2,1)S(1)}, u32[]{:S(2)}, u32[]{:S(2)}) collective-permute-start(bf16[16,512]{1,0:T(8,128)(2,1)} %get-tuple-element.10), channel_id=1, source_target_pairs={{0,8},{8,16},{16,24},{24,0},{1,9},{9,17},{17,25},{25,1},{2,10},{10... | collective-permute-start | bytes 49160 | tf_op jit(solution)/shard_map/ppermute | solution.py:147
  8.5 3.9 %collective-permute-start.1 = (bf16[16,512]{1,0:T(8,128)(2,1)}, bf16[16,512]{1,0:T(8,128)(2,1)S(1)}, u32[]{:S(2)}, u32[]{:S(2)}) collective-permute-start(bf16[16,512]{1,0:T(8,128)(2,1)} %get-tuple-element.11), channel_id=1, source_target_pairs={{0,16},{8,24},{16,0},{24,8},{1,17},{9,25},{17,1},{25,9},{2,18},{10... | collective-permute-start | bytes 49160 | tf_op jit(solution)/shard_map/ppermute | solution.py:147
  10.1 3.9 %collective-permute-start.2 = (bf16[16,512]{1,0:T(8,128)(2,1)}, bf16[16,512]{1,0:T(8,128)(2,1)S(1)}, u32[]{:S(2)}, u32[]{:S(2)}) collective-permute-start(bf16[16,512]{1,0:T(8,128)(2,1)} %get-tuple-element.12), channel_id=1, source_target_pairs={{0,24},{8,0},{16,8},{24,16},{1,25},{9,1},{17,9},{25,17},{2,26},{10... | collective-permute-start | bytes 49160 | tf_op jit(solution)/shard_map/ppermute | solution.py:147
  14.0 8.0 %collective-permute-start.5 = (bf16[16,2048]{1,0:T(8,128)(2,1)S(1)}, bf16[16,2048]{1,0:T(8,128)(2,1)S(1)}, u32[]{:S(2)}, u32[]{:S(2)}) collective-permute-start(bf16[16,2048]{1,0:T(8,128)(2,1)S(1)} %get-tuple-element.43), channel_id=1, source_target_pairs={{6,0},{7,1},{14,8},{15,9},{22,16},{23,17},{30,24},{31,25}} | collective-permute-start | bytes 196616 | tf_op jit(solution)/shard_map/ppermute | solution.py:118
  15.3 8.2 %collective-permute-start.4 = (bf16[16,2048]{1,0:T(8,128)(2,1)S(1)}, bf16[16,2048]{1,0:T(8,128)(2,1)S(1)}, u32[]{:S(2)}, u32[]{:S(2)}) collective-permute-start(bf16[16,2048]{1,0:T(8,128)(2,1)S(1)} %get-tuple-element.43), channel_id=1, source_target_pairs={{4,0},{5,1},{6,2},{7,3},{12,8},{13,9},{14,10},{15,11},{20,16},{21,... | collective-permute-start | bytes 196616 | tf_op jit(solution)/shard_map/ppermute | solution.py:118
  16.6 7.0 %collective-permute-start.3 = (bf16[16,2048]{1,0:T(8,128)(2,1)S(1)}, bf16[16,2048]{1,0:T(8,128)(2,1)S(1)}, u32[]{:S(2)}, u32[]{:S(2)}) collective-permute-start(bf16[16,2048]{1,0:T(8,128)(2,1)S(1)} %get-tuple-element.43), channel_id=1, source_target_pairs={{2,0},{3,1},{4,2},{5,3},{6,4},{7,5},{10,8},{11,9},{12,10},{13,11},... | collective-permute-start | bytes 196616 | tf_op jit(solution)/shard_map/ppermute | solution.py:118
  23.6 1.6 %collective-permute-start.6 = (bf16[64,2048]{1,0:T(8,128)(2,1)S(1)}, bf16[64,2048]{1,0:T(8,128)(2,1)S(1)}, u32[]{:S(2)}, u32[]{:S(2)}) collective-permute-start(bf16[64,2048]{1,0:T(8,128)(2,1)S(1)} %pad_maximum_fusion.3), channel_id=1, source_target_pairs={{0,1},{1,0},{2,3},{3,2},{4,5},{5,4},{6,7},{7,6},{8,9},{9,8},{10,11... | collective-permute-start | bytes 786440 | tf_op jit(solution)/shard_map/ppermute | solution.py:119
  25.3 1.6 %copy-start = (bf16[2]{0:T(256)(128)(2,1)S(1)}, bf16[2]{0:T(256)(128)(2,1)}, u32[]{:S(2)}) copy-start(bf16[2]{0:T(256)(128)(2,1)} %constant.89.clone) | copy-start | bytes 16
  29.6 7.4 %collective-permute-start.9 = (f32[64,512]{1,0:T(8,128)S(1)}, f32[64,512]{1,0:T(8,128)S(1)}, u32[]{:S(2)}, u32[]{:S(2)}) collective-permute-start(f32[64,512]{1,0:T(8,128)S(1)} %get-tuple-element.18), channel_id=1, source_target_pairs={{8,0},{16,8},{9,1},{17,9},{10,2},{18,10},{11,3},{19,11},{12,4},{20... | collective-permute-start | bytes 393224 | tf_op jit(solution)/shard_map/ppermute | solution.py:175
  30.9 11.0 %collective-permute-start.8 = (f32[64,512]{1,0:T(8,128)S(1)}, f32[64,512]{1,0:T(8,128)S(1)}, u32[]{:S(2)}, u32[]{:S(2)}) collective-permute-start(f32[64,512]{1,0:T(8,128)S(1)} %get-tuple-element.19), channel_id=1, source_target_pairs={{16,0},{24,8},{17,1},{25,9},{18,2},{26,10},{19,3},{27,11},{20,4},{... | collective-permute-start | bytes 393224 | tf_op jit(solution)/shard_map/ppermute | solution.py:175
  32.2 9.7 %collective-permute-start.7 = (f32[64,512]{1,0:T(8,128)S(1)}, f32[64,512]{1,0:T(8,128)S(1)}, u32[]{:S(2)}, u32[]{:S(2)}) collective-permute-start(f32[64,512]{1,0:T(8,128)S(1)} %get-tuple-element.20), channel_id=1, source_target_pairs={{0,8},{24,0},{1,9},{25,1},{2,10},{26,2},{3,11},{27,3},{4,12},{28,4... | collective-permute-start | bytes 393224 | tf_op jit(solution)/shard_map/ppermute | solution.py:175

commit v20 on v18

--- a/solution.py
+++ b/solution.py
@@ -179,7 +179,7 @@
     doubled = doubled.reshape(2 * seg_count, per_owner, block, 2, bins_each)
     start = (seg_count - me) % seg_count
     by_bins = [lax.dynamic_index_in_dim(doubled, start + b, 0, keepdims=False) for b in range(seg_count)]
-    return jnp.stack(by_bins, axis=3).reshape(per_owner, block, 2 * NF)
+    return jnp.concatenate([part[:, :, o] for o in range(2) for part in by_bins], axis=-1)
 
 
 def solution(mesh):

time: 44.4 us -> 44.4 us (level)
    concatenate x0 -> x2, local copies, waits for them, and re-layouts: none -> 1.15 us  [shards(): jnp.concatenate([part[:, :, o] for o in range(2) for part in by_bins], ax...]
    reshape x1 -> x0, local copies, waits for them, and re-layouts: 1.14 us -> none  [shards(): return jnp.stack(by_bins, axis=3).reshape(per_owner, block, 2 * NF)]
    unnamed x31 -> x38, local copies, waits for them, and re-layouts: 1.37 us -> 1.44 us
where the time goes in v20:
time: 44.4 us; the launch traced here: 44.1 us
  starting transfers between devices  17 us (38%)
  waiting for transfers between devices  14 us (32%)
  local copies, waits for them, and re-layouts  5.85 us (13%)
  Pallas kernels  5.53 us (12%)
  matrix products  0.72 us (2%)
  between operations  0.53 us (1%)
  other arithmetic  0.45 us (1%)
    ppermute x3, starting transfers between devices, shards(): collected.append(lax.ppermute(sent, 'seg', pairs))  7.13 us
    ppermute x3, starting transfers between devices, shards(): gathered.append(lax.ppermute(split[step], 'seg', pairs))  5.94 us
    ppermute x3, waiting for transfers between devices, halo(): own.append(lax.ppermute(mine, 'fibre', pairs))  5.65 us
    pallas_call x1, Pallas kernels, whiten(): pl.pallas_call(whiten_kernel, out_shape=[jax.ShapeDtypeStruct((channels,...  5.53 us
    ppermute x3, waiting for transfers between devices, shards(): collected.append(lax.ppermute(sent, 'seg', pairs))  5.11 us
    ppermute x3, starting transfers between devices, halo(): own.append(lax.ppermute(mine, 'fibre', pairs))  3.86 us
    ppermute x3, waiting for transfers between devices, shards(): gathered.append(lax.ppermute(split[step], 'seg', pairs))  1.79 us
    unnamed x38, local copies, waits for them, and re-layouts  1.44 us
  transfers between devices with their start and end apart: 10, of which 7 were waited for; matrix products, arithmetic and copies ran while one was open for 2% of the time, Pallas kernels for 0%

profile of v20, /device:TPU:0, one launch (start us, length us, event | category | flops | bytes accessed | tf_op | source)
XLA Modules:
  0.0 44.1 jit_solution(6261066551723350231)
XLA Ops:
  0.0 5.5 %shard_map.73 = (bf16[16,512]{1,0:T(8,128)(2,1)}, bf16[16,512]{1,0:T(8,128)(2,1)}, bf16[16,512]{1,0:T(8,128)(2,1)}, bf16[16,512]{1,0:T(8,128)(2,1)}) custom-call(s32[16]{0:T(128)} %bitcast.149, s32[1]{0:T(128)} %bitcast.1.place_ref, s32[16]{0:T(128)} %live_ref.1, bf16[16,27648]{1,0:T(8,128)(2,1)} %bitcast.129, bf16[3072,128]{1,0:T(8,128)(2,1)} %constant.86.clone.table_ref, ...), custom_call_target="tpu_custom_call" | custom-call | tf_op jit(solution)/shard_map/pallas_call | solution.py:94
  5.5 3.0 %collective-permute-start = (bf16[16,512]{1,0:T(8,128)(2,1)}, bf16[16,512]{1,0:T(8,128)(2,1)S(1)}, u32[]{:S(2)}, u32[]{:S(2)}) collective-permute-start(bf16[16,512]{1,0:T(8,128)(2,1)} %get-tuple-element.10), channel_id=1, source_target_pairs={{0,8},{8,16},{16,24},{24,0},{1,9},{9,17},{17,25},{25,1},{2,10},{10... | collective-permute-start | bytes 49160 | tf_op jit(solution)/shard_map/ppermute | solution.py:147
  8.5 1.5 %collective-permute-start.1 = (bf16[16,512]{1,0:T(8,128)(2,1)}, bf16[16,512]{1,0:T(8,128)(2,1)S(1)}, u32[]{:S(2)}, u32[]{:S(2)}) collective-permute-start(bf16[16,512]{1,0:T(8,128)(2,1)} %get-tuple-element.11), channel_id=1, source_target_pairs={{0,16},{8,24},{16,0},{24,8},{1,17},{9,25},{17,1},{25,9},{2,18},{10... | collective-permute-start | bytes 49160 | tf_op jit(solution)/shard_map/ppermute | solution.py:147
  10.1 1.4 %collective-permute-start.2 = (bf16[16,512]{1,0:T(8,128)(2,1)}, bf16[16,512]{1,0:T(8,128)(2,1)S(1)}, u32[]{:S(2)}, u32[]{:S(2)}) collective-permute-start(bf16[16,512]{1,0:T(8,128)(2,1)} %get-tuple-element.12), channel_id=1, source_target_pairs={{0,24},{8,0},{16,8},{24,16},{1,25},{9,1},{17,9},{25,17},{2,26},{10... | collective-permute-start | bytes 49160 | tf_op jit(solution)/shard_map/ppermute | solution.py:147
  11.5 0.7 %constant_dynamic-update-slice_fusion.3 = (bf16[16,2048]{1,0:T(8,128)(2,1)S(1)}, bf16[128,2048]{1,0:T(8,128)(2,1)S(1)}) fusion(bf16[16,512]{1,0:T(8,128)(2,1)} %get-tuple-element.9), kind=kLoop, calls=%fused_computation.37 | loop fusion | bytes 49152
  12.2 0.3 collective-permute-done.1
  12.5 1.5 %collective-permute-done.2 = bf16[16,512]{1,0:T(8,128)(2,1)S(1)} collective-permute-done((bf16[16,512]{1,0:T(8,128)(2,1)}, bf16[16,512]{1,0:T(8,128)(2,1)S(1)}, u32[]{:S(2)}, u32[]{:S(2)}) %collective-permute-start.2) | collective-permute-done | bytes 16416 | tf_op jit(solution)/shard_map/ppermute | solution.py:147
  14.0 1.3 %collective-permute-start.5 = (bf16[16,2048]{1,0:T(8,128)(2,1)S(1)}, bf16[16,2048]{1,0:T(8,128)(2,1)S(1)}, u32[]{:S(2)}, u32[]{:S(2)}) collective-permute-start(bf16[16,2048]{1,0:T(8,128)(2,1)S(1)} %get-tuple-element.43), channel_id=1, source_target_pairs={{6,0},{7,1},{14,8},{15,9},{22,16},{23,17},{30,24},{31,25}} | collective-permute-start | bytes 196616 | tf_op jit(solution)/shard_map/ppermute | solution.py:118
  15.3 1.3 %collective-permute-start.4 = (bf16[16,2048]{1,0:T(8,128)(2,1)S(1)}, bf16[16,2048]{1,0:T(8,128)(2,1)S(1)}, u32[]{:S(2)}, u32[]{:S(2)}) collective-permute-start(bf16[16,2048]{1,0:T(8,128)(2,1)S(1)} %get-tuple-element.43), channel_id=1, source_target_pairs={{4,0},{5,1},{6,2},{7,3},{12,8},{13,9},{14,10},{15,11},{20,16},{21,... | collective-permute-start | bytes 196616 | tf_op jit(solution)/shard_map/ppermute | solution.py:118
  16.6 1.3 %collective-permute-start.3 = (bf16[16,2048]{1,0:T(8,128)(2,1)S(1)}, bf16[16,2048]{1,0:T(8,128)(2,1)S(1)}, u32[]{:S(2)}, u32[]{:S(2)}) collective-permute-start(bf16[16,2048]{1,0:T(8,128)(2,1)S(1)} %get-tuple-element.43), channel_id=1, source_target_pairs={{2,0},{3,1},{4,2},{5,3},{6,4},{7,5},{10,8},{11,9},{12,10},{13,11},... | collective-permute-start | bytes 196616 | tf_op jit(solution)/shard_map/ppermute | solution.py:118
  17.9 4.2 %collective-permute-done.5 = bf16[16,2048]{1,0:T(8,128)(2,1)S(1)} collective-permute-done((bf16[16,2048]{1,0:T(8,128)(2,1)S(1)}, bf16[16,2048]{1,0:T(8,128)(2,1)S(1)}, u32[]{:S(2)}, u32[]{:S(2)}) %collective-permute-start.5) | collective-permute-done | bytes 65568 | tf_op jit(solution)/shard_map/ppermute | solution.py:118
  22.1 1.5 %collective-permute-done.4 = bf16[16,2048]{1,0:T(8,128)(2,1)S(1)} collective-permute-done((bf16[16,2048]{1,0:T(8,128)(2,1)S(1)}, bf16[16,2048]{1,0:T(8,128)(2,1)S(1)}, u32[]{:S(2)}, u32[]{:S(2)}) %collective-permute-start.4) | collective-permute-done | bytes 65568 | tf_op jit(solution)/shard_map/ppermute | solution.py:118
  23.7 1.4 %collective-permute-done.6 = bf16[64,2048]{1,0:T(8,128)(2,1)S(1)} collective-permute-done((bf16[64,2048]{1,0:T(8,128)(2,1)S(1)}, bf16[64,2048]{1,0:T(8,128)(2,1)S(1)}, u32[]{:S(2)}, u32[]{:S(2)}) %collective-permute-start.6) | collective-permute-done | bytes 262176 | tf_op jit(solution)/shard_map/ppermute | solution.py:119
  25.4 0.3 copy.134
  25.7 0.4 slice.80
  26.1 0.4 stack.25
  26.5 0.4 %copy.78 = bf16[16,64,2,16]{1,0,2,3:T(8,128)(2,1)S(1)} copy(bf16[16,64,2,16]{3,2,1,0:T(2,128)(2,1)S(1)} %slice.80) | data formatting | bytes 131072 | tf_op jit(solution)/shard_map/slice | solution.py:156
  26.9 0.4 %copy.79 = bf16[1,16,64,2,16]{2,1,3,0,4:T(8,128)(2,1)S(1)} copy(bf16[1,16,64,2,16]{4,3,2,1,0:T(2,128)(2,1)S(1)} %stack.25) | data formatting | bytes 131072 | tf_op jit(solution)/shard_map/stack | solution.py:159
  27.4 0.1 concatenate.30.clone
  27.6 0.7 %convolution_bitcast_fusion = f32[16,2,16,144]{3,2,1,0:T(8,128)S(1)} fusion(bf16[144,64,2,16,1]{0,3,2,1,4:T(8,128)(2,1)S(1)} %bitcast.126, bf16[1,16,64,2,16]{2,1,3,0,4:T(8,128)(2,1)S(1)} %multiply_bitcast_fusion.1, bf16[1,16,64,2,16]{2,1,3,0,4:T(8,128)(2,1)S(1)} %copy.79), kind=kOutput, calls=%fused_computation | convolution fusion | flops 18939904 | bytes 1015808 | tf_op jit(solution)/shard_map/ocspn,jspn->nocj/dot_general | solution.py:160
  28.3 0.6 %fusion.13 = (f32[16,2,1,128]{3,2,1,0:T(1,128)S(1)}, f32[16,2,1,128]{3,2,1,0:T(1,128)S(1)}, f32[16,2,1,128]{3,2,1,0:T(1,128)S(1)}, f32[16,2,1,128]{3,2,1,0:T(1,1...) fusion(f32[16,2,16,144]{3,2,1,0:T(8,128)S(1)} %convolution_bitc, ...), kind=kLoop, calls=%fused_computation.78 | loop fusion | bytes 524288 | tf_op jit(solution)/shard_map/slice | solution.py:161
  29.1 0.1 multiply_bitcast_fusion
  29.3 0.1 copy.135
  29.6 1.3 %collective-permute-start.9 = (f32[64,512]{1,0:T(8,128)S(1)}, f32[64,512]{1,0:T(8,128)S(1)}, u32[]{:S(2)}, u32[]{:S(2)}) collective-permute-start(f32[64,512]{1,0:T(8,128)S(1)} %get-tuple-element.18), channel_id=1, source_target_pairs={{8,0},{16,8},{9,1},{17,9},{10,2},{18,10},{11,3},{19,11},{12,4},{20... | collective-permute-start | bytes 393224 | tf_op jit(solution)/shard_map/ppermute | solution.py:173
  30.9 1.3 %collective-permute-start.8 = (f32[64,512]{1,0:T(8,128)S(1)}, f32[64,512]{1,0:T(8,128)S(1)}, u32[]{:S(2)}, u32[]{:S(2)}) collective-permute-start(f32[64,512]{1,0:T(8,128)S(1)} %get-tuple-element.19), channel_id=1, source_target_pairs={{16,0},{24,8},{17,1},{25,9},{18,2},{26,10},{19,3},{27,11},{20,4},{... | collective-permute-start | bytes 393224 | tf_op jit(solution)/shard_map/ppermute | solution.py:173
  32.2 4.6 %collective-permute-start.7 = (f32[64,512]{1,0:T(8,128)S(1)}, f32[64,512]{1,0:T(8,128)S(1)}, u32[]{:S(2)}, u32[]{:S(2)}) collective-permute-start(f32[64,512]{1,0:T(8,128)S(1)} %get-tuple-element.20), channel_id=1, source_target_pairs={{0,8},{24,0},{1,9},{25,1},{2,10},{26,2},{3,11},{27,3},{4,12},{28,4... | collective-permute-start | bytes 393224 | tf_op jit(solution)/shard_map/ppermute | solution.py:173
  36.8 0.2 collective-permute-done.9
  37.0 4.9 %collective-permute-done.8 = f32[64,512]{1,0:T(8,128)S(1)} collective-permute-done((f32[64,512]{1,0:T(8,128)S(1)}, f32[64,512]{1,0:T(8,128)S(1)}, u32[]{:S(2)}, u32[]{:S(2)}) %collective-permute-start.8) | collective-permute-done | bytes 131104 | tf_op jit(solution)/shard_map/ppermute | solution.py:173
  41.9 0.1 pad_maximum_fusion
  42.1 0.6 %copy.99 = f32[8,64,512]{1,2,0:T(8,128)S(1)} copy(f32[8,64,512]{2,1,0:T(8,128)S(1)} %pad_maximum_fusion) | data formatting | bytes 2097152 | tf_op jit(solution)/shard_map/concatenate | solution.py:178
  42.7 0.1 dynamic-slice_bitcast_fusion
  42.9 1.1 %copy.107 = f32[64,16,128]{2,1,0:T(8,128)} copy(f32[64,16,128]{0,2,1:T(8,128)S(1)} %fusion.4) | data formatting | bytes 1048576 | tf_op jit(solution)/shard_map/concatenate | solution.py:182
  (53 shorter events, 0.8 us)
Async XLA Ops:
  5.5 6.7 %collective-permute-start = (bf16[16,512]{1,0:T(8,128)(2,1)}, bf16[16,512]{1,0:T(8,128)(2,1)S(1)}, u32[]{:S(2)}, u32[]{:S(2)}) collective-permute-start(bf16[16,512]{1,0:T(8,128)(2,1)} %get-tuple-element.10), channel_id=1, source_target_pairs={{0,8},{8,16},{16,24},{24,0},{1,9},{9,17},{17,25},{25,1},{2,10},{10... | collective-permute-start | bytes 49160 | tf_op jit(solution)/shard_map/ppermute | solution.py:147
  8.5 3.9 %collective-permute-start.1 = (bf16[16,512]{1,0:T(8,128)(2,1)}, bf16[16,512]{1,0:T(8,128)(2,1)S(1)}, u32[]{:S(2)}, u32[]{:S(2)}) collective-permute-start(bf16[16,512]{1,0:T(8,128)(2,1)} %get-tuple-element.11), channel_id=1, source_target_pairs={{0,16},{8,24},{16,0},{24,8},{1,17},{9,25},{17,1},{25,9},{2,18},{10... | collective-permute-start | bytes 49160 | tf_op jit(solution)/shard_map/ppermute | solution.py:147
  10.1 3.9 %collective-permute-start.2 = (bf16[16,512]{1,0:T(8,128)(2,1)}, bf16[16,512]{1,0:T(8,128)(2,1)S(1)}, u32[]{:S(2)}, u32[]{:S(2)}) collective-permute-start(bf16[16,512]{1,0:T(8,128)(2,1)} %get-tuple-element.12), channel_id=1, source_target_pairs={{0,24},{8,0},{16,8},{24,16},{1,25},{9,1},{17,9},{25,17},{2,26},{10... | collective-permute-start | bytes 49160 | tf_op jit(solution)/shard_map/ppermute | solution.py:147
  14.0 8.0 %collective-permute-start.5 = (bf16[16,2048]{1,0:T(8,128)(2,1)S(1)}, bf16[16,2048]{1,0:T(8,128)(2,1)S(1)}, u32[]{:S(2)}, u32[]{:S(2)}) collective-permute-start(bf16[16,2048]{1,0:T(8,128)(2,1)S(1)} %get-tuple-element.43), channel_id=1, source_target_pairs={{6,0},{7,1},{14,8},{15,9},{22,16},{23,17},{30,24},{31,25}} | collective-permute-start | bytes 196616 | tf_op jit(solution)/shard_map/ppermute | solution.py:118
  15.3 8.2 %collective-permute-start.4 = (bf16[16,2048]{1,0:T(8,128)(2,1)S(1)}, bf16[16,2048]{1,0:T(8,128)(2,1)S(1)}, u32[]{:S(2)}, u32[]{:S(2)}) collective-permute-start(bf16[16,2048]{1,0:T(8,128)(2,1)S(1)} %get-tuple-element.43), channel_id=1, source_target_pairs={{4,0},{5,1},{6,2},{7,3},{12,8},{13,9},{14,10},{15,11},{20,16},{21,... | collective-permute-start | bytes 196616 | tf_op jit(solution)/shard_map/ppermute | solution.py:118
  16.6 7.0 %collective-permute-start.3 = (bf16[16,2048]{1,0:T(8,128)(2,1)S(1)}, bf16[16,2048]{1,0:T(8,128)(2,1)S(1)}, u32[]{:S(2)}, u32[]{:S(2)}) collective-permute-start(bf16[16,2048]{1,0:T(8,128)(2,1)S(1)} %get-tuple-element.43), channel_id=1, source_target_pairs={{2,0},{3,1},{4,2},{5,3},{6,4},{7,5},{10,8},{11,9},{12,10},{13,11},... | collective-permute-start | bytes 196616 | tf_op jit(solution)/shard_map/ppermute | solution.py:118
  23.6 1.6 %collective-permute-start.6 = (bf16[64,2048]{1,0:T(8,128)(2,1)S(1)}, bf16[64,2048]{1,0:T(8,128)(2,1)S(1)}, u32[]{:S(2)}, u32[]{:S(2)}) collective-permute-start(bf16[64,2048]{1,0:T(8,128)(2,1)S(1)} %pad_maximum_fusion.2), channel_id=1, source_target_pairs={{0,1},{1,0},{2,3},{3,2},{4,5},{5,4},{6,7},{7,6},{8,9},{9,8},{10,11... | collective-permute-start | bytes 786440 | tf_op jit(solution)/shard_map/ppermute | solution.py:119
  25.7 1.8 %copy-start = (bf16[2]{0:T(256)(128)(2,1)S(1)}, bf16[2]{0:T(256)(128)(2,1)}, u32[]{:S(2)}) copy-start(bf16[2]{0:T(256)(128)(2,1)} %constant.89.clone) | copy-start | bytes 16
  29.6 7.4 %collective-permute-start.9 = (f32[64,512]{1,0:T(8,128)S(1)}, f32[64,512]{1,0:T(8,128)S(1)}, u32[]{:S(2)}, u32[]{:S(2)}) collective-permute-start(f32[64,512]{1,0:T(8,128)S(1)} %get-tuple-element.18), channel_id=1, source_target_pairs={{8,0},{16,8},{9,1},{17,9},{10,2},{18,10},{11,3},{19,11},{12,4},{20... | collective-permute-start | bytes 393224 | tf_op jit(solution)/shard_map/ppermute | solution.py:173
  30.9 11.0 %collective-permute-start.8 = (f32[64,512]{1,0:T(8,128)S(1)}, f32[64,512]{1,0:T(8,128)S(1)}, u32[]{:S(2)}, u32[]{:S(2)}) collective-permute-start(f32[64,512]{1,0:T(8,128)S(1)} %get-tuple-element.19), channel_id=1, source_target_pairs={{16,0},{24,8},{17,1},{25,9},{18,2},{26,10},{19,3},{27,11},{20,4},{... | collective-permute-start | bytes 393224 | tf_op jit(solution)/shard_map/ppermute | solution.py:173
  32.2 9.7 %collective-permute-start.7 = (f32[64,512]{1,0:T(8,128)S(1)}, f32[64,512]{1,0:T(8,128)S(1)}, u32[]{:S(2)}, u32[]{:S(2)}) collective-permute-start(f32[64,512]{1,0:T(8,128)S(1)} %get-tuple-element.20), channel_id=1, source_target_pairs={{0,8},{24,0},{1,9},{25,1},{2,10},{26,2},{3,11},{27,3},{4,12},{28,4... | collective-permute-start | bytes 393224 | tf_op jit(solution)/shard_map/ppermute | solution.py:173

commit v21 on v16

--- a/solution.py
+++ b/solution.py
@@ -174,9 +174,9 @@
         else:
             collected.append(jnp.zeros_like(sent))
     collected = jnp.stack(collected)
-    holder = (me - jnp.arange(seg_count, dtype=jnp.int32)) % seg_count
-    by_bins = jnp.take(collected, holder, axis=0).reshape(seg_count, per_owner, block, 2, bins_each)
-    return by_bins.transpose(1, 2, 3, 0, 4).reshape(per_owner, block, 2 * NF)
+    collected = collected.reshape(seg_count, per_owner, block, 2, bins_each)
+    by_bins = [lax.dynamic_index_in_dim(collected, (me - b) % seg_count, 0, keepdims=False) for b in range(seg_count)]
+    return jnp.stack(by_bins, axis=3).reshape(per_owner, block, 2 * NF)
 
 
 def solution(mesh):

time: 46.4 us -> 45.6 us (0.983)
  local copies, waits for them, and re-layouts: 6.62 us -> 6.14 us
    gather x2 -> x0, local copies, waits for them, and re-layouts: 0.91 us -> none  [shards(): jnp.take(collected, holder, axis=0)]
where the time goes in v21:
time: 45.6 us; the launch traced here: 45.2 us
  waiting for transfers between devices  16.4 us (36%)
  starting transfers between devices  15.3 us (34%)
  local copies, waits for them, and re-layouts  6.14 us (13%)
  Pallas kernels  5.53 us (12%)
  matrix products  0.73 us (2%)
  other arithmetic  0.54 us (1%)
  between operations  0.52 us (1%)
    ppermute x3, waiting for transfers between devices, halo(): own.append(lax.ppermute(mine, 'fibre', pairs))  7.84 us
    ppermute x3, starting transfers between devices, shards(): gathered.append(lax.ppermute(split[step], 'seg', pairs))  5.94 us
    pallas_call x1, Pallas kernels, whiten(): pl.pallas_call(whiten_kernel, out_shape=[jax.ShapeDtypeStruct((channels,...  5.53 us
    ppermute x3, starting transfers between devices, shards(): collected.append(lax.ppermute(sent, 'seg', pairs))  5.47 us
    ppermute x3, waiting for transfers between devices, shards(): collected.append(lax.ppermute(sent, 'seg', pairs))  5.39 us
    ppermute x3, starting transfers between devices, halo(): own.append(lax.ppermute(mine, 'fibre', pairs))  3.86 us
    unnamed x31, local copies, waits for them, and re-layouts  1.9 us
    ppermute x3, waiting for transfers between devices, shards(): gathered.append(lax.ppermute(split[step], 'seg', pairs))  1.79 us
  transfers between devices with their start and end apart: 10, of which 9 were waited for; matrix products, arithmetic and copies ran while one was open for 2% of the time, Pallas kernels for 0%

profile of v21, /device:TPU:0, one launch (start us, length us, event | category | flops | bytes accessed | tf_op | source)
XLA Modules:
  0.0 45.2 jit_solution(17651215934483239825)
XLA Ops:
  0.0 5.5 %shard_map.73 = (bf16[16,512]{1,0:T(8,128)(2,1)}, bf16[16,512]{1,0:T(8,128)(2,1)}, bf16[16,512]{1,0:T(8,128)(2,1)}, bf16[16,512]{1,0:T(8,128)(2,1)}) custom-call(s32[16]{0:T(128)} %bitcast.105, s32[1]{0:T(128)} %bitcast.1.place_ref, s32[16]{0:T(128)} %live_ref.1, bf16[16,27648]{1,0:T(8,128)(2,1)} %bitcast.88, bf16[3072,128]{1,0:T(8,128)(2,1)} %constant.97.clone.table_ref, ...), custom_call_target="tpu_custom_call" | custom-call | tf_op jit(solution)/shard_map/pallas_call | solution.py:94
  5.5 3.0 %collective-permute-start = (bf16[16,512]{1,0:T(8,128)(2,1)}, bf16[16,512]{1,0:T(8,128)(2,1)S(1)}, u32[]{:S(2)}, u32[]{:S(2)}) collective-permute-start(bf16[16,512]{1,0:T(8,128)(2,1)} %get-tuple-element.10), channel_id=1, source_target_pairs={{0,8},{8,16},{16,24},{24,0},{1,9},{9,17},{17,25},{25,1},{2,10},{10... | collective-permute-start | bytes 49160 | tf_op jit(solution)/shard_map/ppermute | solution.py:147
  8.5 1.5 %collective-permute-start.1 = (bf16[16,512]{1,0:T(8,128)(2,1)}, bf16[16,512]{1,0:T(8,128)(2,1)S(1)}, u32[]{:S(2)}, u32[]{:S(2)}) collective-permute-start(bf16[16,512]{1,0:T(8,128)(2,1)} %get-tuple-element.11), channel_id=1, source_target_pairs={{0,16},{8,24},{16,0},{24,8},{1,17},{9,25},{17,1},{25,9},{2,18},{10... | collective-permute-start | bytes 49160 | tf_op jit(solution)/shard_map/ppermute | solution.py:147
  10.1 1.4 %collective-permute-start.2 = (bf16[16,512]{1,0:T(8,128)(2,1)}, bf16[16,512]{1,0:T(8,128)(2,1)S(1)}, u32[]{:S(2)}, u32[]{:S(2)}) collective-permute-start(bf16[16,512]{1,0:T(8,128)(2,1)} %get-tuple-element.12), channel_id=1, source_target_pairs={{0,24},{8,0},{16,8},{24,16},{1,25},{9,1},{17,9},{25,17},{2,26},{10... | collective-permute-start | bytes 49160 | tf_op jit(solution)/shard_map/ppermute | solution.py:147
  11.5 0.7 %constant_dynamic-update-slice_fusion.3 = (bf16[16,2048]{1,0:T(8,128)(2,1)S(1)}, bf16[128,2048]{1,0:T(8,128)(2,1)S(1)}) fusion(bf16[16,512]{1,0:T(8,128)(2,1)} %get-tuple-element.9), kind=kLoop, calls=%fused_computation.21 | loop fusion | bytes 49152
  12.2 0.3 collective-permute-done.1
  12.5 1.5 %collective-permute-done.2 = bf16[16,512]{1,0:T(8,128)(2,1)S(1)} collective-permute-done((bf16[16,512]{1,0:T(8,128)(2,1)}, bf16[16,512]{1,0:T(8,128)(2,1)S(1)}, u32[]{:S(2)}, u32[]{:S(2)}) %collective-permute-start.2) | collective-permute-done | bytes 16416 | tf_op jit(solution)/shard_map/ppermute | solution.py:147
  14.0 1.3 %collective-permute-start.3 = (bf16[16,2048]{1,0:T(8,128)(2,1)S(1)}, bf16[16,2048]{1,0:T(8,128)(2,1)S(1)}, u32[]{:S(2)}, u32[]{:S(2)}) collective-permute-start(bf16[16,2048]{1,0:T(8,128)(2,1)S(1)} %get-tuple-element.43), channel_id=1, source_target_pairs={{2,0},{3,1},{4,2},{5,3},{6,4},{7,5},{10,8},{11,9},{12,10},{13,11},... | collective-permute-start | bytes 196616 | tf_op jit(solution)/shard_map/ppermute | solution.py:118
  15.3 1.3 %collective-permute-start.4 = (bf16[16,2048]{1,0:T(8,128)(2,1)S(1)}, bf16[16,2048]{1,0:T(8,128)(2,1)S(1)}, u32[]{:S(2)}, u32[]{:S(2)}) collective-permute-start(bf16[16,2048]{1,0:T(8,128)(2,1)S(1)} %get-tuple-element.43), channel_id=1, source_target_pairs={{4,0},{5,1},{6,2},{7,3},{12,8},{13,9},{14,10},{15,11},{20,16},{21,... | collective-permute-start | bytes 196616 | tf_op jit(solution)/shard_map/ppermute | solution.py:118
  16.6 1.3 %collective-permute-start.5 = (bf16[16,2048]{1,0:T(8,128)(2,1)S(1)}, bf16[16,2048]{1,0:T(8,128)(2,1)S(1)}, u32[]{:S(2)}, u32[]{:S(2)}) collective-permute-start(bf16[16,2048]{1,0:T(8,128)(2,1)S(1)} %get-tuple-element.43), channel_id=1, source_target_pairs={{6,0},{7,1},{14,8},{15,9},{22,16},{23,17},{30,24},{31,25}} | collective-permute-start | bytes 196616 | tf_op jit(solution)/shard_map/ppermute | solution.py:118
  17.9 2.7 %collective-permute-done.3 = bf16[16,2048]{1,0:T(8,128)(2,1)S(1)} collective-permute-done((bf16[16,2048]{1,0:T(8,128)(2,1)S(1)}, bf16[16,2048]{1,0:T(8,128)(2,1)S(1)}, u32[]{:S(2)}, u32[]{:S(2)}) %collective-permute-start.3) | collective-permute-done | bytes 65568 | tf_op jit(solution)/shard_map/ppermute | solution.py:118
  20.6 2.7 %collective-permute-done.4 = bf16[16,2048]{1,0:T(8,128)(2,1)S(1)} collective-permute-done((bf16[16,2048]{1,0:T(8,128)(2,1)S(1)}, bf16[16,2048]{1,0:T(8,128)(2,1)S(1)}, u32[]{:S(2)}, u32[]{:S(2)}) %collective-permute-start.4) | collective-permute-done | bytes 65568 | tf_op jit(solution)/shard_map/ppermute | solution.py:118
  23.3 2.5 %collective-permute-done.5 = bf16[16,2048]{1,0:T(8,128)(2,1)S(1)} collective-permute-done((bf16[16,2048]{1,0:T(8,128)(2,1)S(1)}, bf16[16,2048]{1,0:T(8,128)(2,1)S(1)}, u32[]{:S(2)}, u32[]{:S(2)}) %collective-permute-start.5) | collective-permute-done | bytes 65568 | tf_op jit(solution)/shard_map/ppermute | solution.py:118
  25.9 1.4 %collective-permute-done.6 = bf16[64,2048]{1,0:T(8,128)(2,1)S(1)} collective-permute-done((bf16[64,2048]{1,0:T(8,128)(2,1)S(1)}, bf16[64,2048]{1,0:T(8,128)(2,1)S(1)}, u32[]{:S(2)}, u32[]{:S(2)}) %collective-permute-start.6) | collective-permute-done | bytes 262176 | tf_op jit(solution)/shard_map/ppermute | solution.py:119
  27.6 0.3 copy.116
  27.9 0.4 slice.56
  28.3 0.4 stack.42
  28.7 0.4 copy.71
  29.1 0.4 copy.72
  29.7 0.5 %copy-done = bf16[2]{0:T(256)(128)(2,1)S(1)} copy-done((bf16[2]{0:T(256)(128)(2,1)S(1)}, bf16[2]{0:T(256)(128)(2,1)}, u32[]{:S(2)}) %copy-start) | copy-done | bytes 28
  30.3 0.7 %convolution_bitcast_fusion = f32[16,2,16,144]{3,2,1,0:T(8,128)S(1)} fusion(bf16[144,64,2,16,1]{0,3,2,1,4:T(8,128)(2,1)S(1)} %bitcast.80, bf16[1,16,64,2,16]{2,1,3,0,4:T(8,128)(2,1)S(1)} %multiply_bitcast_fusion.1, bf16[1,16,64,2,16]{2,1,3,0,4:T(8,128)(2,1)S(1)} %copy.72), kind=kOutput, calls=%fused_computation | convolution fusion | flops 18939904 | bytes 1015808 | tf_op jit(solution)/shard_map/ocspn,jspn->nocj/dot_general | solution.py:160
  31.0 0.6 %fusion.5 = (f32[16,2,1,128]{3,2,1,0:T(1,128)S(1)}, f32[16,2,1,128]{3,2,1,0:T(1,128)S(1)}, f32[16,2,1,128]{3,2,1,0:T(1,128)S(1)}, f32[16,2,1,128]{3,2,1,0:T(1,12...) fusion(f32[16,2,16,144]{3,2,1,0:T(8,128)S(1)} %convolution_bitc, ...), kind=kLoop, calls=%fused_computation.62 | loop fusion | bytes 524288 | tf_op jit(solution)/shard_map/slice | solution.py:161
  31.9 0.1 multiply_bitcast_fusion
  32.0 0.1 copy.117
  32.3 2.9 %collective-permute-start.7 = (f32[64,512]{1,0:T(8,128)S(1)}, f32[64,512]{1,0:T(8,128)S(1)}, u32[]{:S(2)}, u32[]{:S(2)}) collective-permute-start(f32[64,512]{1,0:T(8,128)S(1)} %get-tuple-element.20), channel_id=1, source_target_pairs={{0,8},{24,0},{1,9},{25,1},{2,10},{26,2},{3,11},{27,3},{4,12},{28,4... | collective-permute-start | bytes 393224 | tf_op jit(solution)/shard_map/ppermute | solution.py:173
  35.2 1.3 %collective-permute-start.8 = (f32[64,512]{1,0:T(8,128)S(1)}, f32[64,512]{1,0:T(8,128)S(1)}, u32[]{:S(2)}, u32[]{:S(2)}) collective-permute-start(f32[64,512]{1,0:T(8,128)S(1)} %get-tuple-element.19), channel_id=1, source_target_pairs={{16,0},{24,8},{17,1},{25,9},{18,2},{26,10},{19,3},{27,11},{20,4},{... | collective-permute-start | bytes 393224 | tf_op jit(solution)/shard_map/ppermute | solution.py:173
  36.5 1.3 %collective-permute-start.9 = (f32[64,512]{1,0:T(8,128)S(1)}, f32[64,512]{1,0:T(8,128)S(1)}, u32[]{:S(2)}, u32[]{:S(2)}) collective-permute-start(f32[64,512]{1,0:T(8,128)S(1)} %get-tuple-element.18), channel_id=1, source_target_pairs={{8,0},{16,8},{9,1},{17,9},{10,2},{18,10},{11,3},{19,11},{12,4},{20... | collective-permute-start | bytes 393224 | tf_op jit(solution)/shard_map/ppermute | solution.py:173
  37.8 0.1 copy.92
  38.0 2.7 %collective-permute-done.7 = f32[64,512]{1,0:T(8,128)S(1)} collective-permute-done((f32[64,512]{1,0:T(8,128)S(1)}, f32[64,512]{1,0:T(8,128)S(1)}, u32[]{:S(2)}, u32[]{:S(2)}) %collective-permute-start.7) | collective-permute-done | bytes 131104 | tf_op jit(solution)/shard_map/ppermute | solution.py:173
  40.8 2.6 %collective-permute-done.8 = f32[64,512]{1,0:T(8,128)S(1)} collective-permute-done((f32[64,512]{1,0:T(8,128)S(1)}, f32[64,512]{1,0:T(8,128)S(1)}, u32[]{:S(2)}, u32[]{:S(2)}) %collective-permute-start.8) | collective-permute-done | bytes 131104 | tf_op jit(solution)/shard_map/ppermute | solution.py:173
  43.8 0.1 pad_maximum_fusion
  44.1 1.1 %copy.96 = f32[64,16,128]{2,1,0:T(8,128)} copy(f32[64,16,128]{0,2,1:T(8,128)S(1)} %bitcast.81) | data formatting | bytes 1048576 | tf_op jit(solution)/shard_map/reshape | solution.py:179
  (47 shorter events, 1.4 us)
Async XLA Ops:
  5.5 6.7 %collective-permute-start = (bf16[16,512]{1,0:T(8,128)(2,1)}, bf16[16,512]{1,0:T(8,128)(2,1)S(1)}, u32[]{:S(2)}, u32[]{:S(2)}) collective-permute-start(bf16[16,512]{1,0:T(8,128)(2,1)} %get-tuple-element.10), channel_id=1, source_target_pairs={{0,8},{8,16},{16,24},{24,0},{1,9},{9,17},{17,25},{25,1},{2,10},{10... | collective-permute-start | bytes 49160 | tf_op jit(solution)/shard_map/ppermute | solution.py:147
  8.5 3.9 %collective-permute-start.1 = (bf16[16,512]{1,0:T(8,128)(2,1)}, bf16[16,512]{1,0:T(8,128)(2,1)S(1)}, u32[]{:S(2)}, u32[]{:S(2)}) collective-permute-start(bf16[16,512]{1,0:T(8,128)(2,1)} %get-tuple-element.11), channel_id=1, source_target_pairs={{0,16},{8,24},{16,0},{24,8},{1,17},{9,25},{17,1},{25,9},{2,18},{10... | collective-permute-start | bytes 49160 | tf_op jit(solution)/shard_map/ppermute | solution.py:147
  10.1 3.9 %collective-permute-start.2 = (bf16[16,512]{1,0:T(8,128)(2,1)}, bf16[16,512]{1,0:T(8,128)(2,1)S(1)}, u32[]{:S(2)}, u32[]{:S(2)}) collective-permute-start(bf16[16,512]{1,0:T(8,128)(2,1)} %get-tuple-element.12), channel_id=1, source_target_pairs={{0,24},{8,0},{16,8},{24,16},{1,25},{9,1},{17,9},{25,17},{2,26},{10... | collective-permute-start | bytes 49160 | tf_op jit(solution)/shard_map/ppermute | solution.py:147
  14.0 6.6 %collective-permute-start.3 = (bf16[16,2048]{1,0:T(8,128)(2,1)S(1)}, bf16[16,2048]{1,0:T(8,128)(2,1)S(1)}, u32[]{:S(2)}, u32[]{:S(2)}) collective-permute-start(bf16[16,2048]{1,0:T(8,128)(2,1)S(1)} %get-tuple-element.43), channel_id=1, source_target_pairs={{2,0},{3,1},{4,2},{5,3},{6,4},{7,5},{10,8},{11,9},{12,10},{13,11},... | collective-permute-start | bytes 196616 | tf_op jit(solution)/shard_map/ppermute | solution.py:118
  15.3 8.0 %collective-permute-start.4 = (bf16[16,2048]{1,0:T(8,128)(2,1)S(1)}, bf16[16,2048]{1,0:T(8,128)(2,1)S(1)}, u32[]{:S(2)}, u32[]{:S(2)}) collective-permute-start(bf16[16,2048]{1,0:T(8,128)(2,1)S(1)} %get-tuple-element.43), channel_id=1, source_target_pairs={{4,0},{5,1},{6,2},{7,3},{12,8},{13,9},{14,10},{15,11},{20,16},{21,... | collective-permute-start | bytes 196616 | tf_op jit(solution)/shard_map/ppermute | solution.py:118
  16.6 9.1 %collective-permute-start.5 = (bf16[16,2048]{1,0:T(8,128)(2,1)S(1)}, bf16[16,2048]{1,0:T(8,128)(2,1)S(1)}, u32[]{:S(2)}, u32[]{:S(2)}) collective-permute-start(bf16[16,2048]{1,0:T(8,128)(2,1)S(1)} %get-tuple-element.43), channel_id=1, source_target_pairs={{6,0},{7,1},{14,8},{15,9},{22,16},{23,17},{30,24},{31,25}} | collective-permute-start | bytes 196616 | tf_op jit(solution)/shard_map/ppermute | solution.py:118
  25.8 1.6 %collective-permute-start.6 = (bf16[64,2048]{1,0:T(8,128)(2,1)S(1)}, bf16[64,2048]{1,0:T(8,128)(2,1)S(1)}, u32[]{:S(2)}, u32[]{:S(2)}) collective-permute-start(bf16[64,2048]{1,0:T(8,128)(2,1)S(1)} %pad_maximum_fusion.2), channel_id=1, source_target_pairs={{0,1},{1,0},{2,3},{3,2},{4,5},{5,4},{6,7},{7,6},{8,9},{9,8},{10,11... | collective-permute-start | bytes 786440 | tf_op jit(solution)/shard_map/ppermute | solution.py:119
  29.6 0.7 %copy-start = (bf16[2]{0:T(256)(128)(2,1)S(1)}, bf16[2]{0:T(256)(128)(2,1)}, u32[]{:S(2)}) copy-start(bf16[2]{0:T(256)(128)(2,1)} %constant.100.clone) | copy-start | bytes 16
  32.3 8.4 %collective-permute-start.7 = (f32[64,512]{1,0:T(8,128)S(1)}, f32[64,512]{1,0:T(8,128)S(1)}, u32[]{:S(2)}, u32[]{:S(2)}) collective-permute-start(f32[64,512]{1,0:T(8,128)S(1)} %get-tuple-element.20), channel_id=1, source_target_pairs={{0,8},{24,0},{1,9},{25,1},{2,10},{26,2},{3,11},{27,3},{4,12},{28,4... | collective-permute-start | bytes 393224 | tf_op jit(solution)/shard_map/ppermute | solution.py:173
  35.2 8.2 %collective-permute-start.8 = (f32[64,512]{1,0:T(8,128)S(1)}, f32[64,512]{1,0:T(8,128)S(1)}, u32[]{:S(2)}, u32[]{:S(2)}) collective-permute-start(f32[64,512]{1,0:T(8,128)S(1)} %get-tuple-element.19), channel_id=1, source_target_pairs={{16,0},{24,8},{17,1},{25,9},{18,2},{26,10},{19,3},{27,11},{20,4},{... | collective-permute-start | bytes 393224 | tf_op jit(solution)/shard_map/ppermute | solution.py:173
  36.5 7.2 %collective-permute-start.9 = (f32[64,512]{1,0:T(8,128)S(1)}, f32[64,512]{1,0:T(8,128)S(1)}, u32[]{:S(2)}, u32[]{:S(2)}) collective-permute-start(f32[64,512]{1,0:T(8,128)S(1)} %get-tuple-element.18), channel_id=1, source_target_pairs={{8,0},{16,8},{9,1},{17,9},{10,2},{18,10},{11,3},{19,11},{12,4},{20... | collective-permute-start | bytes 393224 | tf_op jit(solution)/shard_map/ppermute | solution.py:173

commit v22 on v18

--- a/solution.py
+++ b/solution.py
@@ -116,12 +116,15 @@
     for step in range(1, strides + 1):
         pairs = [(i, i - 2 * step) for i in range(2 * step, fibre_count)]
         own.append(lax.ppermute(mine, "fibre", pairs))
-    swapped = lax.ppermute(jnp.concatenate(own, axis=0), "fibre", [(i, i ^ 1) for i in range(fibre_count)])
+    even_side = lax.axis_index("fibre") % 2 == 0
+    sent = jnp.where(
+        even_side,
+        jnp.concatenate(own[1:] + [jnp.zeros_like(mine)], axis=0),
+        jnp.concatenate(own, axis=0),
+    )
+    swapped = lax.ppermute(sent, "fibre", [(i, i ^ 1) for i in range(fibre_count)])
     swapped = jnp.split(swapped, strides + 1, axis=0)
-    even = [part for pair in zip(own, swapped) for part in pair]
-    odd = [part for pair in zip(own, swapped[1:] + [jnp.zeros_like(mine)]) for part in pair]
-    odd_side = lax.axis_index("fibre") % 2 == 1
-    return jnp.where(odd_side, jnp.concatenate(odd, axis=0), jnp.concatenate(even, axis=0))
+    return jnp.concatenate([part for pair in zip(own, swapped) for part in pair], axis=0)
 
 
 def shards(record, offsets, live_mask):

time: 44.4 us -> 43.3 us (0.975)
  waiting for transfers between devices: 14 us -> 12.8 us
    ppermute x1, waiting for transfers between devices: 1.42 us -> 0.01 us  [halo(): lax.ppermute(sent, 'fibre', [(i, i ^ 1) for i in range(fibre_count)])]
    unnamed x31 -> x28, local copies, waits for them, and re-layouts: 1.37 us -> 1.04 us
  transfers between devices with their start and end apart: 10 -> 10, of which waited for: 7 -> 6; matrix products, arithmetic and copies ran while one was open for 2% -> 6% of each run, Pallas kernels for 0% -> 0%
where the time goes in v22:
time: 43.3 us; the launch traced here: 42.9 us
  starting transfers between devices  17 us (39%)
  waiting for transfers between devices  12.8 us (30%)
  local copies, waits for them, and re-layouts  5.83 us (13%)
  Pallas kernels  5.53 us (13%)
  matrix products  0.73 us (2%)
  other arithmetic  0.54 us (1%)
  between operations  0.45 us (1%)
    ppermute x3, starting transfers between devices, shards(): collected.append(lax.ppermute(sent, 'seg', pairs))  7.13 us
    ppermute x3, starting transfers between devices, shards(): gathered.append(lax.ppermute(split[step], 'seg', pairs))  5.94 us
    ppermute x3, waiting for transfers between devices, halo(): own.append(lax.ppermute(mine, 'fibre', pairs))  5.64 us
    pallas_call x1, Pallas kernels, whiten(): pl.pallas_call(whiten_kernel, out_shape=[jax.ShapeDtypeStruct((channels,...  5.53 us
    ppermute x3, waiting for transfers between devices, shards(): collected.append(lax.ppermute(sent, 'seg', pairs))  5.42 us
    ppermute x3, starting transfers between devices, halo(): own.append(lax.ppermute(mine, 'fibre', pairs))  3.86 us
    ppermute x3, waiting for transfers between devices, shards(): gathered.append(lax.ppermute(split[step], 'seg', pairs))  1.79 us
    reshape x1, local copies, waits for them, and re-layouts, shards(): return jnp.stack(by_bins, axis=3).reshape(per_owner, block, 2 * NF)  1.14 us
  transfers between devices with their start and end apart: 10, of which 6 were waited for; matrix products, arithmetic and copies ran while one was open for 6% of the time, Pallas kernels for 0%

profile of v22, /device:TPU:0, one launch (start us, length us, event | category | flops | bytes accessed | tf_op | source)
XLA Modules:
  0.0 42.9 jit_solution(15281533036007297190)
XLA Ops:
  0.0 5.5 %shard_map.73 = (bf16[16,512]{1,0:T(8,128)(2,1)}, bf16[16,512]{1,0:T(8,128)(2,1)}, bf16[16,512]{1,0:T(8,128)(2,1)}, bf16[16,512]{1,0:T(8,128)(2,1)}) custom-call(s32[16]{0:T(128)} %bitcast.105, s32[1]{0:T(128)} %bitcast.1.place_ref, s32[16]{0:T(128)} %live_ref.1, bf16[16,27648]{1,0:T(8,128)(2,1)} %bitcast.85, bf16[3072,128]{1,0:T(8,128)(2,1)} %constant.87.clone.table_ref, ...), custom_call_target="tpu_custom_call" | custom-call | tf_op jit(solution)/shard_map/pallas_call | solution.py:94
  5.5 3.0 %collective-permute-start = (bf16[16,512]{1,0:T(8,128)(2,1)}, bf16[16,512]{1,0:T(8,128)(2,1)S(1)}, u32[]{:S(2)}, u32[]{:S(2)}) collective-permute-start(bf16[16,512]{1,0:T(8,128)(2,1)} %get-tuple-element.10), channel_id=1, source_target_pairs={{0,8},{8,16},{16,24},{24,0},{1,9},{9,17},{17,25},{25,1},{2,10},{10... | collective-permute-start | bytes 49160 | tf_op jit(solution)/shard_map/ppermute | solution.py:150
  8.5 1.5 %collective-permute-start.1 = (bf16[16,512]{1,0:T(8,128)(2,1)}, bf16[16,512]{1,0:T(8,128)(2,1)S(1)}, u32[]{:S(2)}, u32[]{:S(2)}) collective-permute-start(bf16[16,512]{1,0:T(8,128)(2,1)} %get-tuple-element.11), channel_id=1, source_target_pairs={{0,16},{8,24},{16,0},{24,8},{1,17},{9,25},{17,1},{25,9},{2,18},{10... | collective-permute-start | bytes 49160 | tf_op jit(solution)/shard_map/ppermute | solution.py:150
  10.1 1.4 %collective-permute-start.2 = (bf16[16,512]{1,0:T(8,128)(2,1)}, bf16[16,512]{1,0:T(8,128)(2,1)S(1)}, u32[]{:S(2)}, u32[]{:S(2)}) collective-permute-start(bf16[16,512]{1,0:T(8,128)(2,1)} %get-tuple-element.12), channel_id=1, source_target_pairs={{0,24},{8,0},{16,8},{24,16},{1,25},{9,1},{17,9},{25,17},{2,26},{10... | collective-permute-start | bytes 49160 | tf_op jit(solution)/shard_map/ppermute | solution.py:150
  11.5 0.7 %constant_dynamic-update-slice_fusion.3 = (bf16[16,2048]{1,0:T(8,128)(2,1)S(1)}, bf16[144,2048]{1,0:T(8,128)(2,1)S(1)}) fusion(bf16[16,512]{1,0:T(8,128)(2,1)} %get-tuple-element.9), kind=kLoop, calls=%fused_computation.21 | loop fusion | bytes 49152
  12.2 0.3 collective-permute-done.1
  12.5 1.5 %collective-permute-done.2 = bf16[16,512]{1,0:T(8,128)(2,1)S(1)} collective-permute-done((bf16[16,512]{1,0:T(8,128)(2,1)}, bf16[16,512]{1,0:T(8,128)(2,1)S(1)}, u32[]{:S(2)}, u32[]{:S(2)}) %collective-permute-start.2) | collective-permute-done | bytes 16416 | tf_op jit(solution)/shard_map/ppermute | solution.py:150
  14.0 1.3 %collective-permute-start.5 = (bf16[16,2048]{1,0:T(8,128)(2,1)S(1)}, bf16[16,2048]{1,0:T(8,128)(2,1)S(1)}, u32[]{:S(2)}, u32[]{:S(2)}) collective-permute-start(bf16[16,2048]{1,0:T(8,128)(2,1)S(1)} %get-tuple-element.37), channel_id=1, source_target_pairs={{6,0},{7,1},{14,8},{15,9},{22,16},{23,17},{30,24},{31,25}} | collective-permute-start | bytes 196616 | tf_op jit(solution)/shard_map/ppermute | solution.py:118
  15.3 1.3 %collective-permute-start.4 = (bf16[16,2048]{1,0:T(8,128)(2,1)S(1)}, bf16[16,2048]{1,0:T(8,128)(2,1)S(1)}, u32[]{:S(2)}, u32[]{:S(2)}) collective-permute-start(bf16[16,2048]{1,0:T(8,128)(2,1)S(1)} %get-tuple-element.37), channel_id=1, source_target_pairs={{4,0},{5,1},{6,2},{7,3},{12,8},{13,9},{14,10},{15,11},{20,16},{21,... | collective-permute-start | bytes 196616 | tf_op jit(solution)/shard_map/ppermute | solution.py:118
  16.6 1.3 %collective-permute-start.3 = (bf16[16,2048]{1,0:T(8,128)(2,1)S(1)}, bf16[16,2048]{1,0:T(8,128)(2,1)S(1)}, u32[]{:S(2)}, u32[]{:S(2)}) collective-permute-start(bf16[16,2048]{1,0:T(8,128)(2,1)S(1)} %get-tuple-element.37), channel_id=1, source_target_pairs={{2,0},{3,1},{4,2},{5,3},{6,4},{7,5},{10,8},{11,9},{12,10},{13,11},... | collective-permute-start | bytes 196616 | tf_op jit(solution)/shard_map/ppermute | solution.py:118
  17.9 4.1 %collective-permute-done.5 = bf16[16,2048]{1,0:T(8,128)(2,1)S(1)} collective-permute-done((bf16[16,2048]{1,0:T(8,128)(2,1)S(1)}, bf16[16,2048]{1,0:T(8,128)(2,1)S(1)}, u32[]{:S(2)}, u32[]{:S(2)}) %collective-permute-start.5) | collective-permute-done | bytes 65568 | tf_op jit(solution)/shard_map/ppermute | solution.py:118
  22.1 1.5 %collective-permute-done.4 = bf16[16,2048]{1,0:T(8,128)(2,1)S(1)} collective-permute-done((bf16[16,2048]{1,0:T(8,128)(2,1)S(1)}, bf16[16,2048]{1,0:T(8,128)(2,1)S(1)}, u32[]{:S(2)}, u32[]{:S(2)}) %collective-permute-start.4) | collective-permute-done | bytes 65568 | tf_op jit(solution)/shard_map/ppermute | solution.py:118
  23.8 0.4 slice.52
  24.2 0.4 stack.40
  24.6 0.4 %copy.72 = bf16[16,64,2,16]{1,0,2,3:T(8,128)(2,1)S(1)} copy(bf16[16,64,2,16]{3,2,1,0:T(2,128)(2,1)S(1)} %slice.52) | data formatting | bytes 131072 | tf_op jit(solution)/shard_map/slice | solution.py:159
  25.0 0.4 %copy.73 = bf16[1,16,64,2,16]{2,1,3,0,4:T(8,128)(2,1)S(1)} copy(bf16[1,16,64,2,16]{4,3,2,1,0:T(2,128)(2,1)S(1)} %stack.40) | data formatting | bytes 131072 | tf_op jit(solution)/shard_map/stack | solution.py:162
  25.5 0.1 multiply_bitcast_fusion.1
  25.7 0.5 %copy.74 = bf16[144,2048]{0,1:T(8,128)(2,1)S(1)} copy(bf16[144,2048]{1,0:T(8,128)(2,1)S(1)} %constant_dynamic-update-slice_fusion.4) | data formatting | bytes 1179648 | tf_op jit(solution)/shard_map/concatenate | solution.py:155
  26.2 0.7 %convolution_bitcast_fusion = f32[16,2,16,144]{3,2,1,0:T(8,128)S(1)} fusion(bf16[144,64,2,16,1]{0,3,2,1,4:T(8,128)(2,1)S(1)} %bitcast.81, bf16[1,16,64,2,16]{2,1,3,0,4:T(8,128)(2,1)S(1)} %multiply_bitcast_fusion.1, bf16[1,16,64,2,16]{2,1,3,0,4:T(8,128)(2,1)S(1)} %copy.73), kind=kOutput, calls=%fused_computation | convolution fusion | flops 18939904 | bytes 1015808 | tf_op jit(solution)/shard_map/ocspn,jspn->nocj/dot_general | solution.py:163
  26.9 0.6 %fusion.5 = (f32[16,2,1,128]{3,2,1,0:T(1,128)S(1)}, f32[16,2,1,128]{3,2,1,0:T(1,128)S(1)}, f32[16,2,1,128]{3,2,1,0:T(1,128)S(1)}, f32[16,2,1,128]{3,2,1,0:T(1,12...) fusion(f32[16,2,16,144]{3,2,1,0:T(8,128)S(1)} %convolution_bitc, ...), kind=kLoop, calls=%fused_computation.52 | loop fusion | bytes 524288 | tf_op jit(solution)/shard_map/slice | solution.py:164
  27.7 0.1 multiply_bitcast_fusion
  27.9 0.1 copy.114
  28.2 1.3 %collective-permute-start.9 = (f32[64,512]{1,0:T(8,128)S(1)}, f32[64,512]{1,0:T(8,128)S(1)}, u32[]{:S(2)}, u32[]{:S(2)}) collective-permute-start(f32[64,512]{1,0:T(8,128)S(1)} %get-tuple-element.18), channel_id=1, source_target_pairs={{8,0},{16,8},{9,1},{17,9},{10,2},{18,10},{11,3},{19,11},{12,4},{20... | collective-permute-start | bytes 393224 | tf_op jit(solution)/shard_map/ppermute | solution.py:176
  29.5 1.3 %collective-permute-start.8 = (f32[64,512]{1,0:T(8,128)S(1)}, f32[64,512]{1,0:T(8,128)S(1)}, u32[]{:S(2)}, u32[]{:S(2)}) collective-permute-start(f32[64,512]{1,0:T(8,128)S(1)} %get-tuple-element.19), channel_id=1, source_target_pairs={{16,0},{24,8},{17,1},{25,9},{18,2},{26,10},{19,3},{27,11},{20,4},{... | collective-permute-start | bytes 393224 | tf_op jit(solution)/shard_map/ppermute | solution.py:176
  30.8 4.6 %collective-permute-start.7 = (f32[64,512]{1,0:T(8,128)S(1)}, f32[64,512]{1,0:T(8,128)S(1)}, u32[]{:S(2)}, u32[]{:S(2)}) collective-permute-start(f32[64,512]{1,0:T(8,128)S(1)} %get-tuple-element.20), channel_id=1, source_target_pairs={{0,8},{24,0},{1,9},{25,1},{2,10},{26,2},{3,11},{27,3},{4,12},{28,4... | collective-permute-start | bytes 393224 | tf_op jit(solution)/shard_map/ppermute | solution.py:176
  35.3 0.6 %collective-permute-done.9 = f32[64,512]{1,0:T(8,128)S(1)} collective-permute-done((f32[64,512]{1,0:T(8,128)S(1)}, f32[64,512]{1,0:T(8,128)S(1)}, u32[]{:S(2)}, u32[]{:S(2)}) %collective-permute-start.9) | collective-permute-done | bytes 131104 | tf_op jit(solution)/shard_map/ppermute | solution.py:176
  35.9 4.9 %collective-permute-done.8 = f32[64,512]{1,0:T(8,128)S(1)} collective-permute-done((f32[64,512]{1,0:T(8,128)S(1)}, f32[64,512]{1,0:T(8,128)S(1)}, u32[]{:S(2)}, u32[]{:S(2)}) %collective-permute-start.8) | collective-permute-done | bytes 131104 | tf_op jit(solution)/shard_map/ppermute | solution.py:176
  40.8 0.1 pad_maximum_fusion
  41.0 0.6 %copy.93 = f32[8,64,512]{1,2,0:T(8,128)S(1)} copy(f32[8,64,512]{2,1,0:T(8,128)S(1)} %pad_maximum_fusion) | data formatting | bytes 2097152 | tf_op jit(solution)/shard_map/concatenate | solution.py:181
  41.6 0.1 dynamic-slice_bitcast_fusion.3
  41.7 0.1 pad_maximum_fusion.1
  41.8 1.1 %copy.94 = f32[64,16,128]{2,1,0:T(8,128)} copy(f32[64,16,128]{0,2,1:T(8,128)S(1)} %bitcast.82) | data formatting | bytes 1048576 | tf_op jit(solution)/shard_map/reshape | solution.py:185
  (41 shorter events, 0.5 us)
Async XLA Ops:
  5.5 19.9 %copy-start = (bf16[2]{0:T(256)(128)(2,1)S(1)}, bf16[2]{0:T(256)(128)(2,1)}, u32[]{:S(2)}) copy-start(bf16[2]{0:T(256)(128)(2,1)} %constant.90.clone) | copy-start | bytes 16
  5.5 6.7 %collective-permute-start = (bf16[16,512]{1,0:T(8,128)(2,1)}, bf16[16,512]{1,0:T(8,128)(2,1)S(1)}, u32[]{:S(2)}, u32[]{:S(2)}) collective-permute-start(bf16[16,512]{1,0:T(8,128)(2,1)} %get-tuple-element.10), channel_id=1, source_target_pairs={{0,8},{8,16},{16,24},{24,0},{1,9},{9,17},{17,25},{25,1},{2,10},{10... | collective-permute-start | bytes 49160 | tf_op jit(solution)/shard_map/ppermute | solution.py:150
  8.5 3.9 %collective-permute-start.1 = (bf16[16,512]{1,0:T(8,128)(2,1)}, bf16[16,512]{1,0:T(8,128)(2,1)S(1)}, u32[]{:S(2)}, u32[]{:S(2)}) collective-permute-start(bf16[16,512]{1,0:T(8,128)(2,1)} %get-tuple-element.11), channel_id=1, source_target_pairs={{0,16},{8,24},{16,0},{24,8},{1,17},{9,25},{17,1},{25,9},{2,18},{10... | collective-permute-start | bytes 49160 | tf_op jit(solution)/shard_map/ppermute | solution.py:150
  10.1 3.9 %collective-permute-start.2 = (bf16[16,512]{1,0:T(8,128)(2,1)}, bf16[16,512]{1,0:T(8,128)(2,1)S(1)}, u32[]{:S(2)}, u32[]{:S(2)}) collective-permute-start(bf16[16,512]{1,0:T(8,128)(2,1)} %get-tuple-element.12), channel_id=1, source_target_pairs={{0,24},{8,0},{16,8},{24,16},{1,25},{9,1},{17,9},{25,17},{2,26},{10... | collective-permute-start | bytes 49160 | tf_op jit(solution)/shard_map/ppermute | solution.py:150
  14.0 8.0 %collective-permute-start.5 = (bf16[16,2048]{1,0:T(8,128)(2,1)S(1)}, bf16[16,2048]{1,0:T(8,128)(2,1)S(1)}, u32[]{:S(2)}, u32[]{:S(2)}) collective-permute-start(bf16[16,2048]{1,0:T(8,128)(2,1)S(1)} %get-tuple-element.37), channel_id=1, source_target_pairs={{6,0},{7,1},{14,8},{15,9},{22,16},{23,17},{30,24},{31,25}} | collective-permute-start | bytes 196616 | tf_op jit(solution)/shard_map/ppermute | solution.py:118
  15.3 8.2 %collective-permute-start.4 = (bf16[16,2048]{1,0:T(8,128)(2,1)S(1)}, bf16[16,2048]{1,0:T(8,128)(2,1)S(1)}, u32[]{:S(2)}, u32[]{:S(2)}) collective-permute-start(bf16[16,2048]{1,0:T(8,128)(2,1)S(1)} %get-tuple-element.37), channel_id=1, source_target_pairs={{4,0},{5,1},{6,2},{7,3},{12,8},{13,9},{14,10},{15,11},{20,16},{21,... | collective-permute-start | bytes 196616 | tf_op jit(solution)/shard_map/ppermute | solution.py:118
  16.6 7.0 %collective-permute-start.3 = (bf16[16,2048]{1,0:T(8,128)(2,1)S(1)}, bf16[16,2048]{1,0:T(8,128)(2,1)S(1)}, u32[]{:S(2)}, u32[]{:S(2)}) collective-permute-start(bf16[16,2048]{1,0:T(8,128)(2,1)S(1)} %get-tuple-element.37), channel_id=1, source_target_pairs={{2,0},{3,1},{4,2},{5,3},{6,4},{7,5},{10,8},{11,9},{12,10},{13,11},... | collective-permute-start | bytes 196616 | tf_op jit(solution)/shard_map/ppermute | solution.py:118
  23.6 1.9 %collective-permute-start.6 = (bf16[64,2048]{1,0:T(8,128)(2,1)S(1)}, bf16[64,2048]{1,0:T(8,128)(2,1)S(1)}, u32[]{:S(2)}, u32[]{:S(2)}) collective-permute-start(bf16[64,2048]{1,0:T(8,128)(2,1)S(1)} %maximum_select_fusion), channel_id=1, source_target_pairs={{0,1},{1,0},{2,3},{3,2},{4,5},{5,4},{6,7},{7,6},{8,9},{9,8},{10,11... | collective-permute-start | bytes 786440 | tf_op jit(solution)/shard_map/ppermute | solution.py:125
  28.2 7.7 %collective-permute-start.9 = (f32[64,512]{1,0:T(8,128)S(1)}, f32[64,512]{1,0:T(8,128)S(1)}, u32[]{:S(2)}, u32[]{:S(2)}) collective-permute-start(f32[64,512]{1,0:T(8,128)S(1)} %get-tuple-element.18), channel_id=1, source_target_pairs={{8,0},{16,8},{9,1},{17,9},{10,2},{18,10},{11,3},{19,11},{12,4},{20... | collective-permute-start | bytes 393224 | tf_op jit(solution)/shard_map/ppermute | solution.py:176
  29.5 11.3 %collective-permute-start.8 = (f32[64,512]{1,0:T(8,128)S(1)}, f32[64,512]{1,0:T(8,128)S(1)}, u32[]{:S(2)}, u32[]{:S(2)}) collective-permute-start(f32[64,512]{1,0:T(8,128)S(1)} %get-tuple-element.19), channel_id=1, source_target_pairs={{16,0},{24,8},{17,1},{25,9},{18,2},{26,10},{19,3},{27,11},{20,4},{... | collective-permute-start | bytes 393224 | tf_op jit(solution)/shard_map/ppermute | solution.py:176
  30.8 10.0 %collective-permute-start.7 = (f32[64,512]{1,0:T(8,128)S(1)}, f32[64,512]{1,0:T(8,128)S(1)}, u32[]{:S(2)}, u32[]{:S(2)}) collective-permute-start(f32[64,512]{1,0:T(8,128)S(1)} %get-tuple-element.20), channel_id=1, source_target_pairs={{0,8},{24,0},{1,9},{25,1},{2,10},{26,2},{3,11},{27,3},{4,12},{28,4... | collective-permute-start | bytes 393224 | tf_op jit(solution)/shard_map/ppermute | solution.py:176

commit v23 on v22

--- a/solution.py
+++ b/solution.py
@@ -68,7 +68,7 @@
     per_vreg = LANES // width
     lane = lax.broadcasted_iota(jnp.int32, (channels, LANES), 1)
     for d in range(groups):
-        g = (place_ref[0] + d) % groups
+        g = place_ref[0] ^ d if groups & (groups - 1) == 0 else (place_ref[0] + d) % groups
         for v in range(lanes_out // LANES):
             gathered = jnp.zeros((channels, LANES), jnp.float32)
             for slot in range(per_vreg):
@@ -146,7 +146,10 @@
 
     gathered = [split[0]]
     for step in range(1, seg_count):
-        pairs = [(i, (i + step) % seg_count) for i in range(seg_count)]
+        if seg_count & (seg_count - 1) == 0:
+            pairs = [(i, i ^ step) for i in range(seg_count)]
+        else:
+            pairs = [(i, (i + step) % seg_count) for i in range(seg_count)]
         gathered.append(lax.ppermute(split[step], "seg", pairs))
     mine = jnp.concatenate(gathered, axis=1)
 

time: 43.3 us -> 43.7 us (level)
  waiting for transfers between devices: 12.8 us -> 14.7 us
  starting transfers between devices: 17 us -> 15.6 us
    ppermute x3, waiting for transfers between devices: 1.79 us -> 4.1 us  [shards(): gathered.append(lax.ppermute(split[step], 'seg', pairs))]
    ppermute x3, starting transfers between devices: 5.94 us -> 4.55 us  [shards(): gathered.append(lax.ppermute(split[step], 'seg', pairs))]
    ppermute x3, waiting for transfers between devices: 5.42 us -> 4.96 us  [shards(): collected.append(lax.ppermute(sent, 'seg', pairs))]
  transfers between devices with their start and end apart: 10 -> 10, of which waited for: 6 -> 7; matrix products, arithmetic and copies ran while one was open for 6% -> 6% of each run, Pallas kernels for 0% -> 0%
where the time goes in v23:
time: 43.7 us; the launch traced here: 43.4 us
  starting transfers between devices  15.6 us (36%)
  waiting for transfers between devices  14.7 us (34%)
  local copies, waits for them, and re-layouts  5.83 us (13%)
  Pallas kernels  5.53 us (13%)
  matrix products  0.72 us (2%)
  other arithmetic  0.54 us (1%)
  between operations  0.45 us (1%)
    ppermute x3, starting transfers between devices, shards(): collected.append(lax.ppermute(sent, 'seg', pairs))  7.13 us
    ppermute x3, waiting for transfers between devices, halo(): own.append(lax.ppermute(mine, 'fibre', pairs))  5.64 us
    pallas_call x1, Pallas kernels, whiten(): pl.pallas_call(whiten_kernel, out_shape=[jax.ShapeDtypeStruct((channels,...  5.53 us
    ppermute x3, waiting for transfers between devices, shards(): collected.append(lax.ppermute(sent, 'seg', pairs))  4.96 us
    ppermute x3, starting transfers between devices, shards(): gathered.append(lax.ppermute(split[step], 'seg', pairs))  4.55 us
    ppermute x3, waiting for transfers between devices, shards(): gathered.append(lax.ppermute(split[step], 'seg', pairs))  4.1 us
    ppermute x3, starting transfers between devices, halo(): own.append(lax.ppermute(mine, 'fibre', pairs))  3.86 us
    reshape x1, local copies, waits for them, and re-layouts, shards(): return jnp.stack(by_bins, axis=3).reshape(per_owner, block, 2 * NF)  1.14 us
  transfers between devices with their start and end apart: 10, of which 7 were waited for; matrix products, arithmetic and copies ran while one was open for 6% of the time, Pallas kernels for 0%

profile of v23, /device:TPU:0, one launch (start us, length us, event | category | flops | bytes accessed | tf_op | source)
XLA Modules:
  0.0 43.4 jit_solution(4469814992304612671)
XLA Ops:
  0.0 5.5 %shard_map.73 = (bf16[16,512]{1,0:T(8,128)(2,1)}, bf16[16,512]{1,0:T(8,128)(2,1)}, bf16[16,512]{1,0:T(8,128)(2,1)}, bf16[16,512]{1,0:T(8,128)(2,1)}) custom-call(s32[16]{0:T(128)} %bitcast.105, s32[1]{0:T(128)} %bitcast.1.place_ref, s32[16]{0:T(128)} %live_ref.1, bf16[16,27648]{1,0:T(8,128)(2,1)} %bitcast.85, bf16[3072,128]{1,0:T(8,128)(2,1)} %constant.87.clone.table_ref, ...), custom_call_target="tpu_custom_call" | custom-call | tf_op jit(solution)/shard_map/pallas_call | solution.py:94
  5.5 3.0 %collective-permute-start = (bf16[16,512]{1,0:T(8,128)(2,1)}, bf16[16,512]{1,0:T(8,128)(2,1)S(1)}, u32[]{:S(2)}, u32[]{:S(2)}) collective-permute-start(bf16[16,512]{1,0:T(8,128)(2,1)} %get-tuple-element.10), channel_id=1, source_target_pairs={{0,8},{8,0},{16,24},{24,16},{1,9},{9,1},{17,25},{25,17},{2,10},{10... | collective-permute-start | bytes 49160 | tf_op jit(solution)/shard_map/ppermute | solution.py:153
  8.6 1.5 %collective-permute-start.1 = (bf16[16,512]{1,0:T(8,128)(2,1)}, bf16[16,512]{1,0:T(8,128)(2,1)S(1)}, u32[]{:S(2)}, u32[]{:S(2)}) collective-permute-start(bf16[16,512]{1,0:T(8,128)(2,1)} %get-tuple-element.11), channel_id=1, source_target_pairs={{0,16},{8,24},{16,0},{24,8},{1,17},{9,25},{17,1},{25,9},{2,18},{10... | collective-permute-start | bytes 49160 | tf_op jit(solution)/shard_map/ppermute | solution.py:153
  10.1 0.7 %constant_dynamic-update-slice_fusion.3 = (bf16[16,2048]{1,0:T(8,128)(2,1)S(1)}, bf16[144,2048]{1,0:T(8,128)(2,1)S(1)}) fusion(bf16[16,512]{1,0:T(8,128)(2,1)} %get-tuple-element.9), kind=kLoop, calls=%fused_computation.21 | loop fusion | bytes 49152
  10.8 1.7 %collective-permute-done.1 = bf16[16,512]{1,0:T(8,128)(2,1)S(1)} collective-permute-done((bf16[16,512]{1,0:T(8,128)(2,1)}, bf16[16,512]{1,0:T(8,128)(2,1)S(1)}, u32[]{:S(2)}, u32[]{:S(2)}) %collective-permute-start.1) | collective-permute-done | bytes 16416 | tf_op jit(solution)/shard_map/ppermute | solution.py:153
  12.5 2.4 %collective-permute-done.2 = bf16[16,512]{1,0:T(8,128)(2,1)S(1)} collective-permute-done((bf16[16,512]{1,0:T(8,128)(2,1)}, bf16[16,512]{1,0:T(8,128)(2,1)S(1)}, u32[]{:S(2)}, u32[]{:S(2)}) %collective-permute-start.2) | collective-permute-done | bytes 16416 | tf_op jit(solution)/shard_map/ppermute | solution.py:153
  14.9 1.3 %collective-permute-start.5 = (bf16[16,2048]{1,0:T(8,128)(2,1)S(1)}, bf16[16,2048]{1,0:T(8,128)(2,1)S(1)}, u32[]{:S(2)}, u32[]{:S(2)}) collective-permute-start(bf16[16,2048]{1,0:T(8,128)(2,1)S(1)} %get-tuple-element.37), channel_id=1, source_target_pairs={{6,0},{7,1},{14,8},{15,9},{22,16},{23,17},{30,24},{31,25}} | collective-permute-start | bytes 196616 | tf_op jit(solution)/shard_map/ppermute | solution.py:118
  16.2 1.3 %collective-permute-start.4 = (bf16[16,2048]{1,0:T(8,128)(2,1)S(1)}, bf16[16,2048]{1,0:T(8,128)(2,1)S(1)}, u32[]{:S(2)}, u32[]{:S(2)}) collective-permute-start(bf16[16,2048]{1,0:T(8,128)(2,1)S(1)} %get-tuple-element.37), channel_id=1, source_target_pairs={{4,0},{5,1},{6,2},{7,3},{12,8},{13,9},{14,10},{15,11},{20,16},{21,... | collective-permute-start | bytes 196616 | tf_op jit(solution)/shard_map/ppermute | solution.py:118
  17.5 1.3 %collective-permute-start.3 = (bf16[16,2048]{1,0:T(8,128)(2,1)S(1)}, bf16[16,2048]{1,0:T(8,128)(2,1)S(1)}, u32[]{:S(2)}, u32[]{:S(2)}) collective-permute-start(bf16[16,2048]{1,0:T(8,128)(2,1)S(1)} %get-tuple-element.37), channel_id=1, source_target_pairs={{2,0},{3,1},{4,2},{5,3},{6,4},{7,5},{10,8},{11,9},{12,10},{13,11},... | collective-permute-start | bytes 196616 | tf_op jit(solution)/shard_map/ppermute | solution.py:118
  18.8 4.1 %collective-permute-done.5 = bf16[16,2048]{1,0:T(8,128)(2,1)S(1)} collective-permute-done((bf16[16,2048]{1,0:T(8,128)(2,1)S(1)}, bf16[16,2048]{1,0:T(8,128)(2,1)S(1)}, u32[]{:S(2)}, u32[]{:S(2)}) %collective-permute-start.5) | collective-permute-done | bytes 65568 | tf_op jit(solution)/shard_map/ppermute | solution.py:118
  23.0 1.5 %collective-permute-done.4 = bf16[16,2048]{1,0:T(8,128)(2,1)S(1)} collective-permute-done((bf16[16,2048]{1,0:T(8,128)(2,1)S(1)}, bf16[16,2048]{1,0:T(8,128)(2,1)S(1)}, u32[]{:S(2)}, u32[]{:S(2)}) %collective-permute-start.4) | collective-permute-done | bytes 65568 | tf_op jit(solution)/shard_map/ppermute | solution.py:118
  24.7 0.4 slice.52
  25.1 0.4 stack.40
  25.5 0.4 %copy.72 = bf16[16,64,2,16]{1,0,2,3:T(8,128)(2,1)S(1)} copy(bf16[16,64,2,16]{3,2,1,0:T(2,128)(2,1)S(1)} %slice.52) | data formatting | bytes 131072 | tf_op jit(solution)/shard_map/slice | solution.py:162
  25.9 0.4 %copy.73 = bf16[1,16,64,2,16]{2,1,3,0,4:T(8,128)(2,1)S(1)} copy(bf16[1,16,64,2,16]{4,3,2,1,0:T(2,128)(2,1)S(1)} %stack.40) | data formatting | bytes 131072 | tf_op jit(solution)/shard_map/stack | solution.py:165
  26.4 0.1 multiply_bitcast_fusion.1
  26.6 0.5 %copy.74 = bf16[144,2048]{0,1:T(8,128)(2,1)S(1)} copy(bf16[144,2048]{1,0:T(8,128)(2,1)S(1)} %constant_dynamic-update-slice_fusion.4) | data formatting | bytes 1179648 | tf_op jit(solution)/shard_map/concatenate | solution.py:158
  27.1 0.7 %convolution_bitcast_fusion = f32[16,2,16,144]{3,2,1,0:T(8,128)S(1)} fusion(bf16[144,64,2,16,1]{0,3,2,1,4:T(8,128)(2,1)S(1)} %bitcast.81, bf16[1,16,64,2,16]{2,1,3,0,4:T(8,128)(2,1)S(1)} %multiply_bitcast_fusion.1, bf16[1,16,64,2,16]{2,1,3,0,4:T(8,128)(2,1)S(1)} %copy.73), kind=kOutput, calls=%fused_computation | convolution fusion | flops 18939904 | bytes 1015808 | tf_op jit(solution)/shard_map/ocspn,jspn->nocj/dot_general | solution.py:166
  27.8 0.6 %fusion.5 = (f32[16,2,1,128]{3,2,1,0:T(1,128)S(1)}, f32[16,2,1,128]{3,2,1,0:T(1,128)S(1)}, f32[16,2,1,128]{3,2,1,0:T(1,128)S(1)}, f32[16,2,1,128]{3,2,1,0:T(1,12...) fusion(f32[16,2,16,144]{3,2,1,0:T(8,128)S(1)} %convolution_bitc, ...), kind=kLoop, calls=%fused_computation.52 | loop fusion | bytes 524288 | tf_op jit(solution)/shard_map/slice | solution.py:167
  28.6 0.1 multiply_bitcast_fusion
  28.8 0.1 copy.114
  29.1 1.3 %collective-permute-start.9 = (f32[64,512]{1,0:T(8,128)S(1)}, f32[64,512]{1,0:T(8,128)S(1)}, u32[]{:S(2)}, u32[]{:S(2)}) collective-permute-start(f32[64,512]{1,0:T(8,128)S(1)} %get-tuple-element.18), channel_id=1, source_target_pairs={{8,0},{16,8},{9,1},{17,9},{10,2},{18,10},{11,3},{19,11},{12,4},{20... | collective-permute-start | bytes 393224 | tf_op jit(solution)/shard_map/ppermute | solution.py:179
  30.4 1.3 %collective-permute-start.8 = (f32[64,512]{1,0:T(8,128)S(1)}, f32[64,512]{1,0:T(8,128)S(1)}, u32[]{:S(2)}, u32[]{:S(2)}) collective-permute-start(f32[64,512]{1,0:T(8,128)S(1)} %get-tuple-element.19), channel_id=1, source_target_pairs={{16,0},{24,8},{17,1},{25,9},{18,2},{26,10},{19,3},{27,11},{20,4},{... | collective-permute-start | bytes 393224 | tf_op jit(solution)/shard_map/ppermute | solution.py:179
  31.7 4.6 %collective-permute-start.7 = (f32[64,512]{1,0:T(8,128)S(1)}, f32[64,512]{1,0:T(8,128)S(1)}, u32[]{:S(2)}, u32[]{:S(2)}) collective-permute-start(f32[64,512]{1,0:T(8,128)S(1)} %get-tuple-element.20), channel_id=1, source_target_pairs={{0,8},{24,0},{1,9},{25,1},{2,10},{26,2},{3,11},{27,3},{4,12},{28,4... | collective-permute-start | bytes 393224 | tf_op jit(solution)/shard_map/ppermute | solution.py:179
  36.3 0.6 %collective-permute-done.9 = f32[64,512]{1,0:T(8,128)S(1)} collective-permute-done((f32[64,512]{1,0:T(8,128)S(1)}, f32[64,512]{1,0:T(8,128)S(1)}, u32[]{:S(2)}, u32[]{:S(2)}) %collective-permute-start.9) | collective-permute-done | bytes 131104 | tf_op jit(solution)/shard_map/ppermute | solution.py:179
  36.8 1.3 %collective-permute-done.8 = f32[64,512]{1,0:T(8,128)S(1)} collective-permute-done((f32[64,512]{1,0:T(8,128)S(1)}, f32[64,512]{1,0:T(8,128)S(1)}, u32[]{:S(2)}, u32[]{:S(2)}) %collective-permute-start.8) | collective-permute-done | bytes 131104 | tf_op jit(solution)/shard_map/ppermute | solution.py:179
  38.1 3.1 %collective-permute-done.7 = f32[64,512]{1,0:T(8,128)S(1)} collective-permute-done((f32[64,512]{1,0:T(8,128)S(1)}, f32[64,512]{1,0:T(8,128)S(1)}, u32[]{:S(2)}, u32[]{:S(2)}) %collective-permute-start.7) | collective-permute-done | bytes 131104 | tf_op jit(solution)/shard_map/ppermute | solution.py:179
  41.3 0.1 pad_maximum_fusion
  41.4 0.6 %copy.93 = f32[8,64,512]{1,2,0:T(8,128)S(1)} copy(f32[8,64,512]{2,1,0:T(8,128)S(1)} %pad_maximum_fusion) | data formatting | bytes 2097152 | tf_op jit(solution)/shard_map/concatenate | solution.py:184
  42.0 0.1 dynamic-slice_bitcast_fusion.3
  42.1 0.1 pad_maximum_fusion.1
  42.2 1.1 %copy.94 = f32[64,16,128]{2,1,0:T(8,128)} copy(f32[64,16,128]{0,2,1:T(8,128)S(1)} %bitcast.82) | data formatting | bytes 1048576 | tf_op jit(solution)/shard_map/reshape | solution.py:188
  (41 shorter events, 0.5 us)
Async XLA Ops:
  5.5 20.8 %copy-start = (bf16[2]{0:T(256)(128)(2,1)S(1)}, bf16[2]{0:T(256)(128)(2,1)}, u32[]{:S(2)}) copy-start(bf16[2]{0:T(256)(128)(2,1)} %constant.90.clone) | copy-start | bytes 16
  5.5 5.3 %collective-permute-start = (bf16[16,512]{1,0:T(8,128)(2,1)}, bf16[16,512]{1,0:T(8,128)(2,1)S(1)}, u32[]{:S(2)}, u32[]{:S(2)}) collective-permute-start(bf16[16,512]{1,0:T(8,128)(2,1)} %get-tuple-element.10), channel_id=1, source_target_pairs={{0,8},{8,0},{16,24},{24,16},{1,9},{9,1},{17,25},{25,17},{2,10},{10... | collective-permute-start | bytes 49160 | tf_op jit(solution)/shard_map/ppermute | solution.py:153
  8.6 3.9 %collective-permute-start.1 = (bf16[16,512]{1,0:T(8,128)(2,1)}, bf16[16,512]{1,0:T(8,128)(2,1)S(1)}, u32[]{:S(2)}, u32[]{:S(2)}) collective-permute-start(bf16[16,512]{1,0:T(8,128)(2,1)} %get-tuple-element.11), channel_id=1, source_target_pairs={{0,16},{8,24},{16,0},{24,8},{1,17},{9,25},{17,1},{25,9},{2,18},{10... | collective-permute-start | bytes 49160 | tf_op jit(solution)/shard_map/ppermute | solution.py:153
  10.1 4.8 %collective-permute-start.2 = (bf16[16,512]{1,0:T(8,128)(2,1)}, bf16[16,512]{1,0:T(8,128)(2,1)S(1)}, u32[]{:S(2)}, u32[]{:S(2)}) collective-permute-start(bf16[16,512]{1,0:T(8,128)(2,1)} %get-tuple-element.12), channel_id=1, source_target_pairs={{0,24},{8,16},{16,8},{24,0},{1,25},{9,17},{17,9},{25,1},{2,26},{10... | collective-permute-start | bytes 49160 | tf_op jit(solution)/shard_map/ppermute | solution.py:153
  14.9 8.0 %collective-permute-start.5 = (bf16[16,2048]{1,0:T(8,128)(2,1)S(1)}, bf16[16,2048]{1,0:T(8,128)(2,1)S(1)}, u32[]{:S(2)}, u32[]{:S(2)}) collective-permute-start(bf16[16,2048]{1,0:T(8,128)(2,1)S(1)} %get-tuple-element.37), channel_id=1, source_target_pairs={{6,0},{7,1},{14,8},{15,9},{22,16},{23,17},{30,24},{31,25}} | collective-permute-start | bytes 196616 | tf_op jit(solution)/shard_map/ppermute | solution.py:118
  16.2 8.2 %collective-permute-start.4 = (bf16[16,2048]{1,0:T(8,128)(2,1)S(1)}, bf16[16,2048]{1,0:T(8,128)(2,1)S(1)}, u32[]{:S(2)}, u32[]{:S(2)}) collective-permute-start(bf16[16,2048]{1,0:T(8,128)(2,1)S(1)} %get-tuple-element.37), channel_id=1, source_target_pairs={{4,0},{5,1},{6,2},{7,3},{12,8},{13,9},{14,10},{15,11},{20,16},{21,... | collective-permute-start | bytes 196616 | tf_op jit(solution)/shard_map/ppermute | solution.py:118
  17.5 7.0 %collective-permute-start.3 = (bf16[16,2048]{1,0:T(8,128)(2,1)S(1)}, bf16[16,2048]{1,0:T(8,128)(2,1)S(1)}, u32[]{:S(2)}, u32[]{:S(2)}) collective-permute-start(bf16[16,2048]{1,0:T(8,128)(2,1)S(1)} %get-tuple-element.37), channel_id=1, source_target_pairs={{2,0},{3,1},{4,2},{5,3},{6,4},{7,5},{10,8},{11,9},{12,10},{13,11},... | collective-permute-start | bytes 196616 | tf_op jit(solution)/shard_map/ppermute | solution.py:118
  24.5 1.9 %collective-permute-start.6 = (bf16[64,2048]{1,0:T(8,128)(2,1)S(1)}, bf16[64,2048]{1,0:T(8,128)(2,1)S(1)}, u32[]{:S(2)}, u32[]{:S(2)}) collective-permute-start(bf16[64,2048]{1,0:T(8,128)(2,1)S(1)} %maximum_select_fusion), channel_id=1, source_target_pairs={{0,1},{1,0},{2,3},{3,2},{4,5},{5,4},{6,7},{7,6},{8,9},{9,8},{10,11... | collective-permute-start | bytes 786440 | tf_op jit(solution)/shard_map/ppermute | solution.py:125
  29.1 7.7 %collective-permute-start.9 = (f32[64,512]{1,0:T(8,128)S(1)}, f32[64,512]{1,0:T(8,128)S(1)}, u32[]{:S(2)}, u32[]{:S(2)}) collective-permute-start(f32[64,512]{1,0:T(8,128)S(1)} %get-tuple-element.18), channel_id=1, source_target_pairs={{8,0},{16,8},{9,1},{17,9},{10,2},{18,10},{11,3},{19,11},{12,4},{20... | collective-permute-start | bytes 393224 | tf_op jit(solution)/shard_map/ppermute | solution.py:179
  30.4 7.7 %collective-permute-start.8 = (f32[64,512]{1,0:T(8,128)S(1)}, f32[64,512]{1,0:T(8,128)S(1)}, u32[]{:S(2)}, u32[]{:S(2)}) collective-permute-start(f32[64,512]{1,0:T(8,128)S(1)} %get-tuple-element.19), channel_id=1, source_target_pairs={{16,0},{24,8},{17,1},{25,9},{18,2},{26,10},{19,3},{27,11},{20,4},{... | collective-permute-start | bytes 393224 | tf_op jit(solution)/shard_map/ppermute | solution.py:179
  31.7 9.5 %collective-permute-start.7 = (f32[64,512]{1,0:T(8,128)S(1)}, f32[64,512]{1,0:T(8,128)S(1)}, u32[]{:S(2)}, u32[]{:S(2)}) collective-permute-start(f32[64,512]{1,0:T(8,128)S(1)} %get-tuple-element.20), channel_id=1, source_target_pairs={{0,8},{24,0},{1,9},{25,1},{2,10},{26,2},{3,11},{27,3},{4,12},{28,4... | collective-permute-start | bytes 393224 | tf_op jit(solution)/shard_map/ppermute | solution.py:179
